TPU v7x, 32 devices: a whole 2x2x4 slice. The times are simulated.
32 devices in a mesh: mp: 2 (over y), tx: 4 (over z), ty: 4 (over x, core).
Axes of the slice: x: 2, y: 2, z: 4, core: 2. Of those that a mesh axis runs over, the one named last changes fastest.
Arguments:
- models: float32 [2, 16, 64, 512], P('mp', None, 'ty', 'tx'), may hold values from -6 to 6
- direction: float32 [2, 16, 64, 512], P('mp', None, 'ty', 'tx'), may hold values from -6 to 6
- coupling: float32 [2], replicated, may hold values from 0.1 to 0.4
- tv_weight: float32 [2], replicated, may hold values from 0.5 to 2
Outputs:
- gradient: float32 [2, 16, 64, 512], P('mp', None, 'ty', 'tx')
- hessian_vector: float32 [2, 16, 64, 512], P('mp', None, 'ty', 'tx')
All inputs are finite; a program needn't handle non-finite values.
Results may differ from a plain program's by a relative error of at most 0.0001.
Values sent between devices are 32-bit elements; how exact they have to be, the bound alone decides.
No kernel may reach another device: no remote copies, remote signals or barrier semaphores. Data moves between devices by JAX's collectives and lax.ppermute only.
A program may use at most 64 MiB of HBM per device.

v0:
```python
import jax
import jax.numpy as jnp
from jax import lax
from jax.sharding import PartitionSpec as P

EPS_SQ = 0.25
SYM_PAIRS = ((0, 0), (1, 1), (2, 2), (0, 1), (0, 2), (1, 2))


def passed_along(array, axis, by):
    size = lax.axis_size(axis)
    pairs = [(i, i + by) for i in range(size) if 0 <= i + by < size]
    return lax.ppermute(array, axis, pairs)


def edge_masks(width_y, width_x):
    end_x = lax.axis_index("tx") == lax.axis_size("tx") - 1
    end_y = lax.axis_index("ty") == lax.axis_size("ty") - 1
    col_x = lax.broadcasted_iota(jnp.int32, (1, 1, width_x), 2)
    row_y = lax.broadcasted_iota(jnp.int32, (1, width_y, 1), 1)
    return ((col_x == width_x - 1) & end_x, (row_y == width_y - 1) & end_y)


def fields(tile, rim_x, rim_y):
    last_x, last_y = edge_masks(tile.shape[3], tile.shape[4])
    dx = jnp.concatenate([tile[..., 1:], rim_x], -1) - tile
    dx = jnp.where(last_x, 0.0, dx)
    dy = jnp.concatenate([tile[..., 1:, :], rim_y], -2) - tile
    dy = jnp.where(last_y, 0.0, dy)
    dz = jnp.concatenate(
        [tile[..., 1:, :, :] - tile[..., :-1, :, :], jnp.zeros_like(tile[..., :1, :, :])], -3
    )
    grads = jnp.stack([dx[:, 0], dy[:, 0], dz[:, 0]], 1)
    dirs = jnp.stack([dx[:, 1], dy[:, 1], dz[:, 1]], 1)
    return (grads, dirs)


def moments(grads, dirs, weights):
    wts = weights[:, None, None, None]
    rows = [jnp.sum(wts * grads[:, i] * grads[:, j], 0) for i, j in SYM_PAIRS]
    for i in range(3):
        for j in range(3):
            rows.append(jnp.sum(wts * dirs[:, i] * grads[:, j], 0))
    return jnp.stack(rows, 0)


def couple(moms, grad_own, dir_own):
    trace_m = moms[0] + moms[1] + moms[2]
    mat = [[moms[0], moms[3], moms[4]], [moms[3], moms[1], moms[5]], [moms[4], moms[5], moms[2]]]
    nat = [[moms[6 + 3 * i + j] for j in range(3)] for i in range(3)]
    trace_n = nat[0][0] + nat[1][1] + nat[2][2]
    g_parts = [grad_own[..., i, :, :, :] for i in range(3)]
    e_parts = [dir_own[..., i, :, :, :] for i in range(3)]
    cross_q = []
    cross_p = []
    for i in range(3):
        mg = mat[i][0] * g_parts[0] + mat[i][1] * g_parts[1] + mat[i][2] * g_parts[2]
        me = mat[i][0] * e_parts[0] + mat[i][1] * e_parts[1] + mat[i][2] * e_parts[2]
        ng = nat[i][0] * g_parts[0] + nat[i][1] * g_parts[1] + nat[i][2] * g_parts[2]
        cross_q.append(trace_m * g_parts[i] - mg)
        cross_p.append(trace_m * e_parts[i] - me + trace_n * g_parts[i] - ng)
    return (jnp.stack(cross_q, axis=-4), jnp.stack(cross_p, axis=-4))


def model_split(own, rim_x, rim_y, alpha, beta, own_weights):
    grads, dirs = fields(own, rim_x, rim_y)
    moms = lax.psum(moments(grads, dirs, own_weights), "mp")
    grad_own = grads[0]
    dir_own = dirs[0]
    cross_q, cross_p = couple(moms, grad_own, dir_own)
    size = jnp.sqrt(jnp.sum(grad_own * grad_own, 0) + EPS_SQ)[None]
    flux = jnp.stack(
        [beta * grad_own / size + alpha * cross_q, beta * dir_own / size + alpha * cross_p], 0
    )
    last_x, last_y = edge_masks(flux.shape[3], flux.shape[4])
    flux_x = jnp.where(last_x, 0.0, flux[:, 0])
    flux_y = jnp.where(last_y, 0.0, flux[:, 1])
    flux_z = flux[:, 2]
    flux_z = jnp.concatenate([flux_z[..., :-1, :, :], jnp.zeros_like(flux_z[..., :1, :, :])], -3)
    prev_x = passed_along(flux_x[..., -1:], "tx", 1)
    prev_y = passed_along(flux_y[..., -1:, :], "ty", 1)
    result = jnp.concatenate([prev_x, flux_x[..., :-1]], -1) - flux_x
    result = result + jnp.concatenate([prev_y, flux_y[..., :-1, :]], -2) - flux_y
    result = (
        result
        + jnp.concatenate([jnp.zeros_like(flux_z[..., :1, :, :]), flux_z[..., :-1, :, :]], -3)
        - flux_z
    )
    return (result[0][None], result[1][None])


def shards(models, direction, coupling, tv_weight):
    member = lax.axis_index("mp")
    own_weights = lax.dynamic_slice_in_dim(coupling, member, 1)
    alpha = own_weights[0]
    beta = lax.dynamic_slice_in_dim(tv_weight, member, 1)[0]
    own = jnp.stack([models, direction], 1)
    rim_x = passed_along(own[..., :1], "tx", -1)
    rim_y = passed_along(own[..., :1, :], "ty", -1)
    return model_split(own, rim_x, rim_y, alpha, beta, own_weights)


def solution(mesh):
    placed = (P("mp", None, "ty", "tx"), P("mp", None, "ty", "tx"), P(), P())
    return jax.shard_map(
        shards,
        mesh=mesh,
        in_specs=placed,
        out_specs=(P("mp", None, "ty", "tx"), P("mp", None, "ty", "tx")),
        check_vma=False,
    )
```

profile of v0, /device:TPU:1, one launch (start us, length us, event | category | flops | bytes accessed | tf_op | source)
XLA Modules:
  0.0 115.6 jit_solution(6490164148567552637)
XLA Ops:
  7.2 0.9 fusion.75
  8.2 1.9 %collective-permute-start.1 = (f32[1,2,16,1,128]{4,3,2,1,0:T(1,128)S(1)}, f32[1,2,16,1,128]{4,3,2,1,0:T(1,128)S(1)}, u32[]{:S(2)}, u32[]{:S(2)}) collective-permute-start(f32[1,2,16,1,128]{4,3,2,1,0:T(1,128)S(1)} %fusion.75), channel_id=1, source_target_pairs={{1,0},{2,1},{3,2},{5,4},{6,5},{7,6},{9,8},{10,9},{11,10},{13,12},{... | collective-permute-start | bytes 49160 | tf_op jit(solution)/shard_map/ppermute | solution.py:13
  10.1 1.0 fusion.6
  11.1 1.3 %collective-permute-start = (f32[1,2,16,16,1]{4,3,2,1,0:T(8,128)S(1)}, f32[1,2,16,16,1]{4,3,2,1,0:T(8,128)S(1)}, u32[]{:S(2)}, u32[]{:S(2)}) collective-permute-start(f32[1,2,16,16,1]{4,3,2,1,0:T(8,128)S(1)} %fusion.6), channel_id=1, source_target_pairs={{4,0},{8,4},{12,8},{5,1},{9,5},{13,9},{6,2},{10,6},{14,10},{7,3},{... | collective-permute-start | bytes 6152 | tf_op jit(solution)/shard_map/ppermute | solution.py:13
  12.4 1.0 fusion.7
  13.4 1.1 fusion.5
  14.5 1.1 fusion.22
  16.3 5.7 %collective-permute-done = f32[1,2,16,16,1]{4,3,2,1,0:T(8,128)S(1)} collective-permute-done((f32[1,2,16,16,1]{4,3,2,1,0:T(8,128)S(1)}, f32[1,2,16,16,1]{4,3,2,1,0:T(8,128)S(1)}, u32[]{:S(2)}, u32[]{:S(2)}) %collective-permute-start) | collective-permute-done | bytes 2080 | tf_op jit(solution)/shard_map/ppermute | solution.py:13
  22.1 0.7 fusion.24
  22.8 0.7 fusion.27
  23.4 0.7 fusion.29
  24.1 0.7 fusion.25
  24.8 0.7 fusion.26
  25.4 0.7 fusion.28
  26.1 0.7 fusion.72
  26.8 0.7 fusion.66
  27.5 0.7 fusion.54
  28.1 0.7 fusion.73
  28.8 0.7 fusion.67
  29.5 0.7 fusion.55
  30.1 0.7 fusion.74
  30.8 0.7 fusion.68
  31.5 0.7 fusion.56
  32.2 1.3 %copy-done.3 = f32[15,16,16,128]{3,2,1,0:T(8,128)} copy-done((f32[15,16,16,128]{3,2,1,0:T(8,128)}, f32[15,16,16,128]{3,2,1,0:T(8,128)S(1)}, u32[]{:S(2)}) %copy-start.3) | copy-done | bytes 1966104
  34.2 60.2 %all-reduce.4.cloned.1.call-done = f32[15,16,16,128]{3,2,1,0:T(8,128)} async-done(((f32[15,16,16,128]{3,2,1,0:T(8,128)}), f32[15,16,16,128]{3,2,1,0:T(8,128)}) %all-reduce.4.cloned.1.call-update) | async-done | bytes 1966096 | tf_op jit(solution)/shard_map/psum | solution.py:67
  94.4 1.6 %fusion.40 = (f32[1,1,16,16,128]{4,3,2,0,1:T(8,128)S(1)}, f32[1,16,16,128]{3,2,1,0:T(8,128)S(1)}, f32[1,16,16,128]{3,2,1,0:T(8,128)S(1)}) fusion(f32[15,16,16,128]{3,2,1,0:T(8,128)} %all-reduce.4.cloned.1.call-done, f32[1,2,16,16,128]{4,3,2,1,0:T(8,128)S(1)} %get-tuple-element.17, f32[1,2,16,16,128]{4,3,2,1,0:T(8,128)S(1)} %get-tuple-element.18, ...), kind=kLoop, calls=%fused_computation.79 | loop fusion | flops 622592 | bytes 2473984 | tf_op jit(solution)/shard_map/stack | solution.py:62
  96.8 1.4 %fusion.1 = f32[1,3,16,16,128]{4,3,2,0,1:T(8,128)S(1)} fusion(f32[1,1,16,16,128]{4,3,2,1,0:T(8,128)S(1)} %get-tuple-element.6, f32[1,1,16,16,128]{4,3,2,1,0:T(8,128)S(1)} %get-tuple-element.8, f32[1,1,16,16,128]{4,3,2,1,0:T(8,128)S(1)} %fusion.59, f32[1,1,16,16,128]{4,3,2,1,0:T(8,128)S(1)} %get-tuple-element.20, ...), kind=kLoop, calls=%fused_computation.20 | loop fusion | flops 786432 | bytes 1310728 | tf_op jit(solution)/shard_map/add | solution.py:73
  98.1 1.4 %fusion.4 = f32[1,3,16,16,128]{4,3,2,0,1:T(8,128)S(1)} fusion(f32[1,1,16,16,128]{4,3,2,1,0:T(8,128)S(1)} %get-tuple-element.19, f32[1,1,16,16,128]{4,3,2,1,0:T(8,128)S(1)} %get-tuple-element.22, f32[1,1,16,16,128]{4,3,2,1,0:T(8,128)S(1)} %get-tuple-element.13, f32[1,1,16,16,128]{4,3,2,0,1:T(8,128)S(1)} %get-tuple-element.7, ...), kind=kLoop, calls=%fused_computation.24 | loop fusion | flops 786432 | bytes 1310728 | tf_op jit(solution)/shard_map/add | solution.py:73
  99.7 3.1 %collective-permute-start.2 = (f32[2,16,16,1]{3,2,1,0:T(8,128)S(1)}, f32[2,16,16,1]{3,2,1,0:T(8,128)S(1)}, u32[]{:S(2)}, u32[]{:S(2)}) collective-permute-start(f32[2,16,16,1]{3,2,1,0:T(8,128)S(1)} %slice.200), channel_id=1, source_target_pairs={{0,4},{4,8},{8,12},{1,5},{5,9},{9,13},{2,6},{6,10},{10,14},{3,7},{... | collective-permute-start | bytes 6152 | tf_op jit(solution)/shard_map/ppermute | solution.py:13
  102.9 4.1 %collective-permute-start.3 = (f32[2,16,1,128]{3,2,1,0:T(1,128)S(1)}, f32[2,16,1,128]{3,2,1,0:T(1,128)S(1)}, u32[]{:S(2)}, u32[]{:S(2)}) collective-permute-start(f32[2,16,1,128]{3,2,1,0:T(1,128)S(1)} %slice.204), channel_id=1, source_target_pairs={{0,1},{1,2},{2,3},{4,5},{5,6},{6,7},{8,9},{9,10},{10,11},{12,13},{... | collective-permute-start | bytes 49160 | tf_op jit(solution)/shard_map/ppermute | solution.py:13
  107.1 0.6 collective-permute-done.2
  108.0 0.7 fusion.76
  (35 shorter events, 2.9 us)
Async XLA Ops:
  7.2 14.8 %copy-start.1 = (f32[1,16,16,128]{3,2,1,0:T(8,128)S(1)}, f32[1,16,16,128]{3,2,1,0:T(8,128)}, u32[]{:S(2)}) copy-start(f32[1,16,16,128]{3,2,1,0:T(8,128)} %param.4) | copy-start | bytes 393220
  7.2 14.8 %copy-start.2 = (f32[1,16,16,128]{3,2,1,0:T(8,128)S(1)}, f32[1,16,16,128]{3,2,1,0:T(8,128)}, u32[]{:S(2)}) copy-start(f32[1,16,16,128]{3,2,1,0:T(8,128)} %param.5) | copy-start | bytes 393220
  7.2 8.5 %copy-start.5 = (f32[2]{0:T(128)S(1)}, f32[2]{0:T(128)}, u32[]{:S(2)}) copy-start(f32[2]{0:T(128)} %param.6) | copy-start | bytes 28
  7.2 87.2 %all-reduce.4.cloned.1.call-start = ((), (), s32[]{:S(2)}) async-start(), calls=%async_computation | async-start | bytes 3932160 | tf_op jit(solution)/shard_map/psum | solution.py:67
  8.2 13.7 %collective-permute-start.1 = (f32[1,2,16,1,128]{4,3,2,1,0:T(1,128)S(1)}, f32[1,2,16,1,128]{4,3,2,1,0:T(1,128)S(1)}, u32[]{:S(2)}, u32[]{:S(2)}) collective-permute-start(f32[1,2,16,1,128]{4,3,2,1,0:T(1,128)S(1)} %fusion.75), channel_id=1, source_target_pairs={{1,0},{2,1},{3,2},{5,4},{6,5},{7,6},{9,8},{10,9},{11,10},{13,12},{... | collective-permute-start | bytes 49160 | tf_op jit(solution)/shard_map/ppermute | solution.py:13
  11.1 10.8 %collective-permute-start = (f32[1,2,16,16,1]{4,3,2,1,0:T(8,128)S(1)}, f32[1,2,16,16,1]{4,3,2,1,0:T(8,128)S(1)}, u32[]{:S(2)}, u32[]{:S(2)}) collective-permute-start(f32[1,2,16,16,1]{4,3,2,1,0:T(8,128)S(1)} %fusion.6), channel_id=1, source_target_pairs={{4,0},{8,4},{12,8},{5,1},{9,5},{13,9},{6,2},{10,6},{14,10},{7,3},{... | collective-permute-start | bytes 6152 | tf_op jit(solution)/shard_map/ppermute | solution.py:13
  29.5 4.0 %copy-start.6 = (f32[2]{0:T(128)S(1)}, f32[2]{0:T(128)}, u32[]{:S(2)}) copy-start(f32[2]{0:T(128)} %param.7) | copy-start | bytes 28
  32.2 1.3 %copy-start.3 = (f32[15,16,16,128]{3,2,1,0:T(8,128)}, f32[15,16,16,128]{3,2,1,0:T(8,128)S(1)}, u32[]{:S(2)}) copy-start(f32[15,16,16,128]{3,2,1,0:T(8,128)S(1)} %fusion.56) | copy-start | bytes 5898244
  94.4 2.0 %copy-start = (f32[15,16,16,128]{3,2,1,0:T(8,128)S(1)}, f32[15,16,16,128]{3,2,1,0:T(8,128)}, u32[]{:S(2)}) copy-start(f32[15,16,16,128]{3,2,1,0:T(8,128)} %all-reduce.4.cloned.1.call-done) | copy-start | bytes 5898244
  99.5 8.4 %copy-start.4 = (pred[16]{0:T(512)(128)(4,1)S(1)}, pred[16]{0:T(512)(128)(4,1)}, u32[]{:S(2)}) copy-start(pred[16]{0:T(512)(128)(4,1)} %constant.30.clone.1) | copy-start | bytes 52
  99.7 7.9 %collective-permute-start.2 = (f32[2,16,16,1]{3,2,1,0:T(8,128)S(1)}, f32[2,16,16,1]{3,2,1,0:T(8,128)S(1)}, u32[]{:S(2)}, u32[]{:S(2)}) collective-permute-start(f32[2,16,16,1]{3,2,1,0:T(8,128)S(1)} %slice.200), channel_id=1, source_target_pairs={{0,4},{4,8},{8,12},{1,5},{5,9},{9,13},{2,6},{6,10},{10,14},{3,7},{... | collective-permute-start | bytes 6152 | tf_op jit(solution)/shard_map/ppermute | solution.py:13
  102.9 5.0 %collective-permute-start.3 = (f32[2,16,1,128]{3,2,1,0:T(1,128)S(1)}, f32[2,16,1,128]{3,2,1,0:T(1,128)S(1)}, u32[]{:S(2)}, u32[]{:S(2)}) collective-permute-start(f32[2,16,1,128]{3,2,1,0:T(1,128)S(1)} %slice.204), channel_id=1, source_target_pairs={{0,1},{1,2},{2,3},{4,5},{5,6},{6,7},{8,9},{9,10},{10,11},{12,13},{... | collective-permute-start | bytes 49160 | tf_op jit(solution)/shard_map/ppermute | solution.py:13
Sparse Core Ops, SparseCore 0:
  33.6 60.7 all-reduce.3
where the time goes:
time: 118 us; the launch traced here: 116 us
  waiting for transfers between devices  66.6 us (56%)
  other arithmetic  20.3 us (17%)
  between operations  14.4 us (12%)
  starting transfers between devices  10.5 us (9%)
  local copies, waits for them, and re-layouts  3.79 us (3%)
    psum x1, waiting for transfers between devices, model_split(): moms = lax.psum(moments(grads, dirs, own_weights), 'mp')  60.2 us
    ppermute x4, starting transfers between devices, passed_along(): return lax.ppermute(array, axis, pairs)  10.4 us
    unnamed x14, other arithmetic  9.27 us
    ppermute x4, waiting for transfers between devices, passed_along(): return lax.ppermute(array, axis, pairs)  6.45 us
    another operation x4, other arithmetic, shards(): own = jnp.stack([models, direction], 1)  4.02 us
  transfers between devices with their start and end apart: 5, of which 4 were waited for; matrix products, arithmetic and copies ran while one was open for 5% of the time, Pallas kernels for 0%

commit v1 on v0

--- a/solution.py
+++ b/solution.py
@@ -62,9 +62,9 @@
     return (jnp.stack(cross_q, axis=-4), jnp.stack(cross_p, axis=-4))
 
 
-def model_split(own, rim_x, rim_y, alpha, beta, own_weights):
-    grads, dirs = fields(own, rim_x, rim_y)
-    moms = lax.psum(moments(grads, dirs, own_weights), "mp")
+def model_split(every, rim_x, rim_y, alpha, beta, weights):
+    grads, dirs = fields(every, rim_x, rim_y)
+    moms = moments(grads, dirs, weights)
     grad_own = grads[0]
     dir_own = dirs[0]
     cross_q, cross_p = couple(moms, grad_own, dir_own)
@@ -89,15 +89,41 @@
     return (result[0][None], result[1][None])
 
 
+def rim_from(array, axis, shift):
+    if shift == 0:
+        return passed_along(array, axis, -1)
+    mp = lax.axis_size("mp")
+    size = lax.axis_size(axis)
+    pairs = [
+        (m * size + t, ((m + shift) % mp) * size + t - 1)
+        for m in range(mp)
+        for t in range(1, size)
+    ]
+    return lax.ppermute(array, ("mp", axis), pairs)
+
+
 def shards(models, direction, coupling, tv_weight):
+    mp = lax.axis_size("mp")
     member = lax.axis_index("mp")
-    own_weights = lax.dynamic_slice_in_dim(coupling, member, 1)
+    local = models.shape[0]
+    own_weights = lax.dynamic_slice_in_dim(coupling, member * local, local)
     alpha = own_weights[0]
-    beta = lax.dynamic_slice_in_dim(tv_weight, member, 1)[0]
+    beta = lax.dynamic_slice_in_dim(tv_weight, member * local, local)[0]
     own = jnp.stack([models, direction], 1)
-    rim_x = passed_along(own[..., :1], "tx", -1)
-    rim_y = passed_along(own[..., :1, :], "ty", -1)
-    return model_split(own, rim_x, rim_y, alpha, beta, own_weights)
+    tiles, rims_x, rims_y, weights = [], [], [], []
+    for shift in range(mp):
+        if shift == 0:
+            tiles.append(own)
+        else:
+            tiles.append(lax.ppermute(own, "mp", [(m, (m + shift) % mp) for m in range(mp)]))
+        rims_x.append(rim_from(own[..., :1], "tx", shift))
+        rims_y.append(rim_from(own[..., :1, :], "ty", shift))
+        source = (member - shift) % mp
+        weights.append(lax.dynamic_slice_in_dim(coupling, source * local, local))
+    every = jnp.concatenate(tiles, 0)
+    rim_x = jnp.concatenate(rims_x, 0)
+    rim_y = jnp.concatenate(rims_y, 0)
+    return model_split(every, rim_x, rim_y, alpha, beta, jnp.concatenate(weights, 0))
 
 
 def solution(mesh):

time: 118 us -> 43.6 us (0.37); the launches traced: 116 us -> 42.9 us
  waiting for transfers between devices: 66.6 us -> 13 us
  other arithmetic: 20.3 us -> 6.05 us
  between operations: 14.4 us -> 0.98 us
  starting transfers between devices: 10.5 us -> 18.3 us
    psum x1 -> x0, waiting for transfers between devices: 60.2 us -> none  [model_split(): moms = lax.psum(moments(grads, dirs, own_weights), 'mp')]
    unnamed x14 -> x0, other arithmetic: 9.27 us -> none
    ppermute x0 -> x3, waiting for transfers between devices: none -> 8.05 us  [the longest x1 8.04 us: shards(): lax.ppermute(own, 'mp', [(m, (m + shift) % mp) for m in range(mp)])]
    ppermute x0 -> x3, starting transfers between devices: none -> 5.99 us  [the longest x2 5.18 us: rim_from(): return lax.ppermute(array, ('mp', axis), pairs)]
    another operation x4 -> x3, other arithmetic: 4.02 us -> 1.06 us  [shards(): own = jnp.stack([models, direction], 1)]
    another operation x5 -> x1, other arithmetic: 2.63 us -> 0.05 us  [model_split(): jnp.stack([beta * grad_own / size + alpha * cross_q, beta * dir_own / siz...]
    ppermute x4, starting transfers between devices: 10.4 us -> 12.3 us  [passed_along(): return lax.ppermute(array, axis, pairs)]
    ppermute x4, waiting for transfers between devices: 6.45 us -> 4.97 us  [passed_along(): return lax.ppermute(array, axis, pairs)]
  transfers between devices with their start and end apart: 5 -> 7, of which waited for: 4 -> 2; matrix products, arithmetic and copies ran while one was open for 5% -> 8% of each run, Pallas kernels for 0% -> 0%
where the time goes in v1:
time: 43.6 us; the launch traced here: 42.9 us
  starting transfers between devices  18.3 us (42%)
  waiting for transfers between devices  13 us (30%)
  other arithmetic  6.05 us (14%)
  local copies, waits for them, and re-layouts  4.53 us (10%)
  between operations  0.98 us (2%)
    ppermute x4, starting transfers between devices, passed_along(): return lax.ppermute(array, axis, pairs)  12.3 us
    ppermute x1, waiting for transfers between devices, shards(): lax.ppermute(own, 'mp', [(m, (m + shift) % mp) for m in range(mp)])  8.04 us
    ppermute x2, starting transfers between devices, rim_from(): return lax.ppermute(array, ('mp', axis), pairs)  5.18 us
    ppermute x4, waiting for transfers between devices, passed_along(): return lax.ppermute(array, axis, pairs)  4.97 us
    unnamed x15, local copies, waits for them, and re-layouts  2.79 us
    add x1, other arithmetic, model_split(): beta * dir_own / size + alpha * cross_p  1.46 us
    concatenate x1, other arithmetic, shards(): jnp.concatenate(weights, 0)  1.42 us
    another operation x3, other arithmetic, shards(): own = jnp.stack([models, direction], 1)  1.06 us
  transfers between devices with their start and end apart: 7, of which 2 were waited for; matrix products, arithmetic and copies ran while one was open for 8% of the time, Pallas kernels for 0%

profile of v1, /device:TPU:1, one launch (start us, length us, event | category | flops | bytes accessed | tf_op | source)
XLA Modules:
  0.0 42.9 jit_solution(5391576782539678386)
XLA Ops:
  0.6 1.0 %fusion.9 = f32[1,2,16,16,1]{4,3,2,1,0:T(8,128)S(1)} fusion(f32[1,1,16,16,128]{4,3,2,1,0:T(8,128)} %bitcast.290, f32[1,1,16,16,128]{4,3,2,1,0:T(8,128)} %bitcast.285), kind=kLoop, calls=%fused_computation.39 | loop fusion | flops 512 | bytes 264192 | tf_op jit(solution)/shard_map/stack | solution.py:112
  1.7 1.3 %collective-permute-start.1 = (f32[1,2,16,16,1]{4,3,2,1,0:T(8,128)S(1)}, f32[1,2,16,16,1]{4,3,2,1,0:T(8,128)S(1)}, u32[]{:S(2)}, u32[]{:S(2)}) collective-permute-start(f32[1,2,16,16,1]{4,3,2,1,0:T(8,128)S(1)} %fusion.9), channel_id=1, source_target_pairs={{4,0},{8,4},{12,8},{5,1},{9,5},{13,9},{6,2},{10,6},{14,10},{7,3},{... | collective-permute-start | bytes 6152 | tf_op jit(solution)/shard_map/ppermute | solution.py:13
  3.0 1.3 %collective-permute-start.2 = (f32[1,2,16,16,1]{4,3,2,1,0:T(8,128)S(1)}, f32[1,2,16,16,1]{4,3,2,1,0:T(8,128)S(1)}, u32[]{:S(2)}, u32[]{:S(2)}) collective-permute-start(f32[1,2,16,16,1]{4,3,2,1,0:T(8,128)S(1)} %fusion.9), channel_id=1, source_target_pairs={{4,16},{8,20},{12,24},{20,0},{24,4},{28,8},{5,17},{9,21},{13,25},{... | collective-permute-start | bytes 6152 | tf_op jit(solution)/shard_map/ppermute | solution.py:102
  4.3 1.9 %collective-permute-start.3 = (f32[1,2,16,1,128]{4,2,3,1,0:T(8,128)S(1)}, f32[1,2,16,1,128]{4,2,3,1,0:T(8,128)S(1)}, u32[]{:S(2)}, u32[]{:S(2)}) collective-permute-start(f32[1,2,16,1,128]{4,2,3,1,0:T(8,128)S(1)} %bitcast.297), channel_id=1, source_target_pairs={{1,0},{2,1},{3,2},{5,4},{6,5},{7,6},{9,8},{10,9},{11,10},{13,12},{... | collective-permute-start | bytes 49160 | tf_op jit(solution)/shard_map/ppermute | solution.py:13
  6.3 3.9 %collective-permute-start.4 = (f32[1,2,16,1,128]{4,2,3,1,0:T(8,128)S(1)}, f32[1,2,16,1,128]{4,2,3,1,0:T(8,128)S(1)}, u32[]{:S(2)}, u32[]{:S(2)}) collective-permute-start(f32[1,2,16,1,128]{4,2,3,1,0:T(8,128)S(1)} %bitcast.298), channel_id=1, source_target_pairs={{1,16},{2,17},{3,18},{17,0},{18,1},{19,2},{5,20},{6,21},{7,22},{21... | collective-permute-start | bytes 49160 | tf_op jit(solution)/shard_map/ppermute | solution.py:102
  10.2 0.8 %collective-permute-start = (f32[1,2,16,16,128]{4,3,2,1,0:T(8,128)S(1)}, f32[1,2,16,16,128]{4,3,2,1,0:T(8,128)S(1)}, u32[]{:S(2)}, u32[]{:S(2)}) collective-permute-start(f32[1,2,16,16,128]{4,3,2,1,0:T(8,128)S(1)} %pad_maximum_fusion.5), channel_id=1, source_target_pairs={{0,16},{16,0},{1,17},{17,1},{2,18},{18,2},{3,19},{19,3},{4,20},{20... | collective-permute-start | bytes 786440 | tf_op jit(solution)/shard_map/ppermute | solution.py:118
  11.1 0.6 %copy-done.3 = f32[2]{0:T(128)S(1)} copy-done((f32[2]{0:T(128)S(1)}, f32[2]{0:T(128)}, u32[]{:S(2)}) %copy-start.3) | copy-done | bytes 32
  11.7 0.7 %fusion.63 = (f32[1]{0:T(128)}, f32[1]{0:T(128)}, f32[1]{0:T(128)}) fusion(f32[2]{0:T(128)S(1)} %copy-done.3, s32[]{:T(128)S(6)} %select_n.37, s32[]{:T(128)S(6)} %select_n.43, s32[]{:T(128)S(6)} %select_n.41), kind=kLoop, calls=%fused_computation.150 | loop fusion | bytes 36 | tf_op jit(solution)/shard_map/dynamic_slice | solution.py:109
  12.4 1.4 %pad_maximum_fusion.8 = f32[2]{0:T(128)S(1)} fusion(f32[1]{0:T(128)} %get-tuple-element.52, f32[1]{0:T(128)} %get-tuple-element.53), kind=kLoop, calls=%fused_computation.147 | loop fusion | flops 2 | bytes 16 | tf_op jit(solution)/shard_map/concatenate | solution.py:126
  13.8 0.6 %dynamic_slice.12 = f32[1]{0:T(128)} dynamic-slice(f32[2]{0:T(128)S(1)} %copy-done.5, s32[]{:T(128)S(6)} %select_n.37), dynamic_slice_sizes={1} | dynamic-slice | bytes 12 | tf_op jit(solution)/shard_map/dynamic_slice | solution.py:111
  14.4 8.0 %collective-permute-done = f32[1,2,16,16,128]{4,3,2,1,0:T(8,128)S(1)} collective-permute-done((f32[1,2,16,16,128]{4,3,2,1,0:T(8,128)S(1)}, f32[1,2,16,16,128]{4,3,2,1,0:T(8,128)S(1)}, u32[]{:S(2)}, u32[]{:S(2)}) %collective-permute-start) | collective-permute-done | bytes 262176 | tf_op jit(solution)/shard_map/ppermute | solution.py:118
  22.5 0.2 slice.147
  22.8 0.2 fusion
  23.0 0.1 fusion.1
  23.3 0.5 %fusion.28 = (f32[16,16,128]{2,1,0:T(8,128)S(1)}, f32[16,16,128]{2,1,0:T(8,128)S(1)}, f32[16,16,128]{2,1,0:T(8,128)S(1)}, f32[16,16,128]{2,1,0:T(8,128)S(1)}, f3...) fusion(f32[2,2,16,16,128]{4,3,2,0,1:T(8,128)S(1)} %fusion.1, ...), kind=kLoop, calls=%fused_computation.75 | loop fusion | flops 1998848 | bytes 3506184 | tf_op jit(solution)/shard_map/reduce_sum | solution.py:43
  23.7 0.1 fusion.37
  23.9 0.1 fusion.52
  24.0 0.2 fusion.34
  24.2 0.2 fusion.32
  24.4 1.5 %fusion.4 = (f32[1,3,16,16,128]{4,3,2,1,0:T(8,128)S(1)}, f32[1,3,16,16,128]{4,3,2,1,0:T(8,128)S(1)}) fusion(f32[2,1,16,16,128]{4,3,2,1,0:T(8,128)S(1)} %get-tuple-element.45, f32[2,1,16,16,128]{4,3,2,1,0:T(8,128)S(1)} %get-tuple-element.43, f32[2,1,16,16,128]{4,3,2,1,0:T(8,128)S(1)} %get-tuple-element.41, f32[1,1,16,16,128]{4,3,2,1,0:T(8,128)S(1)} %get-tuple-element.31, ...), kind=kLoop, calls=%fused_computation.17 | loop fusion | flops 1572864 | bytes 3276808 | tf_op jit(solution)/shard_map/add | solution.py:73
  25.8 0.1 pad_maximum_fusion.6
  25.9 0.1 fusion.25
  26.0 5.2 %collective-permute-start.6 = (f32[2,16,1,128]{3,1,2,0:T(8,128)S(1)}, f32[2,16,1,128]{3,1,2,0:T(8,128)S(1)}, u32[]{:S(2)}, u32[]{:S(2)}) collective-permute-start(f32[2,16,1,128]{3,1,2,0:T(8,128)S(1)} %slice.169), channel_id=1, source_target_pairs={{0,1},{1,2},{2,3},{4,5},{5,6},{6,7},{8,9},{9,10},{10,11},{12,13},{... | collective-permute-start | bytes 49160 | tf_op jit(solution)/shard_map/ppermute | solution.py:13
  31.3 0.1 fusion.26
  31.4 0.1 slice.165
  31.5 3.8 %collective-permute-start.5 = (f32[2,16,16,1]{3,1,2,0:T(8,128)S(1)}, f32[2,16,16,1]{3,1,2,0:T(8,128)S(1)}, u32[]{:S(2)}, u32[]{:S(2)}) collective-permute-start(f32[2,16,16,1]{3,1,2,0:T(8,128)S(1)} %slice.165), channel_id=1, source_target_pairs={{0,4},{4,8},{8,12},{1,5},{5,9},{9,13},{2,6},{6,10},{10,14},{3,7},{... | collective-permute-start | bytes 6152 | tf_op jit(solution)/shard_map/ppermute | solution.py:13
  35.3 0.1 copy.117
  35.4 5.0 %collective-permute-done.5 = f32[2,16,16,1]{3,1,2,0:T(8,128)S(1)} collective-permute-done((f32[2,16,16,1]{3,1,2,0:T(8,128)S(1)}, f32[2,16,16,1]{3,1,2,0:T(8,128)S(1)}, u32[]{:S(2)}, u32[]{:S(2)}) %collective-permute-start.5) | collective-permute-done | bytes 2080 | tf_op jit(solution)/shard_map/ppermute | solution.py:13
  40.4 0.7 %copy-done.4 = pred[16]{0:T(512)(128)(4,1)S(1)} copy-done((pred[16]{0:T(512)(128)(4,1)S(1)}, pred[16]{0:T(512)(128)(4,1)}, u32[]{:S(2)}) %copy-start.4) | copy-done | bytes 40
  41.1 0.4 fusion.18
  41.5 0.7 %copy.71 = f32[1,16,16,128]{3,2,1,0:T(8,128)} copy(f32[1,16,16,128]{3,1,2,0:T(8,128)S(1)} %get-tuple-element.48) | data formatting | bytes 262144
  42.2 0.7 %copy.72 = f32[1,16,16,128]{3,2,1,0:T(8,128)} copy(f32[1,16,16,128]{3,1,2,0:T(8,128)S(1)} %get-tuple-element.47) | data formatting | bytes 262144
  (32 shorter events, 0.4 us)
Async XLA Ops:
  0.6 3.7 %copy-start = (f32[1,16,16,128]{3,2,1,0:T(8,128)S(1)}, f32[1,16,16,128]{3,2,1,0:T(8,128)}, u32[]{:S(2)}) copy-start(f32[1,16,16,128]{3,2,1,0:T(8,128)} %param.5) | copy-start | bytes 393220
  0.6 3.7 %copy-start.1 = (f32[1,16,16,128]{3,2,1,0:T(8,128)S(1)}, f32[1,16,16,128]{3,2,1,0:T(8,128)}, u32[]{:S(2)}) copy-start(f32[1,16,16,128]{3,2,1,0:T(8,128)} %param.4) | copy-start | bytes 393220
  1.7 21.1 %collective-permute-start.1 = (f32[1,2,16,16,1]{4,3,2,1,0:T(8,128)S(1)}, f32[1,2,16,16,1]{4,3,2,1,0:T(8,128)S(1)}, u32[]{:S(2)}, u32[]{:S(2)}) collective-permute-start(f32[1,2,16,16,1]{4,3,2,1,0:T(8,128)S(1)} %fusion.9), channel_id=1, source_target_pairs={{4,0},{8,4},{12,8},{5,1},{9,5},{13,9},{6,2},{10,6},{14,10},{7,3},{... | collective-permute-start | bytes 6152 | tf_op jit(solution)/shard_map/ppermute | solution.py:13
  3.0 19.8 %collective-permute-start.2 = (f32[1,2,16,16,1]{4,3,2,1,0:T(8,128)S(1)}, f32[1,2,16,16,1]{4,3,2,1,0:T(8,128)S(1)}, u32[]{:S(2)}, u32[]{:S(2)}) collective-permute-start(f32[1,2,16,16,1]{4,3,2,1,0:T(8,128)S(1)} %fusion.9), channel_id=1, source_target_pairs={{4,16},{8,20},{12,24},{20,0},{24,4},{28,8},{5,17},{9,21},{13,25},{... | collective-permute-start | bytes 6152 | tf_op jit(solution)/shard_map/ppermute | solution.py:102
  4.3 10.0 %collective-permute-start.3 = (f32[1,2,16,1,128]{4,2,3,1,0:T(8,128)S(1)}, f32[1,2,16,1,128]{4,2,3,1,0:T(8,128)S(1)}, u32[]{:S(2)}, u32[]{:S(2)}) collective-permute-start(f32[1,2,16,1,128]{4,2,3,1,0:T(8,128)S(1)} %bitcast.297), channel_id=1, source_target_pairs={{1,0},{2,1},{3,2},{5,4},{6,5},{7,6},{9,8},{10,9},{11,10},{13,12},{... | collective-permute-start | bytes 49160 | tf_op jit(solution)/shard_map/ppermute | solution.py:13
  6.3 8.1 %collective-permute-start.4 = (f32[1,2,16,1,128]{4,2,3,1,0:T(8,128)S(1)}, f32[1,2,16,1,128]{4,2,3,1,0:T(8,128)S(1)}, u32[]{:S(2)}, u32[]{:S(2)}) collective-permute-start(f32[1,2,16,1,128]{4,2,3,1,0:T(8,128)S(1)} %bitcast.298), channel_id=1, source_target_pairs={{1,16},{2,17},{3,18},{17,0},{18,1},{19,2},{5,20},{6,21},{7,22},{21... | collective-permute-start | bytes 49160 | tf_op jit(solution)/shard_map/ppermute | solution.py:102
  10.2 12.3 %collective-permute-start = (f32[1,2,16,16,128]{4,3,2,1,0:T(8,128)S(1)}, f32[1,2,16,16,128]{4,3,2,1,0:T(8,128)S(1)}, u32[]{:S(2)}, u32[]{:S(2)}) collective-permute-start(f32[1,2,16,16,128]{4,3,2,1,0:T(8,128)S(1)} %pad_maximum_fusion.5), channel_id=1, source_target_pairs={{0,16},{16,0},{1,17},{17,1},{2,18},{18,2},{3,19},{19,3},{4,20},{20... | collective-permute-start | bytes 786440 | tf_op jit(solution)/shard_map/ppermute | solution.py:118
  11.0 0.7 %copy-start.3 = (f32[2]{0:T(128)S(1)}, f32[2]{0:T(128)}, u32[]{:S(2)}) copy-start(f32[2]{0:T(128)} %param.6) | copy-start | bytes 28
  12.4 1.4 %copy-start.5 = (f32[2]{0:T(128)S(1)}, f32[2]{0:T(128)}, u32[]{:S(2)}) copy-start(f32[2]{0:T(128)} %param.7) | copy-start | bytes 28
  26.0 9.3 %copy-start.2 = (f32[2,16,16,128]{3,1,2,0:T(8,128)}, f32[2,16,16,128]{3,1,2,0:T(8,128)S(1)}, u32[]{:S(2)}) copy-start(f32[2,16,16,128]{3,1,2,0:T(8,128)S(1)} %fusion.25) | copy-start | bytes 786436
  26.0 14.4 %collective-permute-start.6 = (f32[2,16,1,128]{3,1,2,0:T(8,128)S(1)}, f32[2,16,1,128]{3,1,2,0:T(8,128)S(1)}, u32[]{:S(2)}, u32[]{:S(2)}) collective-permute-start(f32[2,16,1,128]{3,1,2,0:T(8,128)S(1)} %slice.169), channel_id=1, source_target_pairs={{0,1},{1,2},{2,3},{4,5},{5,6},{6,7},{8,9},{9,10},{10,11},{12,13},{... | collective-permute-start | bytes 49160 | tf_op jit(solution)/shard_map/ppermute | solution.py:13
  31.5 8.9 %collective-permute-start.5 = (f32[2,16,16,1]{3,1,2,0:T(8,128)S(1)}, f32[2,16,16,1]{3,1,2,0:T(8,128)S(1)}, u32[]{:S(2)}, u32[]{:S(2)}) collective-permute-start(f32[2,16,16,1]{3,1,2,0:T(8,128)S(1)} %slice.165), channel_id=1, source_target_pairs={{0,4},{4,8},{8,12},{1,5},{5,9},{9,13},{2,6},{6,10},{10,14},{3,7},{... | collective-permute-start | bytes 6152 | tf_op jit(solution)/shard_map/ppermute | solution.py:13
  35.3 5.1 %slice-start = ((f32[2,16,16,128]{3,1,2,0:T(8,128)}), f32[2,16,15,128]{3,1,2,0:T(8,128)S(1)}, s32[]{:S(2)}) async-start(f32[2,16,16,128]{3,1,2,0:T(8,128)} %copy-done.2), calls=%async_computation | async-start | bytes 491520 | tf_op jit(solution)/shard_map/slice | solution.py:83
  40.4 0.7 %copy-start.4 = (pred[16]{0:T(512)(128)(4,1)S(1)}, pred[16]{0:T(512)(128)(4,1)}, u32[]{:S(2)}) copy-start(pred[16]{0:T(512)(128)(4,1)} %constant.47.clone.1) | copy-start | bytes 52

commit v2 on v0

--- a/solution.py
+++ b/solution.py
@@ -62,9 +62,9 @@
     return (jnp.stack(cross_q, axis=-4), jnp.stack(cross_p, axis=-4))
 
 
-def model_split(own, rim_x, rim_y, alpha, beta, own_weights):
-    grads, dirs = fields(own, rim_x, rim_y)
-    moms = lax.psum(moments(grads, dirs, own_weights), "mp")
+def model_split(every, rim_x, rim_y, alpha, beta, weights):
+    grads, dirs = fields(every, rim_x, rim_y)
+    moms = moments(grads, dirs, weights)
     grad_own = grads[0]
     dir_own = dirs[0]
     cross_q, cross_p = couple(moms, grad_own, dir_own)
@@ -90,14 +90,22 @@
 
 
 def shards(models, direction, coupling, tv_weight):
+    mp = lax.axis_size("mp")
     member = lax.axis_index("mp")
-    own_weights = lax.dynamic_slice_in_dim(coupling, member, 1)
+    local = models.shape[0]
+    own_weights = lax.dynamic_slice_in_dim(coupling, member * local, local)
     alpha = own_weights[0]
-    beta = lax.dynamic_slice_in_dim(tv_weight, member, 1)[0]
+    beta = lax.dynamic_slice_in_dim(tv_weight, member * local, local)[0]
     own = jnp.stack([models, direction], 1)
-    rim_x = passed_along(own[..., :1], "tx", -1)
-    rim_y = passed_along(own[..., :1, :], "ty", -1)
-    return model_split(own, rim_x, rim_y, alpha, beta, own_weights)
+    tiles, weights = [own], [own_weights]
+    for shift in range(1, mp):
+        tiles.append(lax.ppermute(own, "mp", [(m, (m + shift) % mp) for m in range(mp)]))
+        source = (member - shift) % mp
+        weights.append(lax.dynamic_slice_in_dim(coupling, source * local, local))
+    every = jnp.concatenate(tiles, 0)
+    rim_x = passed_along(every[..., :1], "tx", -1)
+    rim_y = passed_along(every[..., :1, :], "ty", -1)
+    return model_split(every, rim_x, rim_y, alpha, beta, jnp.concatenate(weights, 0))
 
 
 def solution(mesh):

time: 118 us -> 38.5 us (0.33); the launches traced: 116 us -> 38.2 us
  waiting for transfers between devices: 66.6 us -> 12.9 us
  other arithmetic: 20.3 us -> 5.55 us
  between operations: 14.4 us -> 0.83 us
  starting transfers between devices: 10.5 us -> 15.1 us
    psum x1 -> x0, waiting for transfers between devices: 60.2 us -> none  [model_split(): moms = lax.psum(moments(grads, dirs, own_weights), 'mp')]
    unnamed x14 -> x0, other arithmetic: 9.27 us -> none
    ppermute x4, waiting for transfers between devices: 6.45 us -> 10.2 us  [passed_along(): return lax.ppermute(array, axis, pairs)]
    another operation x4 -> x1, other arithmetic: 4.02 us -> 1.03 us  [shards(): own = jnp.stack([models, direction], 1)]
    ppermute x0 -> x1, waiting for transfers between devices: none -> 2.72 us  [shards(): lax.ppermute(own, 'mp', [(m, (m + shift) % mp) for m in range(mp)])]
    another operation x5 -> x0, other arithmetic: 2.63 us -> none  [the longest x4 1.97 us: couple(): return (jnp.stack(cross_q, axis=-4), jnp.stack(cross_p, axis=-4))]
    ppermute x4, starting transfers between devices: 10.4 us -> 13 us  [passed_along(): return lax.ppermute(array, axis, pairs)]
    ppermute x0 -> x1, starting transfers between devices: none -> 2.12 us  [shards(): lax.ppermute(own, 'mp', [(m, (m + shift) % mp) for m in range(mp)])]
  transfers between devices with their start and end apart: 5 -> 5, of which waited for: 4 -> 3; matrix products, arithmetic and copies ran while one was open for 5% -> 8% of each run, Pallas kernels for 0% -> 0%
where the time goes in v2:
time: 38.5 us; the launch traced here: 38.2 us
  starting transfers between devices  15.1 us (39%)
  waiting for transfers between devices  12.9 us (34%)
  other arithmetic  5.55 us (14%)
  local copies, waits for them, and re-layouts  3.82 us (10%)
  between operations  0.83 us (2%)
    ppermute x4, starting transfers between devices, passed_along(): return lax.ppermute(array, axis, pairs)  13 us
    ppermute x4, waiting for transfers between devices, passed_along(): return lax.ppermute(array, axis, pairs)  10.2 us
    ppermute x1, waiting for transfers between devices, shards(): lax.ppermute(own, 'mp', [(m, (m + shift) % mp) for m in range(mp)])  2.72 us
    ppermute x1, starting transfers between devices, shards(): lax.ppermute(own, 'mp', [(m, (m + shift) % mp) for m in range(mp)])  2.12 us
    add x1, other arithmetic, model_split(): beta * dir_own / size + alpha * cross_p  1.5 us
    concatenate x1, other arithmetic, shards(): jnp.concatenate(weights, 0)  1.37 us
    unnamed x10, local copies, waits for them, and re-layouts  1.32 us
    another operation x1, other arithmetic, shards(): own = jnp.stack([models, direction], 1)  1.03 us
  transfers between devices with their start and end apart: 5, of which 3 were waited for; matrix products, arithmetic and copies ran while one was open for 8% of the time, Pallas kernels for 0%

profile of v2, /device:TPU:1, one launch (start us, length us, event | category | flops | bytes accessed | tf_op | source)
XLA Modules:
  0.0 38.2 jit_solution(2822407033836960108)
XLA Ops:
  0.6 0.0 copy-start
  0.6 0.0 copy-start.1
  0.6 1.0 %pad_maximum_fusion.6 = f32[1,2,16,16,128]{4,3,2,0,1:T(8,128)S(1)} fusion(f32[1,1,16,16,128]{4,3,2,0,1:T(8,128)} %bitcast.243, f32[1,1,16,16,128]{4,3,2,0,1:T(8,128)} %bitcast.246), kind=kLoop, calls=%fused_computation.45 | loop fusion | flops 65536 | bytes 524288 | tf_op jit(solution)/shard_map/stack | solution.py:99
  1.7 2.1 %collective-permute-start = (f32[1,2,16,16,128]{4,3,2,0,1:T(8,128)S(1)}, f32[1,2,16,16,128]{4,3,2,0,1:T(8,128)S(1)}, u32[]{:S(2)}, u32[]{:S(2)}) collective-permute-start(f32[1,2,16,16,128]{4,3,2,0,1:T(8,128)S(1)} %pad_maximum_fusion.6), channel_id=1, source_target_pairs={{0,16},{16,0},{1,17},{17,1},{2,18},{18,2},{3,19},{19,3},{4,20},{20... | collective-permute-start | bytes 786440 | tf_op jit(solution)/shard_map/ppermute | solution.py:102
  3.8 0.7 %copy-done.4 = f32[2]{0:T(128)S(1)} copy-done((f32[2]{0:T(128)S(1)}, f32[2]{0:T(128)}, u32[]{:S(2)}) %copy-start.4) | copy-done | bytes 32
  4.5 0.7 %dynamic_slice.9 = f32[1]{0:T(128)} dynamic-slice(f32[2]{0:T(128)S(1)} %copy-done.4, s32[]{:T(128)S(6)} %select_n.30), dynamic_slice_sizes={1} | dynamic-slice | bytes 12 | tf_op jit(solution)/shard_map/dynamic_slice | solution.py:98
  5.1 0.0 copy-done.2
  5.1 0.6 %fusion.65 = (f32[1]{0:T(128)}, f32[1]{0:T(128)}) fusion(f32[2]{0:T(128)S(1)} %copy-done.2, s32[]{:T(128)S(6)} %select_n.30, s32[]{:T(128)S(6)} %select_n.34), kind=kLoop, calls=%fused_computation.140 | loop fusion | bytes 24 | tf_op jit(solution)/shard_map/dynamic_slice | solution.py:96
  5.7 1.4 %pad_maximum_fusion.7 = f32[2]{0:T(128)S(1)} fusion(f32[1]{0:T(128)} %get-tuple-element.47, f32[1]{0:T(128)} %get-tuple-element.46), kind=kLoop, calls=%fused_computation.136 | loop fusion | flops 2 | bytes 16 | tf_op jit(solution)/shard_map/concatenate | solution.py:108
  7.1 2.7 %collective-permute-done = f32[1,2,16,16,128]{4,3,2,0,1:T(8,128)S(1)} collective-permute-done((f32[1,2,16,16,128]{4,3,2,0,1:T(8,128)S(1)}, f32[1,2,16,16,128]{4,3,2,0,1:T(8,128)S(1)}, u32[]{:S(2)}, u32[]{:S(2)}) %collective-permute-start) | collective-permute-done | bytes 262176 | tf_op jit(solution)/shard_map/ppermute | solution.py:102
  9.9 1.3 %collective-permute-start.1 = (f32[2,2,16,16,1]{4,3,2,0,1:T(8,128)S(1)}, f32[2,2,16,16,1]{4,3,2,0,1:T(8,128)S(1)}, u32[]{:S(2)}, u32[]{:S(2)}) collective-permute-start(f32[2,2,16,16,1]{4,3,2,0,1:T(8,128)S(1)} %bitcast.240), channel_id=1, source_target_pairs={{4,0},{8,4},{12,8},{5,1},{9,5},{13,9},{6,2},{10,6},{14,10},{7,3},{... | collective-permute-start | bytes 12296 | tf_op jit(solution)/shard_map/ppermute | solution.py:13
  11.2 3.2 %collective-permute-start.2 = (f32[2,2,16,1,128]{4,3,2,0,1:T(1,128)S(1)}, f32[2,2,16,1,128]{4,3,2,0,1:T(1,128)S(1)}, u32[]{:S(2)}, u32[]{:S(2)}) collective-permute-start(f32[2,2,16,1,128]{4,3,2,0,1:T(1,128)S(1)} %slice.149), channel_id=1, source_target_pairs={{1,0},{2,1},{3,2},{5,4},{6,5},{7,6},{9,8},{10,9},{11,10},{13,12},{... | collective-permute-start | bytes 98312 | tf_op jit(solution)/shard_map/ppermute | solution.py:13
  14.4 0.2 slice.145
  14.7 9.4 %collective-permute-done.1 = f32[2,2,16,16,1]{4,3,2,0,1:T(8,128)S(1)} collective-permute-done((f32[2,2,16,16,1]{4,3,2,0,1:T(8,128)S(1)}, f32[2,2,16,16,1]{4,3,2,0,1:T(8,128)S(1)}, u32[]{:S(2)}, u32[]{:S(2)}) %collective-permute-start.1) | collective-permute-done | bytes 4128 | tf_op jit(solution)/shard_map/ppermute | solution.py:13
  24.1 0.0 collective-permute-done.2
  24.1 0.3 fusion
  24.4 0.1 fusion.62
  24.4 0.5 %fusion.27 = (f32[16,16,128]{2,1,0:T(8,128)S(1)}, f32[16,16,128]{2,1,0:T(8,128)S(1)}, f32[16,16,128]{2,1,0:T(8,128)S(1)}, f32[16,16,128]{2,1,0:T(8,128)S(1)}, f3...) fusion(f32[2]{0:T(128)S(1)} %pad_maximum_fusion.7, ...), kind=kLoop, calls=%fused_computation.64 | loop fusion | flops 1998848 | bytes 3506184 | tf_op jit(solution)/shard_map/reduce_sum | solution.py:43
  25.0 0.1 fusion.39
  25.1 0.1 fusion.54
  25.2 0.1 fusion.34
  25.3 0.1 fusion.36
  25.5 1.5 %fusion.4 = (f32[1,3,16,16,128]{4,3,2,0,1:T(8,128)S(1)}, f32[1,3,16,16,128]{4,3,2,0,1:T(8,128)S(1)}) fusion(f32[2,1,16,16,128]{4,3,2,0,1:T(8,128)S(1)} %get-tuple-element.40, f32[2,1,16,16,128]{4,3,2,0,1:T(8,128)S(1)} %get-tuple-element.49, f32[2,1,16,16,128]{4,3,2,0,1:T(8,128)S(1)} %get-tuple-element.34, f32[1,1,16,16,128]{4,3,2,0,1:T(8,128)S(1)} %get-tuple-element.25, ...), kind=kLoop, calls=%fused_computation.17 | loop fusion | flops 1572864 | bytes 3276808 | tf_op jit(solution)/shard_map/add | solution.py:73
  27.0 0.1 fusion.17
  27.1 0.1 slice.161
  27.2 2.9 %collective-permute-start.3 = (f32[2,16,16,1]{3,2,1,0:T(8,128)S(1)}, f32[2,16,16,1]{3,2,1,0:T(8,128)S(1)}, u32[]{:S(2)}, u32[]{:S(2)}) collective-permute-start(f32[2,16,16,1]{3,2,1,0:T(8,128)S(1)} %slice.161), channel_id=1, source_target_pairs={{0,4},{4,8},{8,12},{1,5},{5,9},{9,13},{2,6},{6,10},{10,14},{3,7},{... | collective-permute-start | bytes 6152 | tf_op jit(solution)/shard_map/ppermute | solution.py:13
  30.1 5.7 %collective-permute-start.4 = (f32[2,16,1,128]{3,2,1,0:T(1,128)S(1)}, f32[2,16,1,128]{3,2,1,0:T(1,128)S(1)}, u32[]{:S(2)}, u32[]{:S(2)}) collective-permute-start(f32[2,16,1,128]{3,2,1,0:T(1,128)S(1)} %slice.165), channel_id=1, source_target_pairs={{0,1},{1,2},{2,3},{4,5},{5,6},{6,7},{8,9},{9,10},{10,11},{12,13},{... | collective-permute-start | bytes 49160 | tf_op jit(solution)/shard_map/ppermute | solution.py:13
  35.9 0.0 collective-permute-done.3
  35.9 0.8 %collective-permute-done.4 = f32[2,16,1,128]{3,2,1,0:T(1,128)S(1)} collective-permute-done((f32[2,16,1,128]{3,2,1,0:T(1,128)S(1)}, f32[2,16,1,128]{3,2,1,0:T(1,128)S(1)}, u32[]{:S(2)}, u32[]{:S(2)}) %collective-permute-start.4) | collective-permute-done | bytes 16416 | tf_op jit(solution)/shard_map/ppermute | solution.py:13
  36.7 0.7 %copy-done.3 = pred[16]{0:T(512)(128)(4,1)S(1)} copy-done((pred[16]{0:T(512)(128)(4,1)S(1)}, pred[16]{0:T(512)(128)(4,1)}, u32[]{:S(2)}) %copy-start.3) | copy-done | bytes 40
  37.3 0.2 fusion.22
  37.5 0.7 %fusion.64 = (f32[1,16,16,128]{3,2,1,0:T(8,128)}, f32[1,16,16,128]{3,2,1,0:T(8,128)}) fusion(f32[2,16,16,128]{3,2,1,0:T(8,128)S(1)} %fusion.22), kind=kLoop, calls=%fused_computation.139 | loop fusion | bytes 524288 | tf_op jit(solution)/shard_map/slice | solution.py:89
  (17 shorter events, 0.3 us)
Async XLA Ops:
  0.6 9.2 %copy-start = (f32[1,16,16,128]{3,2,1,0:T(8,128)S(1)}, f32[1,16,16,128]{3,2,1,0:T(8,128)}, u32[]{:S(2)}) copy-start(f32[1,16,16,128]{3,2,1,0:T(8,128)} %param.5) | copy-start | bytes 393220
  0.6 9.2 %copy-start.1 = (f32[1,16,16,128]{3,2,1,0:T(8,128)S(1)}, f32[1,16,16,128]{3,2,1,0:T(8,128)}, u32[]{:S(2)}) copy-start(f32[1,16,16,128]{3,2,1,0:T(8,128)} %param.4) | copy-start | bytes 393220
  1.7 8.1 %collective-permute-start = (f32[1,2,16,16,128]{4,3,2,0,1:T(8,128)S(1)}, f32[1,2,16,16,128]{4,3,2,0,1:T(8,128)S(1)}, u32[]{:S(2)}, u32[]{:S(2)}) collective-permute-start(f32[1,2,16,16,128]{4,3,2,0,1:T(8,128)S(1)} %pad_maximum_fusion.6), channel_id=1, source_target_pairs={{0,16},{16,0},{1,17},{17,1},{2,18},{18,2},{3,19},{19,3},{4,20},{20... | collective-permute-start | bytes 786440 | tf_op jit(solution)/shard_map/ppermute | solution.py:102
  3.8 0.7 %copy-start.4 = (f32[2]{0:T(128)S(1)}, f32[2]{0:T(128)}, u32[]{:S(2)}) copy-start(f32[2]{0:T(128)} %param.7) | copy-start | bytes 28
  4.5 0.7 %copy-start.2 = (f32[2]{0:T(128)S(1)}, f32[2]{0:T(128)}, u32[]{:S(2)}) copy-start(f32[2]{0:T(128)} %param.6) | copy-start | bytes 28
  9.9 14.1 %collective-permute-start.1 = (f32[2,2,16,16,1]{4,3,2,0,1:T(8,128)S(1)}, f32[2,2,16,16,1]{4,3,2,0,1:T(8,128)S(1)}, u32[]{:S(2)}, u32[]{:S(2)}) collective-permute-start(f32[2,2,16,16,1]{4,3,2,0,1:T(8,128)S(1)} %bitcast.240), channel_id=1, source_target_pairs={{4,0},{8,4},{12,8},{5,1},{9,5},{13,9},{6,2},{10,6},{14,10},{7,3},{... | collective-permute-start | bytes 12296 | tf_op jit(solution)/shard_map/ppermute | solution.py:13
  11.2 12.8 %collective-permute-start.2 = (f32[2,2,16,1,128]{4,3,2,0,1:T(1,128)S(1)}, f32[2,2,16,1,128]{4,3,2,0,1:T(1,128)S(1)}, u32[]{:S(2)}, u32[]{:S(2)}) collective-permute-start(f32[2,2,16,1,128]{4,3,2,0,1:T(1,128)S(1)} %slice.149), channel_id=1, source_target_pairs={{1,0},{2,1},{3,2},{5,4},{6,5},{7,6},{9,8},{10,9},{11,10},{13,12},{... | collective-permute-start | bytes 98312 | tf_op jit(solution)/shard_map/ppermute | solution.py:13
  27.2 8.6 %collective-permute-start.3 = (f32[2,16,16,1]{3,2,1,0:T(8,128)S(1)}, f32[2,16,16,1]{3,2,1,0:T(8,128)S(1)}, u32[]{:S(2)}, u32[]{:S(2)}) collective-permute-start(f32[2,16,16,1]{3,2,1,0:T(8,128)S(1)} %slice.161), channel_id=1, source_target_pairs={{0,4},{4,8},{8,12},{1,5},{5,9},{9,13},{2,6},{6,10},{10,14},{3,7},{... | collective-permute-start | bytes 6152 | tf_op jit(solution)/shard_map/ppermute | solution.py:13
  30.1 6.5 %collective-permute-start.4 = (f32[2,16,1,128]{3,2,1,0:T(1,128)S(1)}, f32[2,16,1,128]{3,2,1,0:T(1,128)S(1)}, u32[]{:S(2)}, u32[]{:S(2)}) collective-permute-start(f32[2,16,1,128]{3,2,1,0:T(1,128)S(1)} %slice.165), channel_id=1, source_target_pairs={{0,1},{1,2},{2,3},{4,5},{5,6},{6,7},{8,9},{9,10},{10,11},{12,13},{... | collective-permute-start | bytes 49160 | tf_op jit(solution)/shard_map/ppermute | solution.py:13
  36.7 0.7 %copy-start.3 = (pred[16]{0:T(512)(128)(4,1)S(1)}, pred[16]{0:T(512)(128)(4,1)}, u32[]{:S(2)}) copy-start(pred[16]{0:T(512)(128)(4,1)} %constant.43.clone.1) | copy-start | bytes 52

commit v3 on v2

--- a/solution.py
+++ b/solution.py
@@ -11,6 +11,12 @@
     size = lax.axis_size(axis)
     pairs = [(i, i + by) for i in range(size) if 0 <= i + by < size]
     return lax.ppermute(array, axis, pairs)
+
+
+def passed_dense(array, axis, by):
+    count = array.size
+    rows = array.reshape(count // 128, 128) if count % 128 == 0 else array.reshape(count)
+    return passed_along(rows, axis, by).reshape(array.shape)
 
 
 def edge_masks(width_y, width_x):
@@ -77,7 +83,7 @@
     flux_y = jnp.where(last_y, 0.0, flux[:, 1])
     flux_z = flux[:, 2]
     flux_z = jnp.concatenate([flux_z[..., :-1, :, :], jnp.zeros_like(flux_z[..., :1, :, :])], -3)
-    prev_x = passed_along(flux_x[..., -1:], "tx", 1)
+    prev_x = passed_dense(flux_x[..., -1:], "tx", 1)
     prev_y = passed_along(flux_y[..., -1:, :], "ty", 1)
     result = jnp.concatenate([prev_x, flux_x[..., :-1]], -1) - flux_x
     result = result + jnp.concatenate([prev_y, flux_y[..., :-1, :]], -2) - flux_y
@@ -103,7 +109,7 @@
         source = (member - shift) % mp
         weights.append(lax.dynamic_slice_in_dim(coupling, source * local, local))
     every = jnp.concatenate(tiles, 0)
-    rim_x = passed_along(every[..., :1], "tx", -1)
+    rim_x = passed_dense(every[..., :1], "tx", -1)
     rim_y = passed_along(every[..., :1, :], "ty", -1)
     return model_split(every, rim_x, rim_y, alpha, beta, jnp.concatenate(weights, 0))
 

time: 38.5 us -> 30.5 us (0.79)
  waiting for transfers between devices: 12.9 us -> 5.36 us
  starting transfers between devices: 15.1 us -> 13.2 us
  local copies, waits for them, and re-layouts: 3.82 us -> 5.28 us
    ppermute x4, waiting for transfers between devices: 10.2 us -> 2.64 us  [passed_along(): return lax.ppermute(array, axis, pairs)]
    ppermute x4, starting transfers between devices: 13 us -> 11.1 us  [passed_along(): return lax.ppermute(array, axis, pairs)]
    reshape x0 -> x5, local copies, waits for them, and re-layouts: none -> 0.89 us  [the longest x3 0.73 us: passed_dense(): return passed_along(rows, axis, by).reshape(array.shape)]
    slice x1 -> x2, local copies, waits for them, and re-layouts: 0.12 us -> 0.67 us  [the longest x1 0.43 us: shards(): rim_x = passed_dense(every[..., :1], 'tx', -1)]
  transfers between devices with their start and end apart: 5 -> 5, of which waited for: 3 -> 3; matrix products, arithmetic and copies ran while one was open for 8% -> 12% of each run, Pallas kernels for 0% -> 0%
where the time goes in v3:
time: 30.5 us; the launch traced here: 30.3 us
  starting transfers between devices  13.2 us (43%)
  other arithmetic  5.58 us (18%)
  waiting for transfers between devices  5.36 us (18%)
  local copies, waits for them, and re-layouts  5.28 us (17%)
  between operations  0.84 us (3%)
    ppermute x4, starting transfers between devices, passed_along(): return lax.ppermute(array, axis, pairs)  11.1 us
    ppermute x1, waiting for transfers between devices, shards(): lax.ppermute(own, 'mp', [(m, (m + shift) % mp) for m in range(mp)])  2.72 us
    ppermute x4, waiting for transfers between devices, passed_along(): return lax.ppermute(array, axis, pairs)  2.64 us
    ppermute x1, starting transfers between devices, shards(): lax.ppermute(own, 'mp', [(m, (m + shift) % mp) for m in range(mp)])  2.12 us
    add x1, other arithmetic, model_split(): beta * dir_own / size + alpha * cross_p  1.48 us
    concatenate x1, other arithmetic, shards(): jnp.concatenate(weights, 0)  1.37 us
    unnamed x10, local copies, waits for them, and re-layouts  1.32 us
    another operation x1, other arithmetic, shards(): own = jnp.stack([models, direction], 1)  1.03 us
  transfers between devices with their start and end apart: 5, of which 3 were waited for; matrix products, arithmetic and copies ran while one was open for 12% of the time, Pallas kernels for 0%

profile of v3, /device:TPU:1, one launch (start us, length us, event | category | flops | bytes accessed | tf_op | source)
XLA Modules:
  0.0 30.3 jit_solution(15874799241410436556)
XLA Ops:
  0.6 1.0 %pad_maximum_fusion.6 = f32[1,2,16,16,128]{4,3,2,0,1:T(8,128)S(1)} fusion(f32[1,1,16,16,128]{4,3,2,0,1:T(8,128)} %bitcast.247, f32[1,1,16,16,128]{4,3,2,0,1:T(8,128)} %bitcast.250), kind=kLoop, calls=%fused_computation.46 | loop fusion | flops 65536 | bytes 524288 | tf_op jit(solution)/shard_map/stack | solution.py:105
  1.7 2.1 %collective-permute-start = (f32[1,2,16,16,128]{4,3,2,0,1:T(8,128)S(1)}, f32[1,2,16,16,128]{4,3,2,0,1:T(8,128)S(1)}, u32[]{:S(2)}, u32[]{:S(2)}) collective-permute-start(f32[1,2,16,16,128]{4,3,2,0,1:T(8,128)S(1)} %pad_maximum_fusion.6), channel_id=1, source_target_pairs={{0,16},{16,0},{1,17},{17,1},{2,18},{18,2},{3,19},{19,3},{4,20},{20... | collective-permute-start | bytes 786440 | tf_op jit(solution)/shard_map/ppermute | solution.py:108
  3.8 0.7 %copy-done.4 = f32[2]{0:T(128)S(1)} copy-done((f32[2]{0:T(128)S(1)}, f32[2]{0:T(128)}, u32[]{:S(2)}) %copy-start.4) | copy-done | bytes 32
  4.5 0.7 %dynamic_slice.9 = f32[1]{0:T(128)} dynamic-slice(f32[2]{0:T(128)S(1)} %copy-done.4, s32[]{:T(128)S(6)} %select_n.30), dynamic_slice_sizes={1} | dynamic-slice | bytes 12 | tf_op jit(solution)/shard_map/dynamic_slice | solution.py:104
  5.1 0.6 %fusion.65 = (f32[1]{0:T(128)}, f32[1]{0:T(128)}) fusion(f32[2]{0:T(128)S(1)} %copy-done.2, s32[]{:T(128)S(6)} %select_n.30, s32[]{:T(128)S(6)} %select_n.34), kind=kLoop, calls=%fused_computation.141 | loop fusion | bytes 24 | tf_op jit(solution)/shard_map/dynamic_slice | solution.py:102
  5.7 1.4 %pad_maximum_fusion.7 = f32[2]{0:T(128)S(1)} fusion(f32[1]{0:T(128)} %get-tuple-element.47, f32[1]{0:T(128)} %get-tuple-element.46), kind=kLoop, calls=%fused_computation.137 | loop fusion | flops 2 | bytes 16 | tf_op jit(solution)/shard_map/concatenate | solution.py:114
  7.1 2.7 %collective-permute-done = f32[1,2,16,16,128]{4,3,2,0,1:T(8,128)S(1)} collective-permute-done((f32[1,2,16,16,128]{4,3,2,0,1:T(8,128)S(1)}, f32[1,2,16,16,128]{4,3,2,0,1:T(8,128)S(1)}, u32[]{:S(2)}, u32[]{:S(2)}) %collective-permute-start) | collective-permute-done | bytes 262176 | tf_op jit(solution)/shard_map/ppermute | solution.py:108
  9.9 0.4 %copy.6 = f32[2,2,16,16,1]{3,2,1,0,4:T(8,128)S(1)} copy(f32[2,2,16,16,1]{4,3,2,0,1:T(8,128)S(1)} %bitcast.244) | data formatting | bytes 8192 | tf_op jit(solution)/shard_map/slice | solution.py:112
  10.4 0.1 reshape.438
  10.4 1.3 %collective-permute-start.1 = (f32[8,128]{1,0:T(8,128)S(1)}, f32[8,128]{1,0:T(8,128)S(1)}, u32[]{:S(2)}, u32[]{:S(2)}) collective-permute-start(f32[8,128]{1,0:T(8,128)S(1)} %reshape.438), channel_id=1, source_target_pairs={{4,0},{8,4},{12,8},{5,1},{9,5},{13,9},{6,2},{10,6},{14,10},{7,3},{... | collective-permute-start | bytes 12296 | tf_op jit(solution)/shard_map/ppermute | solution.py:13
  11.8 3.2 %collective-permute-start.2 = (f32[2,2,16,1,128]{4,3,2,0,1:T(1,128)S(1)}, f32[2,2,16,1,128]{4,3,2,0,1:T(1,128)S(1)}, u32[]{:S(2)}, u32[]{:S(2)}) collective-permute-start(f32[2,2,16,1,128]{4,3,2,0,1:T(1,128)S(1)} %slice.149), channel_id=1, source_target_pairs={{1,0},{2,1},{3,2},{5,4},{6,5},{7,6},{9,8},{10,9},{11,10},{13,12},{... | collective-permute-start | bytes 98312 | tf_op jit(solution)/shard_map/ppermute | solution.py:13
  15.0 0.2 slice.145
  15.3 0.5 %copy.7 = f32[2,2,16,16,1]{4,3,2,0,1:T(8,128)S(1)} copy(f32[2,2,16,16,1]{3,2,1,0,4:T(8,128)S(1)} %reshape.439) | data formatting | bytes 8192 | tf_op jit(solution)/shard_map/reshape | solution.py:19
  15.8 2.1 %collective-permute-done.2 = f32[2,2,16,1,128]{4,3,2,0,1:T(1,128)S(1)} collective-permute-done((f32[2,2,16,1,128]{4,3,2,0,1:T(1,128)S(1)}, f32[2,2,16,1,128]{4,3,2,0,1:T(1,128)S(1)}, u32[]{:S(2)}, u32[]{:S(2)}) %collective-permute-start.2) | collective-permute-done | bytes 32800 | tf_op jit(solution)/shard_map/ppermute | solution.py:13
  17.8 0.2 fusion
  18.1 0.1 fusion.62
  18.2 0.5 %fusion.27 = (f32[16,16,128]{2,1,0:T(8,128)S(1)}, f32[16,16,128]{2,1,0:T(8,128)S(1)}, f32[16,16,128]{2,1,0:T(8,128)S(1)}, f32[16,16,128]{2,1,0:T(8,128)S(1)}, f3...) fusion(f32[2]{0:T(128)S(1)} %pad_maximum_fusion.7, ...), kind=kLoop, calls=%fused_computation.65 | loop fusion | flops 1998848 | bytes 3506184 | tf_op jit(solution)/shard_map/reduce_sum | solution.py:49
  18.7 0.2 fusion.39
  18.9 0.1 fusion.54
  19.0 0.1 fusion.34
  19.1 0.2 fusion.36
  19.3 1.5 %fusion.4 = (f32[1,3,16,16,128]{4,3,2,0,1:T(8,128)S(1)}, f32[1,3,16,16,128]{4,3,2,0,1:T(8,128)S(1)}) fusion(f32[2,1,16,16,128]{4,3,2,0,1:T(8,128)S(1)} %get-tuple-element.40, f32[2,1,16,16,128]{4,3,2,0,1:T(8,128)S(1)} %get-tuple-element.49, f32[2,1,16,16,128]{4,3,2,0,1:T(8,128)S(1)} %get-tuple-element.34, f32[1,1,16,16,128]{4,3,2,0,1:T(8,128)S(1)} %get-tuple-element.25, ...), kind=kLoop, calls=%fused_computation.17 | loop fusion | flops 1572864 | bytes 3276808 | tf_op jit(solution)/shard_map/add | solution.py:79
  20.8 0.1 fusion.17
  20.9 0.2 slice_reduce_fusion
  21.1 0.1 reshape.440
  21.2 4.3 %collective-permute-start.3 = (f32[4,128]{1,0:T(4,128)S(1)}, f32[4,128]{1,0:T(4,128)S(1)}, u32[]{:S(2)}, u32[]{:S(2)}) collective-permute-start(f32[4,128]{1,0:T(4,128)S(1)} %reshape.440), channel_id=1, source_target_pairs={{0,4},{4,8},{8,12},{1,5},{5,9},{9,13},{2,6},{6,10},{10,14},{3,7},{... | collective-permute-start | bytes 6152 | tf_op jit(solution)/shard_map/ppermute | solution.py:13
  25.5 2.4 %collective-permute-start.4 = (f32[2,16,1,128]{3,2,1,0:T(1,128)S(1)}, f32[2,16,1,128]{3,2,1,0:T(1,128)S(1)}, u32[]{:S(2)}, u32[]{:S(2)}) collective-permute-start(f32[2,16,1,128]{3,2,1,0:T(1,128)S(1)} %slice.165), channel_id=1, source_target_pairs={{0,1},{1,2},{2,3},{4,5},{5,6},{6,7},{8,9},{9,10},{10,11},{12,13},{... | collective-permute-start | bytes 49160 | tf_op jit(solution)/shard_map/ppermute | solution.py:13
  27.9 0.2 reshape.442
  28.1 0.6 %collective-permute-done.4 = f32[2,16,1,128]{3,2,1,0:T(1,128)S(1)} collective-permute-done((f32[2,16,1,128]{3,2,1,0:T(1,128)S(1)}, f32[2,16,1,128]{3,2,1,0:T(1,128)S(1)}, u32[]{:S(2)}, u32[]{:S(2)}) %collective-permute-start.4) | collective-permute-done | bytes 16416 | tf_op jit(solution)/shard_map/ppermute | solution.py:13
  28.7 0.7 %copy-done.3 = pred[16]{0:T(512)(128)(4,1)S(1)} copy-done((pred[16]{0:T(512)(128)(4,1)S(1)}, pred[16]{0:T(512)(128)(4,1)}, u32[]{:S(2)}) %copy-start.3) | copy-done | bytes 40
  29.4 0.2 fusion.22
  29.5 0.7 %fusion.64 = (f32[1,16,16,128]{3,2,1,0:T(8,128)}, f32[1,16,16,128]{3,2,1,0:T(8,128)}) fusion(f32[2,16,16,128]{3,2,1,0:T(8,128)S(1)} %fusion.22), kind=kLoop, calls=%fused_computation.140 | loop fusion | bytes 524288 | tf_op jit(solution)/shard_map/slice | solution.py:95
  (23 shorter events, 0.4 us)
Async XLA Ops:
  0.6 9.2 %copy-start = (f32[1,16,16,128]{3,2,1,0:T(8,128)S(1)}, f32[1,16,16,128]{3,2,1,0:T(8,128)}, u32[]{:S(2)}) copy-start(f32[1,16,16,128]{3,2,1,0:T(8,128)} %param.5) | copy-start | bytes 393220
  0.6 9.2 %copy-start.1 = (f32[1,16,16,128]{3,2,1,0:T(8,128)S(1)}, f32[1,16,16,128]{3,2,1,0:T(8,128)}, u32[]{:S(2)}) copy-start(f32[1,16,16,128]{3,2,1,0:T(8,128)} %param.4) | copy-start | bytes 393220
  1.7 8.1 %collective-permute-start = (f32[1,2,16,16,128]{4,3,2,0,1:T(8,128)S(1)}, f32[1,2,16,16,128]{4,3,2,0,1:T(8,128)S(1)}, u32[]{:S(2)}, u32[]{:S(2)}) collective-permute-start(f32[1,2,16,16,128]{4,3,2,0,1:T(8,128)S(1)} %pad_maximum_fusion.6), channel_id=1, source_target_pairs={{0,16},{16,0},{1,17},{17,1},{2,18},{18,2},{3,19},{19,3},{4,20},{20... | collective-permute-start | bytes 786440 | tf_op jit(solution)/shard_map/ppermute | solution.py:108
  3.8 0.7 %copy-start.4 = (f32[2]{0:T(128)S(1)}, f32[2]{0:T(128)}, u32[]{:S(2)}) copy-start(f32[2]{0:T(128)} %param.7) | copy-start | bytes 28
  4.5 0.7 %copy-start.2 = (f32[2]{0:T(128)S(1)}, f32[2]{0:T(128)}, u32[]{:S(2)}) copy-start(f32[2]{0:T(128)} %param.6) | copy-start | bytes 28
  10.4 4.8 %collective-permute-start.1 = (f32[8,128]{1,0:T(8,128)S(1)}, f32[8,128]{1,0:T(8,128)S(1)}, u32[]{:S(2)}, u32[]{:S(2)}) collective-permute-start(f32[8,128]{1,0:T(8,128)S(1)} %reshape.438), channel_id=1, source_target_pairs={{4,0},{8,4},{12,8},{5,1},{9,5},{13,9},{6,2},{10,6},{14,10},{7,3},{... | collective-permute-start | bytes 12296 | tf_op jit(solution)/shard_map/ppermute | solution.py:13
  11.8 6.1 %collective-permute-start.2 = (f32[2,2,16,1,128]{4,3,2,0,1:T(1,128)S(1)}, f32[2,2,16,1,128]{4,3,2,0,1:T(1,128)S(1)}, u32[]{:S(2)}, u32[]{:S(2)}) collective-permute-start(f32[2,2,16,1,128]{4,3,2,0,1:T(1,128)S(1)} %slice.149), channel_id=1, source_target_pairs={{1,0},{2,1},{3,2},{5,4},{6,5},{7,6},{9,8},{10,9},{11,10},{13,12},{... | collective-permute-start | bytes 98312 | tf_op jit(solution)/shard_map/ppermute | solution.py:13
  21.2 6.7 %collective-permute-start.3 = (f32[4,128]{1,0:T(4,128)S(1)}, f32[4,128]{1,0:T(4,128)S(1)}, u32[]{:S(2)}, u32[]{:S(2)}) collective-permute-start(f32[4,128]{1,0:T(4,128)S(1)} %reshape.440), channel_id=1, source_target_pairs={{0,4},{4,8},{8,12},{1,5},{5,9},{9,13},{2,6},{6,10},{10,14},{3,7},{... | collective-permute-start | bytes 6152 | tf_op jit(solution)/shard_map/ppermute | solution.py:13
  25.5 3.2 %collective-permute-start.4 = (f32[2,16,1,128]{3,2,1,0:T(1,128)S(1)}, f32[2,16,1,128]{3,2,1,0:T(1,128)S(1)}, u32[]{:S(2)}, u32[]{:S(2)}) collective-permute-start(f32[2,16,1,128]{3,2,1,0:T(1,128)S(1)} %slice.165), channel_id=1, source_target_pairs={{0,1},{1,2},{2,3},{4,5},{5,6},{6,7},{8,9},{9,10},{10,11},{12,13},{... | collective-permute-start | bytes 49160 | tf_op jit(solution)/shard_map/ppermute | solution.py:13
  28.7 0.7 %copy-start.3 = (pred[16]{0:T(512)(128)(4,1)S(1)}, pred[16]{0:T(512)(128)(4,1)}, u32[]{:S(2)}) copy-start(pred[16]{0:T(512)(128)(4,1)} %constant.43.clone.1) | copy-start | bytes 52

commit v4 on v3

--- a/solution.py
+++ b/solution.py
@@ -68,23 +68,29 @@
     return (jnp.stack(cross_q, axis=-4), jnp.stack(cross_p, axis=-4))
 
 
-def model_split(every, rim_x, rim_y, alpha, beta, weights):
-    grads, dirs = fields(every, rim_x, rim_y)
+def flux_of(tile, rim_x, rim_y, alpha, beta, weights):
+    grads, dirs = fields(tile, rim_x, rim_y)
     moms = moments(grads, dirs, weights)
     grad_own = grads[0]
     dir_own = dirs[0]
     cross_q, cross_p = couple(moms, grad_own, dir_own)
     size = jnp.sqrt(jnp.sum(grad_own * grad_own, 0) + EPS_SQ)[None]
-    flux = jnp.stack(
+    return jnp.stack(
         [beta * grad_own / size + alpha * cross_q, beta * dir_own / size + alpha * cross_p], 0
     )
+
+
+def model_split(every, rim_x, rim_y, alpha, beta, weights):
+    edge_x = flux_of(every[..., -1:], rim_x, rim_y[..., -1:], alpha, beta, weights)[:, 0]
+    edge_y = flux_of(every[..., -1:, :], rim_x[..., -1:, :], rim_y, alpha, beta, weights)[:, 1]
+    prev_x = passed_dense(edge_x, "tx", 1)
+    prev_y = passed_along(edge_y, "ty", 1)
+    flux = flux_of(every, rim_x, rim_y, alpha, beta, weights)
     last_x, last_y = edge_masks(flux.shape[3], flux.shape[4])
     flux_x = jnp.where(last_x, 0.0, flux[:, 0])
     flux_y = jnp.where(last_y, 0.0, flux[:, 1])
     flux_z = flux[:, 2]
     flux_z = jnp.concatenate([flux_z[..., :-1, :, :], jnp.zeros_like(flux_z[..., :1, :, :])], -3)
-    prev_x = passed_dense(flux_x[..., -1:], "tx", 1)
-    prev_y = passed_along(flux_y[..., -1:, :], "ty", 1)
     result = jnp.concatenate([prev_x, flux_x[..., :-1]], -1) - flux_x
     result = result + jnp.concatenate([prev_y, flux_y[..., :-1, :]], -2) - flux_y
     result = (

time: 30.5 us -> 53.1 us (1.74)
  local copies, waits for them, and re-layouts: 5.28 us -> 20.8 us
  other arithmetic: 5.58 us -> 13.8 us
  waiting for transfers between devices: 5.36 us -> 2.61 us
  starting transfers between devices: 13.2 us -> 14 us
    unnamed x10 -> x65, local copies, waits for them, and re-layouts: 1.32 us -> 10.7 us
    add x1 -> x3, other arithmetic: 1.48 us -> 4.12 us  [the longest x2 2.67 us: flux_of(): beta * grad_own / size + alpha * cross_q]
    ppermute x4, waiting for transfers between devices: 2.64 us -> 0.01 us  [passed_along(): return lax.ppermute(array, axis, pairs)]
    slice x4 -> x9, local copies, waits for them, and re-layouts: 0.71 us -> 3.16 us  [the longest x3 1.22 us: fields(): grads = jnp.stack([dx[:, 0], dy[:, 0], dz[:, 0]], 1)]
    slice x2 -> x3, local copies, waits for them, and re-layouts: 0.13 us -> 2.24 us  [fields(): dirs = jnp.stack([dx[:, 1], dy[:, 1], dz[:, 1]], 1)]
    sub x3 -> x5, other arithmetic: 0.49 us -> 2.19 us  [couple(): cross_p.append(trace_m * e_parts[i] - me + trace_n * g_parts[i] - ng)]
    reduce_sum x1 -> x3, other arithmetic: 0.46 us -> 1.35 us  [moments(): rows.append(jnp.sum(wts * dirs[:, i] * grads[:, j], 0))]
    ppermute x4, starting transfers between devices: 11.1 us -> 11.9 us  [passed_along(): return lax.ppermute(array, axis, pairs)]
  transfers between devices with their start and end apart: 5 -> 5, of which waited for: 3 -> 1; matrix products, arithmetic and copies ran while one was open for 12% -> 32% of each run, Pallas kernels for 0% -> 0%
where the time goes in v4:
time: 53.1 us; the launch traced here: 52.4 us
  local copies, waits for them, and re-layouts  20.8 us (39%)
  starting transfers between devices  14 us (26%)
  other arithmetic  13.8 us (26%)
  waiting for transfers between devices  2.61 us (5%)
  between operations  1.13 us (2%)
    ppermute x4, starting transfers between devices, passed_along(): return lax.ppermute(array, axis, pairs)  11.9 us
    unnamed x65, local copies, waits for them, and re-layouts  10.7 us
    add x2, other arithmetic, flux_of(): beta * grad_own / size + alpha * cross_q  2.67 us
    ppermute x1, waiting for transfers between devices, shards(): lax.ppermute(own, 'mp', [(m, (m + shift) % mp) for m in range(mp)])  2.6 us
    slice x3, local copies, waits for them, and re-layouts, fields(): dirs = jnp.stack([dx[:, 1], dy[:, 1], dz[:, 1]], 1)  2.24 us
    sub x5, other arithmetic, couple(): cross_p.append(trace_m * e_parts[i] - me + trace_n * g_parts[i] - ng)  2.19 us
    ppermute x1, starting transfers between devices, shards(): lax.ppermute(own, 'mp', [(m, (m + shift) % mp) for m in range(mp)])  2.12 us
    add x1, other arithmetic, flux_of(): beta * dir_own / size + alpha * cross_p  1.44 us
  transfers between devices with their start and end apart: 5, of which 1 were waited for; matrix products, arithmetic and copies ran while one was open for 32% of the time, Pallas kernels for 0%

profile of v4, /device:TPU:1, one launch (start us, length us, event | category | flops | bytes accessed | tf_op | source)
XLA Modules:
  0.0 52.4 jit_solution(5910395891648959932)
XLA Ops:
  0.6 1.0 %pad_maximum_fusion.6 = f32[1,2,16,16,128]{4,3,2,1,0:T(8,128)S(1)} fusion(f32[1,1,16,16,128]{4,3,2,1,0:T(8,128)} %bitcast.880, f32[1,1,16,16,128]{4,3,2,1,0:T(8,128)} %bitcast.883), kind=kLoop, calls=%fused_computation.46 | loop fusion | flops 65536 | bytes 524288 | tf_op jit(solution)/shard_map/stack | solution.py:111
  1.7 2.1 %collective-permute-start = (f32[1,2,16,16,128]{4,3,2,1,0:T(8,128)S(1)}, f32[1,2,16,16,128]{4,3,2,1,0:T(8,128)S(1)}, u32[]{:S(2)}, u32[]{:S(2)}) collective-permute-start(f32[1,2,16,16,128]{4,3,2,1,0:T(8,128)S(1)} %pad_maximum_fusion.6), channel_id=1, source_target_pairs={{0,16},{16,0},{1,17},{17,1},{2,18},{18,2},{3,19},{19,3},{4,20},{20... | collective-permute-start | bytes 786440 | tf_op jit(solution)/shard_map/ppermute | solution.py:114
  3.8 0.7 %copy-done.28 = f32[2]{0:T(128)S(1)} copy-done((f32[2]{0:T(128)S(1)}, f32[2]{0:T(128)}, u32[]{:S(2)}) %copy-start.28) | copy-done | bytes 32
  5.1 0.7 %fusion.181 = (f32[1]{0:T(128)}, f32[1]{0:T(128)}) fusion(f32[2]{0:T(128)S(1)} %copy-done.26, s32[]{:T(128)S(6)} %select_n.46, s32[]{:T(128)S(6)} %select_n.50), kind=kLoop, calls=%fused_computation.399 | loop fusion | bytes 24 | tf_op jit(solution)/shard_map/dynamic_slice | solution.py:108
  5.8 1.4 %pad_maximum_fusion.17 = f32[2]{0:T(128)S(1)} fusion(f32[1]{0:T(128)} %get-tuple-element.161, f32[1]{0:T(128)} %get-tuple-element.160), kind=kLoop, calls=%fused_computation.391 | loop fusion | flops 2 | bytes 16 | tf_op jit(solution)/shard_map/concatenate | solution.py:120
  7.2 2.6 %collective-permute-done = f32[1,2,16,16,128]{4,3,2,1,0:T(8,128)S(1)} collective-permute-done((f32[1,2,16,16,128]{4,3,2,1,0:T(8,128)S(1)}, f32[1,2,16,16,128]{4,3,2,1,0:T(8,128)S(1)}, u32[]{:S(2)}, u32[]{:S(2)}) %collective-permute-start) | collective-permute-done | bytes 262176 | tf_op jit(solution)/shard_map/ppermute | solution.py:114
  9.9 0.7 %copy-done.6 = f32[1,2,16,16,128]{4,3,2,1,0:T(8,128)} copy-done((f32[1,2,16,16,128]{4,3,2,1,0:T(8,128)}, f32[1,2,16,16,128]{4,3,2,1,0:T(8,128)S(1)}, u32[]{:S(2)}) %copy-start.6) | copy-done | bytes 262168
  10.9 0.7 %fusion.175 = (f32[2,2,16,1,128]{4,3,2,1,0:T(1,128)}, f32[2,2,16,1,128]{4,3,2,1,0:T(1,128)}) fusion(f32[2,2,16,16,128]{4,3,2,1,0:T(8,128)S(1)} %pad_maximum_fusion), kind=kLoop, calls=%fused_computation.393 | loop fusion | bytes 131072 | tf_op jit(solution)/shard_map/slice | solution.py:85
  12.0 1.3 %collective-permute-start.1 = (f32[8,128]{1,0:T(8,128)S(1)}, f32[8,128]{1,0:T(8,128)}, u32[]{:S(2)}, u32[]{:S(2)}) collective-permute-start(f32[8,128]{1,0:T(8,128)S(1)} %reshape.2579), channel_id=1, source_target_pairs={{4,0},{8,4},{12,8},{5,1},{9,5},{13,9},{6,2},{10,6},{14,10},{7,3},{... | collective-permute-start | bytes 12296 | tf_op jit(solution)/shard_map/ppermute | solution.py:13
  13.3 0.7 %pad_slice_fusion.7 = (f32[2,1,16,16,128]{4,3,2,1,0:T(8,128)}, f32[2,1,16,16,128]{4,3,2,1,0:T(8,128)S(1)}) fusion(f32[2,2,15,16,128]{4,3,2,1,0:T(8,128)S(1)} %slice_subtract_fusion), kind=kLoop, calls=%fused_computation.14 | loop fusion | bytes 1015808 | tf_op jit(solution)/shard_map/slice | solution.py:40
  16.7 3.2 %collective-permute-start.2 = (f32[2,2,16,1,128]{4,2,3,1,0:T(8,128)}, f32[2,2,16,1,128]{4,2,3,1,0:T(8,128)S(1)}, u32[]{:S(2)}, u32[]{:S(2)}) collective-permute-start(f32[2,2,16,1,128]{4,2,3,1,0:T(8,128)} %bitcast.154), channel_id=1, source_target_pairs={{1,0},{2,1},{3,2},{5,4},{6,5},{7,6},{9,8},{10,9},{11,10},{13,12},{... | collective-permute-start | bytes 98312 | tf_op jit(solution)/shard_map/ppermute | solution.py:13
  20.5 1.0 %copy.944 = f32[2,2,16,16,1]{3,2,1,0,4:T(8,128)} copy(f32[2,2,16,16,1]{4,3,2,1,0:T(8,128)S(1)} %get-tuple-element.96) | data formatting | bytes 8192
  21.6 1.1 %copy.946 = f32[2,2,16,15,1]{3,2,1,0,4:T(8,128)} copy(f32[2,2,16,15,1]{4,3,2,1,0:T(8,128)S(1)} %slice.354) | data formatting | bytes 7680
  22.6 0.7 %reshape.2580 = f32[2,2,16,16,1]{3,2,1,0,4:T(8,128)S(1)} reshape(f32[8,128]{1,0:T(8,128)} %collective-permute-done.1) | data formatting | bytes 8192 | tf_op jit(solution)/shard_map/reshape | solution.py:19
  24.6 0.8 %fusion.179 = (f32[2,1,16,16,128]{4,3,2,1,0:T(8,128)}, f32[2,1,16,16,128]{4,3,2,1,0:T(8,128)S(1)}) fusion(f32[2,2,16,16,128]{4,3,2,1,0:T(8,128)S(1)} %fusion), kind=kLoop, calls=%fused_computation.397 | loop fusion | bytes 1048576 | tf_op jit(solution)/shard_map/slice | solution.py:40
  26.1 0.7 %slice_bitcast_fusion = (f32[2,1,16,16,128]{4,3,2,1,0:T(8,128)}, f32[2,1,16,16,128]{4,3,2,1,0:T(8,128)S(1)}) fusion(f32[2,2,16,16,128]{4,3,2,0,1:T(8,128)S(1)} %fusion.1), kind=kLoop, calls=%fused_computation.73 | loop fusion | bytes 1048576 | tf_op jit(solution)/shard_map/slice | solution.py:40
  26.8 1.2 %fusion.30 = (f32[16,16,128]{2,1,0:T(8,128)S(1)}, f32[16,16,128]{2,1,0:T(8,128)S(1)}, f32[16,16,128]{2,1,0:T(8,128)}, f32[16,16,128]{2,1,0:T(8,128)S(1)}, f32[16...) fusion(f32[2,2,16,16,128]{4,3,2,0,1:T(8,128)S(1)} %fusion.1, ...), kind=kLoop, calls=%fused_computation.71 | loop fusion | flops 1998848 | bytes 3506184 | tf_op jit(solution)/shard_map/reduce_sum | solution.py:49
  29.8 0.9 %fusion.39 = (f32[1,1,16,16,128]{4,3,2,1,0:T(8,128)}, f32[1,1,16,16,128]{4,3,2,1,0:T(8,128)}, f32[1,1,16,16,128]{4,3,2,1,0:T(8,128)S(1)}) fusion(f32[16,16,128]{2,1,0:T(8,128)S(1)} %get-tuple-element.28, f32[16,16,128]{2,1,0:T(8,128)S(1)} %get-tuple-element.16, f32[16,16,128]{2,1,0:T(8,128)S(1)} %get-tuple-element.25, ...), kind=kLoop, calls=%fused_computation.89 | loop fusion | flops 622592 | bytes 2719744 | tf_op jit(solution)/shard_map/sub | solution.py:67
  30.7 0.7 %fusion.54 = f32[1,1,16,16,128]{4,3,2,1,0:T(8,128)} fusion(f32[16,16,128]{2,1,0:T(8,128)S(1)} %get-tuple-element.27, f32[16,16,128]{2,1,0:T(8,128)S(1)} %get-tuple-element.17, f32[16,16,128]{2,1,0:T(8,128)S(1)} %get-tuple-element.29, f32[1,1,16,16,128]{4,3,2,1,0:T(8,128)S(1)} %get-tuple-element.80, f32[2,2,16,16,128]{4,3,2,0,1:T(8,128)S(1)} %fusion.1, ...), kind=kLoop, calls=%fused_computation.118 | loop fusion | flops 229376 | bytes 1409024 | tf_op jit(solution)/shard_map/sub | solution.py:66
  31.4 0.7 %add_sqrt_fusion = f32[16,16,128]{2,1,0:T(8,128)} fusion(f32[16,16,128]{2,1,0:T(8,128)S(1)} %multiply_reduce_fusion), kind=kLoop, calls=%fused_computation.138 | loop fusion | flops 32768 | bytes 262144 | tf_op jit(solution)/shard_map/sqrt | solution.py:77
  32.2 0.7 %copy-done.18 = f32[2,1,16,1,128]{4,2,3,1,0:T(8,128)S(1)} copy-done((f32[2,1,16,1,128]{4,2,3,1,0:T(8,128)S(1)}, f32[2,1,16,1,128]{4,2,3,1,0:T(8,128)}, u32[]{:S(2)}) %copy-start.18) | copy-done | bytes 16408
  32.9 1.3 %fusion.73 = (f32[1,3,16,1,128]{4,2,3,1,0:T(8,128)S(1)}, f32[1,3,16,1,128]{4,2,3,1,0:T(8,128)S(1)}) fusion(f32[1,1,16,1,128]{4,2,3,1,0:T(8,128)S(1)} %get-tuple-element.110, f32[1,1,16,1,128]{4,2,3,1,0:T(8,128)S(1)} %get-tuple-element.108, f32[1,1,16,1,128]{4,2,3,1,0:T(8,128)S(1)} %get-tuple-element.70, f32[]{:T(128)} %bitcast.4, ...), kind=kLoop, calls=%fused_computation.175 | loop fusion | flops 98304 | bytes 204808 | tf_op jit(solution)/shard_map/add | solution.py:79
  34.8 3.2 %collective-permute-start.4 = (f32[2,16,1,128]{3,1,2,0:T(8,128)}, f32[2,16,1,128]{3,1,2,0:T(8,128)}, u32[]{:S(2)}, u32[]{:S(2)}) collective-permute-start(f32[2,16,1,128]{3,1,2,0:T(8,128)} %fusion.86), channel_id=1, source_target_pairs={{0,1},{1,2},{2,3},{4,5},{5,6},{6,7},{8,9},{9,10},{10,11},{12,13},{... | collective-permute-start | bytes 49160 | tf_op jit(solution)/shard_map/ppermute | solution.py:13
  38.2 0.7 %copy-done.17 = f32[2,1,16,16,1]{3,2,0,4,1:T(8,128)S(1)} copy-done((f32[2,1,16,16,1]{3,2,0,4,1:T(8,128)S(1)}, f32[2,1,16,16,1]{3,2,0,4,1:T(8,128)}, u32[]{:S(2)}) %copy-start.17) | copy-done | bytes 2072
  38.9 1.4 %fusion.72 = (f32[1,3,16,16,1]{3,2,1,0,4:T(8,128)S(1)}, f32[1,3,16,16,1]{3,2,1,0,4:T(8,128)S(1)}) fusion(f32[1,1,16,16,1]{3,2,1,0,4:T(8,128)S(1)} %get-tuple-element.114, f32[1,1,16,16,1]{3,2,1,0,4:T(8,128)S(1)} %get-tuple-element.112, f32[1,1,16,16,1]{3,2,1,0,4:T(8,128)S(1)} %get-tuple-element.74, f32[]{:T(128)} %bitcast.4, ...), kind=kLoop, calls=%fused_computation.172 | loop fusion | flops 12288 | bytes 25608 | tf_op jit(solution)/shard_map/add | solution.py:79
  40.3 0.7 %reshape_squeeze.3 = f32[4,128]{1,0:T(4,128)} reshape(f32[2,1,16,16,1]{3,2,1,0,4:T(8,128)S(1)} %pad_maximum_fusion.16) | data formatting | bytes 4096 | tf_op jit(solution)/shard_map/reshape;squeeze | solution.py:18
  41.0 4.3 %collective-permute-start.3 = (f32[4,128]{1,0:T(4,128)}, f32[4,128]{1,0:T(4,128)S(1)}, u32[]{:S(2)}, u32[]{:S(2)}) collective-permute-start(f32[4,128]{1,0:T(4,128)} %reshape_squeeze.3), channel_id=1, source_target_pairs={{0,4},{4,8},{8,12},{1,5},{5,9},{9,13},{2,6},{6,10},{10,14},{3,7},{... | collective-permute-start | bytes 6152 | tf_op jit(solution)/shard_map/ppermute | solution.py:13
  45.2 1.1 %fusion.36 = (f32[1,1,16,16,128]{4,3,2,1,0:T(8,128)S(1)}, f32[1,1,16,16,128]{4,3,2,1,0:T(8,128)S(1)}) fusion(f32[16,16,128]{2,1,0:T(8,128)} %get-tuple-element.89, f32[16,16,128]{2,1,0:T(8,128)} %get-tuple-element.18, f32[16,16,128]{2,1,0:T(8,128)S(1)} %get-tuple-element.31, f32[16,16,128]{2,1,0:T(8,128)S(1)} %get-tuple-element.88, ...), kind=kLoop, calls=%fused_computation.84 | loop fusion | flops 720896 | bytes 2326528 | tf_op jit(solution)/shard_map/sub | solution.py:67
  46.6 0.8 %copy-done.3 = f32[2,1,16,16,128]{4,3,2,1,0:T(8,128)S(1)} copy-done((f32[2,1,16,16,128]{4,3,2,1,0:T(8,128)S(1)}, f32[2,1,16,16,128]{4,3,2,1,0:T(8,128)}, u32[]{:S(2)}) %copy-start.3) | copy-done | bytes 262168
  47.6 1.4 %fusion.4 = (f32[1,3,16,16,128]{4,3,2,1,0:T(8,128)S(1)}, f32[1,3,16,16,128]{4,3,2,1,0:T(8,128)S(1)}) fusion(f32[2,1,16,16,128]{4,3,2,1,0:T(8,128)S(1)} %copy-done.3, f32[2,1,16,16,128]{4,3,2,1,0:T(8,128)S(1)} %copy-done.5, f32[2,1,16,16,128]{4,3,2,1,0:T(8,128)S(1)} %copy-done.4, f32[1,1,16,16,128]{4,3,2,1,0:T(8,128)S(1)} %get-tuple-element.83, ...), kind=kLoop, calls=%fused_computation.18 | loop fusion | flops 1572864 | bytes 3276808 | tf_op jit(solution)/shard_map/add | solution.py:79
  50.8 0.9 %fusion.22 = f32[2,16,16,128]{3,2,1,0:T(8,128)S(1)} fusion(f32[2,16,16,128]{3,2,1,0:T(8,128)S(1)} %get-tuple-element.91, f32[2,16,16,128]{3,2,1,0:T(8,128)S(1)} %get-tuple-element.90, f32[2,16,16,127]{3,2,1,0:T(8,128)S(1)} %bitcast.878, f32[2,16,16,1]{3,2,1,0:T(8,128)S(1)} %reshape.2582, f32[2,16,15,128]{3,2,1,0:T(8,128)S(1)} %bitcast.879, ...), kind=kLoop, calls=%fused_computation.51 | loop fusion | flops 524288 | bytes 1818640 | tf_op jit(solution)/shard_map/sub | solution.py:97
  51.7 0.7 %fusion.180 = (f32[1,16,16,128]{3,2,1,0:T(8,128)}, f32[1,16,16,128]{3,2,1,0:T(8,128)}) fusion(f32[2,16,16,128]{3,2,1,0:T(8,128)S(1)} %fusion.22), kind=kLoop, calls=%fused_computation.398 | loop fusion | bytes 524288 | tf_op jit(solution)/shard_map/slice | solution.py:101
  (109 shorter events, 11.3 us)
Async XLA Ops:
  0.6 9.2 %copy-start = (f32[1,16,16,128]{3,2,1,0:T(8,128)S(1)}, f32[1,16,16,128]{3,2,1,0:T(8,128)}, u32[]{:S(2)}) copy-start(f32[1,16,16,128]{3,2,1,0:T(8,128)} %param.5) | copy-start | bytes 393220
  0.6 9.2 %copy-start.1 = (f32[1,16,16,128]{3,2,1,0:T(8,128)S(1)}, f32[1,16,16,128]{3,2,1,0:T(8,128)}, u32[]{:S(2)}) copy-start(f32[1,16,16,128]{3,2,1,0:T(8,128)} %param.4) | copy-start | bytes 393220
  1.7 8.1 %collective-permute-start = (f32[1,2,16,16,128]{4,3,2,1,0:T(8,128)S(1)}, f32[1,2,16,16,128]{4,3,2,1,0:T(8,128)S(1)}, u32[]{:S(2)}, u32[]{:S(2)}) collective-permute-start(f32[1,2,16,16,128]{4,3,2,1,0:T(8,128)S(1)} %pad_maximum_fusion.6), channel_id=1, source_target_pairs={{0,16},{16,0},{1,17},{17,1},{2,18},{18,2},{3,19},{19,3},{4,20},{20... | collective-permute-start | bytes 786440 | tf_op jit(solution)/shard_map/ppermute | solution.py:114
  3.8 24.2 %copy-start.19 = (pred[128]{0:T(512)(128)(4,1)}, pred[128]{0:T(512)(128)(4,1)S(1)}, u32[]{:S(2)}) copy-start(pred[128]{0:T(512)(128)(4,1)S(1)} %compare_and_fusion) | copy-start | bytes 388
  3.8 0.7 %copy-start.28 = (f32[2]{0:T(128)S(1)}, f32[2]{0:T(128)}, u32[]{:S(2)}) copy-start(f32[2]{0:T(128)} %param.7) | copy-start | bytes 28
  4.5 0.7 %copy-start.26 = (f32[2]{0:T(128)S(1)}, f32[2]{0:T(128)}, u32[]{:S(2)}) copy-start(f32[2]{0:T(128)} %param.6) | copy-start | bytes 28
  5.8 20.1 %copy-start.21 = (pred[16]{0:T(512)(128)(4,1)}, pred[16]{0:T(512)(128)(4,1)S(1)}, u32[]{:S(2)}) copy-start(pred[16]{0:T(512)(128)(4,1)S(1)} %compare_and_fusion.1) | copy-start | bytes 52
  7.2 19.6 %copy-start.24 = (f32[2]{0:T(128)}, f32[2]{0:T(128)S(1)}, u32[]{:S(2)}) copy-start(f32[2]{0:T(128)S(1)} %pad_maximum_fusion.17) | copy-start | bytes 28
  9.8 0.7 %copy-start.6 = (f32[1,2,16,16,128]{4,3,2,1,0:T(8,128)}, f32[1,2,16,16,128]{4,3,2,1,0:T(8,128)S(1)}, u32[]{:S(2)}) copy-start(f32[1,2,16,16,128]{4,3,2,1,0:T(8,128)S(1)} %collective-permute-done) | copy-start | bytes 786436
  12.0 10.6 %collective-permute-start.1 = (f32[8,128]{1,0:T(8,128)S(1)}, f32[8,128]{1,0:T(8,128)}, u32[]{:S(2)}, u32[]{:S(2)}) collective-permute-start(f32[8,128]{1,0:T(8,128)S(1)} %reshape.2579), channel_id=1, source_target_pairs={{4,0},{8,4},{12,8},{5,1},{9,5},{13,9},{6,2},{10,6},{14,10},{7,3},{... | collective-permute-start | bytes 12296 | tf_op jit(solution)/shard_map/ppermute | solution.py:13
  16.7 9.1 %collective-permute-start.2 = (f32[2,2,16,1,128]{4,2,3,1,0:T(8,128)}, f32[2,2,16,1,128]{4,2,3,1,0:T(8,128)S(1)}, u32[]{:S(2)}, u32[]{:S(2)}) collective-permute-start(f32[2,2,16,1,128]{4,2,3,1,0:T(8,128)} %bitcast.154), channel_id=1, source_target_pairs={{1,0},{2,1},{3,2},{5,4},{6,5},{7,6},{9,8},{10,9},{11,10},{13,12},{... | collective-permute-start | bytes 98312 | tf_op jit(solution)/shard_map/ppermute | solution.py:13
  23.4 1.0 %copy-start.7 = (f32[1,2,16,16,128]{4,3,2,1,0:T(8,128)S(1)}, f32[1,2,16,16,128]{4,3,2,1,0:T(8,128)}, u32[]{:S(2)}) copy-start(f32[1,2,16,16,128]{4,3,2,1,0:T(8,128)} %copy-done.6) | copy-start | bytes 786436
  26.8 1.2 %copy-start.15 = (f32[2,2,16,1,127]{4,2,0,3,1:T(8,128)S(1)}, f32[2,2,16,1,127]{4,2,0,3,1:T(8,128)}, u32[]{:S(2)}) copy-start(f32[2,2,16,1,127]{4,2,0,3,1:T(8,128)} %copy.961) | copy-start | bytes 97540
  26.8 1.2 %copy-start.16 = (f32[2,2,16,1,128]{4,3,2,1,0:T(1,128)S(1)}, f32[2,2,16,1,128]{4,3,2,1,0:T(1,128)}, u32[]{:S(2)}) copy-start(f32[2,2,16,1,128]{4,3,2,1,0:T(1,128)} %get-tuple-element.92) | copy-start | bytes 98308
  28.8 0.8 %copy-start.13 = (f32[2,2,16,16,1]{3,2,1,0,4:T(8,128)S(1)}, f32[2,2,16,16,1]{3,2,1,0,4:T(8,128)}, u32[]{:S(2)}) copy-start(f32[2,2,16,16,1]{3,2,1,0,4:T(8,128)} %copy.944) | copy-start | bytes 12292
  28.8 0.8 %copy-start.14 = (f32[2,2,16,15,1]{3,2,1,0,4:T(8,128)S(1)}, f32[2,2,16,15,1]{3,2,1,0,4:T(8,128)}, u32[]{:S(2)}) copy-start(f32[2,2,16,15,1]{3,2,1,0,4:T(8,128)} %copy.946) | copy-start | bytes 11524
  32.2 0.7 %copy-start.18 = (f32[2,1,16,1,128]{4,2,3,1,0:T(8,128)S(1)}, f32[2,1,16,1,128]{4,2,3,1,0:T(8,128)}, u32[]{:S(2)}) copy-start(f32[2,1,16,1,128]{4,2,3,1,0:T(8,128)} %get-tuple-element.145) | copy-start | bytes 49156
  34.8 15.3 %collective-permute-start.4 = (f32[2,16,1,128]{3,1,2,0:T(8,128)}, f32[2,16,1,128]{3,1,2,0:T(8,128)}, u32[]{:S(2)}, u32[]{:S(2)}) collective-permute-start(f32[2,16,1,128]{3,1,2,0:T(8,128)} %fusion.86), channel_id=1, source_target_pairs={{0,1},{1,2},{2,3},{4,5},{5,6},{6,7},{8,9},{9,10},{10,11},{12,13},{... | collective-permute-start | bytes 49160 | tf_op jit(solution)/shard_map/ppermute | solution.py:13
  38.2 0.7 %copy-start.17 = (f32[2,1,16,16,1]{3,2,0,4,1:T(8,128)S(1)}, f32[2,1,16,16,1]{3,2,0,4,1:T(8,128)}, u32[]{:S(2)}) copy-start(f32[2,1,16,16,1]{3,2,0,4,1:T(8,128)} %get-tuple-element.153) | copy-start | bytes 6148
  38.9 6.3 %copy-start.2 = (f32[1,1,16,16,128]{4,3,2,1,0:T(8,128)S(1)}, f32[1,1,16,16,128]{4,3,2,1,0:T(8,128)}, u32[]{:S(2)}) copy-start(f32[1,1,16,16,128]{4,3,2,1,0:T(8,128)} %get-tuple-element.79) | copy-start | bytes 393220
  41.0 8.9 %collective-permute-start.3 = (f32[4,128]{1,0:T(4,128)}, f32[4,128]{1,0:T(4,128)S(1)}, u32[]{:S(2)}, u32[]{:S(2)}) collective-permute-start(f32[4,128]{1,0:T(4,128)} %reshape_squeeze.3), channel_id=1, source_target_pairs={{0,4},{4,8},{8,12},{1,5},{5,9},{9,13},{2,6},{6,10},{10,14},{3,7},{... | collective-permute-start | bytes 6152 | tf_op jit(solution)/shard_map/ppermute | solution.py:13
  45.2 1.2 %copy-start.8 = (f32[16,16,128]{2,1,0:T(8,128)S(1)}, f32[16,16,128]{2,1,0:T(8,128)}, u32[]{:S(2)}) copy-start(f32[16,16,128]{2,1,0:T(8,128)} %get-tuple-element.26) | copy-start | bytes 393220
  45.2 1.2 %copy-start.9 = (f32[16,16,128]{2,1,0:T(8,128)S(1)}, f32[16,16,128]{2,1,0:T(8,128)}, u32[]{:S(2)}) copy-start(f32[16,16,128]{2,1,0:T(8,128)} %get-tuple-element.87) | copy-start | bytes 393220
  46.4 1.0 %copy-start.3 = (f32[2,1,16,16,128]{4,3,2,1,0:T(8,128)S(1)}, f32[2,1,16,16,128]{4,3,2,1,0:T(8,128)}, u32[]{:S(2)}) copy-start(f32[2,1,16,16,128]{4,3,2,1,0:T(8,128)} %get-tuple-element.104) | copy-start | bytes 786436
  46.4 1.0 %copy-start.4 = (f32[2,1,16,16,128]{4,3,2,1,0:T(8,128)S(1)}, f32[2,1,16,16,128]{4,3,2,1,0:T(8,128)}, u32[]{:S(2)}) copy-start(f32[2,1,16,16,128]{4,3,2,1,0:T(8,128)} %get-tuple-element.100) | copy-start | bytes 786436
  46.4 1.1 %copy-start.5 = (f32[2,1,16,16,128]{4,3,2,1,0:T(8,128)S(1)}, f32[2,1,16,16,128]{4,3,2,1,0:T(8,128)}, u32[]{:S(2)}) copy-start(f32[2,1,16,16,128]{4,3,2,1,0:T(8,128)} %get-tuple-element.102) | copy-start | bytes 786436
  46.4 1.1 %copy-start.10 = (f32[16,16,128]{2,1,0:T(8,128)S(1)}, f32[16,16,128]{2,1,0:T(8,128)}, u32[]{:S(2)}) copy-start(f32[16,16,128]{2,1,0:T(8,128)} %add_sqrt_fusion) | copy-start | bytes 393220
  46.4 1.1 %copy-start.11 = (f32[1,1,16,16,128]{4,3,2,1,0:T(8,128)S(1)}, f32[1,1,16,16,128]{4,3,2,1,0:T(8,128)}, u32[]{:S(2)}) copy-start(f32[1,1,16,16,128]{4,3,2,1,0:T(8,128)} %fusion.54) | copy-start | bytes 393220
  46.5 1.2 %copy-start.12 = (f32[1,1,16,16,128]{4,3,2,1,0:T(8,128)S(1)}, f32[1,1,16,16,128]{4,3,2,1,0:T(8,128)}, u32[]{:S(2)}) copy-start(f32[1,1,16,16,128]{4,3,2,1,0:T(8,128)} %get-tuple-element.78) | copy-start | bytes 393220
  49.1 0.7 %copy-start.20 = (pred[128]{0:T(512)(128)(4,1)S(1)}, pred[128]{0:T(512)(128)(4,1)}, u32[]{:S(2)}) copy-start(pred[128]{0:T(512)(128)(4,1)} %copy-done.19) | copy-start | bytes 388
  49.1 0.7 %copy-start.23 = (pred[16]{0:T(512)(128)(4,1)S(1)}, pred[16]{0:T(512)(128)(4,1)}, u32[]{:S(2)}) copy-start(pred[16]{0:T(512)(128)(4,1)} %copy-done.21) | copy-start | bytes 52
  50.1 0.7 %copy-start.27 = (pred[16]{0:T(512)(128)(4,1)S(1)}, pred[16]{0:T(512)(128)(4,1)}, u32[]{:S(2)}) copy-start(pred[16]{0:T(512)(128)(4,1)} %constant.47.clone.1) | copy-start | bytes 52
  (2 other events, 1.2 us)

commit v5 on v1

--- a/solution.py
+++ b/solution.py
@@ -11,6 +11,12 @@
     size = lax.axis_size(axis)
     pairs = [(i, i + by) for i in range(size) if 0 <= i + by < size]
     return lax.ppermute(array, axis, pairs)
+
+
+def passed_dense(array, axis, by):
+    count = array.size
+    rows = array.reshape(count // 128, 128) if count % 128 == 0 else array.reshape(count)
+    return passed_along(rows, axis, by).reshape(array.shape)
 
 
 def edge_masks(width_y, width_x):
@@ -77,7 +83,7 @@
     flux_y = jnp.where(last_y, 0.0, flux[:, 1])
     flux_z = flux[:, 2]
     flux_z = jnp.concatenate([flux_z[..., :-1, :, :], jnp.zeros_like(flux_z[..., :1, :, :])], -3)
-    prev_x = passed_along(flux_x[..., -1:], "tx", 1)
+    prev_x = passed_dense(flux_x[..., -1:], "tx", 1)
     prev_y = passed_along(flux_y[..., -1:, :], "ty", 1)
     result = jnp.concatenate([prev_x, flux_x[..., :-1]], -1) - flux_x
     result = result + jnp.concatenate([prev_y, flux_y[..., :-1, :]], -2) - flux_y
@@ -90,8 +96,10 @@
 
 
 def rim_from(array, axis, shift):
+    count = array.size
+    rows = array.reshape(count // 128, 128) if count % 128 == 0 else array.reshape(count)
     if shift == 0:
-        return passed_along(array, axis, -1)
+        return passed_along(rows, axis, -1).reshape(array.shape)
     mp = lax.axis_size("mp")
     size = lax.axis_size(axis)
     pairs = [
@@ -99,7 +107,7 @@
         for m in range(mp)
         for t in range(1, size)
     ]
-    return lax.ppermute(array, ("mp", axis), pairs)
+    return lax.ppermute(rows, ("mp", axis), pairs).reshape(array.shape)
 
 
 def shards(models, direction, coupling, tv_weight):

time: 43.6 us -> 34.4 us (0.79)
  waiting for transfers between devices: 13 us -> 2.34 us
  starting transfers between devices: 18.3 us -> 20 us
    ppermute x1, waiting for transfers between devices: 8.04 us -> 1.75 us  [shards(): lax.ppermute(own, 'mp', [(m, (m + shift) % mp) for m in range(mp)])]
    ppermute x4, waiting for transfers between devices: 4.97 us -> 0.58 us  [passed_along(): return lax.ppermute(array, axis, pairs)]
    ppermute x4, starting transfers between devices: 12.3 us -> 14.1 us  [passed_along(): return lax.ppermute(array, axis, pairs)]
    unnamed x15 -> x10, local copies, waits for them, and re-layouts: 2.79 us -> 1.31 us
    slice x0 -> x1, other arithmetic: none -> 1.15 us  [shards(): rims_x.append(rim_from(own[..., :1], 'tx', shift))]
    another operation x3 -> x2, other arithmetic: 1.06 us -> 0.03 us  [shards(): own = jnp.stack([models, direction], 1)]
    ppermute x1, starting transfers between devices: 0.81 us -> 0.07 us  [shards(): lax.ppermute(own, 'mp', [(m, (m + shift) % mp) for m in range(mp)])]
    slice x1, local copies, waits for them, and re-layouts: 0.02 us -> 0.72 us  [model_split(): return (result[0][None], result[1][None])]
  transfers between devices with their start and end apart: 7 -> 7, of which waited for: 2 -> 2; matrix products, arithmetic and copies ran while one was open for 8% -> 12% of each run, Pallas kernels for 0% -> 0%
where the time goes in v5:
time: 34.4 us; the launch traced here: 33.9 us
  starting transfers between devices  20 us (58%)
  other arithmetic  5.71 us (17%)
  local copies, waits for them, and re-layouts  4.87 us (14%)
  waiting for transfers between devices  2.34 us (7%)
  between operations  0.99 us (3%)
    ppermute x4, starting transfers between devices, passed_along(): return lax.ppermute(array, axis, pairs)  14.1 us
    ppermute x2, starting transfers between devices, rim_from(): return lax.ppermute(rows, ('mp', axis), pairs).reshape(array.shape)  5.81 us
    ppermute x1, waiting for transfers between devices, shards(): lax.ppermute(own, 'mp', [(m, (m + shift) % mp) for m in range(mp)])  1.75 us
    add x1, other arithmetic, model_split(): beta * dir_own / size + alpha * cross_p  1.46 us
    concatenate x1, other arithmetic, shards(): jnp.concatenate(weights, 0)  1.42 us
    unnamed x10, local copies, waits for them, and re-layouts  1.31 us
    slice x1, other arithmetic, shards(): rims_x.append(rim_from(own[..., :1], 'tx', shift))  1.15 us
    slice x1, local copies, waits for them, and re-layouts, model_split(): return (result[0][None], result[1][None])  0.72 us
  transfers between devices with their start and end apart: 7, of which 2 were waited for; matrix products, arithmetic and copies ran while one was open for 12% of the time, Pallas kernels for 0%

profile of v5, /device:TPU:1, one launch (start us, length us, event | category | flops | bytes accessed | tf_op | source)
XLA Modules:
  0.0 33.9 jit_solution(17077628293734466865)
XLA Ops:
  0.6 1.1 %fusion.10 = f32[2,16,16]{2,1,0:T(8,128)S(1)} fusion(f32[1,1,16,16,128]{4,3,2,0,1:T(8,128)} %bitcast.248, f32[1,1,16,16,128]{4,3,2,0,1:T(8,128)} %bitcast.243), kind=kLoop, calls=%fused_computation.40 | loop fusion | flops 512 | bytes 264192 | tf_op jit(solution)/shard_map/slice | solution.py:127
  1.8 0.1 reshape.452
  1.9 1.3 %collective-permute-start.2 = (f32[4,128]{1,0:T(4,128)S(1)}, f32[4,128]{1,0:T(4,128)S(1)}, u32[]{:S(2)}, u32[]{:S(2)}) collective-permute-start(f32[4,128]{1,0:T(4,128)S(1)} %reshape.452), channel_id=1, source_target_pairs={{4,16},{8,20},{12,24},{20,0},{24,4},{28,8},{5,17},{9,21},{13,25},{... | collective-permute-start | bytes 6152 | tf_op jit(solution)/shard_map/ppermute | solution.py:110
  3.2 1.3 %collective-permute-start.1 = (f32[4,128]{1,0:T(4,128)S(1)}, f32[4,128]{1,0:T(4,128)S(1)}, u32[]{:S(2)}, u32[]{:S(2)}) collective-permute-start(f32[4,128]{1,0:T(4,128)S(1)} %reshape.452), channel_id=1, source_target_pairs={{4,0},{8,4},{12,8},{5,1},{9,5},{13,9},{6,2},{10,6},{14,10},{7,3},{... | collective-permute-start | bytes 6152 | tf_op jit(solution)/shard_map/ppermute | solution.py:13
  4.5 4.5 %collective-permute-start.4 = (f32[32,128]{1,0:T(8,128)S(1)}, f32[32,128]{1,0:T(8,128)S(1)}, u32[]{:S(2)}, u32[]{:S(2)}) collective-permute-start(f32[32,128]{1,0:T(8,128)S(1)} %bitcast.256), channel_id=1, source_target_pairs={{1,16},{2,17},{3,18},{17,0},{18,1},{19,2},{5,20},{6,21},{7,22},{21... | collective-permute-start | bytes 49160 | tf_op jit(solution)/shard_map/ppermute | solution.py:110
  9.1 1.9 %collective-permute-start.3 = (f32[32,128]{1,0:T(8,128)S(1)}, f32[32,128]{1,0:T(8,128)S(1)}, u32[]{:S(2)}, u32[]{:S(2)}) collective-permute-start(f32[32,128]{1,0:T(8,128)S(1)} %bitcast.257), channel_id=1, source_target_pairs={{1,0},{2,1},{3,2},{5,4},{6,5},{7,6},{9,8},{10,9},{11,10},{13,12},{... | collective-permute-start | bytes 49160 | tf_op jit(solution)/shard_map/ppermute | solution.py:13
  11.0 0.1 collective-permute-start
  11.2 0.6 %copy-done.2 = f32[2]{0:T(128)S(1)} copy-done((f32[2]{0:T(128)S(1)}, f32[2]{0:T(128)}, u32[]{:S(2)}) %copy-start.2) | copy-done | bytes 32
  11.8 0.7 %fusion.68 = (f32[1]{0:T(128)}, f32[1]{0:T(128)}, f32[1]{0:T(128)}) fusion(f32[2]{0:T(128)S(1)} %copy-done.2, s32[]{:T(128)S(6)} %select_n.37, s32[]{:T(128)S(6)} %select_n.43, s32[]{:T(128)S(6)} %select_n.41), kind=kLoop, calls=%fused_computation.149 | loop fusion | bytes 36 | tf_op jit(solution)/shard_map/dynamic_slice | solution.py:117
  12.5 1.4 %pad_maximum_fusion.8 = f32[2]{0:T(128)S(1)} fusion(f32[1]{0:T(128)} %get-tuple-element.47, f32[1]{0:T(128)} %get-tuple-element.48), kind=kLoop, calls=%fused_computation.145 | loop fusion | flops 2 | bytes 16 | tf_op jit(solution)/shard_map/concatenate | solution.py:134
  13.9 0.6 %dynamic_slice.12 = f32[1]{0:T(128)} dynamic-slice(f32[2]{0:T(128)S(1)} %copy-done.4, s32[]{:T(128)S(6)} %select_n.37), dynamic_slice_sizes={1} | dynamic-slice | bytes 12 | tf_op jit(solution)/shard_map/dynamic_slice | solution.py:119
  14.5 0.1 reshape.454
  14.6 0.1 reshape.453
  14.7 0.4 %copy.6 = f32[2,2,16,16,1]{4,3,2,0,1:T(8,128)S(1)} copy(f32[2,2,16,16,1]{3,2,1,4,0:T(8,128)S(1)} %pad_maximum_fusion.7) | data formatting | bytes 8192 | tf_op jit(solution)/shard_map/concatenate | solution.py:132
  15.1 1.8 %collective-permute-done = f32[1,2,16,16,128]{4,3,2,0,1:T(8,128)S(1)} collective-permute-done((f32[1,2,16,16,128]{4,3,2,0,1:T(8,128)S(1)}, f32[1,2,16,16,128]{4,3,2,0,1:T(8,128)S(1)}, u32[]{:S(2)}, u32[]{:S(2)}) %collective-permute-start) | collective-permute-done | bytes 262176 | tf_op jit(solution)/shard_map/ppermute | solution.py:126
  17.0 0.2 slice.147
  17.3 0.3 fusion
  17.6 0.5 %fusion.29 = (f32[16,16,128]{2,1,0:T(8,128)S(1)}, f32[16,16,128]{2,1,0:T(8,128)S(1)}, f32[16,16,128]{2,1,0:T(8,128)S(1)}, f32[16,16,128]{2,1,0:T(8,128)S(1)}, f3...) fusion(f32[2]{0:T(128)S(1)} %pad_maximum_fusion.8, ...), kind=kLoop, calls=%fused_computation.71 | loop fusion | flops 1998848 | bytes 3506184 | tf_op jit(solution)/shard_map/reduce_sum | solution.py:49
  18.2 0.1 fusion.41
  18.4 0.1 fusion.36
  18.5 0.1 fusion.38
  18.7 1.5 %fusion.4 = (f32[1,3,16,16,128]{4,3,2,0,1:T(8,128)S(1)}, f32[1,3,16,16,128]{4,3,2,0,1:T(8,128)S(1)}) fusion(f32[2,1,16,16,128]{4,3,2,0,1:T(8,128)S(1)} %get-tuple-element.40, f32[2,1,16,16,128]{4,3,2,0,1:T(8,128)S(1)} %get-tuple-element.50, f32[2,1,16,16,128]{4,3,2,0,1:T(8,128)S(1)} %get-tuple-element.34, f32[1,1,16,16,128]{4,3,2,0,1:T(8,128)S(1)} %get-tuple-element.25, ...), kind=kLoop, calls=%fused_computation.17 | loop fusion | flops 1572864 | bytes 3276808 | tf_op jit(solution)/shard_map/add | solution.py:79
  20.1 0.1 fusion.19
  20.2 0.2 slice_reduce_fusion
  20.5 0.1 reshape.458
  20.6 6.2 %collective-permute-start.5 = (f32[4,128]{1,0:T(4,128)S(1)}, f32[4,128]{1,0:T(4,128)S(1)}, u32[]{:S(2)}, u32[]{:S(2)}) collective-permute-start(f32[4,128]{1,0:T(4,128)S(1)} %reshape.458), channel_id=1, source_target_pairs={{0,4},{4,8},{8,12},{1,5},{5,9},{9,13},{2,6},{6,10},{10,14},{3,7},{... | collective-permute-start | bytes 6152 | tf_op jit(solution)/shard_map/ppermute | solution.py:13
  26.8 4.8 %collective-permute-start.6 = (f32[2,16,1,128]{3,2,1,0:T(1,128)S(1)}, f32[2,16,1,128]{3,2,1,0:T(1,128)S(1)}, u32[]{:S(2)}, u32[]{:S(2)}) collective-permute-start(f32[2,16,1,128]{3,2,1,0:T(1,128)S(1)} %slice.169), channel_id=1, source_target_pairs={{0,1},{1,2},{2,3},{4,5},{5,6},{6,7},{8,9},{9,10},{10,11},{12,13},{... | collective-permute-start | bytes 49160 | tf_op jit(solution)/shard_map/ppermute | solution.py:13
  31.6 0.2 reshape.460
  31.8 0.6 %collective-permute-done.6 = f32[2,16,1,128]{3,2,1,0:T(1,128)S(1)} collective-permute-done((f32[2,16,1,128]{3,2,1,0:T(1,128)S(1)}, f32[2,16,1,128]{3,2,1,0:T(1,128)S(1)}, u32[]{:S(2)}, u32[]{:S(2)}) %collective-permute-start.6) | collective-permute-done | bytes 16416 | tf_op jit(solution)/shard_map/ppermute | solution.py:13
  32.4 0.7 %copy-done.3 = pred[16]{0:T(512)(128)(4,1)S(1)} copy-done((pred[16]{0:T(512)(128)(4,1)S(1)}, pred[16]{0:T(512)(128)(4,1)}, u32[]{:S(2)}) %copy-start.3) | copy-done | bytes 40
  33.0 0.2 fusion.24
  33.2 0.7 %fusion.67 = (f32[1,16,16,128]{3,2,1,0:T(8,128)}, f32[1,16,16,128]{3,2,1,0:T(8,128)}) fusion(f32[2,16,16,128]{3,2,1,0:T(8,128)S(1)} %fusion.24), kind=kLoop, calls=%fused_computation.148 | loop fusion | bytes 524288 | tf_op jit(solution)/shard_map/slice | solution.py:95
  (29 shorter events, 0.5 us)
Async XLA Ops:
  0.6 3.9 %copy-start = (f32[1,16,16,128]{3,2,1,0:T(8,128)S(1)}, f32[1,16,16,128]{3,2,1,0:T(8,128)}, u32[]{:S(2)}) copy-start(f32[1,16,16,128]{3,2,1,0:T(8,128)} %param.5) | copy-start | bytes 393220
  0.6 3.9 %copy-start.1 = (f32[1,16,16,128]{3,2,1,0:T(8,128)S(1)}, f32[1,16,16,128]{3,2,1,0:T(8,128)}, u32[]{:S(2)}) copy-start(f32[1,16,16,128]{3,2,1,0:T(8,128)} %param.4) | copy-start | bytes 393220
  1.9 12.6 %collective-permute-start.2 = (f32[4,128]{1,0:T(4,128)S(1)}, f32[4,128]{1,0:T(4,128)S(1)}, u32[]{:S(2)}, u32[]{:S(2)}) collective-permute-start(f32[4,128]{1,0:T(4,128)S(1)} %reshape.452), channel_id=1, source_target_pairs={{4,16},{8,20},{12,24},{20,0},{24,4},{28,8},{5,17},{9,21},{13,25},{... | collective-permute-start | bytes 6152 | tf_op jit(solution)/shard_map/ppermute | solution.py:110
  3.2 11.4 %collective-permute-start.1 = (f32[4,128]{1,0:T(4,128)S(1)}, f32[4,128]{1,0:T(4,128)S(1)}, u32[]{:S(2)}, u32[]{:S(2)}) collective-permute-start(f32[4,128]{1,0:T(4,128)S(1)} %reshape.452), channel_id=1, source_target_pairs={{4,0},{8,4},{12,8},{5,1},{9,5},{13,9},{6,2},{10,6},{14,10},{7,3},{... | collective-permute-start | bytes 6152 | tf_op jit(solution)/shard_map/ppermute | solution.py:13
  4.5 12.7 %collective-permute-start.4 = (f32[32,128]{1,0:T(8,128)S(1)}, f32[32,128]{1,0:T(8,128)S(1)}, u32[]{:S(2)}, u32[]{:S(2)}) collective-permute-start(f32[32,128]{1,0:T(8,128)S(1)} %bitcast.256), channel_id=1, source_target_pairs={{1,16},{2,17},{3,18},{17,0},{18,1},{19,2},{5,20},{6,21},{7,22},{21... | collective-permute-start | bytes 49160 | tf_op jit(solution)/shard_map/ppermute | solution.py:110
  9.1 8.2 %collective-permute-start.3 = (f32[32,128]{1,0:T(8,128)S(1)}, f32[32,128]{1,0:T(8,128)S(1)}, u32[]{:S(2)}, u32[]{:S(2)}) collective-permute-start(f32[32,128]{1,0:T(8,128)S(1)} %bitcast.257), channel_id=1, source_target_pairs={{1,0},{2,1},{3,2},{5,4},{6,5},{7,6},{9,8},{10,9},{11,10},{13,12},{... | collective-permute-start | bytes 49160 | tf_op jit(solution)/shard_map/ppermute | solution.py:13
  11.0 5.9 %collective-permute-start = (f32[1,2,16,16,128]{4,3,2,0,1:T(8,128)S(1)}, f32[1,2,16,16,128]{4,3,2,0,1:T(8,128)S(1)}, u32[]{:S(2)}, u32[]{:S(2)}) collective-permute-start(f32[1,2,16,16,128]{4,3,2,0,1:T(8,128)S(1)} %pad_maximum_fusion.5), channel_id=1, source_target_pairs={{0,16},{16,0},{1,17},{17,1},{2,18},{18,2},{3,19},{19,3},{4,20},{20... | collective-permute-start | bytes 786440 | tf_op jit(solution)/shard_map/ppermute | solution.py:126
  11.2 0.7 %copy-start.2 = (f32[2]{0:T(128)S(1)}, f32[2]{0:T(128)}, u32[]{:S(2)}) copy-start(f32[2]{0:T(128)} %param.6) | copy-start | bytes 28
  12.5 1.4 %copy-start.4 = (f32[2]{0:T(128)S(1)}, f32[2]{0:T(128)}, u32[]{:S(2)}) copy-start(f32[2]{0:T(128)} %param.7) | copy-start | bytes 28
  20.6 11.0 %collective-permute-start.5 = (f32[4,128]{1,0:T(4,128)S(1)}, f32[4,128]{1,0:T(4,128)S(1)}, u32[]{:S(2)}, u32[]{:S(2)}) collective-permute-start(f32[4,128]{1,0:T(4,128)S(1)} %reshape.458), channel_id=1, source_target_pairs={{0,4},{4,8},{8,12},{1,5},{5,9},{9,13},{2,6},{6,10},{10,14},{3,7},{... | collective-permute-start | bytes 6152 | tf_op jit(solution)/shard_map/ppermute | solution.py:13
  26.8 5.6 %collective-permute-start.6 = (f32[2,16,1,128]{3,2,1,0:T(1,128)S(1)}, f32[2,16,1,128]{3,2,1,0:T(1,128)S(1)}, u32[]{:S(2)}, u32[]{:S(2)}) collective-permute-start(f32[2,16,1,128]{3,2,1,0:T(1,128)S(1)} %slice.169), channel_id=1, source_target_pairs={{0,1},{1,2},{2,3},{4,5},{5,6},{6,7},{8,9},{9,10},{10,11},{12,13},{... | collective-permute-start | bytes 49160 | tf_op jit(solution)/shard_map/ppermute | solution.py:13
  32.4 0.7 %copy-start.3 = (pred[16]{0:T(512)(128)(4,1)S(1)}, pred[16]{0:T(512)(128)(4,1)}, u32[]{:S(2)}) copy-start(pred[16]{0:T(512)(128)(4,1)} %constant.47.clone.1) | copy-start | bytes 52

commit v6 on v4

--- a/solution.py
+++ b/solution.py
@@ -68,37 +68,78 @@
     return (jnp.stack(cross_q, axis=-4), jnp.stack(cross_p, axis=-4))
 
 
-def flux_of(tile, rim_x, rim_y, alpha, beta, weights):
-    grads, dirs = fields(tile, rim_x, rim_y)
-    moms = moments(grads, dirs, weights)
-    grad_own = grads[0]
-    dir_own = dirs[0]
-    cross_q, cross_p = couple(moms, grad_own, dir_own)
-    size = jnp.sqrt(jnp.sum(grad_own * grad_own, 0) + EPS_SQ)[None]
-    return jnp.stack(
-        [beta * grad_own / size + alpha * cross_q, beta * dir_own / size + alpha * cross_p], 0
-    )
+def diffs(field, rim_x, rim_y, last):
+    last_x, last_y = last
+    dx = jnp.where(last_x, 0.0, jnp.concatenate([field[..., 1:], rim_x], -1) - field)
+    dy = jnp.where(last_y, 0.0, jnp.concatenate([field[:, 1:, :], rim_y], -2) - field)
+    dz = jnp.concatenate([field[1:], field[-1:]], 0) - field
+    return (dx, dy, dz)
+
+
+def adjoint_of(flux, prev_x, prev_y, masks):
+    last_x, last_y, last_z, first_z = masks
+    fx = jnp.where(last_x, 0.0, flux[0])
+    fy = jnp.where(last_y, 0.0, flux[1])
+    fz = jnp.where(last_z, 0.0, flux[2])
+    res = jnp.concatenate([prev_x, fx[..., :-1]], -1) - fx
+    res = res + jnp.concatenate([prev_y, fy[:, :-1, :]], -2) - fy
+    below = jnp.where(first_z, 0.0, jnp.concatenate([fz[:1], fz[:-1]], 0))
+    return res + below - fz
 
 
 def model_split(every, rim_x, rim_y, alpha, beta, weights):
-    edge_x = flux_of(every[..., -1:], rim_x, rim_y[..., -1:], alpha, beta, weights)[:, 0]
-    edge_y = flux_of(every[..., -1:, :], rim_x[..., -1:, :], rim_y, alpha, beta, weights)[:, 1]
+    depth, width_y, width_x = every.shape[2:]
+    end_x = lax.axis_index("tx") == lax.axis_size("tx") - 1
+    end_y = lax.axis_index("ty") == lax.axis_size("ty") - 1
+    shape = (depth, width_y, width_x)
+    col_x = lax.broadcasted_iota(jnp.int32, shape, 2)
+    row_y = lax.broadcasted_iota(jnp.int32, shape, 1)
+    lev_z = lax.broadcasted_iota(jnp.int32, shape, 0)
+    last_x = (col_x == width_x - 1) & end_x
+    last_y = (row_y == width_y - 1) & end_y
+    last_z = lev_z == depth - 1
+    first_z = lev_z == 0
+    gs, es = [], []
+    for k in range(every.shape[0]):
+        gs.append(diffs(every[k, 0], rim_x[k, 0], rim_y[k, 0], (last_x, last_y)))
+        es.append(diffs(every[k, 1], rim_x[k, 1], rim_y[k, 1], (last_x, last_y)))
+
+    def summed(terms):
+        total = terms[0]
+        for term in terms[1:]:
+            total = total + term
+        return total
+
+    count = len(gs)
+    mom = {}
+    for i, j in SYM_PAIRS:
+        mom[i, j] = summed([weights[k] * gs[k][i] * gs[k][j] for k in range(count)])
+        mom[j, i] = mom[i, j]
+    nat = {}
+    for i in range(3):
+        for j in range(3):
+            nat[i, j] = summed([weights[k] * es[k][i] * gs[k][j] for k in range(count)])
+    trace_m = mom[0, 0] + mom[1, 1] + mom[2, 2]
+    trace_n = nat[0, 0] + nat[1, 1] + nat[2, 2]
+    g, e = gs[0], es[0]
+    size = jnp.sqrt(g[0] * g[0] + g[1] * g[1] + g[2] * g[2] + EPS_SQ)
+    flux_q, flux_p = [], []
+    for i in range(3):
+        mg = mom[i, 0] * g[0] + mom[i, 1] * g[1] + mom[i, 2] * g[2]
+        me = mom[i, 0] * e[0] + mom[i, 1] * e[1] + mom[i, 2] * e[2]
+        ng = nat[i, 0] * g[0] + nat[i, 1] * g[1] + nat[i, 2] * g[2]
+        cross_q = trace_m * g[i] - mg
+        cross_p = trace_m * e[i] - me + trace_n * g[i] - ng
+        flux_q.append(beta * g[i] / size + alpha * cross_q)
+        flux_p.append(beta * e[i] / size + alpha * cross_p)
+    edge_x = jnp.stack([flux_q[0][..., -1:], flux_p[0][..., -1:]], 0)
+    edge_y = jnp.stack([flux_q[1][:, -1:, :], flux_p[1][:, -1:, :]], 0)
     prev_x = passed_dense(edge_x, "tx", 1)
     prev_y = passed_along(edge_y, "ty", 1)
-    flux = flux_of(every, rim_x, rim_y, alpha, beta, weights)
-    last_x, last_y = edge_masks(flux.shape[3], flux.shape[4])
-    flux_x = jnp.where(last_x, 0.0, flux[:, 0])
-    flux_y = jnp.where(last_y, 0.0, flux[:, 1])
-    flux_z = flux[:, 2]
-    flux_z = jnp.concatenate([flux_z[..., :-1, :, :], jnp.zeros_like(flux_z[..., :1, :, :])], -3)
-    result = jnp.concatenate([prev_x, flux_x[..., :-1]], -1) - flux_x
-    result = result + jnp.concatenate([prev_y, flux_y[..., :-1, :]], -2) - flux_y
-    result = (
-        result
-        + jnp.concatenate([jnp.zeros_like(flux_z[..., :1, :, :]), flux_z[..., :-1, :, :]], -3)
-        - flux_z
-    )
-    return (result[0][None], result[1][None])
+    masks = (last_x, last_y, last_z, first_z)
+    gradient = adjoint_of(flux_q, prev_x[0], prev_y[0], masks)
+    hessian = adjoint_of(flux_p, prev_x[1], prev_y[1], masks)
+    return (gradient[None], hessian[None])
 
 
 def shards(models, direction, coupling, tv_weight):

time: 53.1 us -> 52.9 us (level)
  the two profiles are of different devices: /device:TPU:1 before, /device:TPU:0 now
where the time goes in v6:
time: 52.9 us; the launch traced here: 52.3 us
  other arithmetic  20.6 us (39%)
  local copies, waits for them, and re-layouts  15.3 us (29%)
  starting transfers between devices  12.5 us (24%)
  waiting for transfers between devices  2.82 us (5%)
  between operations  1 us (2%)
    ppermute x4, starting transfers between devices, passed_along(): return lax.ppermute(array, axis, pairs)  9.46 us
    sub x2, other arithmetic, adjoint_of(): return res + below - fz  7.27 us
    select_n x2, other arithmetic, adjoint_of(): fz = jnp.where(last_z, 0.0, flux[2])  5.82 us
    add x2, other arithmetic, model_split(): flux_p.append(beta * e[i] / size + alpha * cross_p)  4.34 us
    ppermute x1, starting transfers between devices, shards(): lax.ppermute(own, 'mp', [(m, (m + shift) % mp) for m in range(mp)])  3.06 us
    ppermute x4, waiting for transfers between devices, passed_along(): return lax.ppermute(array, axis, pairs)  2.82 us
    unnamed x48, local copies, waits for them, and re-layouts  2.76 us
    concatenate x8, local copies, waits for them, and re-layouts, diffs(): jnp.concatenate([field[..., 1:], rim_x], -1) - field  1.72 us
  transfers between devices with their start and end apart: 5, of which 2 were waited for; matrix products, arithmetic and copies ran while one was open for 23% of the time, Pallas kernels for 0%

profile of v6, /device:TPU:0, one launch (start us, length us, event | category | flops | bytes accessed | tf_op | source)
XLA Modules:
  0.0 52.3 jit_solution(12038425123001402715)
XLA Ops:
  0.6 1.1 %copy_bitcast_fusion = (f32[1,1,16,16,128]{4,2,3,1,0:T(8,128)S(1)}, f32[1,1,16,16,128]{4,2,3,1,0:T(8,128)S(1)}) fusion(f32[1,16,16,128]{3,2,1,0:T(8,128)} %param.5, f32[1,16,16,128]{3,2,1,0:T(8,128)} %param.4), kind=kLoop, calls=%fused_computation.106 | loop fusion | bytes 524288 | tf_op jit(solution)/shard_map/stack | solution.py:152
  1.8 3.1 %collective-permute-start = (f32[1,2,16,16,128]{4,3,2,1,0:T(8,128)S(1)}, f32[1,2,16,16,128]{4,3,2,1,0:T(8,128)S(1)}, u32[]{:S(2)}, u32[]{:S(2)}) collective-permute-start(f32[1,2,16,16,128]{4,3,2,1,0:T(8,128)S(1)} %copy.435), channel_id=1, source_target_pairs={{0,16},{16,0},{1,17},{17,1},{2,18},{18,2},{3,19},{19,3},{4,20},{20... | collective-permute-start | bytes 786440 | tf_op jit(solution)/shard_map/ppermute | solution.py:155
  4.9 0.7 %fusion.70 = (f32[1,15,16,128]{3,2,1,0:T(8,128)}, f32[15,16,128]{2,1,0:T(8,128)S(1)}, f32[15,16,128]{2,1,0:T(8,128)}, f32[1,15,16,128]{3,2,1,0:T(8,128)S(1)}) fusion(f32[1,16,16,128]{3,2,1,0:T(8,128)S(1)} %copy-done, f32[1,16,16,128]{3,2,1,0:T(8,128)S(1)} %copy-done.1), kind=kLoop, calls=%fused_computation.184 | loop fusion | bytes 737280 | tf_op jit(solution)/shard_map/slice | solution.py:75
  5.6 0.6 %fusion.71 = (f32[1,1,16,128]{3,2,1,0:T(8,128)}, f32[1,16,128]{2,1,0:T(8,128)S(1)}, f32[1,16,128]{2,1,0:T(8,128)}, f32[1,1,16,128]{3,2,1,0:T(8,128)S(1)}) fusion(f32[1,16,16,128]{3,2,1,0:T(8,128)S(1)} %copy-done, f32[1,16,16,128]{3,2,1,0:T(8,128)S(1)} %copy-done.1), kind=kLoop, calls=%fused_computation.185 | loop fusion | bytes 49152 | tf_op jit(solution)/shard_map/slice | solution.py:75
  6.2 0.6 %iota_compare_fusion = pred[16]{0:T(512)(128)(4,1)} fusion(), kind=kLoop, calls=%fused_computation.170 | loop fusion | flops 16 | bytes 16 | tf_op jit(solution)/shard_map/eq | solution.py:101
  6.8 0.6 %broadcast_and_fusion = (pred[16]{0:T(512)(128)(4,1)}, pred[16]{0:T(512)(128)(4,1)}) fusion(pred[]{:T(512)S(6)} %eq.42), kind=kLoop, calls=%fused_computation.169 | loop fusion | flops 32 | bytes 33 | tf_op jit(solution)/shard_map/and | solution.py:99
  7.4 0.8 %slice_bitcast_fusion.29 = (f32[1,16,16,127]{3,2,1,0:T(8,128)S(1)}, f32[16,16,127]{2,1,0:T(8,128)}, f32[16,16,127]{2,1,0:T(8,128)}, f32[1,16,16,127]{3,2,1,0:T(8,128)S(1)}) fusion(f32[16,16,128]{2,1,0:T(8,128)S(1)} %bitcast.191, f32[16,16,128]{2,1,0:T(8,128)S(1)} %bitcast.193), kind=kLoop, calls=%fused_computation.179 | loop fusion | bytes 780288 | tf_op jit(solution)/shard_map/concatenate | solution.py:73
  8.8 0.7 %copy-done.23 = f32[2]{0:T(128)S(1)} copy-done((f32[2]{0:T(128)S(1)}, f32[2]{0:T(128)}, u32[]{:S(2)}) %copy-start.23) | copy-done | bytes 32
  9.5 0.7 %dynamic_slice.9 = f32[1]{0:T(128)} dynamic-slice(f32[2]{0:T(128)S(1)} %copy-done.23, s32[]{:T(128)S(6)} %select_n.189), dynamic_slice_sizes={1} | dynamic-slice | bytes 12 | tf_op jit(solution)/shard_map/dynamic_slice | solution.py:151
  10.2 0.6 %fusion.77 = (f32[1]{0:T(128)}, f32[1]{0:T(128)}) fusion(f32[2]{0:T(128)S(1)} %copy-done.22, s32[]{:T(128)S(6)} %select_n.189, s32[]{:T(128)S(6)} %select_n.193), kind=kLoop, calls=%fused_computation.191 | loop fusion | bytes 24 | tf_op jit(solution)/shard_map/dynamic_slice | solution.py:149
  10.7 0.8 %slice_bitcast_fusion.28 = (f32[1,16,15,128]{3,2,1,0:T(8,128)}, f32[16,15,128]{2,1,0:T(8,128)}, f32[16,15,128]{2,1,0:T(8,128)}, f32[1,16,15,128]{3,2,1,0:T(8,128)S(1)}) fusion(f32[16,16,128]{2,1,0:T(8,128)S(1)} %bitcast.192, f32[16,16,128]{2,1,0:T(8,128)S(1)} %bitcast.194), kind=kLoop, calls=%fused_computation.178 | loop fusion | bytes 737280 | tf_op jit(solution)/shard_map/concatenate | solution.py:74
  11.6 0.6 %pad_maximum_fusion.2 = f32[2,2,16,1,128]{4,2,3,1,0:T(8,128)} fusion(f32[1,2,16,16,128]{4,2,3,1,0:T(8,128)S(1)} %copy.436, f32[1,1,16,16,128]{4,2,3,1,0:T(8,128)S(1)} %get-tuple-element.74, f32[1,1,16,16,128]{4,2,3,1,0:T(8,128)S(1)} %get-tuple-element.75), kind=kLoop, calls=%fused_computation.151 | loop fusion | flops 16384 | bytes 557056 | tf_op jit(solution)/shard_map/slice | solution.py:160
  13.1 1.3 %collective-permute-start.1 = (f32[8,128]{1,0:T(8,128)S(1)}, f32[8,128]{1,0:T(8,128)S(1)}, u32[]{:S(2)}, u32[]{:S(2)}) collective-permute-start(f32[8,128]{1,0:T(8,128)S(1)} %reshape.705), channel_id=1, source_target_pairs={{4,0},{8,4},{12,8},{5,1},{9,5},{13,9},{6,2},{10,6},{14,10},{7,3},{... | collective-permute-start | bytes 12296 | tf_op jit(solution)/shard_map/ppermute | solution.py:13
  14.4 1.3 %collective-permute-start.2 = (f32[2,2,16,1,128]{4,2,3,1,0:T(8,128)}, f32[2,2,16,1,128]{4,2,3,1,0:T(8,128)}, u32[]{:S(2)}, u32[]{:S(2)}) collective-permute-start(f32[2,2,16,1,128]{4,2,3,1,0:T(8,128)} %pad_maximum_fusion.2), channel_id=1, source_target_pairs={{1,0},{2,1},{3,2},{5,4},{6,5},{7,6},{9,8},{10,9},{11,10},{13,12},{... | collective-permute-start | bytes 98312 | tf_op jit(solution)/shard_map/ppermute | solution.py:13
  15.7 0.7 %slice_bitcast_fusion.3 = (f32[1,15,16,128]{3,2,1,0:T(8,128)}, f32[1,15,16,128]{3,2,1,0:T(8,128)S(1)}, f32[15,16,128]{2,1,0:T(8,128)S(1)}, f32[15,16,128]{2,1,0:T(8,128)}) fusion(f32[1,2,16,16,128]{4,3,2,1,0:T(8,128)S(1)} %collective-permute-done), kind=kLoop, calls=%fused_computation.146 | loop fusion | bytes 737280 | tf_op jit(solution)/shard_map/concatenate | solution.py:75
  16.4 0.6 %slice_bitcast_fusion.10 = (f32[1,1,16,128]{3,2,1,0:T(8,128)}, f32[1,1,16,128]{3,2,1,0:T(8,128)S(1)}, f32[1,16,128]{2,1,0:T(8,128)S(1)}, f32[1,16,128]{2,1,0:T(8,128)}) fusion(f32[1,2,16,16,128]{4,3,2,1,0:T(8,128)S(1)} %collective-permute-done), kind=kLoop, calls=%fused_computation.156 | loop fusion | bytes 49152 | tf_op jit(solution)/shard_map/concatenate | solution.py:75
  17.0 1.6 %collective-permute-done.1 = f32[8,128]{1,0:T(8,128)S(1)} collective-permute-done((f32[8,128]{1,0:T(8,128)S(1)}, f32[8,128]{1,0:T(8,128)S(1)}, u32[]{:S(2)}, u32[]{:S(2)}) %collective-permute-start.1) | collective-permute-done | bytes 4128 | tf_op jit(solution)/shard_map/ppermute | solution.py:13
  20.0 0.8 %fusion.74 = (f32[1,1,16,1,128]{4,2,3,1,0:T(8,128)S(1)}, f32[1,1,16,1,128]{4,2,3,1,0:T(8,128)S(1)}, f32[1,1,16,1,128]{4,2,3,1,0:T(8,128)S(1)}, f32[1,1,16,1,128]{4,2,3,1,0:T(8,128)S(1)}) fusion(f32[2,2,16,1,128]{4,2,3,1,0:T(8,128)} %collective-permute-done.2), kind=kLoop, calls=%fused_computation.188 | loop fusion | bytes 65536 | tf_op jit(solution)/shard_map/slice | solution.py:104
  21.5 3.7 %add_select_fusion = (f32[16,16,128]{2,1,0:T(8,128)S(1)}, f32[16,16,128]{2,1,0:T(8,128)S(1)}, f32[16,16,128]{2,1,0:T(8,128)S(1)}, f32[16,16,128]{2,1,0:T(8,128)S...) fusion(f32[]{:T(128)} %bitcast.11, f32[]{:T(128)} %bitcast.10, ...), kind=kLoop, calls=%fused_computation.108 | loop fusion | flops 3407872 | bytes 3539116 | tf_op jit(solution)/shard_map/jit(_where)/select_n | solution.py:83
  25.8 2.1 %add_select_fusion.1 = (f32[16,16,128]{2,1,0:T(8,128)S(1)}, f32[16,16,128]{2,1,0:T(8,128)S(1)}, f32[16,16,128]{2,1,0:T(8,128)S(1)}) fusion(f32[16,16,128]{2,1,0:T(8,128)S(1)} %get-tuple-element.14, f32[16,16,128]{2,1,0:T(8,128)S(1)} %get-tuple-element.13, f32[16,16,128]{2,1,0:T(8,128)S(1)} %get-tuple-element.12, f32[16,16,128]{2,1,0:T(8,128)S(1)} %get-tuple-element.11, ...), kind=kLoop, calls=%fused_computation.130 | loop fusion | flops 2162688 | bytes 1179676 | tf_op jit(solution)/shard_map/jit(_where)/select_n | solution.py:83
  28.0 0.6 %slice_bitcast_fusion.9 = f32[1,1,16,128]{3,2,1,0:T(8,128)} fusion(f32[16,16,128]{2,1,0:T(8,128)S(1)} %get-tuple-element.15), kind=kLoop, calls=%fused_computation.155 | loop fusion | bytes 16384 | tf_op jit(solution)/shard_map/concatenate | solution.py:86
  28.6 2.2 %multiply_add_fusion = f32[16,16,128]{2,1,0:T(8,128)S(1)} fusion(f32[16,16,128]{2,1,0:T(8,128)S(1)} %get-tuple-element.14, f32[16,16,128]{2,1,0:T(8,128)S(1)} %get-tuple-element.5, f32[16,16,128]{2,1,0:T(8,128)S(1)} %get-tuple-element.11, f32[16,16,128]{2,1,0:T(8,128)S(1)} %get-tuple-element.13, f32[16,16,128]{2,1,0:T(8,128)S(1)} %get-tuple-element.12, ...), kind=kLoop, calls=%fused_computation.131 | loop fusion | flops 2392064 | bytes 1966092 | tf_op jit(solution)/shard_map/add | solution.py:134
  30.8 0.6 %pad_maximum_fusion.4 = f32[2,16,1,128]{3,1,2,0:T(8,128)} fusion(f32[1,16,1,128]{3,1,2,0:T(8,128)S(1)} %bitcast.211, f32[1,16,1,128]{3,1,2,0:T(8,128)S(1)} %bitcast.212), kind=kLoop, calls=%fused_computation.153 | loop fusion | flops 4096 | bytes 32768 | tf_op jit(solution)/shard_map/stack | solution.py:136
  31.4 2.2 %collective-permute-start.4 = (f32[2,16,1,128]{3,1,2,0:T(8,128)}, f32[2,16,1,128]{3,1,2,0:T(8,128)}, u32[]{:S(2)}, u32[]{:S(2)}) collective-permute-start(f32[2,16,1,128]{3,1,2,0:T(8,128)} %pad_maximum_fusion.4), channel_id=1, source_target_pairs={{0,1},{1,2},{2,3},{4,5},{5,6},{6,7},{8,9},{9,10},{10,11},{12,13},{... | collective-permute-start | bytes 49160 | tf_op jit(solution)/shard_map/ppermute | solution.py:13
  33.9 2.2 %multiply_add_fusion.3 = f32[16,16,128]{2,1,0:T(8,128)S(1)} fusion(f32[16,16,128]{2,1,0:T(8,128)S(1)} %get-tuple-element.14, f32[16,16,128]{2,1,0:T(8,128)S(1)} %get-tuple-element.8, f32[16,16,128]{2,1,0:T(8,128)S(1)} %get-tuple-element.11, f32[16,16,128]{2,1,0:T(8,128)S(1)} %get-tuple-element.13, f32[16,16,128]{2,1,0:T(8,128)S(1)} %get-tuple-element.10, ...), kind=kLoop, calls=%fused_computation.135 | loop fusion | flops 2392064 | bytes 1966092 | tf_op jit(solution)/shard_map/add | solution.py:134
  36.4 4.7 %collective-permute-start.3 = (f32[4,128]{1,0:T(4,128)S(1)}, f32[4,128]{1,0:T(4,128)S(1)}, u32[]{:S(2)}, u32[]{:S(2)}) collective-permute-start(f32[4,128]{1,0:T(4,128)S(1)} %reshape.707), channel_id=1, source_target_pairs={{0,4},{4,8},{8,12},{1,5},{5,9},{9,13},{2,6},{6,10},{10,14},{3,7},{... | collective-permute-start | bytes 6152 | tf_op jit(solution)/shard_map/ppermute | solution.py:13
  41.1 1.3 %collective-permute-done.3 = f32[4,128]{1,0:T(4,128)S(1)} collective-permute-done((f32[4,128]{1,0:T(4,128)S(1)}, f32[4,128]{1,0:T(4,128)S(1)}, u32[]{:S(2)}, u32[]{:S(2)}) %collective-permute-start.3) | collective-permute-done | bytes 2080 | tf_op jit(solution)/shard_map/ppermute | solution.py:13
  42.8 0.7 %fusion.75 = (f32[1,16,1,128]{3,1,2,0:T(8,128)S(1)}, f32[1,16,1,128]{3,1,2,0:T(8,128)S(1)}) fusion(f32[2,16,1,128]{3,1,2,0:T(8,128)} %collective-permute-done.4), kind=kLoop, calls=%fused_computation.189 | loop fusion | bytes 32768 | tf_op jit(solution)/shard_map/slice | solution.py:141
  43.5 0.7 %copy-done.11 = f32[1,1,16,128]{3,2,1,0:T(8,128)S(1)} copy-done((f32[1,1,16,128]{3,2,1,0:T(8,128)S(1)}, f32[1,1,16,128]{3,2,1,0:T(8,128)}, u32[]{:S(2)}) %copy-start.11) | copy-done | bytes 8216
  44.3 3.8 %fusion.30 = f32[1,16,16,128]{3,2,1,0:T(8,128)} fusion(f32[1,16,16,127]{3,2,1,0:T(8,128)S(1)} %get-tuple-element.71, f32[1,16,16,1]{3,2,1,0:T(8,128)S(1)} %concatenate.337, f32[1,16,15,128]{3,2,1,0:T(8,128)S(1)} %get-tuple-element.69, f32[1,16,1,128]{3,2,1,0:T(1,128)S(1)} %bitcast.208, f32[1,15,16,128]{3,2,1,0:T(8,128)S(1)} %slice_bitcast_fusion.2, ...), kind=kLoop, calls=%fused_computation.75 | loop fusion | flops 3047424 | bytes 1573052 | tf_op jit(solution)/shard_map/sub | solution.py:87
  48.1 0.6 %copy-done.10 = f32[1,1,16,128]{3,2,1,0:T(8,128)S(1)} copy-done((f32[1,1,16,128]{3,2,1,0:T(8,128)S(1)}, f32[1,1,16,128]{3,2,1,0:T(8,128)}, u32[]{:S(2)}) %copy-start.10) | copy-done | bytes 8216
  48.8 3.5 %fusion.38 = f32[1,16,16,128]{3,2,1,0:T(8,128)} fusion(f32[1,16,16,127]{3,2,1,0:T(8,128)S(1)} %get-tuple-element.70, f32[1,16,16,1]{3,2,1,0:T(8,128)S(1)} %concatenate.338, f32[1,16,15,128]{3,2,1,0:T(8,128)S(1)} %get-tuple-element.68, f32[1,16,1,128]{3,2,1,0:T(1,128)S(1)} %bitcast.207, f32[1,15,16,128]{3,2,1,0:T(8,128)S(1)} %slice_bitcast_fusion.1, ...), kind=kLoop, calls=%fused_computation.91 | loop fusion | flops 5505024 | bytes 2621628 | tf_op jit(solution)/shard_map/sub | solution.py:87
  (84 shorter events, 5.4 us)
Async XLA Ops:
  1.7 3.2 %copy-start = (f32[1,16,16,128]{3,2,1,0:T(8,128)S(1)}, f32[1,16,16,128]{3,2,1,0:T(8,128)}, u32[]{:S(2)}) copy-start(f32[1,16,16,128]{3,2,1,0:T(8,128)} %param.5) | copy-start | bytes 393220
  1.7 3.2 %copy-start.1 = (f32[1,16,16,128]{3,2,1,0:T(8,128)S(1)}, f32[1,16,16,128]{3,2,1,0:T(8,128)}, u32[]{:S(2)}) copy-start(f32[1,16,16,128]{3,2,1,0:T(8,128)} %param.4) | copy-start | bytes 393220
  1.8 9.7 %collective-permute-start = (f32[1,2,16,16,128]{4,3,2,1,0:T(8,128)S(1)}, f32[1,2,16,16,128]{4,3,2,1,0:T(8,128)S(1)}, u32[]{:S(2)}, u32[]{:S(2)}) collective-permute-start(f32[1,2,16,16,128]{4,3,2,1,0:T(8,128)S(1)} %copy.435), channel_id=1, source_target_pairs={{0,16},{16,0},{1,17},{17,1},{2,18},{18,2},{3,19},{19,3},{4,20},{20... | collective-permute-start | bytes 786440 | tf_op jit(solution)/shard_map/ppermute | solution.py:155
  8.8 0.7 %copy-start.23 = (f32[2]{0:T(128)S(1)}, f32[2]{0:T(128)}, u32[]{:S(2)}) copy-start(f32[2]{0:T(128)} %param.7) | copy-start | bytes 28
  9.5 0.7 %copy-start.22 = (f32[2]{0:T(128)S(1)}, f32[2]{0:T(128)}, u32[]{:S(2)}) copy-start(f32[2]{0:T(128)} %param.6) | copy-start | bytes 28
  13.1 5.5 %collective-permute-start.1 = (f32[8,128]{1,0:T(8,128)S(1)}, f32[8,128]{1,0:T(8,128)S(1)}, u32[]{:S(2)}, u32[]{:S(2)}) collective-permute-start(f32[8,128]{1,0:T(8,128)S(1)} %reshape.705), channel_id=1, source_target_pairs={{4,0},{8,4},{12,8},{5,1},{9,5},{13,9},{6,2},{10,6},{14,10},{7,3},{... | collective-permute-start | bytes 12296 | tf_op jit(solution)/shard_map/ppermute | solution.py:13
  14.4 5.7 %collective-permute-start.2 = (f32[2,2,16,1,128]{4,2,3,1,0:T(8,128)}, f32[2,2,16,1,128]{4,2,3,1,0:T(8,128)}, u32[]{:S(2)}, u32[]{:S(2)}) collective-permute-start(f32[2,2,16,1,128]{4,2,3,1,0:T(8,128)} %pad_maximum_fusion.2), channel_id=1, source_target_pairs={{1,0},{2,1},{3,2},{5,4},{6,5},{7,6},{9,8},{10,9},{11,10},{13,12},{... | collective-permute-start | bytes 98312 | tf_op jit(solution)/shard_map/ppermute | solution.py:13
  20.0 1.4 %copy-start.4 = (f32[15,16,128]{2,1,0:T(8,128)S(1)}, f32[15,16,128]{2,1,0:T(8,128)}, u32[]{:S(2)}) copy-start(f32[15,16,128]{2,1,0:T(8,128)} %get-tuple-element.82) | copy-start | bytes 368644
  20.8 0.6 %copy-start.6 = (f32[1,1,16,1,128]{4,2,3,1,0:T(8,128)}, f32[1,1,16,1,128]{4,2,3,1,0:T(8,128)S(1)}, u32[]{:S(2)}) copy-start(f32[1,1,16,1,128]{4,2,3,1,0:T(8,128)S(1)} %get-tuple-element.61) | copy-start | bytes 24580
  20.8 0.6 %copy-start.8 = (f32[1,1,16,1,128]{4,2,3,1,0:T(8,128)}, f32[1,1,16,1,128]{4,2,3,1,0:T(8,128)S(1)}, u32[]{:S(2)}) copy-start(f32[1,1,16,1,128]{4,2,3,1,0:T(8,128)S(1)} %get-tuple-element.62) | copy-start | bytes 24580
  20.8 0.7 %copy-start.14 = (pred[16]{0:T(512)(128)(4,1)S(1)}, pred[16]{0:T(512)(128)(4,1)}, u32[]{:S(2)}) copy-start(pred[16]{0:T(512)(128)(4,1)} %get-tuple-element.76) | copy-start | bytes 52
  20.8 0.7 %copy-start.16 = (pred[16]{0:T(512)(128)(4,1)S(1)}, pred[16]{0:T(512)(128)(4,1)}, u32[]{:S(2)}) copy-start(pred[16]{0:T(512)(128)(4,1)} %get-tuple-element.77) | copy-start | bytes 52
  20.8 0.7 %copy-start.18 = (pred[128]{0:T(512)(128)(4,1)S(1)}, pred[128]{0:T(512)(128)(4,1)}, u32[]{:S(2)}) copy-start(pred[128]{0:T(512)(128)(4,1)} %compare_and_fusion) | copy-start | bytes 388
  31.4 11.4 %collective-permute-start.4 = (f32[2,16,1,128]{3,1,2,0:T(8,128)}, f32[2,16,1,128]{3,1,2,0:T(8,128)}, u32[]{:S(2)}, u32[]{:S(2)}) collective-permute-start(f32[2,16,1,128]{3,1,2,0:T(8,128)} %pad_maximum_fusion.4), channel_id=1, source_target_pairs={{0,1},{1,2},{2,3},{4,5},{5,6},{6,7},{8,9},{9,10},{10,11},{12,13},{... | collective-permute-start | bytes 49160 | tf_op jit(solution)/shard_map/ppermute | solution.py:13
  36.4 4.7 %copy-start.19 = (pred[128]{0:T(512)(128)(4,1)S(1)}, pred[128]{0:T(512)(128)(4,1)}, u32[]{:S(2)}) copy-start(pred[128]{0:T(512)(128)(4,1)} %compare_and_fusion) | copy-start | bytes 388
  36.4 6.0 %collective-permute-start.3 = (f32[4,128]{1,0:T(4,128)S(1)}, f32[4,128]{1,0:T(4,128)S(1)}, u32[]{:S(2)}, u32[]{:S(2)}) collective-permute-start(f32[4,128]{1,0:T(4,128)S(1)} %reshape.707), channel_id=1, source_target_pairs={{0,4},{4,8},{8,12},{1,5},{5,9},{9,13},{2,6},{6,10},{10,14},{3,7},{... | collective-permute-start | bytes 6152 | tf_op jit(solution)/shard_map/ppermute | solution.py:13
  43.5 0.7 %copy-start.11 = (f32[1,1,16,128]{3,2,1,0:T(8,128)S(1)}, f32[1,1,16,128]{3,2,1,0:T(8,128)}, u32[]{:S(2)}) copy-start(f32[1,1,16,128]{3,2,1,0:T(8,128)} %slice_bitcast_fusion.9) | copy-start | bytes 24580
  43.5 0.7 %copy-start.15 = (pred[16]{0:T(512)(128)(4,1)S(1)}, pred[16]{0:T(512)(128)(4,1)}, u32[]{:S(2)}) copy-start(pred[16]{0:T(512)(128)(4,1)} %get-tuple-element.76) | copy-start | bytes 52
  43.5 0.7 %copy-start.17 = (pred[16]{0:T(512)(128)(4,1)S(1)}, pred[16]{0:T(512)(128)(4,1)}, u32[]{:S(2)}) copy-start(pred[16]{0:T(512)(128)(4,1)} %get-tuple-element.77) | copy-start | bytes 52
  43.5 0.7 %copy-start.20 = (pred[128]{0:T(512)(128)(4,1)S(1)}, pred[128]{0:T(512)(128)(4,1)}, u32[]{:S(2)}) copy-start(pred[128]{0:T(512)(128)(4,1)} %compare_and_fusion) | copy-start | bytes 388
  44.2 3.9 %copy-start.2 = (f32[1,16,15,128]{3,2,1,0:T(8,128)S(1)}, f32[1,16,15,128]{3,2,1,0:T(8,128)}, u32[]{:S(2)}) copy-start(f32[1,16,15,128]{3,2,1,0:T(8,128)} %get-tuple-element.30) | copy-start | bytes 368644
  44.2 3.9 %copy-start.3 = (f32[1,15,16,128]{3,2,1,0:T(8,128)S(1)}, f32[1,15,16,128]{3,2,1,0:T(8,128)}, u32[]{:S(2)}) copy-start(f32[1,15,16,128]{3,2,1,0:T(8,128)} %get-tuple-element.32) | copy-start | bytes 368644
  44.2 3.9 %copy-start.5 = (f32[1,15,16,128]{3,2,1,0:T(8,128)S(1)}, f32[1,15,16,128]{3,2,1,0:T(8,128)}, u32[]{:S(2)}) copy-start(f32[1,15,16,128]{3,2,1,0:T(8,128)} %get-tuple-element.18) | copy-start | bytes 368644
  44.2 3.9 %copy-start.12 = (f32[1,1,16,128]{3,2,1,0:T(8,128)S(1)}, f32[1,1,16,128]{3,2,1,0:T(8,128)}, u32[]{:S(2)}) copy-start(f32[1,1,16,128]{3,2,1,0:T(8,128)} %get-tuple-element.34) | copy-start | bytes 24580
  44.2 3.9 %copy-start.13 = (f32[1,1,16,128]{3,2,1,0:T(8,128)S(1)}, f32[1,1,16,128]{3,2,1,0:T(8,128)}, u32[]{:S(2)}) copy-start(f32[1,1,16,128]{3,2,1,0:T(8,128)} %get-tuple-element.22) | copy-start | bytes 24580
  48.1 0.7 %copy-start.10 = (f32[1,1,16,128]{3,2,1,0:T(8,128)S(1)}, f32[1,1,16,128]{3,2,1,0:T(8,128)}, u32[]{:S(2)}) copy-start(f32[1,1,16,128]{3,2,1,0:T(8,128)} %slice_bitcast_fusion.8) | copy-start | bytes 24580
  48.1 0.7 %copy-start.9 = (f32[1,1,16,1,128]{4,2,3,1,0:T(8,128)S(1)}, f32[1,1,16,1,128]{4,2,3,1,0:T(8,128)}, u32[]{:S(2)}) copy-start(f32[1,1,16,1,128]{4,2,3,1,0:T(8,128)} %copy-done.8) | copy-start | bytes 24580
  48.1 0.7 %copy-start.7 = (f32[1,1,16,1,128]{4,2,3,1,0:T(8,128)S(1)}, f32[1,1,16,1,128]{4,2,3,1,0:T(8,128)}, u32[]{:S(2)}) copy-start(f32[1,1,16,1,128]{4,2,3,1,0:T(8,128)} %copy-done.6) | copy-start | bytes 24580
  48.1 0.7 %copy-start.21 = (pred[16]{0:T(512)(128)(4,1)S(1)}, pred[16]{0:T(512)(128)(4,1)}, u32[]{:S(2)}) copy-start(pred[16]{0:T(512)(128)(4,1)} %iota_compare_fusion) | copy-start | bytes 52

commit v7 on v3

--- a/solution.py
+++ b/solution.py
@@ -81,18 +81,19 @@
     last_x, last_y = edge_masks(flux.shape[3], flux.shape[4])
     flux_x = jnp.where(last_x, 0.0, flux[:, 0])
     flux_y = jnp.where(last_y, 0.0, flux[:, 1])
-    flux_z = flux[:, 2]
-    flux_z = jnp.concatenate([flux_z[..., :-1, :, :], jnp.zeros_like(flux_z[..., :1, :, :])], -3)
+    levels = lax.broadcasted_iota(jnp.int32, (flux.shape[2], 1, 1), 0)
+    flux_z = jnp.where(levels == flux.shape[2] - 1, 0.0, flux[:, 2])
     prev_x = passed_dense(flux_x[..., -1:], "tx", 1)
     prev_y = passed_along(flux_y[..., -1:, :], "ty", 1)
-    result = jnp.concatenate([prev_x, flux_x[..., :-1]], -1) - flux_x
-    result = result + jnp.concatenate([prev_y, flux_y[..., :-1, :]], -2) - flux_y
-    result = (
-        result
-        + jnp.concatenate([jnp.zeros_like(flux_z[..., :1, :, :]), flux_z[..., :-1, :, :]], -3)
-        - flux_z
-    )
-    return (result[0][None], result[1][None])
+
+    def adjoint_one(out):
+        fx, fy, fz = flux_x[out], flux_y[out], flux_z[out]
+        res = jnp.concatenate([prev_x[out], fx[..., :-1]], -1) - fx
+        res = res + jnp.concatenate([prev_y[out], fy[..., :-1, :]], -2) - fy
+        below = jnp.where(levels == 0, 0.0, jnp.concatenate([fz[:1], fz[:-1]], 0))
+        return (res + below - fz)[None]
+
+    return (adjoint_one(0), adjoint_one(1))
 
 
 def shards(models, direction, coupling, tv_weight):

time: 30.5 us -> 30 us (0.984)
  local copies, waits for them, and re-layouts: 5.28 us -> 4.2 us
  other arithmetic: 5.58 us -> 6.29 us
    sub x1, other arithmetic: 0.16 us -> 0.88 us  [adjoint_one(): return (res + below - fz)[None]]
    slice x4 -> x6, local copies, waits for them, and re-layouts: 0.87 us -> 0.17 us  [the longest x2 0.14 us: fields(): grads = jnp.stack([dx[:, 0], dy[:, 0], dz[:, 0]], 1)]
    unnamed x10 -> x8, local copies, waits for them, and re-layouts: 1.32 us -> 0.66 us
    concatenate x0 -> x6, local copies, waits for them, and re-layouts: none -> 0.44 us  [the longest x4 0.42 us: adjoint_one(): res = jnp.concatenate([prev_x[out], fx[..., :-1]], -1) - fx]
    sub x3 -> x1, other arithmetic: 0.49 us -> 0.15 us  [couple(): cross_p.append(trace_m * e_parts[i] - me + trace_n * g_parts[i] - ng)]
    sub x1 -> x3, other arithmetic: 0.08 us -> 0.42 us  [couple(): cross_q.append(trace_m * g_parts[i] - mg)]
    reshape x3 -> x2, local copies, waits for them, and re-layouts: 0.73 us -> 0.52 us  [passed_dense(): return passed_along(rows, axis, by).reshape(array.shape)]
  transfers between devices with their start and end apart: 5 -> 5, of which waited for: 3 -> 3; matrix products, arithmetic and copies ran while one was open for 12% -> 13% of each run, Pallas kernels for 0% -> 0%
where the time goes in v7:
time: 30 us; the launch traced here: 29.7 us
  starting transfers between devices  13.2 us (44%)
  other arithmetic  6.29 us (21%)
  waiting for transfers between devices  5.08 us (17%)
  local copies, waits for them, and re-layouts  4.2 us (14%)
  between operations  0.95 us (3%)
    ppermute x4, starting transfers between devices, passed_along(): return lax.ppermute(array, axis, pairs)  11.1 us
    ppermute x1, waiting for transfers between devices, shards(): lax.ppermute(own, 'mp', [(m, (m + shift) % mp) for m in range(mp)])  2.67 us
    ppermute x4, waiting for transfers between devices, passed_along(): return lax.ppermute(array, axis, pairs)  2.41 us
    ppermute x1, starting transfers between devices, shards(): lax.ppermute(own, 'mp', [(m, (m + shift) % mp) for m in range(mp)])  2.12 us
    add x1, other arithmetic, model_split(): beta * grad_own / size + alpha * cross_q  1.48 us
    concatenate x1, other arithmetic, shards(): jnp.concatenate(weights, 0)  1.37 us
    another operation x1, other arithmetic, shards(): own = jnp.stack([models, direction], 1)  1.03 us
    sub x1, other arithmetic, adjoint_one(): return (res + below - fz)[None]  0.88 us
  transfers between devices with their start and end apart: 5, of which 3 were waited for; matrix products, arithmetic and copies ran while one was open for 13% of the time, Pallas kernels for 0%

profile of v7, /device:TPU:1, one launch (start us, length us, event | category | flops | bytes accessed | tf_op | source)
XLA Modules:
  0.0 29.7 jit_solution(16646324630490461237)
XLA Ops:
  0.6 1.0 %pad_maximum_fusion.6 = f32[1,2,16,16,128]{4,3,2,0,1:T(8,128)S(1)} fusion(f32[1,1,16,16,128]{4,3,2,0,1:T(8,128)} %bitcast.261, f32[1,1,16,16,128]{4,3,2,0,1:T(8,128)} %bitcast.264), kind=kLoop, calls=%fused_computation.47 | loop fusion | flops 65536 | bytes 524288 | tf_op jit(solution)/shard_map/stack | solution.py:106
  1.7 2.1 %collective-permute-start = (f32[1,2,16,16,128]{4,3,2,0,1:T(8,128)S(1)}, f32[1,2,16,16,128]{4,3,2,0,1:T(8,128)S(1)}, u32[]{:S(2)}, u32[]{:S(2)}) collective-permute-start(f32[1,2,16,16,128]{4,3,2,0,1:T(8,128)S(1)} %pad_maximum_fusion.6), channel_id=1, source_target_pairs={{0,16},{16,0},{1,17},{17,1},{2,18},{18,2},{3,19},{19,3},{4,20},{20... | collective-permute-start | bytes 786440 | tf_op jit(solution)/shard_map/ppermute | solution.py:109
  3.9 0.6 %copy-done.3 = f32[2]{0:T(128)S(1)} copy-done((f32[2]{0:T(128)S(1)}, f32[2]{0:T(128)}, u32[]{:S(2)}) %copy-start.3) | copy-done | bytes 32
  4.5 0.7 %dynamic_slice.9 = f32[1]{0:T(128)} dynamic-slice(f32[2]{0:T(128)S(1)} %copy-done.3, s32[]{:T(128)S(6)} %select_n.55), dynamic_slice_sizes={1} | dynamic-slice | bytes 12 | tf_op jit(solution)/shard_map/dynamic_slice | solution.py:105
  5.2 0.6 %fusion.71 = (f32[1]{0:T(128)}, f32[1]{0:T(128)}) fusion(f32[2]{0:T(128)S(1)} %copy-done.2, s32[]{:T(128)S(6)} %select_n.55, s32[]{:T(128)S(6)} %select_n.59), kind=kLoop, calls=%fused_computation.162 | loop fusion | bytes 24 | tf_op jit(solution)/shard_map/dynamic_slice | solution.py:103
  5.8 1.4 %pad_maximum_fusion.7 = f32[2]{0:T(128)S(1)} fusion(f32[1]{0:T(128)} %get-tuple-element.61, f32[1]{0:T(128)} %get-tuple-element.60), kind=kLoop, calls=%fused_computation.153 | loop fusion | flops 2 | bytes 16 | tf_op jit(solution)/shard_map/concatenate | solution.py:115
  7.1 2.7 %collective-permute-done = f32[1,2,16,16,128]{4,3,2,0,1:T(8,128)S(1)} collective-permute-done((f32[1,2,16,16,128]{4,3,2,0,1:T(8,128)S(1)}, f32[1,2,16,16,128]{4,3,2,0,1:T(8,128)S(1)}, u32[]{:S(2)}, u32[]{:S(2)}) %collective-permute-start) | collective-permute-done | bytes 262176 | tf_op jit(solution)/shard_map/ppermute | solution.py:109
  9.9 0.4 %copy.6 = f32[2,2,16,16,1]{3,2,1,0,4:T(8,128)S(1)} copy(f32[2,2,16,16,1]{4,3,2,0,1:T(8,128)S(1)} %bitcast.260) | data formatting | bytes 8192 | tf_op jit(solution)/shard_map/slice | solution.py:113
  10.4 0.1 reshape.515
  10.4 1.3 %collective-permute-start.1 = (f32[8,128]{1,0:T(8,128)S(1)}, f32[8,128]{1,0:T(8,128)S(1)}, u32[]{:S(2)}, u32[]{:S(2)}) collective-permute-start(f32[8,128]{1,0:T(8,128)S(1)} %reshape.515), channel_id=1, source_target_pairs={{4,0},{8,4},{12,8},{5,1},{9,5},{13,9},{6,2},{10,6},{14,10},{7,3},{... | collective-permute-start | bytes 12296 | tf_op jit(solution)/shard_map/ppermute | solution.py:13
  11.8 3.2 %collective-permute-start.2 = (f32[2,2,16,1,128]{4,3,2,0,1:T(1,128)S(1)}, f32[2,2,16,1,128]{4,3,2,0,1:T(1,128)S(1)}, u32[]{:S(2)}, u32[]{:S(2)}) collective-permute-start(f32[2,2,16,1,128]{4,3,2,0,1:T(1,128)S(1)} %slice.210), channel_id=1, source_target_pairs={{1,0},{2,1},{3,2},{5,4},{6,5},{7,6},{9,8},{10,9},{11,10},{13,12},{... | collective-permute-start | bytes 98312 | tf_op jit(solution)/shard_map/ppermute | solution.py:13
  15.0 0.2 slice.206
  15.2 0.1 reshape.516
  15.3 0.5 %copy.7 = f32[2,2,16,16,1]{4,3,2,0,1:T(8,128)S(1)} copy(f32[2,2,16,16,1]{3,2,1,0,4:T(8,128)S(1)} %reshape.516) | data formatting | bytes 8192 | tf_op jit(solution)/shard_map/reshape | solution.py:19
  15.8 2.1 %collective-permute-done.2 = f32[2,2,16,1,128]{4,3,2,0,1:T(1,128)S(1)} collective-permute-done((f32[2,2,16,1,128]{4,3,2,0,1:T(1,128)S(1)}, f32[2,2,16,1,128]{4,3,2,0,1:T(1,128)S(1)}, u32[]{:S(2)}, u32[]{:S(2)}) %collective-permute-start.2) | collective-permute-done | bytes 32800 | tf_op jit(solution)/shard_map/ppermute | solution.py:13
  17.8 0.2 fusion
  18.1 0.1 fusion.65
  18.2 0.5 %fusion.24 = (f32[16,16,128]{2,1,0:T(8,128)S(1)}, f32[16,16,128]{2,1,0:T(8,128)S(1)}, f32[16,16,128]{2,1,0:T(8,128)S(1)}, f32[16,16,128]{2,1,0:T(8,128)S(1)}, f3...) fusion(f32[2]{0:T(128)S(1)} %pad_maximum_fusion.7, ...), kind=kLoop, calls=%fused_computation.61 | loop fusion | flops 1998848 | bytes 3506184 | tf_op jit(solution)/shard_map/reduce_sum | solution.py:49
  18.7 0.1 fusion.57
  18.8 0.2 fusion.42
  19.0 0.2 fusion.48
  19.1 0.2 fusion.45
  19.3 1.5 %fusion.5 = (f32[1,3,16,16,128]{4,3,2,0,1:T(8,128)S(1)}, f32[1,3,16,16,128]{4,3,2,0,1:T(8,128)S(1)}) fusion(f32[1,1,16,16,128]{4,3,2,0,1:T(8,128)S(1)} %get-tuple-element.26, f32[1,1,16,16,128]{4,3,2,0,1:T(8,128)S(1)} %get-tuple-element.24, f32[1,1,16,16,128]{4,3,2,0,1:T(8,128)S(1)} %get-tuple-element.20, f32[]{:T(128)} %bitcast.3, ...), kind=kLoop, calls=%fused_computation.22 | loop fusion | flops 1572864 | bytes 3276808 | tf_op jit(solution)/shard_map/add | solution.py:79
  20.8 0.1 fusion.14
  20.9 0.2 slice_reduce_fusion
  21.3 0.1 reshape.517
  21.3 4.3 %collective-permute-start.3 = (f32[4,128]{1,0:T(4,128)S(1)}, f32[4,128]{1,0:T(4,128)S(1)}, u32[]{:S(2)}, u32[]{:S(2)}) collective-permute-start(f32[4,128]{1,0:T(4,128)S(1)} %reshape.517), channel_id=1, source_target_pairs={{0,4},{4,8},{8,12},{1,5},{5,9},{9,13},{2,6},{6,10},{10,14},{3,7},{... | collective-permute-start | bytes 6152 | tf_op jit(solution)/shard_map/ppermute | solution.py:13
  25.6 2.4 %collective-permute-start.4 = (f32[2,16,1,128]{3,2,1,0:T(1,128)S(1)}, f32[2,16,1,128]{3,2,1,0:T(1,128)S(1)}, u32[]{:S(2)}, u32[]{:S(2)}) collective-permute-start(f32[2,16,1,128]{3,2,1,0:T(1,128)S(1)} %slice.227), channel_id=1, source_target_pairs={{0,1},{1,2},{2,3},{4,5},{5,6},{6,7},{8,9},{9,10},{10,11},{12,13},{... | collective-permute-start | bytes 49160 | tf_op jit(solution)/shard_map/ppermute | solution.py:13
  28.1 0.2 concatenate.95
  28.3 0.2 concatenate.94
  28.5 0.3 %collective-permute-done.4 = f32[2,16,1,128]{3,2,1,0:T(1,128)S(1)} collective-permute-done((f32[2,16,1,128]{3,2,1,0:T(1,128)S(1)}, f32[2,16,1,128]{3,2,1,0:T(1,128)S(1)}, u32[]{:S(2)}, u32[]{:S(2)}) %collective-permute-start.4) | collective-permute-done | bytes 16416 | tf_op jit(solution)/shard_map/ppermute | solution.py:13
  28.8 0.9 %slice_subtract_fusion.1 = (f32[1,16,16,128]{3,2,1,0:T(8,128)}, f32[1,16,16,128]{3,2,1,0:T(8,128)}) fusion(f32[2,16,16,128]{3,2,1,0:T(8,128)S(1)} %get-tuple-element.37, f32[1,16,16,127]{3,2,1,0:T(8,128)S(1)} %slice_bitcast_fusion.1, f32[1,16,16,1]{3,2,1,0:T(8,128)S(1)} %concatenate.95, f32[1,16,15,128]{3,2,1,0:T(8,128)S(1)} %slice_bitcast_fusion, ...), kind=kLoop, calls=%fused_computation.69 | loop fusion | flops 589824 | bytes 1835024 | tf_op jit(solution)/shard_map/sub | solution.py:94
  (31 shorter events, 0.4 us)
Async XLA Ops:
  0.6 9.2 %copy-start = (f32[1,16,16,128]{3,2,1,0:T(8,128)S(1)}, f32[1,16,16,128]{3,2,1,0:T(8,128)}, u32[]{:S(2)}) copy-start(f32[1,16,16,128]{3,2,1,0:T(8,128)} %param.5) | copy-start | bytes 393220
  0.6 9.2 %copy-start.1 = (f32[1,16,16,128]{3,2,1,0:T(8,128)S(1)}, f32[1,16,16,128]{3,2,1,0:T(8,128)}, u32[]{:S(2)}) copy-start(f32[1,16,16,128]{3,2,1,0:T(8,128)} %param.4) | copy-start | bytes 393220
  1.7 8.1 %collective-permute-start = (f32[1,2,16,16,128]{4,3,2,0,1:T(8,128)S(1)}, f32[1,2,16,16,128]{4,3,2,0,1:T(8,128)S(1)}, u32[]{:S(2)}, u32[]{:S(2)}) collective-permute-start(f32[1,2,16,16,128]{4,3,2,0,1:T(8,128)S(1)} %pad_maximum_fusion.6), channel_id=1, source_target_pairs={{0,16},{16,0},{1,17},{17,1},{2,18},{18,2},{3,19},{19,3},{4,20},{20... | collective-permute-start | bytes 786440 | tf_op jit(solution)/shard_map/ppermute | solution.py:109
  3.9 0.7 %copy-start.3 = (f32[2]{0:T(128)S(1)}, f32[2]{0:T(128)}, u32[]{:S(2)}) copy-start(f32[2]{0:T(128)} %param.7) | copy-start | bytes 28
  4.5 0.7 %copy-start.2 = (f32[2]{0:T(128)S(1)}, f32[2]{0:T(128)}, u32[]{:S(2)}) copy-start(f32[2]{0:T(128)} %param.6) | copy-start | bytes 28
  10.4 4.8 %collective-permute-start.1 = (f32[8,128]{1,0:T(8,128)S(1)}, f32[8,128]{1,0:T(8,128)S(1)}, u32[]{:S(2)}, u32[]{:S(2)}) collective-permute-start(f32[8,128]{1,0:T(8,128)S(1)} %reshape.515), channel_id=1, source_target_pairs={{4,0},{8,4},{12,8},{5,1},{9,5},{13,9},{6,2},{10,6},{14,10},{7,3},{... | collective-permute-start | bytes 12296 | tf_op jit(solution)/shard_map/ppermute | solution.py:13
  11.8 6.1 %collective-permute-start.2 = (f32[2,2,16,1,128]{4,3,2,0,1:T(1,128)S(1)}, f32[2,2,16,1,128]{4,3,2,0,1:T(1,128)S(1)}, u32[]{:S(2)}, u32[]{:S(2)}) collective-permute-start(f32[2,2,16,1,128]{4,3,2,0,1:T(1,128)S(1)} %slice.210), channel_id=1, source_target_pairs={{1,0},{2,1},{3,2},{5,4},{6,5},{7,6},{9,8},{10,9},{11,10},{13,12},{... | collective-permute-start | bytes 98312 | tf_op jit(solution)/shard_map/ppermute | solution.py:13
  21.3 6.7 %collective-permute-start.3 = (f32[4,128]{1,0:T(4,128)S(1)}, f32[4,128]{1,0:T(4,128)S(1)}, u32[]{:S(2)}, u32[]{:S(2)}) collective-permute-start(f32[4,128]{1,0:T(4,128)S(1)} %reshape.517), channel_id=1, source_target_pairs={{0,4},{4,8},{8,12},{1,5},{5,9},{9,13},{2,6},{6,10},{10,14},{3,7},{... | collective-permute-start | bytes 6152 | tf_op jit(solution)/shard_map/ppermute | solution.py:13
  25.6 3.2 %collective-permute-start.4 = (f32[2,16,1,128]{3,2,1,0:T(1,128)S(1)}, f32[2,16,1,128]{3,2,1,0:T(1,128)S(1)}, u32[]{:S(2)}, u32[]{:S(2)}) collective-permute-start(f32[2,16,1,128]{3,2,1,0:T(1,128)S(1)} %slice.227), channel_id=1, source_target_pairs={{0,1},{1,2},{2,3},{4,5},{5,6},{6,7},{8,9},{9,10},{10,11},{12,13},{... | collective-permute-start | bytes 49160 | tf_op jit(solution)/shard_map/ppermute | solution.py:13

commit v8 on v7

--- a/solution.py
+++ b/solution.py
@@ -47,7 +47,7 @@
     for i in range(3):
         for j in range(3):
             rows.append(jnp.sum(wts * dirs[:, i] * grads[:, j], 0))
-    return jnp.stack(rows, 0)
+    return rows
 
 
 def couple(moms, grad_own, dir_own):
@@ -68,11 +68,13 @@
     return (jnp.stack(cross_q, axis=-4), jnp.stack(cross_p, axis=-4))
 
 
-def model_split(every, rim_x, rim_y, alpha, beta, weights):
-    grads, dirs = fields(every, rim_x, rim_y)
-    moms = moments(grads, dirs, weights)
-    grad_own = grads[0]
-    dir_own = dirs[0]
+def model_split(own, own_rims, others, other_rims, alpha, beta, own_weights, other_weights):
+    own_grads, own_dirs = fields(own, *own_rims)
+    own_moms = moments(own_grads, own_dirs, own_weights)
+    other_grads, other_dirs = fields(others, *other_rims)
+    moms = [a + b for a, b in zip(own_moms, moments(other_grads, other_dirs, other_weights))]
+    grad_own = own_grads[0]
+    dir_own = own_dirs[0]
     cross_q, cross_p = couple(moms, grad_own, dir_own)
     size = jnp.sqrt(jnp.sum(grad_own * grad_own, 0) + EPS_SQ)[None]
     flux = jnp.stack(
@@ -104,15 +106,24 @@
     alpha = own_weights[0]
     beta = lax.dynamic_slice_in_dim(tv_weight, member * local, local)[0]
     own = jnp.stack([models, direction], 1)
-    tiles, weights = [own], [own_weights]
+    width_y, width_x = own.shape[3], own.shape[4]
+    rim_x = passed_dense(own[..., :1], "tx", -1)
+    rim_y = passed_along(own[..., :1, :], "ty", -1)
+    lanes = jnp.pad(rim_x[..., 0], ((0, 0),) * 3 + ((0, width_x - width_y),))[..., None, :]
+    packed = jnp.concatenate([own, rim_y, lanes], -2)
+    tiles, weights = [], []
     for shift in range(1, mp):
-        tiles.append(lax.ppermute(own, "mp", [(m, (m + shift) % mp) for m in range(mp)]))
+        tiles.append(lax.ppermute(packed, "mp", [(m, (m + shift) % mp) for m in range(mp)]))
         source = (member - shift) % mp
         weights.append(lax.dynamic_slice_in_dim(coupling, source * local, local))
     every = jnp.concatenate(tiles, 0)
-    rim_x = passed_dense(every[..., :1], "tx", -1)
-    rim_y = passed_along(every[..., :1, :], "ty", -1)
-    return model_split(every, rim_x, rim_y, alpha, beta, jnp.concatenate(weights, 0))
+    others = every[..., :width_y, :]
+    other_rim_y = every[..., width_y : width_y + 1, :]
+    other_rim_x = every[..., width_y + 1, :width_y][..., None]
+    return model_split(
+        own, (rim_x, rim_y), others, (other_rim_x, other_rim_y),
+        alpha, beta, own_weights, jnp.concatenate(weights, 0),
+    )
 
 
 def solution(mesh):

time: 30 us -> 39 us (1.30)
  waiting for transfers between devices: 5.08 us -> 11.5 us
  other arithmetic: 6.29 us -> 10.3 us
  starting transfers between devices: 13.2 us -> 12.4 us
  local copies, waits for them, and re-layouts: 4.2 us -> 3.52 us
    ppermute x1, waiting for transfers between devices: 2.67 us -> 9.19 us  [shards(): lax.ppermute(packed, 'mp', [(m, (m + shift) % mp) for m in range(mp)])]
    sub x1 -> x2, other arithmetic: 0.15 us -> 3.11 us  [couple(): cross_p.append(trace_m * e_parts[i] - me + trace_n * g_parts[i] - ng)]
    sub x3 -> x2, other arithmetic: 0.42 us -> 3.07 us  [couple(): cross_q.append(trace_m * g_parts[i] - mg)]
    concatenate x2 -> x1, other arithmetic: 1.4 us -> 0.04 us  [shards(): packed = jnp.concatenate([own, rim_y, lanes], -2)]
    slice x0 -> x1, other arithmetic: none -> 1.15 us  [shards(): rim_x = passed_dense(own[..., :1], 'tx', -1)]
    another operation x1 -> x3, other arithmetic: 1.03 us -> 0.16 us  [shards(): own = jnp.stack([models, direction], 1)]
    ppermute x1, starting transfers between devices: 2.12 us -> 1.3 us  [shards(): lax.ppermute(packed, 'mp', [(m, (m + shift) % mp) for m in range(mp)])]
    slice x5 -> x1, local copies, waits for them, and re-layouts: 0.64 us -> 0.02 us  [shards(): other_rim_x = every[..., width_y + 1, :width_y][..., None]]
  transfers between devices with their start and end apart: 5 -> 5, of which waited for: 3 -> 3; matrix products, arithmetic and copies ran while one was open for 13% -> 5% of each run, Pallas kernels for 0% -> 0%
where the time goes in v8:
time: 39 us; the launch traced here: 38.7 us
  starting transfers between devices  12.4 us (32%)
  waiting for transfers between devices  11.5 us (29%)
  other arithmetic  10.3 us (26%)
  local copies, waits for them, and re-layouts  3.52 us (9%)
  between operations  1 us (3%)
    ppermute x4, starting transfers between devices, passed_along(): return lax.ppermute(array, axis, pairs)  11.1 us
    ppermute x1, waiting for transfers between devices, shards(): lax.ppermute(packed, 'mp', [(m, (m + shift) % mp) for m in range(mp)])  9.19 us
    sub x2, other arithmetic, couple(): cross_p.append(trace_m * e_parts[i] - me + trace_n * g_parts[i] - ng)  3.11 us
    sub x2, other arithmetic, couple(): cross_q.append(trace_m * g_parts[i] - mg)  3.07 us
    ppermute x4, waiting for transfers between devices, passed_along(): return lax.ppermute(array, axis, pairs)  2.3 us
    add x1, other arithmetic, model_split(): beta * grad_own / size + alpha * cross_q  1.4 us
    ppermute x1, starting transfers between devices, shards(): lax.ppermute(packed, 'mp', [(m, (m + shift) % mp) for m in range(mp)])  1.3 us
    slice x1, other arithmetic, shards(): rim_x = passed_dense(own[..., :1], 'tx', -1)  1.15 us
  transfers between devices with their start and end apart: 5, of which 3 were waited for; matrix products, arithmetic and copies ran while one was open for 5% of the time, Pallas kernels for 0%

profile of v8, /device:TPU:1, one launch (start us, length us, event | category | flops | bytes accessed | tf_op | source)
XLA Modules:
  0.0 38.7 jit_solution(15273365860577270138)
XLA Ops:
  0.6 1.1 %fusion.5 = f32[2,16,16]{2,1,0:T(8,128)S(1)} fusion(f32[1,1,16,16,128]{4,3,2,0,1:T(8,128)} %bitcast.35, f32[1,1,16,16,128]{4,3,2,0,1:T(8,128)} %bitcast.42), kind=kLoop, calls=%fused_computation.28 | loop fusion | flops 512 | bytes 264192 | tf_op jit(solution)/shard_map/slice | solution.py:110
  1.8 0.1 reshape.1224
  1.9 1.3 %collective-permute-start = (f32[4,128]{1,0:T(4,128)S(1)}, f32[4,128]{1,0:T(4,128)S(1)}, u32[]{:S(2)}, u32[]{:S(2)}) collective-permute-start(f32[4,128]{1,0:T(4,128)S(1)} %reshape.1224), channel_id=1, source_target_pairs={{4,0},{8,4},{12,8},{5,1},{9,5},{13,9},{6,2},{10,6},{14,10},{7,3},{... | collective-permute-start | bytes 6152 | tf_op jit(solution)/shard_map/ppermute | solution.py:13
  3.2 1.9 %collective-permute-start.1 = (f32[1,2,16,1,128]{4,3,2,0,1:T(1,128)S(1)}, f32[1,2,16,1,128]{4,3,2,0,1:T(1,128)S(1)}, u32[]{:S(2)}, u32[]{:S(2)}) collective-permute-start(f32[1,2,16,1,128]{4,3,2,0,1:T(1,128)S(1)} %fusion.35), channel_id=1, source_target_pairs={{1,0},{2,1},{3,2},{5,4},{6,5},{7,6},{9,8},{10,9},{11,10},{13,12},{... | collective-permute-start | bytes 49160 | tf_op jit(solution)/shard_map/ppermute | solution.py:13
  5.3 0.0 copy-start.3
  5.3 0.6 %copy-done.3 = f32[2]{0:T(128)S(1)} copy-done((f32[2]{0:T(128)S(1)}, f32[2]{0:T(128)}, u32[]{:S(2)}) %copy-start.3) | copy-done | bytes 32
  5.9 0.6 %dynamic_slice.9 = f32[1]{0:T(128)} dynamic-slice(f32[2]{0:T(128)S(1)} %copy-done.3, s32[]{:T(128)S(6)} %select_n.77), dynamic_slice_sizes={1} | dynamic-slice | bytes 12 | tf_op jit(solution)/shard_map/dynamic_slice | solution.py:107
  6.5 0.0 copy-done.2
  6.6 0.6 %fusion.40 = (f32[1]{0:T(128)}, f32[1]{0:T(128)}) fusion(f32[2]{0:T(128)S(1)} %copy-done.2, s32[]{:T(128)S(6)} %select_n.77, s32[]{:T(128)S(6)} %select_n.81), kind=kLoop, calls=%fused_computation.118 | loop fusion | bytes 24 | tf_op jit(solution)/shard_map/dynamic_slice | solution.py:105
  7.2 0.1 squeeze_reshape.3
  7.2 1.9 %collective-permute-done.1 = f32[1,2,16,1,128]{4,3,2,0,1:T(1,128)S(1)} collective-permute-done((f32[1,2,16,1,128]{4,3,2,0,1:T(1,128)S(1)}, f32[1,2,16,1,128]{4,3,2,0,1:T(1,128)S(1)}, u32[]{:S(2)}, u32[]{:S(2)}) %collective-permute-start.1) | collective-permute-done | bytes 16416 | tf_op jit(solution)/shard_map/ppermute | solution.py:13
  9.2 1.3 %collective-permute-start.2 = (f32[1,2,16,18,128]{4,3,2,0,1:T(8,128)S(1)}, f32[1,2,16,18,128]{4,3,2,0,1:T(8,128)S(1)}, u32[]{:S(2)}, u32[]{:S(2)}) collective-permute-start(f32[1,2,16,18,128]{4,3,2,0,1:T(8,128)S(1)} %pad_maximum_fusion.2), channel_id=1, source_target_pairs={{0,16},{16,0},{1,17},{17,1},{2,18},{18,2},{3,19},{19,3},{4,20},{20... | collective-permute-start | bytes 884744 | tf_op jit(solution)/shard_map/ppermute | solution.py:116
  10.5 0.1 fusion.3
  10.7 0.2 concatenate.149
  10.9 9.2 %collective-permute-done.2 = f32[1,2,16,18,128]{4,3,2,0,1:T(8,128)S(1)} collective-permute-done((f32[1,2,16,18,128]{4,3,2,0,1:T(8,128)S(1)}, f32[1,2,16,18,128]{4,3,2,0,1:T(8,128)S(1)}, u32[]{:S(2)}, u32[]{:S(2)}) %collective-permute-start.2) | collective-permute-done | bytes 294944 | tf_op jit(solution)/shard_map/ppermute | solution.py:116
  20.1 0.3 copy.8
  20.3 0.1 slice.227
  20.5 0.3 fusion.16
  20.8 1.6 %add_subtract_fusion.2 = f32[1,1,16,16,128]{4,3,2,0,1:T(8,128)S(1)} fusion(f32[1,2,16,16,128]{4,3,2,0,1:T(8,128)S(1)} %get-tuple-element.35, f32[1,2,16,16,128]{4,3,2,0,1:T(8,128)S(1)} %get-tuple-element.36, f32[1,2,15,16,128]{4,3,2,0,1:T(8,128)S(1)} %slice_subtract_fusion.1, f32[]{:T(128)} %bitcast.4, f32[]{:T(128)} %bitcast.3, ...), kind=kLoop, calls=%fused_computation.95 | loop fusion | flops 1998848 | bytes 1671176 | tf_op jit(solution)/shard_map/sub | solution.py:67
  22.3 1.6 %add_subtract_fusion = f32[1,1,16,16,128]{4,3,2,0,1:T(8,128)S(1)} fusion(f32[1,2,16,16,128]{4,3,2,0,1:T(8,128)S(1)} %get-tuple-element.35, f32[1,2,16,16,128]{4,3,2,0,1:T(8,128)S(1)} %get-tuple-element.36, f32[1,2,15,16,128]{4,3,2,0,1:T(8,128)S(1)} %slice_subtract_fusion.1, f32[]{:T(128)} %bitcast.4, f32[]{:T(128)} %bitcast.3, ...), kind=kLoop, calls=%fused_computation.93 | loop fusion | flops 1998848 | bytes 1671176 | tf_op jit(solution)/shard_map/sub | solution.py:67
  23.9 1.5 %add_subtract_fusion.5 = (f32[1,1,16,16,128]{4,3,2,0,1:T(8,128)S(1)}, f32[1,1,16,16,128]{4,3,2,0,1:T(8,128)S(1)}, f32[1,1,16,16,128]{4,3,2,0,1:T(8,128)S(1)}, f3...) fusion(f32[1,2,16,16,128]{4,3,2,0,1:T(8,128)S(1)} %get-tuple-el, ...), kind=kLoop, calls=%fused_computation.102 | loop fusion | flops 1507328 | bytes 2195464 | tf_op jit(solution)/shard_map/sub | solution.py:66
  25.4 1.6 %add_subtract_fusion.3 = (f32[1,1,16,16,128]{4,3,2,0,1:T(8,128)S(1)}, f32[1,1,16,16,128]{4,3,2,0,1:T(8,128)S(1)}, f32[1,1,16,16,128]{4,3,2,0,1:T(8,128)S(1)}) fusion(f32[1,2,16,16,128]{4,3,2,0,1:T(8,128)S(1)} %get-tuple-element.36, f32[1,2,16,16,128]{4,3,2,0,1:T(8,128)S(1)} %get-tuple-element.35, f32[]{:T(128)} %bitcast.4, f32[]{:T(128)} %bitcast.3, ...), kind=kLoop, calls=%fused_computation.100 | loop fusion | flops 2621440 | bytes 1933320 | tf_op jit(solution)/shard_map/sub | solution.py:66
  27.0 1.4 %fusion = (f32[1,3,16,16,128]{4,3,2,0,1:T(8,128)S(1)}, f32[1,3,16,16,128]{4,3,2,0,1:T(8,128)S(1)}) fusion(f32[1,1,16,16,128]{4,3,2,0,1:T(8,128)S(1)} %get-tuple-element.4, f32[1,1,16,16,128]{4,3,2,0,1:T(8,128)S(1)} %get-tuple-element.3, f32[1,1,16,16,128]{4,3,2,0,1:T(8,128)S(1)} %get-tuple-element.2, f32[1,1,16,16,128]{4,3,2,0,1:T(8,128)S(1)} %get-tuple-element.28, ...), kind=kLoop, calls=%fused_computation.20 | loop fusion | flops 1572864 | bytes 2490376 | tf_op jit(solution)/shard_map/add | solution.py:81
  28.5 0.1 fusion.9
  28.6 0.2 slice_reduce_fusion
  29.0 0.1 reshape.1225
  29.0 3.5 %collective-permute-start.3 = (f32[4,128]{1,0:T(4,128)S(1)}, f32[4,128]{1,0:T(4,128)S(1)}, u32[]{:S(2)}, u32[]{:S(2)}) collective-permute-start(f32[4,128]{1,0:T(4,128)S(1)} %reshape.1225), channel_id=1, source_target_pairs={{0,4},{4,8},{8,12},{1,5},{5,9},{9,13},{2,6},{6,10},{10,14},{3,7},{... | collective-permute-start | bytes 6152 | tf_op jit(solution)/shard_map/ppermute | solution.py:13
  32.6 4.4 %collective-permute-start.4 = (f32[2,16,1,128]{3,2,1,0:T(1,128)S(1)}, f32[2,16,1,128]{3,2,1,0:T(1,128)S(1)}, u32[]{:S(2)}, u32[]{:S(2)}) collective-permute-start(f32[2,16,1,128]{3,2,1,0:T(1,128)S(1)} %slice.245), channel_id=1, source_target_pairs={{0,1},{1,2},{2,3},{4,5},{5,6},{6,7},{8,9},{9,10},{10,11},{12,13},{... | collective-permute-start | bytes 49160 | tf_op jit(solution)/shard_map/ppermute | solution.py:13
  37.0 0.2 concatenate.150
  37.2 0.2 concatenate.151
  37.4 0.4 %collective-permute-done.4 = f32[2,16,1,128]{3,2,1,0:T(1,128)S(1)} collective-permute-done((f32[2,16,1,128]{3,2,1,0:T(1,128)S(1)}, f32[2,16,1,128]{3,2,1,0:T(1,128)S(1)}, u32[]{:S(2)}, u32[]{:S(2)}) %collective-permute-start.4) | collective-permute-done | bytes 16416 | tf_op jit(solution)/shard_map/ppermute | solution.py:13
  37.8 0.9 %slice_subtract_fusion.2 = (f32[1,16,16,128]{3,2,1,0:T(8,128)}, f32[1,16,16,128]{3,2,1,0:T(8,128)}) fusion(f32[2,16,16,128]{3,2,1,0:T(8,128)S(1)} %get-tuple-element.10, f32[1,16,16,127]{3,2,1,0:T(8,128)S(1)} %slice_bitcast_fusion.1, f32[1,16,16,1]{3,2,1,0:T(8,128)S(1)} %concatenate.151, f32[1,16,15,128]{3,2,1,0:T(8,128)S(1)} %slice_bitcast_fusion, ...), kind=kLoop, calls=%fused_computation.75 | loop fusion | flops 589824 | bytes 1835024 | tf_op jit(solution)/shard_map/sub | solution.py:96
  (30 shorter events, 0.4 us)
Async XLA Ops:
  0.6 2.6 %copy-start = (f32[1,16,16,128]{3,2,1,0:T(8,128)S(1)}, f32[1,16,16,128]{3,2,1,0:T(8,128)}, u32[]{:S(2)}) copy-start(f32[1,16,16,128]{3,2,1,0:T(8,128)} %param.4) | copy-start | bytes 393220
  0.6 2.6 %copy-start.1 = (f32[1,16,16,128]{3,2,1,0:T(8,128)S(1)}, f32[1,16,16,128]{3,2,1,0:T(8,128)}, u32[]{:S(2)}) copy-start(f32[1,16,16,128]{3,2,1,0:T(8,128)} %param.5) | copy-start | bytes 393220
  1.9 5.3 %collective-permute-start = (f32[4,128]{1,0:T(4,128)S(1)}, f32[4,128]{1,0:T(4,128)S(1)}, u32[]{:S(2)}, u32[]{:S(2)}) collective-permute-start(f32[4,128]{1,0:T(4,128)S(1)} %reshape.1224), channel_id=1, source_target_pairs={{4,0},{8,4},{12,8},{5,1},{9,5},{13,9},{6,2},{10,6},{14,10},{7,3},{... | collective-permute-start | bytes 6152 | tf_op jit(solution)/shard_map/ppermute | solution.py:13
  3.2 5.9 %collective-permute-start.1 = (f32[1,2,16,1,128]{4,3,2,0,1:T(1,128)S(1)}, f32[1,2,16,1,128]{4,3,2,0,1:T(1,128)S(1)}, u32[]{:S(2)}, u32[]{:S(2)}) collective-permute-start(f32[1,2,16,1,128]{4,3,2,0,1:T(1,128)S(1)} %fusion.35), channel_id=1, source_target_pairs={{1,0},{2,1},{3,2},{5,4},{6,5},{7,6},{9,8},{10,9},{11,10},{13,12},{... | collective-permute-start | bytes 49160 | tf_op jit(solution)/shard_map/ppermute | solution.py:13
  5.3 0.7 %copy-start.3 = (f32[2]{0:T(128)S(1)}, f32[2]{0:T(128)}, u32[]{:S(2)}) copy-start(f32[2]{0:T(128)} %param.7) | copy-start | bytes 28
  5.9 0.7 %copy-start.2 = (f32[2]{0:T(128)S(1)}, f32[2]{0:T(128)}, u32[]{:S(2)}) copy-start(f32[2]{0:T(128)} %param.6) | copy-start | bytes 28
  9.2 10.9 %collective-permute-start.2 = (f32[1,2,16,18,128]{4,3,2,0,1:T(8,128)S(1)}, f32[1,2,16,18,128]{4,3,2,0,1:T(8,128)S(1)}, u32[]{:S(2)}, u32[]{:S(2)}) collective-permute-start(f32[1,2,16,18,128]{4,3,2,0,1:T(8,128)S(1)} %pad_maximum_fusion.2), channel_id=1, source_target_pairs={{0,16},{16,0},{1,17},{17,1},{2,18},{18,2},{3,19},{19,3},{4,20},{20... | collective-permute-start | bytes 884744 | tf_op jit(solution)/shard_map/ppermute | solution.py:116
  29.0 7.9 %collective-permute-start.3 = (f32[4,128]{1,0:T(4,128)S(1)}, f32[4,128]{1,0:T(4,128)S(1)}, u32[]{:S(2)}, u32[]{:S(2)}) collective-permute-start(f32[4,128]{1,0:T(4,128)S(1)} %reshape.1225), channel_id=1, source_target_pairs={{0,4},{4,8},{8,12},{1,5},{5,9},{9,13},{2,6},{6,10},{10,14},{3,7},{... | collective-permute-start | bytes 6152 | tf_op jit(solution)/shard_map/ppermute | solution.py:13
  32.6 5.2 %collective-permute-start.4 = (f32[2,16,1,128]{3,2,1,0:T(1,128)S(1)}, f32[2,16,1,128]{3,2,1,0:T(1,128)S(1)}, u32[]{:S(2)}, u32[]{:S(2)}) collective-permute-start(f32[2,16,1,128]{3,2,1,0:T(1,128)S(1)} %slice.245), channel_id=1, source_target_pairs={{0,1},{1,2},{2,3},{4,5},{5,6},{6,7},{8,9},{9,10},{10,11},{12,13},{... | collective-permute-start | bytes 49160 | tf_op jit(solution)/shard_map/ppermute | solution.py:13

commit v9 on v7

--- a/solution.py
+++ b/solution.py
@@ -75,9 +75,8 @@
     dir_own = dirs[0]
     cross_q, cross_p = couple(moms, grad_own, dir_own)
     size = jnp.sqrt(jnp.sum(grad_own * grad_own, 0) + EPS_SQ)[None]
-    flux = jnp.stack(
-        [beta * grad_own / size + alpha * cross_q, beta * dir_own / size + alpha * cross_p], 0
-    )
+    scale = beta / size
+    flux = jnp.stack([grad_own * scale + alpha * cross_q, dir_own * scale + alpha * cross_p], 0)
     last_x, last_y = edge_masks(flux.shape[3], flux.shape[4])
     flux_x = jnp.where(last_x, 0.0, flux[:, 0])
     flux_y = jnp.where(last_y, 0.0, flux[:, 1])

time: 30 us -> 30 us (level)
    div x0 -> x1, other arithmetic: none -> 0.71 us  [model_split(): scale = beta / size]
    add x1, other arithmetic: 1.48 us -> 0.77 us  [model_split(): grad_own * scale + alpha * cross_q]
where the time goes in v9:
time: 30 us; the launch traced here: 29.7 us
  starting transfers between devices  13.2 us (44%)
  other arithmetic  6.26 us (21%)
  waiting for transfers between devices  5.08 us (17%)
  local copies, waits for them, and re-layouts  4.2 us (14%)
  between operations  0.94 us (3%)
    ppermute x4, starting transfers between devices, passed_along(): return lax.ppermute(array, axis, pairs)  11.1 us
    ppermute x1, waiting for transfers between devices, shards(): lax.ppermute(own, 'mp', [(m, (m + shift) % mp) for m in range(mp)])  2.67 us
    ppermute x4, waiting for transfers between devices, passed_along(): return lax.ppermute(array, axis, pairs)  2.41 us
    ppermute x1, starting transfers between devices, shards(): lax.ppermute(own, 'mp', [(m, (m + shift) % mp) for m in range(mp)])  2.12 us
    concatenate x1, other arithmetic, shards(): jnp.concatenate(weights, 0)  1.37 us
    another operation x1, other arithmetic, shards(): own = jnp.stack([models, direction], 1)  1.03 us
    sub x1, other arithmetic, adjoint_one(): return (res + below - fz)[None]  0.88 us
    add x1, other arithmetic, model_split(): grad_own * scale + alpha * cross_q  0.77 us
  transfers between devices with their start and end apart: 5, of which 3 were waited for; matrix products, arithmetic and copies ran while one was open for 13% of the time, Pallas kernels for 0%

profile of v9, /device:TPU:1, one launch (start us, length us, event | category | flops | bytes accessed | tf_op | source)
XLA Modules:
  0.0 29.7 jit_solution(12428988680624340095)
XLA Ops:
  0.6 1.0 %pad_maximum_fusion.6 = f32[1,2,16,16,128]{4,3,2,0,1:T(8,128)S(1)} fusion(f32[1,1,16,16,128]{4,3,2,0,1:T(8,128)} %bitcast.261, f32[1,1,16,16,128]{4,3,2,0,1:T(8,128)} %bitcast.264), kind=kLoop, calls=%fused_computation.46 | loop fusion | flops 65536 | bytes 524288 | tf_op jit(solution)/shard_map/stack | solution.py:105
  1.7 2.1 %collective-permute-start = (f32[1,2,16,16,128]{4,3,2,0,1:T(8,128)S(1)}, f32[1,2,16,16,128]{4,3,2,0,1:T(8,128)S(1)}, u32[]{:S(2)}, u32[]{:S(2)}) collective-permute-start(f32[1,2,16,16,128]{4,3,2,0,1:T(8,128)S(1)} %pad_maximum_fusion.6), channel_id=1, source_target_pairs={{0,16},{16,0},{1,17},{17,1},{2,18},{18,2},{3,19},{19,3},{4,20},{20... | collective-permute-start | bytes 786440 | tf_op jit(solution)/shard_map/ppermute | solution.py:108
  3.9 0.6 %copy-done.3 = f32[2]{0:T(128)S(1)} copy-done((f32[2]{0:T(128)S(1)}, f32[2]{0:T(128)}, u32[]{:S(2)}) %copy-start.3) | copy-done | bytes 32
  4.5 0.7 %dynamic_slice.9 = f32[1]{0:T(128)} dynamic-slice(f32[2]{0:T(128)S(1)} %copy-done.3, s32[]{:T(128)S(6)} %select_n.57), dynamic_slice_sizes={1} | dynamic-slice | bytes 12 | tf_op jit(solution)/shard_map/dynamic_slice | solution.py:104
  5.2 0.6 %fusion.70 = (f32[1]{0:T(128)}, f32[1]{0:T(128)}) fusion(f32[2]{0:T(128)S(1)} %copy-done.2, s32[]{:T(128)S(6)} %select_n.57, s32[]{:T(128)S(6)} %select_n.59), kind=kLoop, calls=%fused_computation.161 | loop fusion | bytes 24 | tf_op jit(solution)/shard_map/dynamic_slice | solution.py:102
  5.8 1.4 %pad_maximum_fusion.7 = f32[2]{0:T(128)S(1)} fusion(f32[1]{0:T(128)} %get-tuple-element.61, f32[1]{0:T(128)} %get-tuple-element.60), kind=kLoop, calls=%fused_computation.152 | loop fusion | flops 2 | bytes 16 | tf_op jit(solution)/shard_map/concatenate | solution.py:114
  7.1 2.7 %collective-permute-done = f32[1,2,16,16,128]{4,3,2,0,1:T(8,128)S(1)} collective-permute-done((f32[1,2,16,16,128]{4,3,2,0,1:T(8,128)S(1)}, f32[1,2,16,16,128]{4,3,2,0,1:T(8,128)S(1)}, u32[]{:S(2)}, u32[]{:S(2)}) %collective-permute-start) | collective-permute-done | bytes 262176 | tf_op jit(solution)/shard_map/ppermute | solution.py:108
  9.9 0.4 %copy.6 = f32[2,2,16,16,1]{3,2,1,0,4:T(8,128)S(1)} copy(f32[2,2,16,16,1]{4,3,2,0,1:T(8,128)S(1)} %bitcast.260) | data formatting | bytes 8192 | tf_op jit(solution)/shard_map/slice | solution.py:112
  10.4 0.1 reshape.517
  10.4 1.3 %collective-permute-start.1 = (f32[8,128]{1,0:T(8,128)S(1)}, f32[8,128]{1,0:T(8,128)S(1)}, u32[]{:S(2)}, u32[]{:S(2)}) collective-permute-start(f32[8,128]{1,0:T(8,128)S(1)} %reshape.517), channel_id=1, source_target_pairs={{4,0},{8,4},{12,8},{5,1},{9,5},{13,9},{6,2},{10,6},{14,10},{7,3},{... | collective-permute-start | bytes 12296 | tf_op jit(solution)/shard_map/ppermute | solution.py:13
  11.8 3.2 %collective-permute-start.2 = (f32[2,2,16,1,128]{4,3,2,0,1:T(1,128)S(1)}, f32[2,2,16,1,128]{4,3,2,0,1:T(1,128)S(1)}, u32[]{:S(2)}, u32[]{:S(2)}) collective-permute-start(f32[2,2,16,1,128]{4,3,2,0,1:T(1,128)S(1)} %slice.210), channel_id=1, source_target_pairs={{1,0},{2,1},{3,2},{5,4},{6,5},{7,6},{9,8},{10,9},{11,10},{13,12},{... | collective-permute-start | bytes 98312 | tf_op jit(solution)/shard_map/ppermute | solution.py:13
  15.0 0.2 slice.206
  15.3 0.5 %copy.7 = f32[2,2,16,16,1]{4,3,2,0,1:T(8,128)S(1)} copy(f32[2,2,16,16,1]{3,2,1,0,4:T(8,128)S(1)} %reshape.518) | data formatting | bytes 8192 | tf_op jit(solution)/shard_map/reshape | solution.py:19
  15.8 2.1 %collective-permute-done.2 = f32[2,2,16,1,128]{4,3,2,0,1:T(1,128)S(1)} collective-permute-done((f32[2,2,16,1,128]{4,3,2,0,1:T(1,128)S(1)}, f32[2,2,16,1,128]{4,3,2,0,1:T(1,128)S(1)}, u32[]{:S(2)}, u32[]{:S(2)}) %collective-permute-start.2) | collective-permute-done | bytes 32800 | tf_op jit(solution)/shard_map/ppermute | solution.py:13
  17.8 0.2 fusion
  18.1 0.1 fusion.64
  18.2 0.5 %fusion.23 = (f32[16,16,128]{2,1,0:T(8,128)S(1)}, f32[16,16,128]{2,1,0:T(8,128)S(1)}, f32[16,16,128]{2,1,0:T(8,128)S(1)}, f32[16,16,128]{2,1,0:T(8,128)S(1)}, f3...) fusion(f32[2]{0:T(128)S(1)} %pad_maximum_fusion.7, ...), kind=kLoop, calls=%fused_computation.60 | loop fusion | flops 1998848 | bytes 3506184 | tf_op jit(solution)/shard_map/reduce_sum | solution.py:49
  18.7 0.1 fusion.56
  18.7 0.2 fusion.41
  18.9 0.2 fusion.47
  19.1 0.2 fusion.44
  19.3 0.7 %rsqrt_multiply_fusion = f32[16,16,128]{2,1,0:T(8,128)S(1)} fusion(f32[16,16,128]{2,1,0:T(8,128)S(1)} %multiply_reduce_fusion, f32[]{:T(128)} %bitcast.2), kind=kLoop, calls=%fused_computation.145 | loop fusion | flops 65536 | bytes 262148 | tf_op jit(solution)/shard_map/div | solution.py:78
  20.0 0.8 %fusion.4 = (f32[1,3,16,16,128]{4,3,2,0,1:T(8,128)S(1)}, f32[1,3,16,16,128]{4,3,2,0,1:T(8,128)S(1)}) fusion(f32[1,1,16,16,128]{4,3,2,0,1:T(8,128)S(1)} %get-tuple-element.26, f32[1,1,16,16,128]{4,3,2,0,1:T(8,128)S(1)} %get-tuple-element.24, f32[1,1,16,16,128]{4,3,2,0,1:T(8,128)S(1)} %get-tuple-element.20, f32[]{:T(128)} %bitcast.3, ...), kind=kLoop, calls=%fused_computation.21 | loop fusion | flops 1376256 | bytes 3276804 | tf_op jit(solution)/shard_map/add | solution.py:79
  20.8 0.1 fusion.13
  20.9 0.2 slice_reduce_fusion
  21.2 0.1 reshape.519
  21.3 4.3 %collective-permute-start.3 = (f32[4,128]{1,0:T(4,128)S(1)}, f32[4,128]{1,0:T(4,128)S(1)}, u32[]{:S(2)}, u32[]{:S(2)}) collective-permute-start(f32[4,128]{1,0:T(4,128)S(1)} %reshape.519), channel_id=1, source_target_pairs={{0,4},{4,8},{8,12},{1,5},{5,9},{9,13},{2,6},{6,10},{10,14},{3,7},{... | collective-permute-start | bytes 6152 | tf_op jit(solution)/shard_map/ppermute | solution.py:13
  25.6 2.4 %collective-permute-start.4 = (f32[2,16,1,128]{3,2,1,0:T(1,128)S(1)}, f32[2,16,1,128]{3,2,1,0:T(1,128)S(1)}, u32[]{:S(2)}, u32[]{:S(2)}) collective-permute-start(f32[2,16,1,128]{3,2,1,0:T(1,128)S(1)} %slice.227), channel_id=1, source_target_pairs={{0,1},{1,2},{2,3},{4,5},{5,6},{6,7},{8,9},{9,10},{10,11},{12,13},{... | collective-permute-start | bytes 49160 | tf_op jit(solution)/shard_map/ppermute | solution.py:13
  28.0 0.2 concatenate.95
  28.3 0.2 concatenate.94
  28.5 0.3 %collective-permute-done.4 = f32[2,16,1,128]{3,2,1,0:T(1,128)S(1)} collective-permute-done((f32[2,16,1,128]{3,2,1,0:T(1,128)S(1)}, f32[2,16,1,128]{3,2,1,0:T(1,128)S(1)}, u32[]{:S(2)}, u32[]{:S(2)}) %collective-permute-start.4) | collective-permute-done | bytes 16416 | tf_op jit(solution)/shard_map/ppermute | solution.py:13
  28.8 0.9 %slice_subtract_fusion.1 = (f32[1,16,16,128]{3,2,1,0:T(8,128)}, f32[1,16,16,128]{3,2,1,0:T(8,128)}) fusion(f32[2,16,16,128]{3,2,1,0:T(8,128)S(1)} %get-tuple-element.37, f32[1,16,16,127]{3,2,1,0:T(8,128)S(1)} %slice_bitcast_fusion.1, f32[1,16,16,1]{3,2,1,0:T(8,128)S(1)} %concatenate.95, f32[1,16,15,128]{3,2,1,0:T(8,128)S(1)} %slice_bitcast_fusion, ...), kind=kLoop, calls=%fused_computation.68 | loop fusion | flops 589824 | bytes 1835024 | tf_op jit(solution)/shard_map/sub | solution.py:93
  (31 shorter events, 0.4 us)
Async XLA Ops:
  0.6 9.2 %copy-start = (f32[1,16,16,128]{3,2,1,0:T(8,128)S(1)}, f32[1,16,16,128]{3,2,1,0:T(8,128)}, u32[]{:S(2)}) copy-start(f32[1,16,16,128]{3,2,1,0:T(8,128)} %param.5) | copy-start | bytes 393220
  0.6 9.2 %copy-start.1 = (f32[1,16,16,128]{3,2,1,0:T(8,128)S(1)}, f32[1,16,16,128]{3,2,1,0:T(8,128)}, u32[]{:S(2)}) copy-start(f32[1,16,16,128]{3,2,1,0:T(8,128)} %param.4) | copy-start | bytes 393220
  1.7 8.1 %collective-permute-start = (f32[1,2,16,16,128]{4,3,2,0,1:T(8,128)S(1)}, f32[1,2,16,16,128]{4,3,2,0,1:T(8,128)S(1)}, u32[]{:S(2)}, u32[]{:S(2)}) collective-permute-start(f32[1,2,16,16,128]{4,3,2,0,1:T(8,128)S(1)} %pad_maximum_fusion.6), channel_id=1, source_target_pairs={{0,16},{16,0},{1,17},{17,1},{2,18},{18,2},{3,19},{19,3},{4,20},{20... | collective-permute-start | bytes 786440 | tf_op jit(solution)/shard_map/ppermute | solution.py:108
  3.9 0.7 %copy-start.3 = (f32[2]{0:T(128)S(1)}, f32[2]{0:T(128)}, u32[]{:S(2)}) copy-start(f32[2]{0:T(128)} %param.7) | copy-start | bytes 28
  4.5 0.7 %copy-start.2 = (f32[2]{0:T(128)S(1)}, f32[2]{0:T(128)}, u32[]{:S(2)}) copy-start(f32[2]{0:T(128)} %param.6) | copy-start | bytes 28
  10.4 4.8 %collective-permute-start.1 = (f32[8,128]{1,0:T(8,128)S(1)}, f32[8,128]{1,0:T(8,128)S(1)}, u32[]{:S(2)}, u32[]{:S(2)}) collective-permute-start(f32[8,128]{1,0:T(8,128)S(1)} %reshape.517), channel_id=1, source_target_pairs={{4,0},{8,4},{12,8},{5,1},{9,5},{13,9},{6,2},{10,6},{14,10},{7,3},{... | collective-permute-start | bytes 12296 | tf_op jit(solution)/shard_map/ppermute | solution.py:13
  11.8 6.1 %collective-permute-start.2 = (f32[2,2,16,1,128]{4,3,2,0,1:T(1,128)S(1)}, f32[2,2,16,1,128]{4,3,2,0,1:T(1,128)S(1)}, u32[]{:S(2)}, u32[]{:S(2)}) collective-permute-start(f32[2,2,16,1,128]{4,3,2,0,1:T(1,128)S(1)} %slice.210), channel_id=1, source_target_pairs={{1,0},{2,1},{3,2},{5,4},{6,5},{7,6},{9,8},{10,9},{11,10},{13,12},{... | collective-permute-start | bytes 98312 | tf_op jit(solution)/shard_map/ppermute | solution.py:13
  21.3 6.7 %collective-permute-start.3 = (f32[4,128]{1,0:T(4,128)S(1)}, f32[4,128]{1,0:T(4,128)S(1)}, u32[]{:S(2)}, u32[]{:S(2)}) collective-permute-start(f32[4,128]{1,0:T(4,128)S(1)} %reshape.519), channel_id=1, source_target_pairs={{0,4},{4,8},{8,12},{1,5},{5,9},{9,13},{2,6},{6,10},{10,14},{3,7},{... | collective-permute-start | bytes 6152 | tf_op jit(solution)/shard_map/ppermute | solution.py:13
  25.6 3.2 %collective-permute-start.4 = (f32[2,16,1,128]{3,2,1,0:T(1,128)S(1)}, f32[2,16,1,128]{3,2,1,0:T(1,128)S(1)}, u32[]{:S(2)}, u32[]{:S(2)}) collective-permute-start(f32[2,16,1,128]{3,2,1,0:T(1,128)S(1)} %slice.227), channel_id=1, source_target_pairs={{0,1},{1,2},{2,3},{4,5},{5,6},{6,7},{8,9},{9,10},{10,11},{12,13},{... | collective-permute-start | bytes 49160 | tf_op jit(solution)/shard_map/ppermute | solution.py:13

commit v10 on v7

--- a/solution.py
+++ b/solution.py
@@ -104,14 +104,22 @@
     alpha = own_weights[0]
     beta = lax.dynamic_slice_in_dim(tv_weight, member * local, local)[0]
     own = jnp.stack([models, direction], 1)
-    tiles, weights = [own], [own_weights]
+    rim_x = passed_dense(own[..., :1], "tx", -1)
+    rim_y = passed_along(own[..., :1, :], "ty", -1)
+    rims = jnp.concatenate([rim_x.reshape(-1), rim_y.reshape(-1)])
+    rims = rims.reshape(-1, 128) if rims.size % 128 == 0 else rims
+    tiles, rims_x, rims_y, weights = [own], [rim_x], [rim_y], [own_weights]
     for shift in range(1, mp):
-        tiles.append(lax.ppermute(own, "mp", [(m, (m + shift) % mp) for m in range(mp)]))
+        pairs = [(m, (m + shift) % mp) for m in range(mp)]
+        tiles.append(lax.ppermute(own, "mp", pairs))
+        theirs = lax.ppermute(rims, "mp", pairs).reshape(-1)
+        rims_x.append(theirs[: rim_x.size].reshape(rim_x.shape))
+        rims_y.append(theirs[rim_x.size :].reshape(rim_y.shape))
         source = (member - shift) % mp
         weights.append(lax.dynamic_slice_in_dim(coupling, source * local, local))
     every = jnp.concatenate(tiles, 0)
-    rim_x = passed_dense(every[..., :1], "tx", -1)
-    rim_y = passed_along(every[..., :1, :], "ty", -1)
+    rim_x = jnp.concatenate(rims_x, 0)
+    rim_y = jnp.concatenate(rims_y, 0)
     return model_split(every, rim_x, rim_y, alpha, beta, jnp.concatenate(weights, 0))
 
 

time: 30 us -> 29.4 us (0.980)
  waiting for transfers between devices: 5.08 us -> 2.08 us
  starting transfers between devices: 13.2 us -> 16.1 us
  local copies, waits for them, and re-layouts: 4.2 us -> 3.71 us
    ppermute x1 -> x2, starting transfers between devices: 2.12 us -> 4.24 us  [the longest x1 2.78 us: shards(): tiles.append(lax.ppermute(own, 'mp', pairs))]
    ppermute x4, waiting for transfers between devices: 2.41 us -> 0.86 us  [passed_along(): return lax.ppermute(array, axis, pairs)]
    ppermute x1 -> x2, waiting for transfers between devices: 2.67 us -> 1.22 us  [the longest x1 1.22 us: shards(): theirs = lax.ppermute(rims, 'mp', pairs).reshape(-1)]
    ppermute x4, starting transfers between devices: 11.1 us -> 11.8 us  [passed_along(): return lax.ppermute(array, axis, pairs)]
    concatenate x0 -> x1, local copies, waits for them, and re-layouts: none -> 0.45 us  [shards(): rim_x = jnp.concatenate(rims_x, 0)]
    reshape x2 -> x1, local copies, waits for them, and re-layouts: 0.52 us -> 0.08 us  [passed_dense(): return passed_along(rows, axis, by).reshape(array.shape)]
    slice x2, local copies, waits for them, and re-layouts: 0.45 us -> 0.01 us  [the longest x1 0.01 us: shards(): rims_y.append(theirs[rim_x.size:].reshape(rim_y.shape))]
    another operation x1 -> x2, other arithmetic: 1.03 us -> 0.94 us  [shards(): own = jnp.stack([models, direction], 1)]
  transfers between devices with their start and end apart: 5 -> 6, of which waited for: 3 -> 3; matrix products, arithmetic and copies ran while one was open for 13% -> 13% of each run, Pallas kernels for 0% -> 0%
where the time goes in v10:
time: 29.4 us; the launch traced here: 29.2 us
  starting transfers between devices  16.1 us (55%)
  other arithmetic  6.32 us (21%)
  local copies, waits for them, and re-layouts  3.71 us (13%)
  waiting for transfers between devices  2.08 us (7%)
  between operations  0.99 us (3%)
    ppermute x4, starting transfers between devices, passed_along(): return lax.ppermute(array, axis, pairs)  11.8 us
    ppermute x1, starting transfers between devices, shards(): tiles.append(lax.ppermute(own, 'mp', pairs))  2.78 us
    ppermute x1, starting transfers between devices, shards(): theirs = lax.ppermute(rims, 'mp', pairs).reshape(-1)  1.46 us
    add x1, other arithmetic, model_split(): beta * grad_own / size + alpha * cross_q  1.46 us
    concatenate x1, other arithmetic, shards(): jnp.concatenate(weights, 0)  1.38 us
    ppermute x1, waiting for transfers between devices, shards(): theirs = lax.ppermute(rims, 'mp', pairs).reshape(-1)  1.22 us
    another operation x2, other arithmetic, shards(): own = jnp.stack([models, direction], 1)  0.94 us
    sub x1, other arithmetic, adjoint_one(): return (res + below - fz)[None]  0.88 us
  transfers between devices with their start and end apart: 6, of which 3 were waited for; matrix products, arithmetic and copies ran while one was open for 13% of the time, Pallas kernels for 0%

profile of v10, /device:TPU:1, one launch (start us, length us, event | category | flops | bytes accessed | tf_op | source)
XLA Modules:
  0.0 29.2 jit_solution(11151300363726261875)
XLA Ops:
  0.6 0.9 %fusion.67 = f32[1,2,16,1,128]{4,3,2,0,1:T(1,128)S(1)} fusion(f32[1,1,16,16,128]{4,3,2,0,1:T(8,128)} %bitcast.260, f32[1,1,16,16,128]{4,3,2,0,1:T(8,128)} %bitcast.265), kind=kLoop, calls=%fused_computation.159 | loop fusion | flops 4096 | bytes 278528 | tf_op jit(solution)/shard_map/stack | solution.py:106
  1.6 1.9 %collective-permute-start.2 = (f32[1,2,16,1,128]{4,3,2,0,1:T(1,128)S(1)}, f32[1,2,16,1,128]{4,3,2,0,1:T(1,128)S(1)}, u32[]{:S(2)}, u32[]{:S(2)}) collective-permute-start(f32[1,2,16,1,128]{4,3,2,0,1:T(1,128)S(1)} %fusion.67), channel_id=1, source_target_pairs={{1,0},{2,1},{3,2},{5,4},{6,5},{7,6},{9,8},{10,9},{11,10},{13,12},{... | collective-permute-start | bytes 49160 | tf_op jit(solution)/shard_map/ppermute | solution.py:13
  3.5 0.1 fusion.10
  3.7 0.1 reshape.532
  3.8 1.3 %collective-permute-start.1 = (f32[4,128]{1,0:T(4,128)S(1)}, f32[4,128]{1,0:T(4,128)S(1)}, u32[]{:S(2)}, u32[]{:S(2)}) collective-permute-start(f32[4,128]{1,0:T(4,128)S(1)} %reshape.532), channel_id=1, source_target_pairs={{4,0},{8,4},{12,8},{5,1},{9,5},{13,9},{6,2},{10,6},{14,10},{7,3},{... | collective-permute-start | bytes 6152 | tf_op jit(solution)/shard_map/ppermute | solution.py:13
  5.1 2.8 %collective-permute-start = (f32[1,2,16,16,128]{4,3,2,0,1:T(8,128)S(1)}, f32[1,2,16,16,128]{4,3,2,0,1:T(8,128)S(1)}, u32[]{:S(2)}, u32[]{:S(2)}) collective-permute-start(f32[1,2,16,16,128]{4,3,2,0,1:T(8,128)S(1)} %pad_maximum_fusion.5), channel_id=1, source_target_pairs={{0,16},{16,0},{1,17},{17,1},{2,18},{18,2},{3,19},{19,3},{4,20},{20... | collective-permute-start | bytes 786440 | tf_op jit(solution)/shard_map/ppermute | solution.py:114
  7.9 0.6 %copy-done.2 = f32[2]{0:T(128)S(1)} copy-done((f32[2]{0:T(128)S(1)}, f32[2]{0:T(128)}, u32[]{:S(2)}) %copy-start.2) | copy-done | bytes 32
  8.6 0.6 %fusion.74 = (f32[1]{0:T(128)}, f32[1]{0:T(128)}) fusion(f32[2]{0:T(128)S(1)} %copy-done.2, s32[]{:T(128)S(6)} %select_n.55, s32[]{:T(128)S(6)} %select_n.59), kind=kLoop, calls=%fused_computation.171 | loop fusion | bytes 24 | tf_op jit(solution)/shard_map/dynamic_slice | solution.py:103
  9.2 0.5 %collective-permute-done.1 = f32[4,128]{1,0:T(4,128)S(1)} collective-permute-done((f32[4,128]{1,0:T(4,128)S(1)}, f32[4,128]{1,0:T(4,128)S(1)}, u32[]{:S(2)}, u32[]{:S(2)}) %collective-permute-start.1) | collective-permute-done | bytes 2080 | tf_op jit(solution)/shard_map/ppermute | solution.py:13
  9.7 1.5 %collective-permute-start.3 = (f32[36,128]{1,0:T(8,128)S(1)}, f32[36,128]{1,0:T(8,128)S(1)}, u32[]{:S(2)}, u32[]{:S(2)}) collective-permute-start(f32[36,128]{1,0:T(8,128)S(1)} %maximum_bitcast_fusion), channel_id=1, source_target_pairs={{0,16},{16,0},{1,17},{17,1},{2,18},{18,2},{3,19},{19,3},{4,20},{20... | collective-permute-start | bytes 55304 | tf_op jit(solution)/shard_map/ppermute | solution.py:115
  11.2 1.4 %pad_maximum_fusion.8 = f32[2]{0:T(128)S(1)} fusion(f32[1]{0:T(128)} %get-tuple-element.61, f32[1]{0:T(128)} %get-tuple-element.60), kind=kLoop, calls=%fused_computation.162 | loop fusion | flops 2 | bytes 16 | tf_op jit(solution)/shard_map/concatenate | solution.py:123
  12.6 0.6 %dynamic_slice.9 = f32[1]{0:T(128)} dynamic-slice(f32[2]{0:T(128)S(1)} %copy-done.3, s32[]{:T(128)S(6)} %select_n.55), dynamic_slice_sizes={1} | dynamic-slice | bytes 12 | tf_op jit(solution)/shard_map/dynamic_slice | solution.py:105
  13.1 0.1 reshape.533
  13.2 1.2 %collective-permute-done.3 = f32[36,128]{1,0:T(8,128)S(1)} collective-permute-done((f32[36,128]{1,0:T(8,128)S(1)}, f32[36,128]{1,0:T(8,128)S(1)}, u32[]{:S(2)}, u32[]{:S(2)}) %collective-permute-start.3) | collective-permute-done | bytes 18464 | tf_op jit(solution)/shard_map/ppermute | solution.py:115
  14.4 0.1 reshape.536
  14.5 0.4 %copy.6 = f32[2,2,16,16,1]{4,3,2,0,1:T(8,128)S(1)} copy(f32[2,2,16,16,1]{3,2,1,4,0:T(8,128)S(1)} %pad_maximum_fusion.7) | data formatting | bytes 8192 | tf_op jit(solution)/shard_map/concatenate | solution.py:121
  15.0 0.2 slice.216
  15.4 0.3 fusion
  15.7 0.5 %fusion.26 = (f32[16,16,128]{2,1,0:T(8,128)S(1)}, f32[16,16,128]{2,1,0:T(8,128)S(1)}, f32[16,16,128]{2,1,0:T(8,128)S(1)}, f32[16,16,128]{2,1,0:T(8,128)S(1)}, f3...) fusion(f32[2]{0:T(128)S(1)} %pad_maximum_fusion.8, ...), kind=kLoop, calls=%fused_computation.67 | loop fusion | flops 1998848 | bytes 3506184 | tf_op jit(solution)/shard_map/reduce_sum | solution.py:49
  16.4 0.1 fusion.44
  16.5 0.1 fusion.50
  16.6 0.1 fusion.47
  16.8 1.5 %fusion.5 = (f32[1,3,16,16,128]{4,3,2,0,1:T(8,128)S(1)}, f32[1,3,16,16,128]{4,3,2,0,1:T(8,128)S(1)}) fusion(f32[1,1,16,16,128]{4,3,2,0,1:T(8,128)S(1)} %get-tuple-element.26, f32[1,1,16,16,128]{4,3,2,0,1:T(8,128)S(1)} %get-tuple-element.24, f32[1,1,16,16,128]{4,3,2,0,1:T(8,128)S(1)} %get-tuple-element.20, f32[]{:T(128)} %bitcast.7, ...), kind=kLoop, calls=%fused_computation.22 | loop fusion | flops 1572864 | bytes 3276808 | tf_op jit(solution)/shard_map/add | solution.py:79
  18.3 0.1 fusion.16
  18.4 0.2 slice_reduce_fusion
  18.7 0.1 reshape.538
  18.8 4.5 %collective-permute-start.4 = (f32[4,128]{1,0:T(4,128)S(1)}, f32[4,128]{1,0:T(4,128)S(1)}, u32[]{:S(2)}, u32[]{:S(2)}) collective-permute-start(f32[4,128]{1,0:T(4,128)S(1)} %reshape.538), channel_id=1, source_target_pairs={{0,4},{4,8},{8,12},{1,5},{5,9},{9,13},{2,6},{6,10},{10,14},{3,7},{... | collective-permute-start | bytes 6152 | tf_op jit(solution)/shard_map/ppermute | solution.py:13
  23.3 4.1 %collective-permute-start.5 = (f32[2,16,1,128]{3,2,1,0:T(1,128)S(1)}, f32[2,16,1,128]{3,2,1,0:T(1,128)S(1)}, u32[]{:S(2)}, u32[]{:S(2)}) collective-permute-start(f32[2,16,1,128]{3,2,1,0:T(1,128)S(1)} %slice.241), channel_id=1, source_target_pairs={{0,1},{1,2},{2,3},{4,5},{5,6},{6,7},{8,9},{9,10},{10,11},{12,13},{... | collective-permute-start | bytes 49160 | tf_op jit(solution)/shard_map/ppermute | solution.py:13
  27.5 0.2 concatenate.107
  27.7 0.2 concatenate.106
  28.0 0.3 %collective-permute-done.5 = f32[2,16,1,128]{3,2,1,0:T(1,128)S(1)} collective-permute-done((f32[2,16,1,128]{3,2,1,0:T(1,128)S(1)}, f32[2,16,1,128]{3,2,1,0:T(1,128)S(1)}, u32[]{:S(2)}, u32[]{:S(2)}) %collective-permute-start.5) | collective-permute-done | bytes 16416 | tf_op jit(solution)/shard_map/ppermute | solution.py:13
  28.3 0.9 %slice_subtract_fusion.1 = (f32[1,16,16,128]{3,2,1,0:T(8,128)}, f32[1,16,16,128]{3,2,1,0:T(8,128)}) fusion(f32[2,16,16,128]{3,2,1,0:T(8,128)S(1)} %get-tuple-element.37, f32[1,16,16,127]{3,2,1,0:T(8,128)S(1)} %slice_bitcast_fusion.1, f32[1,16,16,1]{3,2,1,0:T(8,128)S(1)} %concatenate.107, f32[1,16,15,128]{3,2,1,0:T(8,128)S(1)} %slice_bitcast_fusion, ...), kind=kLoop, calls=%fused_computation.75 | loop fusion | flops 589824 | bytes 1835024 | tf_op jit(solution)/shard_map/sub | solution.py:94
  (38 shorter events, 0.6 us)
Async XLA Ops:
  0.6 2.9 %copy-start = (f32[1,16,16,128]{3,2,1,0:T(8,128)S(1)}, f32[1,16,16,128]{3,2,1,0:T(8,128)}, u32[]{:S(2)}) copy-start(f32[1,16,16,128]{3,2,1,0:T(8,128)} %param.4) | copy-start | bytes 393220
  0.6 2.9 %copy-start.1 = (f32[1,16,16,128]{3,2,1,0:T(8,128)S(1)}, f32[1,16,16,128]{3,2,1,0:T(8,128)}, u32[]{:S(2)}) copy-start(f32[1,16,16,128]{3,2,1,0:T(8,128)} %param.5) | copy-start | bytes 393220
  1.6 8.1 %collective-permute-start.2 = (f32[1,2,16,1,128]{4,3,2,0,1:T(1,128)S(1)}, f32[1,2,16,1,128]{4,3,2,0,1:T(1,128)S(1)}, u32[]{:S(2)}, u32[]{:S(2)}) collective-permute-start(f32[1,2,16,1,128]{4,3,2,0,1:T(1,128)S(1)} %fusion.67), channel_id=1, source_target_pairs={{1,0},{2,1},{3,2},{5,4},{6,5},{7,6},{9,8},{10,9},{11,10},{13,12},{... | collective-permute-start | bytes 49160 | tf_op jit(solution)/shard_map/ppermute | solution.py:13
  3.8 5.9 %collective-permute-start.1 = (f32[4,128]{1,0:T(4,128)S(1)}, f32[4,128]{1,0:T(4,128)S(1)}, u32[]{:S(2)}, u32[]{:S(2)}) collective-permute-start(f32[4,128]{1,0:T(4,128)S(1)} %reshape.532), channel_id=1, source_target_pairs={{4,0},{8,4},{12,8},{5,1},{9,5},{13,9},{6,2},{10,6},{14,10},{7,3},{... | collective-permute-start | bytes 6152 | tf_op jit(solution)/shard_map/ppermute | solution.py:13
  5.1 9.9 %collective-permute-start = (f32[1,2,16,16,128]{4,3,2,0,1:T(8,128)S(1)}, f32[1,2,16,16,128]{4,3,2,0,1:T(8,128)S(1)}, u32[]{:S(2)}, u32[]{:S(2)}) collective-permute-start(f32[1,2,16,16,128]{4,3,2,0,1:T(8,128)S(1)} %pad_maximum_fusion.5), channel_id=1, source_target_pairs={{0,16},{16,0},{1,17},{17,1},{2,18},{18,2},{3,19},{19,3},{4,20},{20... | collective-permute-start | bytes 786440 | tf_op jit(solution)/shard_map/ppermute | solution.py:114
  7.9 0.7 %copy-start.2 = (f32[2]{0:T(128)S(1)}, f32[2]{0:T(128)}, u32[]{:S(2)}) copy-start(f32[2]{0:T(128)} %param.6) | copy-start | bytes 28
  9.7 4.7 %collective-permute-start.3 = (f32[36,128]{1,0:T(8,128)S(1)}, f32[36,128]{1,0:T(8,128)S(1)}, u32[]{:S(2)}, u32[]{:S(2)}) collective-permute-start(f32[36,128]{1,0:T(8,128)S(1)} %maximum_bitcast_fusion), channel_id=1, source_target_pairs={{0,16},{16,0},{1,17},{17,1},{2,18},{18,2},{3,19},{19,3},{4,20},{20... | collective-permute-start | bytes 55304 | tf_op jit(solution)/shard_map/ppermute | solution.py:115
  11.2 1.4 %copy-start.3 = (f32[2]{0:T(128)S(1)}, f32[2]{0:T(128)}, u32[]{:S(2)}) copy-start(f32[2]{0:T(128)} %param.7) | copy-start | bytes 28
  18.8 8.7 %collective-permute-start.4 = (f32[4,128]{1,0:T(4,128)S(1)}, f32[4,128]{1,0:T(4,128)S(1)}, u32[]{:S(2)}, u32[]{:S(2)}) collective-permute-start(f32[4,128]{1,0:T(4,128)S(1)} %reshape.538), channel_id=1, source_target_pairs={{0,4},{4,8},{8,12},{1,5},{5,9},{9,13},{2,6},{6,10},{10,14},{3,7},{... | collective-permute-start | bytes 6152 | tf_op jit(solution)/shard_map/ppermute | solution.py:13
  23.3 5.0 %collective-permute-start.5 = (f32[2,16,1,128]{3,2,1,0:T(1,128)S(1)}, f32[2,16,1,128]{3,2,1,0:T(1,128)S(1)}, u32[]{:S(2)}, u32[]{:S(2)}) collective-permute-start(f32[2,16,1,128]{3,2,1,0:T(1,128)S(1)} %slice.241), channel_id=1, source_target_pairs={{0,1},{1,2},{2,3},{4,5},{5,6},{6,7},{8,9},{9,10},{10,11},{12,13},{... | collective-permute-start | bytes 49160 | tf_op jit(solution)/shard_map/ppermute | solution.py:13

commit v11 on v10

--- a/solution.py
+++ b/solution.py
@@ -2,6 +2,10 @@
 import jax.numpy as jnp
 from jax import lax
 from jax.sharding import PartitionSpec as P
+from jax.experimental import pallas as pl
+from jax.experimental.pallas import tpu as pltpu
+
+INTERPRET = False
 
 EPS_SQ = 0.25
 SYM_PAIRS = ((0, 0), (1, 1), (2, 2), (0, 1), (0, 2), (1, 2))
@@ -68,32 +72,106 @@
     return (jnp.stack(cross_q, axis=-4), jnp.stack(cross_p, axis=-4))
 
 
+def flux_kernel(scal_ref, flag_ref, ev_ref, rx_ref, ry_ref, pg_ref, ph_ref, ex_ref, ey_ref):
+    count, _, depth, width_y, width_x = ev_ref.shape
+    lane = lax.broadcasted_iota(jnp.int32, (width_y, width_x), 1)
+    row = lax.broadcasted_iota(jnp.int32, (width_y, width_x), 0)
+    last_x = (lane == width_x - 1) & (flag_ref[0] == 1)
+    last_y = (row == width_y - 1) & (flag_ref[1] == 1)
+    alpha = scal_ref[0]
+    beta = scal_ref[1]
+
+    def diffs(k, c, z):
+        here = ev_ref[k, c, z]
+        above = ev_ref[k, c, jnp.minimum(z + 1, depth - 1)]
+        next_x = jnp.where(lane == width_x - 1, rx_ref[k, c, z], pltpu.roll(here, width_x - 1, 1))
+        next_y = jnp.where(row == width_y - 1, ry_ref[k, c, z], pltpu.roll(here, width_y - 1, 0))
+        dx = jnp.where(last_x, 0.0, next_x - here)
+        dy = jnp.where(last_y, 0.0, next_y - here)
+        return (dx, dy, above - here)
+
+    def adjoint(flux, below, z):
+        fx = jnp.where(last_x, 0.0, flux[0])
+        fy = jnp.where(last_y, 0.0, flux[1])
+        fz = jnp.where(z == depth - 1, 0.0, flux[2])
+        res = jnp.where(lane == 0, 0.0, pltpu.roll(fx, 1, 1)) - fx
+        res = res + jnp.where(row == 0, 0.0, pltpu.roll(fy, 1, 0)) - fy
+        return (res + below - fz, fz)
+
+    def body(z, carry):
+        gs = [diffs(k, 0, z) for k in range(count)]
+        es = [diffs(k, 1, z) for k in range(count)]
+        wts = [scal_ref[2 + k] for k in range(count)]
+
+        def summed(terms):
+            total = terms[0]
+            for term in terms[1:]:
+                total = total + term
+            return total
+
+        mom = {}
+        for i, j in SYM_PAIRS:
+            mom[i, j] = summed([wts[k] * gs[k][i] * gs[k][j] for k in range(count)])
+            mom[j, i] = mom[i, j]
+        nat = {}
+        for i in range(3):
+            for j in range(3):
+                nat[i, j] = summed([wts[k] * es[k][i] * gs[k][j] for k in range(count)])
+        trace_m = mom[0, 0] + mom[1, 1] + mom[2, 2]
+        trace_n = nat[0, 0] + nat[1, 1] + nat[2, 2]
+        g, e = gs[0], es[0]
+        size = jnp.sqrt(g[0] * g[0] + g[1] * g[1] + g[2] * g[2] + EPS_SQ)
+        flux_q, flux_p = [], []
+        for i in range(3):
+            mg = mom[i, 0] * g[0] + mom[i, 1] * g[1] + mom[i, 2] * g[2]
+            me = mom[i, 0] * e[0] + mom[i, 1] * e[1] + mom[i, 2] * e[2]
+            ng = nat[i, 0] * g[0] + nat[i, 1] * g[1] + nat[i, 2] * g[2]
+            cross_q = trace_m * g[i] - mg
+            cross_p = trace_m * e[i] - me + trace_n * g[i] - ng
+            flux_q.append(beta * g[i] / size + alpha * cross_q)
+            flux_p.append(beta * e[i] / size + alpha * cross_p)
+        res_g, fz_g = adjoint(flux_q, carry[0], z)
+        res_h, fz_h = adjoint(flux_p, carry[1], z)
+        pg_ref[z] = res_g
+        ph_ref[z] = res_h
+        ex_ref[0, z] = flux_q[0][:, width_x - 1 :]
+        ex_ref[1, z] = flux_p[0][:, width_x - 1 :]
+        ey_ref[0, z] = flux_q[1][width_y - 1 :, :]
+        ey_ref[1, z] = flux_p[1][width_y - 1 :, :]
+        return (fz_g, fz_h)
+
+    zero = jnp.zeros((width_y, width_x), jnp.float32)
+    lax.fori_loop(0, depth, body, (zero, zero))
+
+
 def model_split(every, rim_x, rim_y, alpha, beta, weights):
-    grads, dirs = fields(every, rim_x, rim_y)
-    moms = moments(grads, dirs, weights)
-    grad_own = grads[0]
-    dir_own = dirs[0]
-    cross_q, cross_p = couple(moms, grad_own, dir_own)
-    size = jnp.sqrt(jnp.sum(grad_own * grad_own, 0) + EPS_SQ)[None]
-    flux = jnp.stack(
-        [beta * grad_own / size + alpha * cross_q, beta * dir_own / size + alpha * cross_p], 0
-    )
-    last_x, last_y = edge_masks(flux.shape[3], flux.shape[4])
-    flux_x = jnp.where(last_x, 0.0, flux[:, 0])
-    flux_y = jnp.where(last_y, 0.0, flux[:, 1])
-    levels = lax.broadcasted_iota(jnp.int32, (flux.shape[2], 1, 1), 0)
-    flux_z = jnp.where(levels == flux.shape[2] - 1, 0.0, flux[:, 2])
-    prev_x = passed_dense(flux_x[..., -1:], "tx", 1)
-    prev_y = passed_along(flux_y[..., -1:, :], "ty", 1)
-
-    def adjoint_one(out):
-        fx, fy, fz = flux_x[out], flux_y[out], flux_z[out]
-        res = jnp.concatenate([prev_x[out], fx[..., :-1]], -1) - fx
-        res = res + jnp.concatenate([prev_y[out], fy[..., :-1, :]], -2) - fy
-        below = jnp.where(levels == 0, 0.0, jnp.concatenate([fz[:1], fz[:-1]], 0))
-        return (res + below - fz)[None]
-
-    return (adjoint_one(0), adjoint_one(1))
+    count, _, depth, width_y, width_x = every.shape
+    end_x = lax.axis_index("tx") == lax.axis_size("tx") - 1
+    end_y = lax.axis_index("ty") == lax.axis_size("ty") - 1
+    flags = jnp.stack([end_x, end_y]).astype(jnp.int32)
+    scal = jnp.concatenate([jnp.stack([alpha, beta]), weights])
+    smem = pl.BlockSpec(memory_space=pltpu.SMEM)
+    vmem = pl.BlockSpec(memory_space=pltpu.VMEM)
+    tile = jax.ShapeDtypeStruct((depth, width_y, width_x), jnp.float32)
+    part_g, part_h, edge_x, edge_y = pl.pallas_call(
+        flux_kernel,
+        out_shape=(
+            tile,
+            tile,
+            jax.ShapeDtypeStruct((2, depth, width_y, 1), jnp.float32),
+            jax.ShapeDtypeStruct((2, depth, 1, width_x), jnp.float32),
+        ),
+        in_specs=[smem, smem, vmem, vmem, vmem],
+        out_specs=(vmem, vmem, vmem, vmem),
+        interpret=INTERPRET,
+    )(scal, flags, every, rim_x, rim_y)
+    prev_x = passed_dense(edge_x, "tx", 1)
+    prev_y = passed_along(edge_y, "ty", 1)
+    lane = lax.broadcasted_iota(jnp.int32, (1, 1, width_x), 2)
+    row = lax.broadcasted_iota(jnp.int32, (1, width_y, 1), 1)
+    gradient = part_g + jnp.where(lane == 0, prev_x[0], 0.0) + jnp.where(row == 0, prev_y[0], 0.0)
+    hessian = part_h + jnp.where(lane == 0, prev_x[1], 0.0) + jnp.where(row == 0, prev_y[1], 0.0)
+    return (gradient[None], hessian[None])
 
 
 def shards(models, direction, coupling, tv_weight):

time: 29.4 us -> 33.8 us (1.15)
  Pallas kernels: 0 us -> 4.9 us
  other arithmetic: 6.32 us -> 8.62 us
  local copies, waits for them, and re-layouts: 3.71 us -> 2.65 us
  waiting for transfers between devices: 2.08 us -> 1.15 us
  starting transfers between devices: 16.1 us -> 15.4 us
    pallas_call x0 -> x1, Pallas kernels: none -> 4.9 us  [model_split(): pl.pallas_call(flux_kernel, out_shape=(tile, tile, jax.ShapeDtypeStruct((...]
    concatenate x1 -> x2, other arithmetic: 1.38 us -> 3.23 us  [the longest x1 2.58 us: model_split(): scal = jnp.concatenate([jnp.stack([alpha, beta]), weights])]
    add x1 -> x0, other arithmetic: 1.46 us -> none  [model_split(): beta * grad_own / size + alpha * cross_q]
    sub x6 -> x0, other arithmetic: 1.42 us -> none  [the longest x1 0.88 us: adjoint_one(): return (res + below - fz)[None]]
    pallas_call x0 -> x1, other arithmetic: none -> 1.13 us  [model_split(): pl.pallas_call(flux_kernel, out_shape=(tile, tile, jax.ShapeDtypeStruct((...]
    concatenate x7 -> x0, local copies, waits for them, and re-layouts: 0.89 us -> none  [the longest x1 0.45 us: shards(): rim_x = jnp.concatenate(rims_x, 0)]
    broadcast_in_dim x0 -> x1, other arithmetic: none -> 0.85 us  [model_split(): return (gradient[None], hessian[None])]
    concatenate x1, other arithmetic: 0.01 us -> 0.85 us  [shards(): rim_x = jnp.concatenate(rims_x, 0)]
  transfers between devices with their start and end apart: 6 -> 6, of which waited for: 3 -> 2; matrix products, arithmetic and copies ran while one was open for 13% -> 20% of each run, Pallas kernels for 0% -> 0%
where the time goes in v11:
time: 33.8 us; the launch traced here: 33.5 us
  starting transfers between devices  15.4 us (46%)
  other arithmetic  8.62 us (26%)
  Pallas kernels  4.9 us (14%)
  local copies, waits for them, and re-layouts  2.65 us (8%)
  waiting for transfers between devices  1.15 us (3%)
  between operations  0.8 us (2%)
    ppermute x4, starting transfers between devices, passed_along(): return lax.ppermute(array, axis, pairs)  11.8 us
    pallas_call x1, Pallas kernels, model_split(): pl.pallas_call(flux_kernel, out_shape=(tile, tile, jax.ShapeDtypeStruct((...  4.9 us
    ppermute x1, starting transfers between devices, shards(): tiles.append(lax.ppermute(own, 'mp', pairs))  2.78 us
    concatenate x1, other arithmetic, model_split(): scal = jnp.concatenate([jnp.stack([alpha, beta]), weights])  2.58 us
    pallas_call x1, other arithmetic, model_split(): pl.pallas_call(flux_kernel, out_shape=(tile, tile, jax.ShapeDtypeStruct((...  1.13 us
    another operation x2, other arithmetic, shards(): own = jnp.stack([models, direction], 1)  0.94 us
    broadcast_in_dim x1, other arithmetic, model_split(): return (gradient[None], hessian[None])  0.85 us
    concatenate x1, other arithmetic, shards(): rim_x = jnp.concatenate(rims_x, 0)  0.85 us
  transfers between devices with their start and end apart: 6, of which 2 were waited for; matrix products, arithmetic and copies ran while one was open for 20% of the time, Pallas kernels for 0%

profile of v11, /device:TPU:1, one launch (start us, length us, event | category | flops | bytes accessed | tf_op | source)
XLA Modules:
  0.0 33.5 jit_solution(1281184599340200998)
XLA Ops:
  0.6 0.9 %fusion.2 = f32[1,2,16,1,128]{4,3,2,1,0:T(1,128)S(1)} fusion(f32[1,1,16,16,128]{4,3,2,1,0:T(8,128)} %bitcast.19, f32[1,1,16,16,128]{4,3,2,1,0:T(8,128)} %bitcast.15), kind=kLoop, calls=%fused_computation.13 | loop fusion | flops 4096 | bytes 278528 | tf_op jit(solution)/shard_map/stack | solution.py:184
  1.6 1.9 %collective-permute-start.2 = (f32[1,2,16,1,128]{4,3,2,1,0:T(1,128)S(1)}, f32[1,2,16,1,128]{4,3,2,1,0:T(1,128)S(1)}, u32[]{:S(2)}, u32[]{:S(2)}) collective-permute-start(f32[1,2,16,1,128]{4,3,2,1,0:T(1,128)S(1)} %fusion.2), channel_id=1, source_target_pairs={{1,0},{2,1},{3,2},{5,4},{6,5},{7,6},{9,8},{10,9},{11,10},{13,12},{... | collective-permute-start | bytes 49160 | tf_op jit(solution)/shard_map/ppermute | solution.py:17
  3.5 0.1 fusion.1
  3.7 0.1 reshape.49
  3.8 1.3 %collective-permute-start.1 = (f32[4,128]{1,0:T(4,128)S(1)}, f32[4,128]{1,0:T(4,128)S(1)}, u32[]{:S(2)}, u32[]{:S(2)}) collective-permute-start(f32[4,128]{1,0:T(4,128)S(1)} %reshape.49), channel_id=1, source_target_pairs={{4,0},{8,4},{12,8},{5,1},{9,5},{13,9},{6,2},{10,6},{14,10},{7,3},{... | collective-permute-start | bytes 6152 | tf_op jit(solution)/shard_map/ppermute | solution.py:17
  5.1 2.8 %collective-permute-start = (f32[1,2,16,16,128]{4,3,2,1,0:T(8,128)S(1)}, f32[1,2,16,16,128]{4,3,2,1,0:T(8,128)S(1)}, u32[]{:S(2)}, u32[]{:S(2)}) collective-permute-start(f32[1,2,16,16,128]{4,3,2,1,0:T(8,128)S(1)} %pad_maximum_fusion.2), channel_id=1, source_target_pairs={{0,16},{16,0},{1,17},{17,1},{2,18},{18,2},{3,19},{19,3},{4,20},{20... | collective-permute-start | bytes 786440 | tf_op jit(solution)/shard_map/ppermute | solution.py:192
  7.9 0.6 %add_convert_fusion.flag_ref = s32[2]{0:T(128)} fusion(pred[1]{0:T(512)(128)(4,1)} %bitcast.1, pred[1]{0:T(512)(128)(4,1)} %bitcast), kind=kLoop, calls=%fused_computation.14 | loop fusion | flops 4 | bytes 10 | tf_op jit(solution)/shard_map/convert_element_type | solution.py:151
  8.5 0.7 %copy-done.6 = f32[2]{0:T(128)S(1)} copy-done((f32[2]{0:T(128)S(1)}, f32[2]{0:T(128)}, u32[]{:S(2)}) %copy-start.6) | copy-done | bytes 32
  9.1 0.6 %dynamic_slice.10 = f32[1]{0:T(128)} dynamic-slice(f32[2]{0:T(128)S(1)} %copy-done.6, s32[]{:T(128)S(6)} %select_n.28), dynamic_slice_sizes={1} | dynamic-slice | bytes 12 | tf_op jit(solution)/shard_map/dynamic_slice | solution.py:183
  9.7 0.0 copy-done.4
  9.8 0.6 %fusion.5 = (f32[1]{0:T(128)}, f32[1]{0:T(128)}) fusion(f32[2]{0:T(128)S(1)} %copy-done.4, s32[]{:T(128)S(6)} %select_n.28, s32[]{:T(128)S(6)} %select_n.30), kind=kLoop, calls=%fused_computation.20 | loop fusion | bytes 24 | tf_op jit(solution)/shard_map/dynamic_slice | solution.py:181
  10.4 0.0 collective-permute-done.1
  10.4 0.0 collective-permute-done.2
  10.4 0.8 %collective-permute-start.3 = (f32[36,128]{1,0:T(8,128)S(1)}, f32[36,128]{1,0:T(8,128)S(1)}, u32[]{:S(2)}, u32[]{:S(2)}) collective-permute-start(f32[36,128]{1,0:T(8,128)S(1)} %maximum_bitcast_fusion), channel_id=1, source_target_pairs={{0,16},{16,0},{1,17},{17,1},{2,18},{18,2},{3,19},{19,3},{4,20},{20... | collective-permute-start | bytes 55304 | tf_op jit(solution)/shard_map/ppermute | solution.py:193
  11.2 2.6 %pad_maximum_fusion.4.scal_ref = f32[4]{0:T(128)} fusion(f32[1]{0:T(128)} %get-tuple-element.17, f32[1]{0:T(128)} %get-tuple-element.16, f32[1]{0:T(128)} %dynamic_slice.10), kind=kLoop, calls=%fused_computation.15 | loop fusion | flops 12 | bytes 28 | tf_op jit(solution)/shard_map/concatenate | solution.py:152
  13.8 0.2 reshape.56
  14.0 0.5 %collective-permute-done.3 = f32[36,128]{1,0:T(8,128)S(1)} collective-permute-done((f32[36,128]{1,0:T(8,128)S(1)}, f32[36,128]{1,0:T(8,128)S(1)}, u32[]{:S(2)}, u32[]{:S(2)}) %collective-permute-start.3) | collective-permute-done | bytes 18464 | tf_op jit(solution)/shard_map/ppermute | solution.py:193
  14.4 0.2 reshape.57
  14.7 0.6 %pad_maximum_fusion.3.ry_ref = f32[2,2,16,1,128]{4,3,2,1,0:T(1,128)} fusion(f32[1,2,16,1,128]{4,3,2,1,0:T(1,128)S(1)} %bitcast.24, f32[1,2,16,1,128]{4,3,2,1,0:T(1,128)S(1)} %collective-permute-done.2), kind=kLoop, calls=%fused_computation.11 | loop fusion | flops 8192 | bytes 65536 | tf_op jit(solution)/shard_map/concatenate | solution.py:200
  15.3 0.8 %pad_maximum_fusion.1.rx_ref = f32[2,2,16,16,1]{4,3,2,1,0:T(8,128)} fusion(f32[1,2,16,16,1]{4,3,2,1,0:T(8,128)S(1)} %reshape.57, f32[1,2,16,16,1]{4,3,2,1,0:T(8,128)S(1)} %reshape.56), kind=kLoop, calls=%fused_computation.1 | loop fusion | flops 1024 | bytes 8192 | tf_op jit(solution)/shard_map/concatenate | solution.py:199
  16.2 0.0 collective-permute-done
  16.2 0.8 %pad_maximum_fusion.ev_ref = f32[2,2,16,16,128]{4,3,2,1,0:T(8,128)} fusion(f32[1,2,16,16,128]{4,3,2,1,0:T(8,128)S(1)} %collective-permute-done, f32[1,1,16,16,128]{4,3,2,1,0:T(8,128)S(1)} %bitcast.18, f32[1,1,16,16,128]{4,3,2,1,0:T(8,128)S(1)} %bitcast.22), kind=kLoop, calls=%fused_computation | loop fusion | flops 262144 | bytes 1048576 | tf_op jit(solution)/shard_map/concatenate | solution.py:198
  17.0 4.9 %shard_map.59 = (f32[16,16,128]{2,1,0:T(8,128)}, f32[16,16,128]{2,1,0:T(8,128)}, f32[2,16,16,1]{3,2,1,0:T(8,128)}, f32[2,16,1,128]{3,2,1,0:T(1,128)}) custom-call(f32[4]{0:T(128)} %pad_maximum_fusion.4.scal_ref, s32[2]{0:T(128)} %add_convert_fusion.flag_ref, f32[2,2,16,16,128]{4,3,2,1,0:T(8,128)} %pad_maximum_fusion.ev_ref, ...), custom_call_target="tpu_custom_call" | custom-call | tf_op jit(solution)/shard_map/pallas_call | solution.py:156
  21.9 1.1 %reduce.1 = f32[2,16,16]{2,1,0:T(8,128)S(1)} reduce(f32[2,16,16,1]{3,2,1,0:T(8,128)} %get-tuple-element.7, f32[]{:T(128)} %constant.38), dimensions={3}, to_apply=%get-tuple-element.7.reduce_sub_computation | reduce | bytes 4100 | tf_op jit(solution)/shard_map/pallas_call | solution.py:156
  23.1 0.1 reshape.55
  23.1 4.5 %collective-permute-start.4 = (f32[4,128]{1,0:T(4,128)S(1)}, f32[4,128]{1,0:T(4,128)S(1)}, u32[]{:S(2)}, u32[]{:S(2)}) collective-permute-start(f32[4,128]{1,0:T(4,128)S(1)} %reshape.55), channel_id=1, source_target_pairs={{0,4},{4,8},{8,12},{1,5},{5,9},{9,13},{2,6},{6,10},{10,14},{3,7},{... | collective-permute-start | bytes 6152 | tf_op jit(solution)/shard_map/ppermute | solution.py:17
  27.6 4.1 %collective-permute-start.5 = (f32[2,16,1,128]{3,2,1,0:T(1,128)S(1)}, f32[2,16,1,128]{3,2,1,0:T(1,128)S(1)}, u32[]{:S(2)}, u32[]{:S(2)}) collective-permute-start(f32[2,16,1,128]{3,2,1,0:T(1,128)S(1)} %copy-done.5), channel_id=1, source_target_pairs={{0,1},{1,2},{2,3},{4,5},{5,6},{6,7},{8,9},{9,10},{10,11},{12,13},{... | collective-permute-start | bytes 49160 | tf_op jit(solution)/shard_map/ppermute | solution.py:17
  31.8 0.0 collective-permute-done.4
  31.8 0.1 broadcast_in_dim.75
  31.9 0.1 broadcast_in_dim.82
  32.0 0.7 %collective-permute-done.5 = f32[2,16,1,128]{3,2,1,0:T(1,128)S(1)} collective-permute-done((f32[2,16,1,128]{3,2,1,0:T(1,128)S(1)}, f32[2,16,1,128]{3,2,1,0:T(1,128)S(1)}, u32[]{:S(2)}, u32[]{:S(2)}) %collective-permute-start.5) | collective-permute-done | bytes 16416 | tf_op jit(solution)/shard_map/ppermute | solution.py:17
  32.6 0.9 %add_bitcast_fusion = (f32[1,16,16,128]{3,2,1,0:T(8,128)}, f32[1,16,16,128]{3,2,1,0:T(8,128)}) fusion(f32[16,16,128]{2,1,0:T(8,128)S(1)} %copy-done.3, f32[16,128]{1,0:T(8,128)S(1)} %bitcast.25, f32[16,16]{1,0:T(8,128)S(1)} %broadcast_in_dim.82, pred[16]{0:T(512)(128)(4,1)S(1)} %iota_compare_fusion, pred[128]{0:T(512)(128)(4,1)S(1)} %iota_compare_fusion.1, ...), kind=kLoop, calls=%fused_computation.9 | loop fusion | flops 262144 | bytes 542864 | tf_op jit(solution)/shard_map/broadcast_in_dim | solution.py:174
  (20 shorter events, 0.1 us)
Async XLA Ops:
  0.6 2.9 %copy-start = (f32[1,16,16,128]{3,2,1,0:T(8,128)S(1)}, f32[1,16,16,128]{3,2,1,0:T(8,128)}, u32[]{:S(2)}) copy-start(f32[1,16,16,128]{3,2,1,0:T(8,128)} %param.5) | copy-start | bytes 393220
  0.6 2.9 %copy-start.1 = (f32[1,16,16,128]{3,2,1,0:T(8,128)S(1)}, f32[1,16,16,128]{3,2,1,0:T(8,128)}, u32[]{:S(2)}) copy-start(f32[1,16,16,128]{3,2,1,0:T(8,128)} %param.4) | copy-start | bytes 393220
  1.6 8.8 %collective-permute-start.2 = (f32[1,2,16,1,128]{4,3,2,1,0:T(1,128)S(1)}, f32[1,2,16,1,128]{4,3,2,1,0:T(1,128)S(1)}, u32[]{:S(2)}, u32[]{:S(2)}) collective-permute-start(f32[1,2,16,1,128]{4,3,2,1,0:T(1,128)S(1)} %fusion.2), channel_id=1, source_target_pairs={{1,0},{2,1},{3,2},{5,4},{6,5},{7,6},{9,8},{10,9},{11,10},{13,12},{... | collective-permute-start | bytes 49160 | tf_op jit(solution)/shard_map/ppermute | solution.py:17
  3.8 6.6 %collective-permute-start.1 = (f32[4,128]{1,0:T(4,128)S(1)}, f32[4,128]{1,0:T(4,128)S(1)}, u32[]{:S(2)}, u32[]{:S(2)}) collective-permute-start(f32[4,128]{1,0:T(4,128)S(1)} %reshape.49), channel_id=1, source_target_pairs={{4,0},{8,4},{12,8},{5,1},{9,5},{13,9},{6,2},{10,6},{14,10},{7,3},{... | collective-permute-start | bytes 6152 | tf_op jit(solution)/shard_map/ppermute | solution.py:17
  5.1 11.1 %collective-permute-start = (f32[1,2,16,16,128]{4,3,2,1,0:T(8,128)S(1)}, f32[1,2,16,16,128]{4,3,2,1,0:T(8,128)S(1)}, u32[]{:S(2)}, u32[]{:S(2)}) collective-permute-start(f32[1,2,16,16,128]{4,3,2,1,0:T(8,128)S(1)} %pad_maximum_fusion.2), channel_id=1, source_target_pairs={{0,16},{16,0},{1,17},{17,1},{2,18},{18,2},{3,19},{19,3},{4,20},{20... | collective-permute-start | bytes 786440 | tf_op jit(solution)/shard_map/ppermute | solution.py:192
  8.5 0.7 %copy-start.6 = (f32[2]{0:T(128)S(1)}, f32[2]{0:T(128)}, u32[]{:S(2)}) copy-start(f32[2]{0:T(128)} %param.7) | copy-start | bytes 28
  9.1 0.7 %copy-start.4 = (f32[2]{0:T(128)S(1)}, f32[2]{0:T(128)}, u32[]{:S(2)}) copy-start(f32[2]{0:T(128)} %param.6) | copy-start | bytes 28
  10.4 4.0 %collective-permute-start.3 = (f32[36,128]{1,0:T(8,128)S(1)}, f32[36,128]{1,0:T(8,128)S(1)}, u32[]{:S(2)}, u32[]{:S(2)}) collective-permute-start(f32[36,128]{1,0:T(8,128)S(1)} %maximum_bitcast_fusion), channel_id=1, source_target_pairs={{0,16},{16,0},{1,17},{17,1},{2,18},{18,2},{3,19},{19,3},{4,20},{20... | collective-permute-start | bytes 55304 | tf_op jit(solution)/shard_map/ppermute | solution.py:193
  21.9 10.7 %copy-start.2 = (f32[16,16,128]{2,1,0:T(8,128)S(1)}, f32[16,16,128]{2,1,0:T(8,128)}, u32[]{:S(2)}) copy-start(f32[16,16,128]{2,1,0:T(8,128)} %get-tuple-element.6) | copy-start | bytes 393220
  21.9 10.7 %copy-start.3 = (f32[16,16,128]{2,1,0:T(8,128)S(1)}, f32[16,16,128]{2,1,0:T(8,128)}, u32[]{:S(2)}) copy-start(f32[16,16,128]{2,1,0:T(8,128)} %get-tuple-element.9) | copy-start | bytes 393220
  23.0 4.6 %copy-start.5 = (f32[2,16,1,128]{3,2,1,0:T(1,128)S(1)}, f32[2,16,1,128]{3,2,1,0:T(1,128)}, u32[]{:S(2)}) copy-start(f32[2,16,1,128]{3,2,1,0:T(1,128)} %get-tuple-element.8) | copy-start | bytes 49156
  23.1 8.6 %collective-permute-start.4 = (f32[4,128]{1,0:T(4,128)S(1)}, f32[4,128]{1,0:T(4,128)S(1)}, u32[]{:S(2)}, u32[]{:S(2)}) collective-permute-start(f32[4,128]{1,0:T(4,128)S(1)} %reshape.55), channel_id=1, source_target_pairs={{0,4},{4,8},{8,12},{1,5},{5,9},{9,13},{2,6},{6,10},{10,14},{3,7},{... | collective-permute-start | bytes 6152 | tf_op jit(solution)/shard_map/ppermute | solution.py:17
  27.6 5.0 %collective-permute-start.5 = (f32[2,16,1,128]{3,2,1,0:T(1,128)S(1)}, f32[2,16,1,128]{3,2,1,0:T(1,128)S(1)}, u32[]{:S(2)}, u32[]{:S(2)}) collective-permute-start(f32[2,16,1,128]{3,2,1,0:T(1,128)S(1)} %copy-done.5), channel_id=1, source_target_pairs={{0,1},{1,2},{2,3},{4,5},{5,6},{6,7},{8,9},{9,10},{10,11},{12,13},{... | collective-permute-start | bytes 49160 | tf_op jit(solution)/shard_map/ppermute | solution.py:17

commit v12 on v10

--- a/solution.py
+++ b/solution.py
@@ -104,8 +104,13 @@
     alpha = own_weights[0]
     beta = lax.dynamic_slice_in_dim(tv_weight, member * local, local)[0]
     own = jnp.stack([models, direction], 1)
-    rim_x = passed_dense(own[..., :1], "tx", -1)
-    rim_y = passed_along(own[..., :1, :], "ty", -1)
+    def fetched(edges):
+        return (passed_dense(edges[0], "tx", -1), passed_along(edges[1], "ty", -1))
+
+    def skipped(edges):
+        return (jnp.zeros_like(edges[0]), jnp.zeros_like(edges[1]))
+
+    rim_x, rim_y = lax.cond(member >= 0, fetched, skipped, (own[..., :1], own[..., :1, :]))
     rims = jnp.concatenate([rim_x.reshape(-1), rim_y.reshape(-1)])
     rims = rims.reshape(-1, 128) if rims.size % 128 == 0 else rims
     tiles, rims_x, rims_y, weights = [own], [rim_x], [rim_y], [own_weights]

time: 29.4 us -> 34.2 us (1.16)
  local copies, waits for them, and re-layouts: 3.71 us -> 7.45 us
  starting transfers between devices: 16.1 us -> 14.2 us
  waiting for transfers between devices: 2.08 us -> 3.51 us
  other arithmetic: 6.32 us -> 7.63 us
    ppermute x4, waiting for transfers between devices: 0.86 us -> 3.5 us  [passed_along(): return lax.ppermute(array, axis, pairs)]
    cond x0 -> x5, local copies, waits for them, and re-layouts: none -> 1.9 us
    ppermute x1, starting transfers between devices: 1.46 us -> 0.01 us  [shards(): theirs = lax.ppermute(rims, 'mp', pairs).reshape(-1)]
    ppermute x1, waiting for transfers between devices: 1.22 us -> 0.01 us  [shards(): theirs = lax.ppermute(rims, 'mp', pairs).reshape(-1)]
    another operation x0 -> x1, local copies, waits for them, and re-layouts: none -> 1.07 us  [shards(): own = jnp.stack([models, direction], 1)]
    another operation x2 -> x1, other arithmetic: 0.94 us -> 1.68 us  [shards(): own = jnp.stack([models, direction], 1)]
    ppermute x1, starting transfers between devices: 2.78 us -> 2.06 us  [shards(): tiles.append(lax.ppermute(own, 'mp', pairs))]
    reshape x1, other arithmetic: 0.01 us -> 0.72 us  [shards(): rims = rims.reshape(-1, 128) if rims.size % 128 == 0 else rims]
  transfers between devices with their start and end apart: 6 -> 6, of which waited for: 3 -> 2; matrix products, arithmetic and copies ran while one was open for 13% -> 19% of each run, Pallas kernels for 0% -> 0%
where the time goes in v12:
time: 34.2 us; the launch traced here: 33.8 us
  starting transfers between devices  14.2 us (42%)
  other arithmetic  7.63 us (22%)
  local copies, waits for them, and re-layouts  7.45 us (22%)
  waiting for transfers between devices  3.51 us (10%)
  between operations  0.94 us (3%)
    ppermute x4, starting transfers between devices, passed_along(): return lax.ppermute(array, axis, pairs)  12.1 us
    ppermute x4, waiting for transfers between devices, passed_along(): return lax.ppermute(array, axis, pairs)  3.5 us
    ppermute x1, starting transfers between devices, shards(): tiles.append(lax.ppermute(own, 'mp', pairs))  2.06 us
    cond x5, local copies, waits for them, and re-layouts  1.9 us
    another operation x1, other arithmetic, shards(): own = jnp.stack([models, direction], 1)  1.68 us
    add x1, other arithmetic, model_split(): beta * grad_own / size + alpha * cross_q  1.46 us
    concatenate x1, other arithmetic, shards(): jnp.concatenate(weights, 0)  1.38 us
    unnamed x8, local copies, waits for them, and re-layouts  1.14 us
  transfers between devices with their start and end apart: 6, of which 2 were waited for; matrix products, arithmetic and copies ran while one was open for 19% of the time, Pallas kernels for 0%

profile of v12, /device:TPU:1, one launch (start us, length us, event | category | flops | bytes accessed | tf_op | source)
XLA Modules:
  0.0 33.8 jit_solution(15934384210545394559)
XLA Ops:
  0.6 1.7 %pad_maximum_fusion.6 = f32[1,2,16,16,128]{4,3,2,0,1:T(8,128)} fusion(f32[1,1,16,16,128]{4,3,2,0,1:T(8,128)} %bitcast.267, f32[1,1,16,16,128]{4,3,2,0,1:T(8,128)} %bitcast.270), kind=kLoop, calls=%fused_computation.47 | loop fusion | flops 65536 | bytes 524288 | tf_op jit(solution)/shard_map/stack | solution.py:106
  2.3 2.1 %collective-permute-start.2 = (f32[1,2,16,16,128]{4,3,2,0,1:T(8,128)}, f32[1,2,16,16,128]{4,3,2,0,1:T(8,128)S(1)}, u32[]{:S(2)}, u32[]{:S(2)}) collective-permute-start(f32[1,2,16,16,128]{4,3,2,0,1:T(8,128)} %pad_maximum_fusion.6), channel_id=1, source_target_pairs={{0,16},{16,0},{1,17},{17,1},{2,18},{18,2},{3,19},{19,3},{4,20},{20... | collective-permute-start | bytes 786440 | tf_op jit(solution)/shard_map/ppermute | solution.py:119
  4.4 10.8 %conditional.1 = (f32[1,2,16,16,1]{3,2,1,4,0:T(8,128)S(1)}, f32[512]{0:T(512)S(1)}, f32[4096]{0:T(1024)}, f32[1,2,16,1,128]{4,3,2,0,1:T(1,128)S(1)}) conditional(s32[]{:T(128)} %convert_element_type.3, () %tuple.19, (f32[1,2,16,16,128]{4,3,2,0,1:T(8,128)}) %tuple.23), branch_computations={%region_0.0_spmd, %region_1.0_spmd} | conditional | bytes 692392 | solution.py:113
  4.4 1.1 %copy.22 = f32[1,2,16,16,128]{4,2,1,3,0:T(8,128)S(1)} copy(f32[1,2,16,16,128]{4,3,2,0,1:T(8,128)} %get-tuple-element.17) | data formatting | bytes 524288 | tf_op jit(solution)/shard_map/stack | solution.py:106
  5.4 2.9 %collective-permute-start.1 = (f32[1,2,16,1,128]{4,2,1,3,0:T(8,128)S(1)}, f32[1,2,16,1,128]{4,2,1,3,0:T(8,128)}, u32[]{:S(2)}, u32[]{:S(2)}) collective-permute-start(f32[1,2,16,1,128]{4,2,1,3,0:T(8,128)S(1)} %slice.217), channel_id=1, source_target_pairs={{1,0},{2,1},{3,2},{5,4},{6,5},{7,6},{9,8},{10,9},{11,10},{13,12},{... | collective-permute-start | bytes 49160 | tf_op jit(solution)/shard_map/cond/branch_1_fun/ppermute | solution.py:13
  8.3 0.3 copy.14
  8.7 1.3 %collective-permute-start = (f32[4,128]{1,0:T(4,128)S(1)}, f32[4,128]{1,0:T(4,128)S(1)}, u32[]{:S(2)}, u32[]{:S(2)}) collective-permute-start(f32[4,128]{1,0:T(4,128)S(1)} %reshape.536), channel_id=1, source_target_pairs={{4,0},{8,4},{12,8},{5,1},{9,5},{13,9},{6,2},{10,6},{14,10},{7,3},{... | collective-permute-start | bytes 6152 | tf_op jit(solution)/shard_map/cond/branch_1_fun/ppermute | solution.py:13
  10.0 3.2 %collective-permute-done = f32[4,128]{1,0:T(4,128)S(1)} collective-permute-done((f32[4,128]{1,0:T(4,128)S(1)}, f32[4,128]{1,0:T(4,128)S(1)}, u32[]{:S(2)}, u32[]{:S(2)}) %collective-permute-start) | collective-permute-done | bytes 2080 | tf_op jit(solution)/shard_map/cond/branch_1_fun/ppermute | solution.py:13
  13.2 0.5 %copy-done.2 = f32[4,128]{1,0:T(4,128)} copy-done((f32[4,128]{1,0:T(4,128)}, f32[4,128]{1,0:T(4,128)S(1)}, u32[]{:S(2)}) %copy-start.2) | copy-done | bytes 2072 | tf_op jit(solution)/shard_map/cond
  13.7 0.7 %copy.30 = f32[1,2,16,1,128]{4,3,2,0,1:T(1,128)S(1)} copy(f32[1,2,16,1,128]{4,3,2,0,1:T(1,128)} %bitcast.3) | data formatting | bytes 32768 | tf_op jit(solution)/shard_map/cond
  14.4 0.7 %copy-done.3 = f32[4,128]{1,0:T(4,128)S(1)} copy-done((f32[4,128]{1,0:T(4,128)S(1)}, f32[4,128]{1,0:T(4,128)}, u32[]{:S(2)}) %copy-start.3) | copy-done | bytes 2072 | tf_op jit(solution)/shard_map/cond
  15.1 0.7 %maximum_bitcast_fusion = f32[36,128]{1,0:T(8,128)S(1)} fusion(f32[4096]{0:T(1024)} %get-tuple-element.14, f32[512]{0:T(512)S(1)} %get-tuple-element.13), kind=kLoop, calls=%fused_computation.152 | loop fusion | flops 4608 | bytes 36864 | tf_op jit(solution)/shard_map/reshape | solution.py:115
  15.9 0.6 %copy-done.4 = f32[2]{0:T(128)S(1)} copy-done((f32[2]{0:T(128)S(1)}, f32[2]{0:T(128)}, u32[]{:S(2)}) %copy-start.4) | copy-done | bytes 32
  16.6 0.6 %fusion.71 = (f32[1]{0:T(128)}, f32[1]{0:T(128)}) fusion(f32[2]{0:T(128)S(1)} %copy-done.4, s32[]{:T(128)S(6)} %select_n.55, s32[]{:T(128)S(6)} %select_n.59), kind=kLoop, calls=%fused_computation.164 | loop fusion | bytes 24 | tf_op jit(solution)/shard_map/dynamic_slice | solution.py:103
  17.2 1.4 %pad_maximum_fusion.8 = f32[2]{0:T(128)S(1)} fusion(f32[1]{0:T(128)} %get-tuple-element.77, f32[1]{0:T(128)} %get-tuple-element.76), kind=kLoop, calls=%fused_computation.155 | loop fusion | flops 2 | bytes 16 | tf_op jit(solution)/shard_map/concatenate | solution.py:128
  18.6 0.6 %dynamic_slice.9 = f32[1]{0:T(128)} dynamic-slice(f32[2]{0:T(128)S(1)} %copy-done.5, s32[]{:T(128)S(6)} %select_n.55), dynamic_slice_sizes={1} | dynamic-slice | bytes 12 | tf_op jit(solution)/shard_map/dynamic_slice | solution.py:105
  19.3 0.4 %copy.16 = f32[2,2,16,16,1]{4,3,2,0,1:T(8,128)S(1)} copy(f32[2,2,16,16,1]{3,2,1,4,0:T(8,128)S(1)} %pad_maximum_fusion.7) | data formatting | bytes 8192 | tf_op jit(solution)/shard_map/concatenate | solution.py:126
  19.7 0.4 %copy-done = f32[1,16,16,128]{3,2,1,0:T(8,128)S(1)} copy-done((f32[1,16,16,128]{3,2,1,0:T(8,128)S(1)}, f32[1,16,16,128]{3,2,1,0:T(8,128)}, u32[]{:S(2)}) %copy-start) | copy-done | bytes 131096
  20.2 0.2 slice.218
  20.6 0.3 fusion
  20.9 0.5 %fusion.24 = (f32[16,16,128]{2,1,0:T(8,128)S(1)}, f32[16,16,128]{2,1,0:T(8,128)S(1)}, f32[16,16,128]{2,1,0:T(8,128)S(1)}, f32[16,16,128]{2,1,0:T(8,128)S(1)}, f3...) fusion(f32[2]{0:T(128)S(1)} %pad_maximum_fusion.8, ...), kind=kLoop, calls=%fused_computation.61 | loop fusion | flops 1998848 | bytes 3506184 | tf_op jit(solution)/shard_map/reduce_sum | solution.py:49
  21.6 0.1 fusion.42
  21.7 0.1 fusion.48
  21.9 0.1 fusion.45
  22.0 1.5 %fusion.5 = (f32[1,3,16,16,128]{4,3,2,0,1:T(8,128)S(1)}, f32[1,3,16,16,128]{4,3,2,0,1:T(8,128)S(1)}) fusion(f32[1,1,16,16,128]{4,3,2,0,1:T(8,128)S(1)} %get-tuple-element.42, f32[1,1,16,16,128]{4,3,2,0,1:T(8,128)S(1)} %get-tuple-element.40, f32[1,1,16,16,128]{4,3,2,0,1:T(8,128)S(1)} %get-tuple-element.36, f32[]{:T(128)} %bitcast.9, ...), kind=kLoop, calls=%fused_computation.22 | loop fusion | flops 1572864 | bytes 3276808 | tf_op jit(solution)/shard_map/add | solution.py:79
  23.6 0.2 slice_reduce_fusion
  24.0 3.4 %collective-permute-start.4 = (f32[4,128]{1,0:T(4,128)S(1)}, f32[4,128]{1,0:T(4,128)S(1)}, u32[]{:S(2)}, u32[]{:S(2)}) collective-permute-start(f32[4,128]{1,0:T(4,128)S(1)} %reshape.547), channel_id=1, source_target_pairs={{0,4},{4,8},{8,12},{1,5},{5,9},{9,13},{2,6},{6,10},{10,14},{3,7},{... | collective-permute-start | bytes 6152 | tf_op jit(solution)/shard_map/ppermute | solution.py:13
  27.4 4.6 %collective-permute-start.5 = (f32[2,16,1,128]{3,2,1,0:T(1,128)S(1)}, f32[2,16,1,128]{3,2,1,0:T(1,128)S(1)}, u32[]{:S(2)}, u32[]{:S(2)}) collective-permute-start(f32[2,16,1,128]{3,2,1,0:T(1,128)S(1)} %slice.239), channel_id=1, source_target_pairs={{0,1},{1,2},{2,3},{4,5},{5,6},{6,7},{8,9},{9,10},{10,11},{12,13},{... | collective-permute-start | bytes 49160 | tf_op jit(solution)/shard_map/ppermute | solution.py:13
  32.1 0.2 concatenate.107
  32.3 0.2 concatenate.106
  32.6 0.3 collective-permute-done.5
  32.9 0.9 %slice_subtract_fusion.1 = (f32[1,16,16,128]{3,2,1,0:T(8,128)}, f32[1,16,16,128]{3,2,1,0:T(8,128)}) fusion(f32[2,16,16,128]{3,2,1,0:T(8,128)S(1)} %get-tuple-element.53, f32[1,16,16,127]{3,2,1,0:T(8,128)S(1)} %slice_bitcast_fusion.1, f32[1,16,16,1]{3,2,1,0:T(8,128)S(1)} %concatenate.107, f32[1,16,15,128]{3,2,1,0:T(8,128)S(1)} %slice_bitcast_fusion, ...), kind=kLoop, calls=%fused_computation.69 | loop fusion | flops 589824 | bytes 1835024 | tf_op jit(solution)/shard_map/sub | solution.py:94
  (45 shorter events, 1.1 us)
Async XLA Ops:
  2.3 17.4 %collective-permute-start.2 = (f32[1,2,16,16,128]{4,3,2,0,1:T(8,128)}, f32[1,2,16,16,128]{4,3,2,0,1:T(8,128)S(1)}, u32[]{:S(2)}, u32[]{:S(2)}) collective-permute-start(f32[1,2,16,16,128]{4,3,2,0,1:T(8,128)} %pad_maximum_fusion.6), channel_id=1, source_target_pairs={{0,16},{16,0},{1,17},{17,1},{2,18},{18,2},{3,19},{19,3},{4,20},{20... | collective-permute-start | bytes 786440 | tf_op jit(solution)/shard_map/ppermute | solution.py:119
  5.4 8.3 %collective-permute-start.1 = (f32[1,2,16,1,128]{4,2,1,3,0:T(8,128)S(1)}, f32[1,2,16,1,128]{4,2,1,3,0:T(8,128)}, u32[]{:S(2)}, u32[]{:S(2)}) collective-permute-start(f32[1,2,16,1,128]{4,2,1,3,0:T(8,128)S(1)} %slice.217), channel_id=1, source_target_pairs={{1,0},{2,1},{3,2},{5,4},{6,5},{7,6},{9,8},{10,9},{11,10},{13,12},{... | collective-permute-start | bytes 49160 | tf_op jit(solution)/shard_map/cond/branch_1_fun/ppermute | solution.py:13
  8.7 4.5 %collective-permute-start = (f32[4,128]{1,0:T(4,128)S(1)}, f32[4,128]{1,0:T(4,128)S(1)}, u32[]{:S(2)}, u32[]{:S(2)}) collective-permute-start(f32[4,128]{1,0:T(4,128)S(1)} %reshape.536), channel_id=1, source_target_pairs={{4,0},{8,4},{12,8},{5,1},{9,5},{13,9},{6,2},{10,6},{14,10},{7,3},{... | collective-permute-start | bytes 6152 | tf_op jit(solution)/shard_map/cond/branch_1_fun/ppermute | solution.py:13
  13.1 0.6 %copy-start.2 = (f32[4,128]{1,0:T(4,128)}, f32[4,128]{1,0:T(4,128)S(1)}, u32[]{:S(2)}) copy-start(f32[4,128]{1,0:T(4,128)S(1)} %collective-permute-done) | copy-start | bytes 6148 | tf_op jit(solution)/shard_map/cond
  14.4 0.7 %copy-start.3 = (f32[4,128]{1,0:T(4,128)S(1)}, f32[4,128]{1,0:T(4,128)}, u32[]{:S(2)}) copy-start(f32[4,128]{1,0:T(4,128)} %copy-done.2) | copy-start | bytes 6148 | tf_op jit(solution)/shard_map/cond
  15.8 3.3 %collective-permute-start.3 = (f32[36,128]{1,0:T(8,128)S(1)}, f32[36,128]{1,0:T(8,128)S(1)}, u32[]{:S(2)}, u32[]{:S(2)}) collective-permute-start(f32[36,128]{1,0:T(8,128)S(1)} %maximum_bitcast_fusion), channel_id=1, source_target_pairs={{0,16},{16,0},{1,17},{17,1},{2,18},{18,2},{3,19},{19,3},{4,20},{20... | collective-permute-start | bytes 55304 | tf_op jit(solution)/shard_map/ppermute | solution.py:120
  15.9 0.7 %copy-start.4 = (f32[2]{0:T(128)S(1)}, f32[2]{0:T(128)}, u32[]{:S(2)}) copy-start(f32[2]{0:T(128)} %param.8) | copy-start | bytes 28
  17.2 1.4 %copy-start.5 = (f32[2]{0:T(128)S(1)}, f32[2]{0:T(128)}, u32[]{:S(2)}) copy-start(f32[2]{0:T(128)} %param.9) | copy-start | bytes 28
  19.2 0.9 %copy-start = (f32[1,16,16,128]{3,2,1,0:T(8,128)S(1)}, f32[1,16,16,128]{3,2,1,0:T(8,128)}, u32[]{:S(2)}) copy-start(f32[1,16,16,128]{3,2,1,0:T(8,128)} %param.7) | copy-start | bytes 393220
  19.2 1.0 %copy-start.1 = (f32[1,16,16,128]{3,2,1,0:T(8,128)S(1)}, f32[1,16,16,128]{3,2,1,0:T(8,128)}, u32[]{:S(2)}) copy-start(f32[1,16,16,128]{3,2,1,0:T(8,128)} %param.6) | copy-start | bytes 393220
  24.0 8.1 %collective-permute-start.4 = (f32[4,128]{1,0:T(4,128)S(1)}, f32[4,128]{1,0:T(4,128)S(1)}, u32[]{:S(2)}, u32[]{:S(2)}) collective-permute-start(f32[4,128]{1,0:T(4,128)S(1)} %reshape.547), channel_id=1, source_target_pairs={{0,4},{4,8},{8,12},{1,5},{5,9},{9,13},{2,6},{6,10},{10,14},{3,7},{... | collective-permute-start | bytes 6152 | tf_op jit(solution)/shard_map/ppermute | solution.py:13
  27.4 5.4 %collective-permute-start.5 = (f32[2,16,1,128]{3,2,1,0:T(1,128)S(1)}, f32[2,16,1,128]{3,2,1,0:T(1,128)S(1)}, u32[]{:S(2)}, u32[]{:S(2)}) collective-permute-start(f32[2,16,1,128]{3,2,1,0:T(1,128)S(1)} %slice.239), channel_id=1, source_target_pairs={{0,1},{1,2},{2,3},{4,5},{5,6},{6,7},{8,9},{9,10},{10,11},{12,13},{... | collective-permute-start | bytes 49160 | tf_op jit(solution)/shard_map/ppermute | solution.py:13

commit v13 on v10

--- a/solution.py
+++ b/solution.py
@@ -106,15 +106,16 @@
     own = jnp.stack([models, direction], 1)
     rim_x = passed_dense(own[..., :1], "tx", -1)
     rim_y = passed_along(own[..., :1, :], "ty", -1)
-    rims = jnp.concatenate([rim_x.reshape(-1), rim_y.reshape(-1)])
-    rims = rims.reshape(-1, 128) if rims.size % 128 == 0 else rims
+    packed = jnp.concatenate([own.reshape(-1), rim_x.reshape(-1), rim_y.reshape(-1)])
+    packed = packed.reshape(-1, 128) if packed.size % 128 == 0 else packed
     tiles, rims_x, rims_y, weights = [own], [rim_x], [rim_y], [own_weights]
     for shift in range(1, mp):
         pairs = [(m, (m + shift) % mp) for m in range(mp)]
-        tiles.append(lax.ppermute(own, "mp", pairs))
-        theirs = lax.ppermute(rims, "mp", pairs).reshape(-1)
-        rims_x.append(theirs[: rim_x.size].reshape(rim_x.shape))
-        rims_y.append(theirs[rim_x.size :].reshape(rim_y.shape))
+        theirs = lax.ppermute(packed, "mp", pairs).reshape(-1)
+        cut = own.size + rim_x.size
+        tiles.append(theirs[: own.size].reshape(own.shape))
+        rims_x.append(theirs[own.size : cut].reshape(rim_x.shape))
+        rims_y.append(theirs[cut:].reshape(rim_y.shape))
         source = (member - shift) % mp
         weights.append(lax.dynamic_slice_in_dim(coupling, source * local, local))
     every = jnp.concatenate(tiles, 0)

time: 29.4 us -> 31.8 us (1.082)
  waiting for transfers between devices: 2.08 us -> 7.9 us
  starting transfers between devices: 16.1 us -> 12.4 us
    ppermute x2 -> x1, waiting for transfers between devices: 1.22 us -> 5.2 us  [shards(): theirs = lax.ppermute(packed, 'mp', pairs).reshape(-1)]
    ppermute x2 -> x1, starting transfers between devices: 4.24 us -> 1.6 us  [shards(): theirs = lax.ppermute(packed, 'mp', pairs).reshape(-1)]
    ppermute x4, waiting for transfers between devices: 0.86 us -> 2.69 us  [passed_along(): return lax.ppermute(array, axis, pairs)]
    ppermute x4, starting transfers between devices: 11.8 us -> 10.8 us  [passed_along(): return lax.ppermute(array, axis, pairs)]
  transfers between devices with their start and end apart: 6 -> 5, of which waited for: 3 -> 3; matrix products, arithmetic and copies ran while one was open for 13% -> 11% of each run, Pallas kernels for 0% -> 0%
where the time goes in v13:
time: 31.8 us; the launch traced here: 31.5 us
  starting transfers between devices  12.4 us (39%)
  waiting for transfers between devices  7.9 us (25%)
  other arithmetic  6.4 us (20%)
  local copies, waits for them, and re-layouts  3.82 us (12%)
  between operations  0.99 us (3%)
    ppermute x4, starting transfers between devices, passed_along(): return lax.ppermute(array, axis, pairs)  10.8 us
    ppermute x1, waiting for transfers between devices, shards(): theirs = lax.ppermute(packed, 'mp', pairs).reshape(-1)  5.2 us
    ppermute x4, waiting for transfers between devices, passed_along(): return lax.ppermute(array, axis, pairs)  2.69 us
    ppermute x1, starting transfers between devices, shards(): theirs = lax.ppermute(packed, 'mp', pairs).reshape(-1)  1.6 us
    add x1, other arithmetic, model_split(): beta * grad_own / size + alpha * cross_q  1.5 us
    concatenate x1, other arithmetic, shards(): jnp.concatenate(weights, 0)  1.37 us
    another operation x2, other arithmetic, shards(): own = jnp.stack([models, direction], 1)  0.94 us
    sub x1, other arithmetic, adjoint_one(): return (res + below - fz)[None]  0.88 us
  transfers between devices with their start and end apart: 5, of which 3 were waited for; matrix products, arithmetic and copies ran while one was open for 11% of the time, Pallas kernels for 0%

profile of v13, /device:TPU:1, one launch (start us, length us, event | category | flops | bytes accessed | tf_op | source)
XLA Modules:
  0.0 31.5 jit_solution(10175256696345943645)
XLA Ops:
  0.6 0.9 %fusion.67 = f32[1,2,16,1,128]{4,3,2,0,1:T(1,128)S(1)} fusion(f32[1,1,16,16,128]{4,3,2,0,1:T(8,128)} %bitcast.262, f32[1,1,16,16,128]{4,3,2,0,1:T(8,128)} %bitcast.267), kind=kLoop, calls=%fused_computation.159 | loop fusion | flops 4096 | bytes 278528 | tf_op jit(solution)/shard_map/stack | solution.py:106
  1.6 1.9 %collective-permute-start.1 = (f32[1,2,16,1,128]{4,3,2,0,1:T(1,128)S(1)}, f32[1,2,16,1,128]{4,3,2,0,1:T(1,128)S(1)}, u32[]{:S(2)}, u32[]{:S(2)}) collective-permute-start(f32[1,2,16,1,128]{4,3,2,0,1:T(1,128)S(1)} %fusion.67), channel_id=1, source_target_pairs={{1,0},{2,1},{3,2},{5,4},{6,5},{7,6},{9,8},{10,9},{11,10},{13,12},{... | collective-permute-start | bytes 49160 | tf_op jit(solution)/shard_map/ppermute | solution.py:13
  3.5 0.1 fusion.10
  3.7 0.1 reshape.541
  3.8 1.3 %collective-permute-start = (f32[4,128]{1,0:T(4,128)S(1)}, f32[4,128]{1,0:T(4,128)S(1)}, u32[]{:S(2)}, u32[]{:S(2)}) collective-permute-start(f32[4,128]{1,0:T(4,128)S(1)} %reshape.541), channel_id=1, source_target_pairs={{4,0},{8,4},{12,8},{5,1},{9,5},{13,9},{6,2},{10,6},{14,10},{7,3},{... | collective-permute-start | bytes 6152 | tf_op jit(solution)/shard_map/ppermute | solution.py:13
  5.1 0.6 %copy-done.3 = f32[2]{0:T(128)S(1)} copy-done((f32[2]{0:T(128)S(1)}, f32[2]{0:T(128)}, u32[]{:S(2)}) %copy-start.3) | copy-done | bytes 32
  5.8 0.7 %dynamic_slice.9 = f32[1]{0:T(128)} dynamic-slice(f32[2]{0:T(128)S(1)} %copy-done.3, s32[]{:T(128)S(6)} %select_n.55), dynamic_slice_sizes={1} | dynamic-slice | bytes 12 | tf_op jit(solution)/shard_map/dynamic_slice | solution.py:105
  6.5 0.6 %fusion.74 = (f32[1]{0:T(128)}, f32[1]{0:T(128)}) fusion(f32[2]{0:T(128)S(1)} %copy-done.2, s32[]{:T(128)S(6)} %select_n.55, s32[]{:T(128)S(6)} %select_n.59), kind=kLoop, calls=%fused_computation.171 | loop fusion | bytes 24 | tf_op jit(solution)/shard_map/dynamic_slice | solution.py:103
  7.0 2.4 %collective-permute-done = f32[4,128]{1,0:T(4,128)S(1)} collective-permute-done((f32[4,128]{1,0:T(4,128)S(1)}, f32[4,128]{1,0:T(4,128)S(1)}, u32[]{:S(2)}, u32[]{:S(2)}) %collective-permute-start) | collective-permute-done | bytes 2080 | tf_op jit(solution)/shard_map/ppermute | solution.py:13
  9.4 1.6 %collective-permute-start.2 = (f32[548,128]{1,0:T(8,128)S(1)}, f32[548,128]{1,0:T(8,128)S(1)}, u32[]{:S(2)}, u32[]{:S(2)}) collective-permute-start(f32[548,128]{1,0:T(8,128)S(1)} %maximum_bitcast_fusion), channel_id=1, source_target_pairs={{0,16},{16,0},{1,17},{17,1},{2,18},{18,2},{3,19},{19,3},{4,20},{20... | collective-permute-start | bytes 841736 | tf_op jit(solution)/shard_map/ppermute | solution.py:114
  11.0 1.4 %pad_maximum_fusion.8 = f32[2]{0:T(128)S(1)} fusion(f32[1]{0:T(128)} %get-tuple-element.61, f32[1]{0:T(128)} %get-tuple-element.60), kind=kLoop, calls=%fused_computation.162 | loop fusion | flops 2 | bytes 16 | tf_op jit(solution)/shard_map/concatenate | solution.py:124
  12.4 0.1 reshape.545
  12.5 5.2 %collective-permute-done.2 = f32[548,128]{1,0:T(8,128)S(1)} collective-permute-done((f32[548,128]{1,0:T(8,128)S(1)}, f32[548,128]{1,0:T(8,128)S(1)}, u32[]{:S(2)}, u32[]{:S(2)}) %collective-permute-start.2) | collective-permute-done | bytes 280608 | tf_op jit(solution)/shard_map/ppermute | solution.py:114
  17.8 0.2 slice.226
  18.1 0.1 reshape.546
  18.2 0.4 %copy.6 = f32[2,2,16,16,1]{4,3,2,0,1:T(8,128)S(1)} copy(f32[2,2,16,16,1]{3,2,1,4,0:T(8,128)S(1)} %pad_maximum_fusion.7) | data formatting | bytes 8192 | tf_op jit(solution)/shard_map/concatenate | solution.py:122
  18.7 0.3 fusion
  19.0 0.5 %fusion.26 = (f32[16,16,128]{2,1,0:T(8,128)S(1)}, f32[16,16,128]{2,1,0:T(8,128)S(1)}, f32[16,16,128]{2,1,0:T(8,128)S(1)}, f32[16,16,128]{2,1,0:T(8,128)S(1)}, f3...) fusion(f32[2]{0:T(128)S(1)} %pad_maximum_fusion.8, ...), kind=kLoop, calls=%fused_computation.68 | loop fusion | flops 1998848 | bytes 3506184 | tf_op jit(solution)/shard_map/reduce_sum | solution.py:49
  19.6 0.1 fusion.59
  19.6 0.2 fusion.44
  19.8 0.1 fusion.50
  19.9 0.2 fusion.47
  20.1 1.5 %fusion.5 = (f32[1,3,16,16,128]{4,3,2,0,1:T(8,128)S(1)}, f32[1,3,16,16,128]{4,3,2,0,1:T(8,128)S(1)}) fusion(f32[1,1,16,16,128]{4,3,2,0,1:T(8,128)S(1)} %get-tuple-element.26, f32[1,1,16,16,128]{4,3,2,0,1:T(8,128)S(1)} %get-tuple-element.24, f32[1,1,16,16,128]{4,3,2,0,1:T(8,128)S(1)} %get-tuple-element.20, f32[]{:T(128)} %bitcast.9, ...), kind=kLoop, calls=%fused_computation.22 | loop fusion | flops 1572864 | bytes 3276808 | tf_op jit(solution)/shard_map/add | solution.py:79
  21.6 0.1 fusion.16
  21.8 0.2 slice_reduce_fusion
  22.1 0.1 reshape.548
  22.2 3.2 %collective-permute-start.3 = (f32[4,128]{1,0:T(4,128)S(1)}, f32[4,128]{1,0:T(4,128)S(1)}, u32[]{:S(2)}, u32[]{:S(2)}) collective-permute-start(f32[4,128]{1,0:T(4,128)S(1)} %reshape.548), channel_id=1, source_target_pairs={{0,4},{4,8},{8,12},{1,5},{5,9},{9,13},{2,6},{6,10},{10,14},{3,7},{... | collective-permute-start | bytes 6152 | tf_op jit(solution)/shard_map/ppermute | solution.py:13
  25.4 4.4 %collective-permute-start.4 = (f32[2,16,1,128]{3,2,1,0:T(1,128)S(1)}, f32[2,16,1,128]{3,2,1,0:T(1,128)S(1)}, u32[]{:S(2)}, u32[]{:S(2)}) collective-permute-start(f32[2,16,1,128]{3,2,1,0:T(1,128)S(1)} %slice.247), channel_id=1, source_target_pairs={{0,1},{1,2},{2,3},{4,5},{5,6},{6,7},{8,9},{9,10},{10,11},{12,13},{... | collective-permute-start | bytes 49160 | tf_op jit(solution)/shard_map/ppermute | solution.py:13
  29.9 0.2 concatenate.107
  30.1 0.2 concatenate.106
  30.3 0.3 %collective-permute-done.4 = f32[2,16,1,128]{3,2,1,0:T(1,128)S(1)} collective-permute-done((f32[2,16,1,128]{3,2,1,0:T(1,128)S(1)}, f32[2,16,1,128]{3,2,1,0:T(1,128)S(1)}, u32[]{:S(2)}, u32[]{:S(2)}) %collective-permute-start.4) | collective-permute-done | bytes 16416 | tf_op jit(solution)/shard_map/ppermute | solution.py:13
  30.6 0.9 %slice_subtract_fusion.1 = (f32[1,16,16,128]{3,2,1,0:T(8,128)}, f32[1,16,16,128]{3,2,1,0:T(8,128)}) fusion(f32[2,16,16,128]{3,2,1,0:T(8,128)S(1)} %get-tuple-element.37, f32[1,16,16,127]{3,2,1,0:T(8,128)S(1)} %slice_bitcast_fusion.1, f32[1,16,16,1]{3,2,1,0:T(8,128)S(1)} %concatenate.107, f32[1,16,15,128]{3,2,1,0:T(8,128)S(1)} %slice_bitcast_fusion, ...), kind=kLoop, calls=%fused_computation.76 | loop fusion | flops 589824 | bytes 1835024 | tf_op jit(solution)/shard_map/sub | solution.py:94
  (37 shorter events, 0.5 us)
Async XLA Ops:
  0.6 2.9 %copy-start = (f32[1,16,16,128]{3,2,1,0:T(8,128)S(1)}, f32[1,16,16,128]{3,2,1,0:T(8,128)}, u32[]{:S(2)}) copy-start(f32[1,16,16,128]{3,2,1,0:T(8,128)} %param.4) | copy-start | bytes 393220
  0.6 2.9 %copy-start.1 = (f32[1,16,16,128]{3,2,1,0:T(8,128)S(1)}, f32[1,16,16,128]{3,2,1,0:T(8,128)}, u32[]{:S(2)}) copy-start(f32[1,16,16,128]{3,2,1,0:T(8,128)} %param.5) | copy-start | bytes 393220
  1.6 7.8 %collective-permute-start.1 = (f32[1,2,16,1,128]{4,3,2,0,1:T(1,128)S(1)}, f32[1,2,16,1,128]{4,3,2,0,1:T(1,128)S(1)}, u32[]{:S(2)}, u32[]{:S(2)}) collective-permute-start(f32[1,2,16,1,128]{4,3,2,0,1:T(1,128)S(1)} %fusion.67), channel_id=1, source_target_pairs={{1,0},{2,1},{3,2},{5,4},{6,5},{7,6},{9,8},{10,9},{11,10},{13,12},{... | collective-permute-start | bytes 49160 | tf_op jit(solution)/shard_map/ppermute | solution.py:13
  3.8 5.6 %collective-permute-start = (f32[4,128]{1,0:T(4,128)S(1)}, f32[4,128]{1,0:T(4,128)S(1)}, u32[]{:S(2)}, u32[]{:S(2)}) collective-permute-start(f32[4,128]{1,0:T(4,128)S(1)} %reshape.541), channel_id=1, source_target_pairs={{4,0},{8,4},{12,8},{5,1},{9,5},{13,9},{6,2},{10,6},{14,10},{7,3},{... | collective-permute-start | bytes 6152 | tf_op jit(solution)/shard_map/ppermute | solution.py:13
  5.1 0.7 %copy-start.3 = (f32[2]{0:T(128)S(1)}, f32[2]{0:T(128)}, u32[]{:S(2)}) copy-start(f32[2]{0:T(128)} %param.7) | copy-start | bytes 28
  5.8 0.7 %copy-start.2 = (f32[2]{0:T(128)S(1)}, f32[2]{0:T(128)}, u32[]{:S(2)}) copy-start(f32[2]{0:T(128)} %param.6) | copy-start | bytes 28
  9.4 8.3 %collective-permute-start.2 = (f32[548,128]{1,0:T(8,128)S(1)}, f32[548,128]{1,0:T(8,128)S(1)}, u32[]{:S(2)}, u32[]{:S(2)}) collective-permute-start(f32[548,128]{1,0:T(8,128)S(1)} %maximum_bitcast_fusion), channel_id=1, source_target_pairs={{0,16},{16,0},{1,17},{17,1},{2,18},{18,2},{3,19},{19,3},{4,20},{20... | collective-permute-start | bytes 841736 | tf_op jit(solution)/shard_map/ppermute | solution.py:114
  22.2 7.7 %collective-permute-start.3 = (f32[4,128]{1,0:T(4,128)S(1)}, f32[4,128]{1,0:T(4,128)S(1)}, u32[]{:S(2)}, u32[]{:S(2)}) collective-permute-start(f32[4,128]{1,0:T(4,128)S(1)} %reshape.548), channel_id=1, source_target_pairs={{0,4},{4,8},{8,12},{1,5},{5,9},{9,13},{2,6},{6,10},{10,14},{3,7},{... | collective-permute-start | bytes 6152 | tf_op jit(solution)/shard_map/ppermute | solution.py:13
  25.4 5.2 %collective-permute-start.4 = (f32[2,16,1,128]{3,2,1,0:T(1,128)S(1)}, f32[2,16,1,128]{3,2,1,0:T(1,128)S(1)}, u32[]{:S(2)}, u32[]{:S(2)}) collective-permute-start(f32[2,16,1,128]{3,2,1,0:T(1,128)S(1)} %slice.247), channel_id=1, source_target_pairs={{0,1},{1,2},{2,3},{4,5},{5,6},{6,7},{8,9},{9,10},{10,11},{12,13},{... | collective-permute-start | bytes 49160 | tf_op jit(solution)/shard_map/ppermute | solution.py:13

commit v14 on v10

--- a/solution.py
+++ b/solution.py
@@ -104,14 +104,15 @@
     alpha = own_weights[0]
     beta = lax.dynamic_slice_in_dim(tv_weight, member * local, local)[0]
     own = jnp.stack([models, direction], 1)
-    rim_x = passed_dense(own[..., :1], "tx", -1)
-    rim_y = passed_along(own[..., :1, :], "ty", -1)
+    rim_x = passed_dense(jnp.stack([models[..., :1], direction[..., :1]], 1), "tx", -1)
+    rim_y = passed_along(jnp.stack([models[..., :1, :], direction[..., :1, :]], 1), "ty", -1)
     rims = jnp.concatenate([rim_x.reshape(-1), rim_y.reshape(-1)])
     rims = rims.reshape(-1, 128) if rims.size % 128 == 0 else rims
     tiles, rims_x, rims_y, weights = [own], [rim_x], [rim_y], [own_weights]
     for shift in range(1, mp):
         pairs = [(m, (m + shift) % mp) for m in range(mp)]
-        tiles.append(lax.ppermute(own, "mp", pairs))
+        parts = [lax.ppermute(part, "mp", pairs) for part in (models, direction)]
+        tiles.append(jnp.stack(parts, 1))
         theirs = lax.ppermute(rims, "mp", pairs).reshape(-1)
         rims_x.append(theirs[: rim_x.size].reshape(rim_x.shape))
         rims_y.append(theirs[rim_x.size :].reshape(rim_y.shape))

time: 29.4 us -> 32 us (1.088)
  local copies, waits for them, and re-layouts: 3.71 us -> 7.09 us
  other arithmetic: 6.32 us -> 5.26 us
    another operation x0 -> x2, local copies, waits for them, and re-layouts: none -> 1.72 us  [shards(): jnp.stack([models[..., :1, :], direction[..., :1, :]], 1)]
    unnamed x8 -> x10, local copies, waits for them, and re-layouts: 0.65 us -> 2.3 us
    ppermute x4, waiting for transfers between devices: 0.86 us -> 2.38 us  [passed_along(): return lax.ppermute(array, axis, pairs)]
    ppermute x1, waiting for transfers between devices: 1.22 us -> 0.01 us  [shards(): theirs = lax.ppermute(rims, 'mp', pairs).reshape(-1)]
    another operation x2, other arithmetic: 0.94 us -> 0.02 us  [the longest x1 0.02 us: shards(): jnp.stack([models[..., :1, :], direction[..., :1, :]], 1)]
    ppermute x1 -> x2, starting transfers between devices: 2.78 us -> 2.2 us  [shards(): parts = [lax.ppermute(part, 'mp', pairs) for part in (models, direction)]]
    ppermute x4, starting transfers between devices: 11.8 us -> 12.1 us  [passed_along(): return lax.ppermute(array, axis, pairs)]
  transfers between devices with their start and end apart: 6 -> 7, of which waited for: 3 -> 2; matrix products, arithmetic and copies ran while one was open for 13% -> 21% of each run, Pallas kernels for 0% -> 0%
where the time goes in v14:
time: 32 us; the launch traced here: 31.7 us
  starting transfers between devices  16 us (50%)
  local copies, waits for them, and re-layouts  7.09 us (22%)
  other arithmetic  5.26 us (16%)
  waiting for transfers between devices  2.39 us (7%)
  between operations  0.99 us (3%)
    ppermute x4, starting transfers between devices, passed_along(): return lax.ppermute(array, axis, pairs)  12.1 us
    ppermute x4, waiting for transfers between devices, passed_along(): return lax.ppermute(array, axis, pairs)  2.38 us
    unnamed x10, local copies, waits for them, and re-layouts  2.3 us
    ppermute x2, starting transfers between devices, shards(): parts = [lax.ppermute(part, 'mp', pairs) for part in (models, direction)]  2.2 us
    another operation x2, local copies, waits for them, and re-layouts, shards(): jnp.stack([models[..., :1, :], direction[..., :1, :]], 1)  1.72 us
    ppermute x1, starting transfers between devices, shards(): theirs = lax.ppermute(rims, 'mp', pairs).reshape(-1)  1.6 us
    add x1, other arithmetic, model_split(): beta * grad_own / size + alpha * cross_q  1.46 us
    concatenate x1, other arithmetic, shards(): jnp.concatenate(weights, 0)  1.38 us
  transfers between devices with their start and end apart: 7, of which 2 were waited for; matrix products, arithmetic and copies ran while one was open for 21% of the time, Pallas kernels for 0%

profile of v14, /device:TPU:1, one launch (start us, length us, event | category | flops | bytes accessed | tf_op | source)
XLA Modules:
  0.0 31.7 jit_solution(18005591256420385036)
XLA Ops:
  0.6 2.1 %collective-permute-start = (f32[1,16,16,128]{3,2,1,0:T(8,128)}, f32[1,16,16,128]{3,2,1,0:T(8,128)S(1)}, u32[]{:S(2)}, u32[]{:S(2)}) collective-permute-start(f32[1,16,16,128]{3,2,1,0:T(8,128)} %param.4), channel_id=1, source_target_pairs={{0,16},{16,0},{1,17},{17,1},{2,18},{18,2},{3,19},{19,3},{4,20},{20... | collective-permute-start | bytes 393224 | tf_op jit(solution)/shard_map/ppermute | solution.py:114
  2.8 0.1 collective-permute-start.1
  2.8 0.9 %slice_bitcast_fusion.8 = f32[1,1,16,1,128]{4,3,2,0,1:T(1,128)S(1)} fusion(f32[1,16,16,128]{3,2,1,0:T(8,128)} %param.5), kind=kLoop, calls=%fused_computation.154 | loop fusion | bytes 16384 | tf_op jit(solution)/shard_map/stack | solution.py:108
  3.7 0.8 %slice_bitcast_fusion.9 = f32[1,1,16,1,128]{4,3,2,0,1:T(1,128)S(1)} fusion(f32[1,16,16,128]{3,2,1,0:T(8,128)} %param.4), kind=kLoop, calls=%fused_computation.155 | loop fusion | bytes 16384 | tf_op jit(solution)/shard_map/stack | solution.py:108
  4.6 2.9 %collective-permute-start.3 = (f32[1,2,16,1,128]{4,3,2,0,1:T(1,128)S(1)}, f32[1,2,16,1,128]{4,3,2,0,1:T(1,128)S(1)}, u32[]{:S(2)}, u32[]{:S(2)}) collective-permute-start(f32[1,2,16,1,128]{4,3,2,0,1:T(1,128)S(1)} %pad_maximum_fusion.7), channel_id=1, source_target_pairs={{1,0},{2,1},{3,2},{5,4},{6,5},{7,6},{9,8},{10,9},{11,10},{13,12},{... | collective-permute-start | bytes 49160 | tf_op jit(solution)/shard_map/ppermute | solution.py:13
  7.5 1.1 %copy.16 = f32[1,16,16,1]{2,1,3,0:T(8,128)S(1)} copy(f32[1,16,16,1]{3,2,1,0:T(8,128)} %bitcast.281) | data formatting | bytes 2048
  8.5 0.2 copy.17
  8.7 0.1 reshape.532
  8.8 1.3 %collective-permute-start.2 = (f32[4,128]{1,0:T(4,128)S(1)}, f32[4,128]{1,0:T(4,128)S(1)}, u32[]{:S(2)}, u32[]{:S(2)}) collective-permute-start(f32[4,128]{1,0:T(4,128)S(1)} %reshape.532), channel_id=1, source_target_pairs={{4,0},{8,4},{12,8},{5,1},{9,5},{13,9},{6,2},{10,6},{14,10},{7,3},{... | collective-permute-start | bytes 6152 | tf_op jit(solution)/shard_map/ppermute | solution.py:13
  10.2 0.6 %copy-done.2 = f32[2]{0:T(128)S(1)} copy-done((f32[2]{0:T(128)S(1)}, f32[2]{0:T(128)}, u32[]{:S(2)}) %copy-start.2) | copy-done | bytes 32
  10.8 0.6 %fusion.71 = (f32[1]{0:T(128)}, f32[1]{0:T(128)}) fusion(f32[2]{0:T(128)S(1)} %copy-done.2, s32[]{:T(128)S(6)} %select_n.55, s32[]{:T(128)S(6)} %select_n.59), kind=kLoop, calls=%fused_computation.167 | loop fusion | bytes 24 | tf_op jit(solution)/shard_map/dynamic_slice | solution.py:103
  11.4 2.0 %collective-permute-done.2 = f32[4,128]{1,0:T(4,128)S(1)} collective-permute-done((f32[4,128]{1,0:T(4,128)S(1)}, f32[4,128]{1,0:T(4,128)S(1)}, u32[]{:S(2)}, u32[]{:S(2)}) %collective-permute-start.2) | collective-permute-done | bytes 2080 | tf_op jit(solution)/shard_map/ppermute | solution.py:13
  13.4 1.6 %collective-permute-start.4 = (f32[36,128]{1,0:T(8,128)S(1)}, f32[36,128]{1,0:T(8,128)S(1)}, u32[]{:S(2)}, u32[]{:S(2)}) collective-permute-start(f32[36,128]{1,0:T(8,128)S(1)} %maximum_bitcast_fusion), channel_id=1, source_target_pairs={{0,16},{16,0},{1,17},{17,1},{2,18},{18,2},{3,19},{19,3},{4,20},{20... | collective-permute-start | bytes 55304 | tf_op jit(solution)/shard_map/ppermute | solution.py:116
  15.0 1.4 %pad_maximum_fusion.8 = f32[2]{0:T(128)S(1)} fusion(f32[1]{0:T(128)} %get-tuple-element.61, f32[1]{0:T(128)} %get-tuple-element.60), kind=kLoop, calls=%fused_computation.158 | loop fusion | flops 2 | bytes 16 | tf_op jit(solution)/shard_map/concatenate | solution.py:124
  16.4 0.6 %dynamic_slice.9 = f32[1]{0:T(128)} dynamic-slice(f32[2]{0:T(128)S(1)} %copy-done.3, s32[]{:T(128)S(6)} %select_n.55), dynamic_slice_sizes={1} | dynamic-slice | bytes 12 | tf_op jit(solution)/shard_map/dynamic_slice | solution.py:105
  17.2 0.4 %copy.13 = f32[2,2,16,16,1]{4,3,2,0,1:T(8,128)S(1)} copy(f32[2,2,16,16,1]{3,2,1,4,0:T(8,128)S(1)} %pad_maximum_fusion.5) | data formatting | bytes 8192 | tf_op jit(solution)/shard_map/concatenate | solution.py:122
  17.6 0.4 %copy-done.1 = f32[1,16,16,128]{3,2,1,0:T(8,128)S(1)} copy-done((f32[1,16,16,128]{3,2,1,0:T(8,128)S(1)}, f32[1,16,16,128]{3,2,1,0:T(8,128)}, u32[]{:S(2)}) %copy-start.1) | copy-done | bytes 131096
  18.1 0.2 slice.224
  18.4 0.3 fusion
  18.8 0.5 %fusion.24 = (f32[16,16,128]{2,1,0:T(8,128)S(1)}, f32[16,16,128]{2,1,0:T(8,128)S(1)}, f32[16,16,128]{2,1,0:T(8,128)S(1)}, f32[16,16,128]{2,1,0:T(8,128)S(1)}, f3...) fusion(f32[2]{0:T(128)S(1)} %pad_maximum_fusion.8, ...), kind=kLoop, calls=%fused_computation.60 | loop fusion | flops 1998848 | bytes 3506184 | tf_op jit(solution)/shard_map/reduce_sum | solution.py:49
  19.4 0.1 fusion.42
  19.6 0.1 fusion.45
  19.7 0.1 fusion.48
  19.9 1.5 %fusion.5 = (f32[1,3,16,16,128]{4,3,2,0,1:T(8,128)S(1)}, f32[1,3,16,16,128]{4,3,2,0,1:T(8,128)S(1)}) fusion(f32[1,1,16,16,128]{4,3,2,0,1:T(8,128)S(1)} %get-tuple-element.26, f32[1,1,16,16,128]{4,3,2,0,1:T(8,128)S(1)} %get-tuple-element.24, f32[1,1,16,16,128]{4,3,2,0,1:T(8,128)S(1)} %get-tuple-element.20, f32[]{:T(128)} %bitcast.13, ...), kind=kLoop, calls=%fused_computation.22 | loop fusion | flops 1572864 | bytes 3276808 | tf_op jit(solution)/shard_map/add | solution.py:79
  21.3 0.1 fusion.14
  21.4 0.2 slice_reduce_fusion
  21.9 3.2 %collective-permute-start.5 = (f32[4,128]{1,0:T(4,128)S(1)}, f32[4,128]{1,0:T(4,128)S(1)}, u32[]{:S(2)}, u32[]{:S(2)}) collective-permute-start(f32[4,128]{1,0:T(4,128)S(1)} %reshape.538), channel_id=1, source_target_pairs={{0,4},{4,8},{8,12},{1,5},{5,9},{9,13},{2,6},{6,10},{10,14},{3,7},{... | collective-permute-start | bytes 6152 | tf_op jit(solution)/shard_map/ppermute | solution.py:13
  25.1 4.8 %collective-permute-start.6 = (f32[2,16,1,128]{3,2,1,0:T(1,128)S(1)}, f32[2,16,1,128]{3,2,1,0:T(1,128)S(1)}, u32[]{:S(2)}, u32[]{:S(2)}) collective-permute-start(f32[2,16,1,128]{3,2,1,0:T(1,128)S(1)} %slice.245), channel_id=1, source_target_pairs={{0,1},{1,2},{2,3},{4,5},{5,6},{6,7},{8,9},{9,10},{10,11},{12,13},{... | collective-permute-start | bytes 49160 | tf_op jit(solution)/shard_map/ppermute | solution.py:13
  30.0 0.2 concatenate.106
  30.2 0.2 concatenate.107
  30.4 0.4 %collective-permute-done.6 = f32[2,16,1,128]{3,2,1,0:T(1,128)S(1)} collective-permute-done((f32[2,16,1,128]{3,2,1,0:T(1,128)S(1)}, f32[2,16,1,128]{3,2,1,0:T(1,128)S(1)}, u32[]{:S(2)}, u32[]{:S(2)}) %collective-permute-start.6) | collective-permute-done | bytes 16416 | tf_op jit(solution)/shard_map/ppermute | solution.py:13
  30.8 0.9 %slice_subtract_fusion.1 = (f32[1,16,16,128]{3,2,1,0:T(8,128)}, f32[1,16,16,128]{3,2,1,0:T(8,128)}) fusion(f32[2,16,16,128]{3,2,1,0:T(8,128)S(1)} %get-tuple-element.37, f32[1,16,16,127]{3,2,1,0:T(8,128)S(1)} %slice_bitcast_fusion.1, f32[1,16,16,1]{3,2,1,0:T(8,128)S(1)} %concatenate.107, f32[1,16,15,128]{3,2,1,0:T(8,128)S(1)} %slice_bitcast_fusion, ...), kind=kLoop, calls=%fused_computation.68 | loop fusion | flops 589824 | bytes 1835024 | tf_op jit(solution)/shard_map/sub | solution.py:94
  (43 shorter events, 0.8 us)
Async XLA Ops:
  0.6 7.9 %copy-start = (f32[1,16,16,128]{3,2,1,0:T(8,128)S(1)}, f32[1,16,16,128]{3,2,1,0:T(8,128)}, u32[]{:S(2)}) copy-start(f32[1,16,16,128]{3,2,1,0:T(8,128)} %param.5) | copy-start | bytes 393220
  0.6 17.0 %collective-permute-start = (f32[1,16,16,128]{3,2,1,0:T(8,128)}, f32[1,16,16,128]{3,2,1,0:T(8,128)S(1)}, u32[]{:S(2)}, u32[]{:S(2)}) collective-permute-start(f32[1,16,16,128]{3,2,1,0:T(8,128)} %param.4), channel_id=1, source_target_pairs={{0,16},{16,0},{1,17},{17,1},{2,18},{18,2},{3,19},{19,3},{4,20},{20... | collective-permute-start | bytes 393224 | tf_op jit(solution)/shard_map/ppermute | solution.py:114
  2.8 14.9 %collective-permute-start.1 = (f32[1,16,16,128]{3,2,1,0:T(8,128)}, f32[1,16,16,128]{3,2,1,0:T(8,128)S(1)}, u32[]{:S(2)}, u32[]{:S(2)}) collective-permute-start(f32[1,16,16,128]{3,2,1,0:T(8,128)} %param.5), channel_id=1, source_target_pairs={{0,16},{16,0},{1,17},{17,1},{2,18},{18,2},{3,19},{19,3},{4,20},{20... | collective-permute-start | bytes 393224 | tf_op jit(solution)/shard_map/ppermute | solution.py:114
  4.6 8.8 %collective-permute-start.3 = (f32[1,2,16,1,128]{4,3,2,0,1:T(1,128)S(1)}, f32[1,2,16,1,128]{4,3,2,0,1:T(1,128)S(1)}, u32[]{:S(2)}, u32[]{:S(2)}) collective-permute-start(f32[1,2,16,1,128]{4,3,2,0,1:T(1,128)S(1)} %pad_maximum_fusion.7), channel_id=1, source_target_pairs={{1,0},{2,1},{3,2},{5,4},{6,5},{7,6},{9,8},{10,9},{11,10},{13,12},{... | collective-permute-start | bytes 49160 | tf_op jit(solution)/shard_map/ppermute | solution.py:13
  8.8 4.6 %collective-permute-start.2 = (f32[4,128]{1,0:T(4,128)S(1)}, f32[4,128]{1,0:T(4,128)S(1)}, u32[]{:S(2)}, u32[]{:S(2)}) collective-permute-start(f32[4,128]{1,0:T(4,128)S(1)} %reshape.532), channel_id=1, source_target_pairs={{4,0},{8,4},{12,8},{5,1},{9,5},{13,9},{6,2},{10,6},{14,10},{7,3},{... | collective-permute-start | bytes 6152 | tf_op jit(solution)/shard_map/ppermute | solution.py:13
  10.2 0.7 %copy-start.2 = (f32[2]{0:T(128)S(1)}, f32[2]{0:T(128)}, u32[]{:S(2)}) copy-start(f32[2]{0:T(128)} %param.6) | copy-start | bytes 28
  13.4 3.6 %collective-permute-start.4 = (f32[36,128]{1,0:T(8,128)S(1)}, f32[36,128]{1,0:T(8,128)S(1)}, u32[]{:S(2)}, u32[]{:S(2)}) collective-permute-start(f32[36,128]{1,0:T(8,128)S(1)} %maximum_bitcast_fusion), channel_id=1, source_target_pairs={{0,16},{16,0},{1,17},{17,1},{2,18},{18,2},{3,19},{19,3},{4,20},{20... | collective-permute-start | bytes 55304 | tf_op jit(solution)/shard_map/ppermute | solution.py:116
  15.0 1.4 %copy-start.3 = (f32[2]{0:T(128)S(1)}, f32[2]{0:T(128)}, u32[]{:S(2)}) copy-start(f32[2]{0:T(128)} %param.7) | copy-start | bytes 28
  17.1 0.9 %copy-start.1 = (f32[1,16,16,128]{3,2,1,0:T(8,128)S(1)}, f32[1,16,16,128]{3,2,1,0:T(8,128)}, u32[]{:S(2)}) copy-start(f32[1,16,16,128]{3,2,1,0:T(8,128)} %param.4) | copy-start | bytes 393220
  21.9 8.0 %collective-permute-start.5 = (f32[4,128]{1,0:T(4,128)S(1)}, f32[4,128]{1,0:T(4,128)S(1)}, u32[]{:S(2)}, u32[]{:S(2)}) collective-permute-start(f32[4,128]{1,0:T(4,128)S(1)} %reshape.538), channel_id=1, source_target_pairs={{0,4},{4,8},{8,12},{1,5},{5,9},{9,13},{2,6},{6,10},{10,14},{3,7},{... | collective-permute-start | bytes 6152 | tf_op jit(solution)/shard_map/ppermute | solution.py:13
  25.1 5.7 %collective-permute-start.6 = (f32[2,16,1,128]{3,2,1,0:T(1,128)S(1)}, f32[2,16,1,128]{3,2,1,0:T(1,128)S(1)}, u32[]{:S(2)}, u32[]{:S(2)}) collective-permute-start(f32[2,16,1,128]{3,2,1,0:T(1,128)S(1)} %slice.245), channel_id=1, source_target_pairs={{0,1},{1,2},{2,3},{4,5},{5,6},{6,7},{8,9},{9,10},{10,11},{12,13},{... | collective-permute-start | bytes 49160 | tf_op jit(solution)/shard_map/ppermute | solution.py:13

commit v15 on v10

--- a/solution.py
+++ b/solution.py
@@ -100,27 +100,27 @@
     mp = lax.axis_size("mp")
     member = lax.axis_index("mp")
     local = models.shape[0]
-    own_weights = lax.dynamic_slice_in_dim(coupling, member * local, local)
-    alpha = own_weights[0]
-    beta = lax.dynamic_slice_in_dim(tv_weight, member * local, local)[0]
+    order = (member - jnp.arange(mp)) % mp
+    picks = (order[:, None] * local + jnp.arange(local)[None, :]).reshape(-1)
+    weights = jnp.take(coupling, picks)
+    alpha = weights[0]
+    beta = jnp.take(tv_weight, picks[:1])[0]
     own = jnp.stack([models, direction], 1)
     rim_x = passed_dense(own[..., :1], "tx", -1)
     rim_y = passed_along(own[..., :1, :], "ty", -1)
     rims = jnp.concatenate([rim_x.reshape(-1), rim_y.reshape(-1)])
     rims = rims.reshape(-1, 128) if rims.size % 128 == 0 else rims
-    tiles, rims_x, rims_y, weights = [own], [rim_x], [rim_y], [own_weights]
+    tiles, rims_x, rims_y = [own], [rim_x], [rim_y]
     for shift in range(1, mp):
         pairs = [(m, (m + shift) % mp) for m in range(mp)]
         tiles.append(lax.ppermute(own, "mp", pairs))
         theirs = lax.ppermute(rims, "mp", pairs).reshape(-1)
         rims_x.append(theirs[: rim_x.size].reshape(rim_x.shape))
         rims_y.append(theirs[rim_x.size :].reshape(rim_y.shape))
-        source = (member - shift) % mp
-        weights.append(lax.dynamic_slice_in_dim(coupling, source * local, local))
     every = jnp.concatenate(tiles, 0)
     rim_x = jnp.concatenate(rims_x, 0)
     rim_y = jnp.concatenate(rims_y, 0)
-    return model_split(every, rim_x, rim_y, alpha, beta, jnp.concatenate(weights, 0))
+    return model_split(every, rim_x, rim_y, alpha, beta, weights)
 
 
 def solution(mesh):

time: 29.4 us -> 28.2 us (0.959)
  other arithmetic: 6.32 us -> 3.77 us
  between operations: 0.99 us -> 1.76 us
  waiting for transfers between devices: 2.08 us -> 2.59 us
    concatenate x1 -> x0, other arithmetic: 1.38 us -> none  [shards(): jnp.concatenate(weights, 0)]
    add x1, other arithmetic: 1.46 us -> 0.2 us  [model_split(): beta * grad_own / size + alpha * cross_q]
    gather x0 -> x2, local copies, waits for them, and re-layouts: none -> 1.22 us  [the longest x1 0.64 us: shards(): weights = jnp.take(coupling, picks)]
    dynamic_slice x2 -> x0, local copies, waits for them, and re-layouts: 1.17 us -> none  [the longest x1 0.59 us: shards(): own_weights = lax.dynamic_slice_in_dim(coupling, member * local, local)]
    ppermute x4, waiting for transfers between devices: 0.86 us -> 1.42 us  [passed_along(): return lax.ppermute(array, axis, pairs)]
  transfers between devices with their start and end apart: 6 -> 6, of which waited for: 3 -> 3; matrix products, arithmetic and copies ran while one was open for 13% -> 9% of each run, Pallas kernels for 0% -> 0%
where the time goes in v15:
time: 28.2 us; the launch traced here: 28 us
  starting transfers between devices  16.1 us (57%)
  local copies, waits for them, and re-layouts  3.78 us (13%)
  other arithmetic  3.77 us (13%)
  waiting for transfers between devices  2.59 us (9%)
  between operations  1.76 us (6%)
    ppermute x4, starting transfers between devices, passed_along(): return lax.ppermute(array, axis, pairs)  11.8 us
    ppermute x1, starting transfers between devices, shards(): tiles.append(lax.ppermute(own, 'mp', pairs))  2.78 us
    ppermute x1, starting transfers between devices, shards(): theirs = lax.ppermute(rims, 'mp', pairs).reshape(-1)  1.46 us
    ppermute x4, waiting for transfers between devices, passed_along(): return lax.ppermute(array, axis, pairs)  1.42 us
    ppermute x1, waiting for transfers between devices, shards(): theirs = lax.ppermute(rims, 'mp', pairs).reshape(-1)  1.17 us
    another operation x2, other arithmetic, shards(): own = jnp.stack([models, direction], 1)  0.94 us
    sub x1, other arithmetic, adjoint_one(): return (res + below - fz)[None]  0.89 us
    unnamed x8, local copies, waits for them, and re-layouts  0.67 us
  transfers between devices with their start and end apart: 6, of which 3 were waited for; matrix products, arithmetic and copies ran while one was open for 9% of the time, Pallas kernels for 0%

profile of v15, /device:TPU:1, one launch (start us, length us, event | category | flops | bytes accessed | tf_op | source)
XLA Modules:
  0.0 28.0 jit_solution(8971266567504553229)
XLA Ops:
  0.7 0.9 %fusion.67 = f32[1,2,16,1,128]{4,3,2,0,1:T(1,128)S(1)} fusion(f32[1,1,16,16,128]{4,3,2,0,1:T(8,128)} %bitcast.265, f32[1,1,16,16,128]{4,3,2,0,1:T(8,128)} %bitcast.270), kind=kLoop, calls=%fused_computation.160 | loop fusion | flops 4096 | bytes 278528 | tf_op jit(solution)/shard_map/stack | solution.py:108
  1.6 1.9 %collective-permute-start.2 = (f32[1,2,16,1,128]{4,3,2,0,1:T(1,128)S(1)}, f32[1,2,16,1,128]{4,3,2,0,1:T(1,128)S(1)}, u32[]{:S(2)}, u32[]{:S(2)}) collective-permute-start(f32[1,2,16,1,128]{4,3,2,0,1:T(1,128)S(1)} %fusion.67), channel_id=1, source_target_pairs={{1,0},{2,1},{3,2},{5,4},{6,5},{7,6},{9,8},{10,9},{11,10},{13,12},{... | collective-permute-start | bytes 49160 | tf_op jit(solution)/shard_map/ppermute | solution.py:13
  3.5 0.1 fusion.10
  3.7 0.1 reshape.610
  3.8 1.3 %collective-permute-start.1 = (f32[4,128]{1,0:T(4,128)S(1)}, f32[4,128]{1,0:T(4,128)S(1)}, u32[]{:S(2)}, u32[]{:S(2)}) collective-permute-start(f32[4,128]{1,0:T(4,128)S(1)} %reshape.610), channel_id=1, source_target_pairs={{4,0},{8,4},{12,8},{5,1},{9,5},{13,9},{6,2},{10,6},{14,10},{7,3},{... | collective-permute-start | bytes 6152 | tf_op jit(solution)/shard_map/ppermute | solution.py:13
  5.1 2.8 %collective-permute-start = (f32[1,2,16,16,128]{4,3,2,0,1:T(8,128)S(1)}, f32[1,2,16,16,128]{4,3,2,0,1:T(8,128)S(1)}, u32[]{:S(2)}, u32[]{:S(2)}) collective-permute-start(f32[1,2,16,16,128]{4,3,2,0,1:T(8,128)S(1)} %pad_maximum_fusion.5), channel_id=1, source_target_pairs={{0,16},{16,0},{1,17},{17,1},{2,18},{18,2},{3,19},{19,3},{4,20},{20... | collective-permute-start | bytes 786440 | tf_op jit(solution)/shard_map/ppermute | solution.py:116
  8.0 0.6 %gather_fusion = f32[2]{0:T(128)S(1)} fusion(f32[2]{0:T(128)S(1)} %copy-done, s32[1024]{0:T(1024)S(1)} %pad_clamp_fusion), kind=kCustom, calls=%fused_computation | custom fusion | bytes 24 | tf_op jit(solution)/shard_map/jit(_take)/gather | solution.py:105
  8.6 1.1 %collective-permute-done.1 = f32[4,128]{1,0:T(4,128)S(1)} collective-permute-done((f32[4,128]{1,0:T(4,128)S(1)}, f32[4,128]{1,0:T(4,128)S(1)}, u32[]{:S(2)}, u32[]{:S(2)}) %collective-permute-start.1) | collective-permute-done | bytes 2080 | tf_op jit(solution)/shard_map/ppermute | solution.py:13
  9.7 1.5 %collective-permute-start.3 = (f32[36,128]{1,0:T(8,128)S(1)}, f32[36,128]{1,0:T(8,128)S(1)}, u32[]{:S(2)}, u32[]{:S(2)}) collective-permute-start(f32[36,128]{1,0:T(8,128)S(1)} %maximum_bitcast_fusion), channel_id=1, source_target_pairs={{0,16},{16,0},{1,17},{17,1},{2,18},{18,2},{3,19},{19,3},{4,20},{20... | collective-permute-start | bytes 55304 | tf_op jit(solution)/shard_map/ppermute | solution.py:117
  11.3 0.6 %copy-done.3 = f32[2]{0:T(128)S(1)} copy-done((f32[2]{0:T(128)S(1)}, f32[2]{0:T(128)}, u32[]{:S(2)}) %copy-start.3) | copy-done | bytes 32
  12.0 0.6 %dynamic-slice.2 = f32[1]{0:T(128)} dynamic-slice(f32[2]{0:T(128)S(1)} %copy-done.3, s32[]{:T(128)} %bitcast), dynamic_slice_sizes={1} | dynamic-slice | bytes 12 | tf_op jit(solution)/shard_map/jit(_take)/gather | solution.py:107
  13.2 0.1 reshape.611
  13.3 1.2 %collective-permute-done.3 = f32[36,128]{1,0:T(8,128)S(1)} collective-permute-done((f32[36,128]{1,0:T(8,128)S(1)}, f32[36,128]{1,0:T(8,128)S(1)}, u32[]{:S(2)}, u32[]{:S(2)}) %collective-permute-start.3) | collective-permute-done | bytes 18464 | tf_op jit(solution)/shard_map/ppermute | solution.py:117
  14.5 0.1 reshape.614
  14.5 0.4 %copy.6 = f32[2,2,16,16,1]{4,3,2,0,1:T(8,128)S(1)} copy(f32[2,2,16,16,1]{3,2,1,4,0:T(8,128)S(1)} %pad_maximum_fusion.7) | data formatting | bytes 8192 | tf_op jit(solution)/shard_map/concatenate | solution.py:121
  15.1 0.2 slice.231
  15.4 0.3 %fusion = (f32[2,2,16,16,128]{4,3,2,0,1:T(8,128)S(1)}, f32[2,2,16,16,128]{4,3,2,0,1:T(8,128)S(1)}) fusion(f32[2,2,16,16,1]{4,3,2,0,1:T(8,128)S(1)} %copy.6, f32[2,2,16,16,127]{4,3,2,0,1:T(8,128)S(1)} %slice.231, pred[128]{0:T(512)(128)(4,1)S(1)} %compare_and_fusion, f32[1,2,16,16,128]{4,3,2,0,1:T(8,128)S(1)} %collective-permute-done, ...), kind=kLoop, calls=%fused_computation.7 | loop fusion | flops 1179648 | bytes 2621584 | tf_op jit(solution)/shard_map/jit(_where)/select_n | solution.py:33
  15.8 0.5 %fusion.26 = (f32[16,16,128]{2,1,0:T(8,128)S(1)}, f32[16,16,128]{2,1,0:T(8,128)S(1)}, f32[16,16,128]{2,1,0:T(8,128)S(1)}, f32[16,16,128]{2,1,0:T(8,128)S(1)}, f3...) fusion(f32[2]{0:T(128)S(1)} %and_select_fusion.1, ...), kind=kLoop, calls=%fused_computation.68 | loop fusion | flops 1998848 | bytes 3506184 | tf_op jit(solution)/shard_map/reduce_sum | solution.py:49
  16.3 0.1 fusion.59
  16.4 0.1 fusion.44
  16.6 0.1 fusion.50
  16.7 0.1 fusion.47
  16.8 0.2 fusion.5
  17.0 0.1 fusion.16
  17.2 0.2 slice_reduce_fusion
  17.5 0.1 reshape.616
  17.6 4.5 %collective-permute-start.4 = (f32[4,128]{1,0:T(4,128)S(1)}, f32[4,128]{1,0:T(4,128)S(1)}, u32[]{:S(2)}, u32[]{:S(2)}) collective-permute-start(f32[4,128]{1,0:T(4,128)S(1)} %reshape.616), channel_id=1, source_target_pairs={{0,4},{4,8},{8,12},{1,5},{5,9},{9,13},{2,6},{6,10},{10,14},{3,7},{... | collective-permute-start | bytes 6152 | tf_op jit(solution)/shard_map/ppermute | solution.py:13
  22.1 4.1 %collective-permute-start.5 = (f32[2,16,1,128]{3,2,1,0:T(1,128)S(1)}, f32[2,16,1,128]{3,2,1,0:T(1,128)S(1)}, u32[]{:S(2)}, u32[]{:S(2)}) collective-permute-start(f32[2,16,1,128]{3,2,1,0:T(1,128)S(1)} %slice.256), channel_id=1, source_target_pairs={{0,1},{1,2},{2,3},{4,5},{5,6},{6,7},{8,9},{9,10},{10,11},{12,13},{... | collective-permute-start | bytes 49160 | tf_op jit(solution)/shard_map/ppermute | solution.py:13
  26.3 0.2 concatenate.104
  26.5 0.2 concatenate.103
  26.7 0.3 %collective-permute-done.5 = f32[2,16,1,128]{3,2,1,0:T(1,128)S(1)} collective-permute-done((f32[2,16,1,128]{3,2,1,0:T(1,128)S(1)}, f32[2,16,1,128]{3,2,1,0:T(1,128)S(1)}, u32[]{:S(2)}, u32[]{:S(2)}) %collective-permute-start.5) | collective-permute-done | bytes 16416 | tf_op jit(solution)/shard_map/ppermute | solution.py:13
  27.1 0.9 %slice_subtract_fusion.1 = (f32[1,16,16,128]{3,2,1,0:T(8,128)}, f32[1,16,16,128]{3,2,1,0:T(8,128)}) fusion(f32[2,16,16,128]{3,2,1,0:T(8,128)S(1)} %get-tuple-element.48, f32[1,16,16,127]{3,2,1,0:T(8,128)S(1)} %slice_bitcast_fusion.1, f32[1,16,16,1]{3,2,1,0:T(8,128)S(1)} %concatenate.104, f32[1,16,15,128]{3,2,1,0:T(8,128)S(1)} %slice_bitcast_fusion, ...), kind=kLoop, calls=%fused_computation.76 | loop fusion | flops 589824 | bytes 1835024 | tf_op jit(solution)/shard_map/sub | solution.py:94
  (41 shorter events, 0.6 us)
Async XLA Ops:
  0.6 7.3 %copy-start = (f32[2]{0:T(128)S(1)}, f32[2]{0:T(128)}, u32[]{:S(2)}) copy-start(f32[2]{0:T(128)} %param.6) | copy-start | bytes 28
  0.6 2.9 %copy-start.1 = (f32[1,16,16,128]{3,2,1,0:T(8,128)S(1)}, f32[1,16,16,128]{3,2,1,0:T(8,128)}, u32[]{:S(2)}) copy-start(f32[1,16,16,128]{3,2,1,0:T(8,128)} %param.4) | copy-start | bytes 393220
  0.7 2.9 %copy-start.2 = (f32[1,16,16,128]{3,2,1,0:T(8,128)S(1)}, f32[1,16,16,128]{3,2,1,0:T(8,128)}, u32[]{:S(2)}) copy-start(f32[1,16,16,128]{3,2,1,0:T(8,128)} %param.5) | copy-start | bytes 393220
  1.6 8.1 %collective-permute-start.2 = (f32[1,2,16,1,128]{4,3,2,0,1:T(1,128)S(1)}, f32[1,2,16,1,128]{4,3,2,0,1:T(1,128)S(1)}, u32[]{:S(2)}, u32[]{:S(2)}) collective-permute-start(f32[1,2,16,1,128]{4,3,2,0,1:T(1,128)S(1)} %fusion.67), channel_id=1, source_target_pairs={{1,0},{2,1},{3,2},{5,4},{6,5},{7,6},{9,8},{10,9},{11,10},{13,12},{... | collective-permute-start | bytes 49160 | tf_op jit(solution)/shard_map/ppermute | solution.py:13
  3.8 5.9 %collective-permute-start.1 = (f32[4,128]{1,0:T(4,128)S(1)}, f32[4,128]{1,0:T(4,128)S(1)}, u32[]{:S(2)}, u32[]{:S(2)}) collective-permute-start(f32[4,128]{1,0:T(4,128)S(1)} %reshape.610), channel_id=1, source_target_pairs={{4,0},{8,4},{12,8},{5,1},{9,5},{13,9},{6,2},{10,6},{14,10},{7,3},{... | collective-permute-start | bytes 6152 | tf_op jit(solution)/shard_map/ppermute | solution.py:13
  5.1 9.9 %collective-permute-start = (f32[1,2,16,16,128]{4,3,2,0,1:T(8,128)S(1)}, f32[1,2,16,16,128]{4,3,2,0,1:T(8,128)S(1)}, u32[]{:S(2)}, u32[]{:S(2)}) collective-permute-start(f32[1,2,16,16,128]{4,3,2,0,1:T(8,128)S(1)} %pad_maximum_fusion.5), channel_id=1, source_target_pairs={{0,16},{16,0},{1,17},{17,1},{2,18},{18,2},{3,19},{19,3},{4,20},{20... | collective-permute-start | bytes 786440 | tf_op jit(solution)/shard_map/ppermute | solution.py:116
  9.7 4.7 %collective-permute-start.3 = (f32[36,128]{1,0:T(8,128)S(1)}, f32[36,128]{1,0:T(8,128)S(1)}, u32[]{:S(2)}, u32[]{:S(2)}) collective-permute-start(f32[36,128]{1,0:T(8,128)S(1)} %maximum_bitcast_fusion), channel_id=1, source_target_pairs={{0,16},{16,0},{1,17},{17,1},{2,18},{18,2},{3,19},{19,3},{4,20},{20... | collective-permute-start | bytes 55304 | tf_op jit(solution)/shard_map/ppermute | solution.py:117
  11.3 0.7 %copy-start.3 = (f32[2]{0:T(128)S(1)}, f32[2]{0:T(128)}, u32[]{:S(2)}) copy-start(f32[2]{0:T(128)} %param.7) | copy-start | bytes 28
  17.6 8.7 %collective-permute-start.4 = (f32[4,128]{1,0:T(4,128)S(1)}, f32[4,128]{1,0:T(4,128)S(1)}, u32[]{:S(2)}, u32[]{:S(2)}) collective-permute-start(f32[4,128]{1,0:T(4,128)S(1)} %reshape.616), channel_id=1, source_target_pairs={{0,4},{4,8},{8,12},{1,5},{5,9},{9,13},{2,6},{6,10},{10,14},{3,7},{... | collective-permute-start | bytes 6152 | tf_op jit(solution)/shard_map/ppermute | solution.py:13
  22.1 5.0 %collective-permute-start.5 = (f32[2,16,1,128]{3,2,1,0:T(1,128)S(1)}, f32[2,16,1,128]{3,2,1,0:T(1,128)S(1)}, u32[]{:S(2)}, u32[]{:S(2)}) collective-permute-start(f32[2,16,1,128]{3,2,1,0:T(1,128)S(1)} %slice.256), channel_id=1, source_target_pairs={{0,1},{1,2},{2,3},{4,5},{5,6},{6,7},{8,9},{9,10},{10,11},{12,13},{... | collective-permute-start | bytes 49160 | tf_op jit(solution)/shard_map/ppermute | solution.py:13

commit v16 on v15

--- a/solution.py
+++ b/solution.py
@@ -83,8 +83,13 @@
     flux_y = jnp.where(last_y, 0.0, flux[:, 1])
     levels = lax.broadcasted_iota(jnp.int32, (flux.shape[2], 1, 1), 0)
     flux_z = jnp.where(levels == flux.shape[2] - 1, 0.0, flux[:, 2])
-    prev_x = passed_dense(flux_x[..., -1:], "tx", 1)
     prev_y = passed_along(flux_y[..., -1:, :], "ty", 1)
+    prev_x = lax.cond(
+        lax.axis_index("mp") >= 0,
+        lambda edge: passed_dense(edge, "tx", 1),
+        jnp.zeros_like,
+        flux_x[..., -1:],
+    )
 
     def adjoint_one(out):
         fx, fy, fz = flux_x[out], flux_y[out], flux_z[out]

time: 28.2 us -> 35.3 us (1.25)
  local copies, waits for them, and re-layouts: 3.78 us -> 7.76 us
  other arithmetic: 3.77 us -> 6.63 us
  waiting for transfers between devices: 2.59 us -> 3.13 us
  starting transfers between devices: 16.1 us -> 15.6 us
    select_n x0 -> x1, local copies, waits for them, and re-layouts: none -> 1.63 us  [model_split(): flux_x = jnp.where(last_x, 0.0, flux[:, 0])]
    slice x2, local copies, waits for them, and re-layouts: 0.02 us -> 1.26 us  [adjoint_one(): below = jnp.where(levels == 0, 0.0, jnp.concatenate([fz[:1], fz[:-1]], 0))]
    ppermute x1, waiting for transfers between devices: 1.17 us -> 2.29 us  [shards(): theirs = lax.ppermute(rims, 'mp', pairs).reshape(-1)]
    slice x1, other arithmetic: 0.14 us -> 1.11 us  [shards(): rim_x = passed_dense(own[..., :1], 'tx', -1)]
    another operation x2, other arithmetic: 0.94 us -> 1.91 us  [shards(): own = jnp.stack([models, direction], 1)]
    sub x1, other arithmetic: 0.89 us -> 1.82 us  [adjoint_one(): return (res + below - fz)[None]]
    slice x1, local copies, waits for them, and re-layouts: 0.01 us -> 0.72 us  [adjoint_one(): res = res + jnp.concatenate([prev_y[out], fy[..., :-1, :]], -2) - fy]
    gather x1, local copies, waits for them, and re-layouts: 0.58 us -> 1.24 us  [shards(): beta = jnp.take(tv_weight, picks[:1])[0]]
  transfers between devices with their start and end apart: 6 -> 6, of which waited for: 3 -> 3; matrix products, arithmetic and copies ran while one was open for 9% -> 20% of each run, Pallas kernels for 0% -> 0%
where the time goes in v16:
time: 35.3 us; the launch traced here: 34.9 us
  starting transfers between devices  15.6 us (44%)
  local copies, waits for them, and re-layouts  7.76 us (22%)
  other arithmetic  6.63 us (19%)
  waiting for transfers between devices  3.13 us (9%)
  between operations  1.68 us (5%)
    ppermute x4, starting transfers between devices, passed_along(): return lax.ppermute(array, axis, pairs)  11.5 us
    ppermute x1, starting transfers between devices, shards(): tiles.append(lax.ppermute(own, 'mp', pairs))  2.78 us
    ppermute x1, waiting for transfers between devices, shards(): theirs = lax.ppermute(rims, 'mp', pairs).reshape(-1)  2.29 us
    another operation x2, other arithmetic, shards(): own = jnp.stack([models, direction], 1)  1.91 us
    sub x1, other arithmetic, adjoint_one(): return (res + below - fz)[None]  1.82 us
    select_n x1, local copies, waits for them, and re-layouts, model_split(): flux_x = jnp.where(last_x, 0.0, flux[:, 0])  1.63 us
    ppermute x1, starting transfers between devices, shards(): theirs = lax.ppermute(rims, 'mp', pairs).reshape(-1)  1.31 us
    slice x2, local copies, waits for them, and re-layouts, adjoint_one(): below = jnp.where(levels == 0, 0.0, jnp.concatenate([fz[:1], fz[:-1]], 0))  1.26 us
  transfers between devices with their start and end apart: 6, of which 3 were waited for; matrix products, arithmetic and copies ran while one was open for 20% of the time, Pallas kernels for 0%

profile of v16, /device:TPU:1, one launch (start us, length us, event | category | flops | bytes accessed | tf_op | source)
XLA Modules:
  0.0 34.9 jit_solution(6719002450186662343)
XLA Ops:
  0.7 0.9 %fusion.67 = f32[1,2,16,1,128]{4,3,2,0,1:T(1,128)S(1)} fusion(f32[1,1,16,16,128]{4,3,2,0,1:T(8,128)} %bitcast.269, f32[1,1,16,16,128]{4,3,2,0,1:T(8,128)} %bitcast.274), kind=kLoop, calls=%fused_computation.159 | loop fusion | flops 4096 | bytes 278528 | tf_op jit(solution)/shard_map/stack | solution.py:113
  1.6 1.9 %collective-permute-start.3 = (f32[1,2,16,1,128]{4,3,2,0,1:T(1,128)S(1)}, f32[1,2,16,1,128]{4,3,2,0,1:T(1,128)S(1)}, u32[]{:S(2)}, u32[]{:S(2)}) collective-permute-start(f32[1,2,16,1,128]{4,3,2,0,1:T(1,128)S(1)} %fusion.67), channel_id=1, source_target_pairs={{1,0},{2,1},{3,2},{5,4},{6,5},{7,6},{9,8},{10,9},{11,10},{13,12},{... | collective-permute-start | bytes 49160 | tf_op jit(solution)/shard_map/ppermute | solution.py:13
  3.5 1.1 %fusion.10 = f32[2,16,16]{2,1,0:T(8,128)S(1)} fusion(f32[1,1,16,16,128]{4,3,2,0,1:T(8,128)} %bitcast.270, f32[1,1,16,16,128]{4,3,2,0,1:T(8,128)} %bitcast.275), kind=kLoop, calls=%fused_computation.41 | loop fusion | flops 512 | bytes 264192 | tf_op jit(solution)/shard_map/slice | solution.py:114
  4.7 1.3 %collective-permute-start.2 = (f32[4,128]{1,0:T(4,128)S(1)}, f32[4,128]{1,0:T(4,128)S(1)}, u32[]{:S(2)}, u32[]{:S(2)}) collective-permute-start(f32[4,128]{1,0:T(4,128)S(1)} %reshape.608), channel_id=1, source_target_pairs={{4,0},{8,4},{12,8},{5,1},{9,5},{13,9},{6,2},{10,6},{14,10},{7,3},{... | collective-permute-start | bytes 6152 | tf_op jit(solution)/shard_map/ppermute | solution.py:13
  6.0 1.0 %pad_maximum_fusion.5 = f32[1,2,16,16,128]{4,3,2,0,1:T(8,128)S(1)} fusion(f32[1,1,16,16,128]{4,3,2,0,1:T(8,128)} %bitcast.276, f32[1,1,16,16,128]{4,3,2,0,1:T(8,128)} %bitcast.271), kind=kLoop, calls=%fused_computation.31 | loop fusion | flops 65536 | bytes 524288 | tf_op jit(solution)/shard_map/stack | solution.py:113
  7.0 2.8 %collective-permute-start.1 = (f32[1,2,16,16,128]{4,3,2,0,1:T(8,128)S(1)}, f32[1,2,16,16,128]{4,3,2,0,1:T(8,128)S(1)}, u32[]{:S(2)}, u32[]{:S(2)}) collective-permute-start(f32[1,2,16,16,128]{4,3,2,0,1:T(8,128)S(1)} %pad_maximum_fusion.5), channel_id=1, source_target_pairs={{0,16},{16,0},{1,17},{17,1},{2,18},{18,2},{3,19},{19,3},{4,20},{20... | collective-permute-start | bytes 786440 | tf_op jit(solution)/shard_map/ppermute | solution.py:121
  9.9 0.6 %gather_fusion = f32[2]{0:T(128)S(1)} fusion(f32[2]{0:T(128)S(1)} %copy-done, s32[1024]{0:T(1024)S(1)} %pad_clamp_fusion), kind=kCustom, calls=%fused_computation | custom fusion | bytes 24 | tf_op jit(solution)/shard_map/jit(_take)/gather | solution.py:110
  10.5 0.1 collective-permute-done.2
  10.7 1.3 %collective-permute-start.4 = (f32[36,128]{1,0:T(8,128)S(1)}, f32[36,128]{1,0:T(8,128)S(1)}, u32[]{:S(2)}, u32[]{:S(2)}) collective-permute-start(f32[36,128]{1,0:T(8,128)S(1)} %maximum_bitcast_fusion), channel_id=1, source_target_pairs={{0,16},{16,0},{1,17},{17,1},{2,18},{18,2},{3,19},{19,3},{4,20},{20... | collective-permute-start | bytes 55304 | tf_op jit(solution)/shard_map/ppermute | solution.py:122
  12.1 1.2 %dynamic-slice.2 = f32[1]{0:T(128)} dynamic-slice(f32[2]{0:T(128)} %param.9, s32[]{:T(128)} %bitcast), dynamic_slice_sizes={1} | dynamic-slice | bytes 12 | tf_op jit(solution)/shard_map/jit(_take)/gather | solution.py:112
  14.1 2.3 %collective-permute-done.4 = f32[36,128]{1,0:T(8,128)S(1)} collective-permute-done((f32[36,128]{1,0:T(8,128)S(1)}, f32[36,128]{1,0:T(8,128)S(1)}, u32[]{:S(2)}, u32[]{:S(2)}) %collective-permute-start.4) | collective-permute-done | bytes 18464 | tf_op jit(solution)/shard_map/ppermute | solution.py:122
  16.5 0.4 %copy.8 = f32[2,2,16,16,1]{4,3,2,0,1:T(8,128)S(1)} copy(f32[2,2,16,16,1]{3,2,1,4,0:T(8,128)S(1)} %pad_maximum_fusion.7) | data formatting | bytes 8192 | tf_op jit(solution)/shard_map/concatenate | solution.py:126
  17.0 0.2 slice.232
  17.3 0.3 fusion
  17.7 0.5 %fusion.26 = (f32[16,16,128]{2,1,0:T(8,128)S(1)}, f32[16,16,128]{2,1,0:T(8,128)S(1)}, f32[16,16,128]{2,1,0:T(8,128)S(1)}, f32[16,16,128]{2,1,0:T(8,128)S(1)}, f3...) fusion(f32[2]{0:T(128)S(1)} %and_select_fusion.1, ...), kind=kLoop, calls=%fused_computation.67 | loop fusion | flops 1998848 | bytes 3506184 | tf_op jit(solution)/shard_map/reduce_sum | solution.py:49
  18.3 0.1 fusion.44
  18.5 0.1 fusion.50
  18.6 0.1 fusion.47
  18.8 0.2 fusion.5
  19.0 0.1 fusion.16
  19.1 0.6 %slice.257 = f32[2,16,1,128]{3,2,1,0:T(1,128)} slice(f32[2,16,16,128]{3,2,1,0:T(8,128)S(1)} %get-tuple-element.52), slice={[0:2], [0:16], [15:16], [0:128]} | slice | bytes 32768 | tf_op jit(solution)/shard_map/slice | solution.py:86
  19.8 0.7 %fusion.74 = (f32[1,15,16,128]{3,2,1,0:T(8,128)S(1)}, f32[1,15,16,128]{3,2,1,0:T(8,128)}) fusion(f32[2,16,16,128]{3,2,1,0:T(8,128)S(1)} %get-tuple-element.54), kind=kLoop, calls=%fused_computation.180 | loop fusion | bytes 491520 | tf_op jit(solution)/shard_map/slice | solution.py:98
  20.4 0.6 %fusion.73 = (f32[1,1,16,128]{3,2,1,0:T(8,128)}, f32[1,1,16,128]{3,2,1,0:T(8,128)}) fusion(f32[2,16,16,128]{3,2,1,0:T(8,128)S(1)} %get-tuple-element.54), kind=kLoop, calls=%fused_computation.179 | loop fusion | bytes 32768 | tf_op jit(solution)/shard_map/slice | solution.py:98
  21.1 4.3 %collective-permute-start.5 = (f32[2,16,1,128]{3,2,1,0:T(1,128)}, f32[2,16,1,128]{3,2,1,0:T(1,128)}, u32[]{:S(2)}, u32[]{:S(2)}) collective-permute-start(f32[2,16,1,128]{3,2,1,0:T(1,128)} %slice.257), channel_id=1, source_target_pairs={{0,1},{1,2},{2,3},{4,5},{5,6},{6,7},{8,9},{9,10},{10,11},{12,13},{... | collective-permute-start | bytes 49160 | tf_op jit(solution)/shard_map/ppermute | solution.py:13
  25.4 6.5 %conditional.1 = (f32[2,16,16,1]{2,1,0,3:T(8,128)S(1)}) conditional(s32[]{:T(128)} %convert_element_type.3, () %tuple.14, (f32[2,16,16,128]{3,2,1,0:T(8,128)S(1)}) %tuple.21), branch_computations={%region_16.17_spmd, %region_17.18_spmd} | conditional | bytes 544816 | solution.py:87
  25.5 1.6 %copy.12 = f32[2,16,16,128]{2,1,0,3:T(8,128)S(1)} copy(f32[2,16,16,128]{3,2,1,0:T(8,128)S(1)} %get-tuple-element.18) | data formatting | bytes 524288 | tf_op jit(solution)/shard_map/jit(_where)/select_n | solution.py:82
  27.2 4.0 %collective-permute-start = (f32[4,128]{1,0:T(4,128)S(1)}, f32[4,128]{1,0:T(4,128)S(1)}, u32[]{:S(2)}, u32[]{:S(2)}) collective-permute-start(f32[4,128]{1,0:T(4,128)S(1)} %reshape.600), channel_id=1, source_target_pairs={{0,4},{4,8},{8,12},{1,5},{5,9},{9,13},{2,6},{6,10},{10,14},{3,7},{... | collective-permute-start | bytes 6152 | tf_op jit(solution)/shard_map/cond/branch_1_fun/ppermute | solution.py:13
  31.2 0.7 %collective-permute-done = f32[4,128]{1,0:T(4,128)S(1)} collective-permute-done((f32[4,128]{1,0:T(4,128)S(1)}, f32[4,128]{1,0:T(4,128)S(1)}, u32[]{:S(2)}, u32[]{:S(2)}) %collective-permute-start) | collective-permute-done | bytes 2080 | tf_op jit(solution)/shard_map/cond/branch_1_fun/ppermute | solution.py:13
  32.0 0.2 copy.11
  32.1 0.2 copy.10
  32.3 0.7 %fusion.75 = (f32[1,16,1,128]{3,2,1,0:T(1,128)S(1)}, f32[1,16,1,128]{3,2,1,0:T(1,128)S(1)}) fusion(f32[2,16,1,128]{3,2,1,0:T(1,128)} %collective-permute-done.5), kind=kLoop, calls=%fused_computation.181 | loop fusion | bytes 32768 | tf_op jit(solution)/shard_map/slice | solution.py:97
  33.0 1.8 %slice_subtract_fusion.1 = (f32[1,16,16,128]{3,2,1,0:T(8,128)}, f32[1,16,16,128]{3,2,1,0:T(8,128)}) fusion(f32[2,16,16,128]{3,2,1,0:T(8,128)S(1)} %get-tuple-element.54, f32[1,16,16,127]{3,2,1,0:T(8,128)S(1)} %slice_bitcast_fusion.1, f32[1,16,16,1]{3,2,1,0:T(8,128)S(1)} %copy.11, f32[1,16,15,128]{3,2,1,0:T(8,128)S(1)} %slice_bitcast_fusion, ...), kind=kLoop, calls=%fused_computation.75 | loop fusion | flops 589824 | bytes 1835024 | tf_op jit(solution)/shard_map/sub | solution.py:99
  (42 shorter events, 1.0 us)
Async XLA Ops:
  0.6 9.2 %copy-start = (f32[2]{0:T(128)S(1)}, f32[2]{0:T(128)}, u32[]{:S(2)}) copy-start(f32[2]{0:T(128)} %param.8) | copy-start | bytes 28
  0.6 16.3 %copy-start.1 = (f32[1,16,16,128]{3,2,1,0:T(8,128)S(1)}, f32[1,16,16,128]{3,2,1,0:T(8,128)}, u32[]{:S(2)}) copy-start(f32[1,16,16,128]{3,2,1,0:T(8,128)} %param.6) | copy-start | bytes 393220
  0.7 16.3 %copy-start.2 = (f32[1,16,16,128]{3,2,1,0:T(8,128)S(1)}, f32[1,16,16,128]{3,2,1,0:T(8,128)}, u32[]{:S(2)}) copy-start(f32[1,16,16,128]{3,2,1,0:T(8,128)} %param.7) | copy-start | bytes 393220
  1.6 9.1 %collective-permute-start.3 = (f32[1,2,16,1,128]{4,3,2,0,1:T(1,128)S(1)}, f32[1,2,16,1,128]{4,3,2,0,1:T(1,128)S(1)}, u32[]{:S(2)}, u32[]{:S(2)}) collective-permute-start(f32[1,2,16,1,128]{4,3,2,0,1:T(1,128)S(1)} %fusion.67), channel_id=1, source_target_pairs={{1,0},{2,1},{3,2},{5,4},{6,5},{7,6},{9,8},{10,9},{11,10},{13,12},{... | collective-permute-start | bytes 49160 | tf_op jit(solution)/shard_map/ppermute | solution.py:13
  4.7 5.9 %collective-permute-start.2 = (f32[4,128]{1,0:T(4,128)S(1)}, f32[4,128]{1,0:T(4,128)S(1)}, u32[]{:S(2)}, u32[]{:S(2)}) collective-permute-start(f32[4,128]{1,0:T(4,128)S(1)} %reshape.608), channel_id=1, source_target_pairs={{4,0},{8,4},{12,8},{5,1},{9,5},{13,9},{6,2},{10,6},{14,10},{7,3},{... | collective-permute-start | bytes 6152 | tf_op jit(solution)/shard_map/ppermute | solution.py:13
  7.0 9.9 %collective-permute-start.1 = (f32[1,2,16,16,128]{4,3,2,0,1:T(8,128)S(1)}, f32[1,2,16,16,128]{4,3,2,0,1:T(8,128)S(1)}, u32[]{:S(2)}, u32[]{:S(2)}) collective-permute-start(f32[1,2,16,16,128]{4,3,2,0,1:T(8,128)S(1)} %pad_maximum_fusion.5), channel_id=1, source_target_pairs={{0,16},{16,0},{1,17},{17,1},{2,18},{18,2},{3,19},{19,3},{4,20},{20... | collective-permute-start | bytes 786440 | tf_op jit(solution)/shard_map/ppermute | solution.py:121
  10.7 5.7 %collective-permute-start.4 = (f32[36,128]{1,0:T(8,128)S(1)}, f32[36,128]{1,0:T(8,128)S(1)}, u32[]{:S(2)}, u32[]{:S(2)}) collective-permute-start(f32[36,128]{1,0:T(8,128)S(1)} %maximum_bitcast_fusion), channel_id=1, source_target_pairs={{0,16},{16,0},{1,17},{17,1},{2,18},{18,2},{3,19},{19,3},{4,20},{20... | collective-permute-start | bytes 55304 | tf_op jit(solution)/shard_map/ppermute | solution.py:122
  21.1 11.3 %collective-permute-start.5 = (f32[2,16,1,128]{3,2,1,0:T(1,128)}, f32[2,16,1,128]{3,2,1,0:T(1,128)}, u32[]{:S(2)}, u32[]{:S(2)}) collective-permute-start(f32[2,16,1,128]{3,2,1,0:T(1,128)} %slice.257), channel_id=1, source_target_pairs={{0,1},{1,2},{2,3},{4,5},{5,6},{6,7},{8,9},{9,10},{10,11},{12,13},{... | collective-permute-start | bytes 49160 | tf_op jit(solution)/shard_map/ppermute | solution.py:13
  27.2 4.7 %collective-permute-start = (f32[4,128]{1,0:T(4,128)S(1)}, f32[4,128]{1,0:T(4,128)S(1)}, u32[]{:S(2)}, u32[]{:S(2)}) collective-permute-start(f32[4,128]{1,0:T(4,128)S(1)} %reshape.600), channel_id=1, source_target_pairs={{0,4},{4,8},{8,12},{1,5},{5,9},{9,13},{2,6},{6,10},{10,14},{3,7},{... | collective-permute-start | bytes 6152 | tf_op jit(solution)/shard_map/cond/branch_1_fun/ppermute | solution.py:13

commit v17 on v15

--- a/solution.py
+++ b/solution.py
@@ -88,8 +88,14 @@
 
     def adjoint_one(out):
         fx, fy, fz = flux_x[out], flux_y[out], flux_z[out]
-        res = jnp.concatenate([prev_x[out], fx[..., :-1]], -1) - fx
-        res = res + jnp.concatenate([prev_y[out], fy[..., :-1, :]], -2) - fy
+        lane = lax.broadcasted_iota(jnp.int32, (1, 1, fx.shape[-1]), 2)
+        row = lax.broadcasted_iota(jnp.int32, (1, fy.shape[-2], 1), 1)
+        left = jnp.pad(fx[..., :-1], ((0, 0), (0, 0), (1, 0)))
+        left = jnp.where(lane == 0, prev_x[out], left)
+        above = jnp.pad(fy[..., :-1, :], ((0, 0), (1, 0), (0, 0)))
+        above = jnp.where(row == 0, prev_y[out], above)
+        res = left - fx
+        res = res + above - fy
         below = jnp.where(levels == 0, 0.0, jnp.concatenate([fz[:1], fz[:-1]], 0))
         return (res + below - fz)[None]
 

time: 28.2 us -> 29 us (1.028)
  other arithmetic: 3.77 us -> 4.55 us
  waiting for transfers between devices: 2.59 us -> 2.92 us
    broadcast_in_dim x0 -> x2, other arithmetic: none -> 1.66 us  [adjoint_one(): return (res + below - fz)[None]]
    sub x1 -> x0, other arithmetic: 0.89 us -> none  [adjoint_one(): return (res + below - fz)[None]]
    concatenate x6 -> x0, local copies, waits for them, and re-layouts: 0.44 us -> none  [the longest x4 0.42 us: adjoint_one(): res = jnp.concatenate([prev_x[out], fx[..., :-1]], -1) - fx]
    ppermute x4, waiting for transfers between devices: 1.42 us -> 1.74 us  [passed_along(): return lax.ppermute(array, axis, pairs)]
  transfers between devices with their start and end apart: 6 -> 6, of which waited for: 3 -> 3; matrix products, arithmetic and copies ran while one was open for 9% -> 8% of each run, Pallas kernels for 0% -> 0%
where the time goes in v17:
time: 29 us; the launch traced here: 28.7 us
  starting transfers between devices  16.1 us (56%)
  other arithmetic  4.55 us (16%)
  local copies, waits for them, and re-layouts  3.49 us (12%)
  waiting for transfers between devices  2.92 us (10%)
  between operations  1.73 us (6%)
    ppermute x4, starting transfers between devices, passed_along(): return lax.ppermute(array, axis, pairs)  11.8 us
    ppermute x1, starting transfers between devices, shards(): tiles.append(lax.ppermute(own, 'mp', pairs))  2.78 us
    ppermute x4, waiting for transfers between devices, passed_along(): return lax.ppermute(array, axis, pairs)  1.74 us
    broadcast_in_dim x2, other arithmetic, adjoint_one(): return (res + below - fz)[None]  1.66 us
    ppermute x1, starting transfers between devices, shards(): theirs = lax.ppermute(rims, 'mp', pairs).reshape(-1)  1.46 us
    ppermute x1, waiting for transfers between devices, shards(): theirs = lax.ppermute(rims, 'mp', pairs).reshape(-1)  1.17 us
    another operation x2, other arithmetic, shards(): own = jnp.stack([models, direction], 1)  0.94 us
    unnamed x8, local copies, waits for them, and re-layouts  0.67 us
  transfers between devices with their start and end apart: 6, of which 3 were waited for; matrix products, arithmetic and copies ran while one was open for 8% of the time, Pallas kernels for 0%

profile of v17, /device:TPU:1, one launch (start us, length us, event | category | flops | bytes accessed | tf_op | source)
XLA Modules:
  0.0 28.7 jit_solution(754772349644571421)
XLA Ops:
  0.7 0.9 %fusion.67 = f32[1,2,16,1,128]{4,3,2,0,1:T(1,128)S(1)} fusion(f32[1,1,16,16,128]{4,3,2,0,1:T(8,128)} %bitcast.295, f32[1,1,16,16,128]{4,3,2,0,1:T(8,128)} %bitcast.300), kind=kLoop, calls=%fused_computation.156 | loop fusion | flops 4096 | bytes 278528 | tf_op jit(solution)/shard_map/stack | solution.py:114
  1.6 1.9 %collective-permute-start.2 = (f32[1,2,16,1,128]{4,3,2,0,1:T(1,128)S(1)}, f32[1,2,16,1,128]{4,3,2,0,1:T(1,128)S(1)}, u32[]{:S(2)}, u32[]{:S(2)}) collective-permute-start(f32[1,2,16,1,128]{4,3,2,0,1:T(1,128)S(1)} %fusion.67), channel_id=1, source_target_pairs={{1,0},{2,1},{3,2},{5,4},{6,5},{7,6},{9,8},{10,9},{11,10},{13,12},{... | collective-permute-start | bytes 49160 | tf_op jit(solution)/shard_map/ppermute | solution.py:13
  3.5 0.1 fusion.10
  3.7 0.1 reshape.562
  3.8 1.3 %collective-permute-start.1 = (f32[4,128]{1,0:T(4,128)S(1)}, f32[4,128]{1,0:T(4,128)S(1)}, u32[]{:S(2)}, u32[]{:S(2)}) collective-permute-start(f32[4,128]{1,0:T(4,128)S(1)} %reshape.562), channel_id=1, source_target_pairs={{4,0},{8,4},{12,8},{5,1},{9,5},{13,9},{6,2},{10,6},{14,10},{7,3},{... | collective-permute-start | bytes 6152 | tf_op jit(solution)/shard_map/ppermute | solution.py:13
  5.1 2.8 %collective-permute-start = (f32[1,2,16,16,128]{4,3,2,0,1:T(8,128)S(1)}, f32[1,2,16,16,128]{4,3,2,0,1:T(8,128)S(1)}, u32[]{:S(2)}, u32[]{:S(2)}) collective-permute-start(f32[1,2,16,16,128]{4,3,2,0,1:T(8,128)S(1)} %pad_maximum_fusion.5), channel_id=1, source_target_pairs={{0,16},{16,0},{1,17},{17,1},{2,18},{18,2},{3,19},{19,3},{4,20},{20... | collective-permute-start | bytes 786440 | tf_op jit(solution)/shard_map/ppermute | solution.py:122
  8.0 0.6 %gather_fusion = f32[2]{0:T(128)S(1)} fusion(f32[2]{0:T(128)S(1)} %copy-done, s32[1024]{0:T(1024)S(1)} %pad_clamp_fusion), kind=kCustom, calls=%fused_computation | custom fusion | bytes 24 | tf_op jit(solution)/shard_map/jit(_take)/gather | solution.py:111
  8.6 1.1 %collective-permute-done.1 = f32[4,128]{1,0:T(4,128)S(1)} collective-permute-done((f32[4,128]{1,0:T(4,128)S(1)}, f32[4,128]{1,0:T(4,128)S(1)}, u32[]{:S(2)}, u32[]{:S(2)}) %collective-permute-start.1) | collective-permute-done | bytes 2080 | tf_op jit(solution)/shard_map/ppermute | solution.py:13
  9.7 1.5 %collective-permute-start.3 = (f32[36,128]{1,0:T(8,128)S(1)}, f32[36,128]{1,0:T(8,128)S(1)}, u32[]{:S(2)}, u32[]{:S(2)}) collective-permute-start(f32[36,128]{1,0:T(8,128)S(1)} %maximum_bitcast_fusion), channel_id=1, source_target_pairs={{0,16},{16,0},{1,17},{17,1},{2,18},{18,2},{3,19},{19,3},{4,20},{20... | collective-permute-start | bytes 55304 | tf_op jit(solution)/shard_map/ppermute | solution.py:123
  11.3 0.6 %copy-done.3 = f32[2]{0:T(128)S(1)} copy-done((f32[2]{0:T(128)S(1)}, f32[2]{0:T(128)}, u32[]{:S(2)}) %copy-start.3) | copy-done | bytes 32
  12.0 0.6 %dynamic-slice.2 = f32[1]{0:T(128)} dynamic-slice(f32[2]{0:T(128)S(1)} %copy-done.3, s32[]{:T(128)} %bitcast), dynamic_slice_sizes={1} | dynamic-slice | bytes 12 | tf_op jit(solution)/shard_map/jit(_take)/gather | solution.py:113
  13.2 0.1 reshape.563
  13.3 1.2 %collective-permute-done.3 = f32[36,128]{1,0:T(8,128)S(1)} collective-permute-done((f32[36,128]{1,0:T(8,128)S(1)}, f32[36,128]{1,0:T(8,128)S(1)}, u32[]{:S(2)}, u32[]{:S(2)}) %collective-permute-start.3) | collective-permute-done | bytes 18464 | tf_op jit(solution)/shard_map/ppermute | solution.py:123
  14.5 0.1 reshape.566
  14.5 0.4 %copy.6 = f32[2,2,16,16,1]{4,3,2,0,1:T(8,128)S(1)} copy(f32[2,2,16,16,1]{3,2,1,4,0:T(8,128)S(1)} %pad_maximum_fusion.7) | data formatting | bytes 8192 | tf_op jit(solution)/shard_map/concatenate | solution.py:127
  15.1 0.2 slice.243
  15.4 0.3 %fusion = (f32[2,2,16,16,128]{4,3,2,0,1:T(8,128)S(1)}, f32[2,2,16,16,128]{4,3,2,0,1:T(8,128)S(1)}) fusion(f32[2,2,16,16,1]{4,3,2,0,1:T(8,128)S(1)} %copy.6, f32[2,2,16,16,127]{4,3,2,0,1:T(8,128)S(1)} %slice.243, pred[128]{0:T(512)(128)(4,1)S(1)} %compare_and_fusion, f32[1,2,16,16,128]{4,3,2,0,1:T(8,128)S(1)} %collective-permute-done, ...), kind=kLoop, calls=%fused_computation.7 | loop fusion | flops 1179648 | bytes 2621584 | tf_op jit(solution)/shard_map/jit(_where)/select_n | solution.py:33
  15.8 0.5 %fusion.26 = (f32[16,16,128]{2,1,0:T(8,128)S(1)}, f32[16,16,128]{2,1,0:T(8,128)S(1)}, f32[16,16,128]{2,1,0:T(8,128)S(1)}, f32[16,16,128]{2,1,0:T(8,128)S(1)}, f3...) fusion(f32[2]{0:T(128)S(1)} %and_select_fusion.1, ...), kind=kLoop, calls=%fused_computation.68 | loop fusion | flops 1998848 | bytes 3506184 | tf_op jit(solution)/shard_map/reduce_sum | solution.py:49
  16.4 0.1 fusion.44
  16.6 0.1 fusion.50
  16.7 0.1 fusion.47
  16.8 0.2 fusion.5
  17.0 0.1 fusion.19
  17.2 0.2 slice_reduce_fusion
  17.5 0.1 reshape.568
  17.6 4.5 %collective-permute-start.4 = (f32[4,128]{1,0:T(4,128)S(1)}, f32[4,128]{1,0:T(4,128)S(1)}, u32[]{:S(2)}, u32[]{:S(2)}) collective-permute-start(f32[4,128]{1,0:T(4,128)S(1)} %reshape.568), channel_id=1, source_target_pairs={{0,4},{4,8},{8,12},{1,5},{5,9},{9,13},{2,6},{6,10},{10,14},{3,7},{... | collective-permute-start | bytes 6152 | tf_op jit(solution)/shard_map/ppermute | solution.py:13
  22.1 4.1 %collective-permute-start.5 = (f32[2,16,1,128]{3,2,1,0:T(1,128)S(1)}, f32[2,16,1,128]{3,2,1,0:T(1,128)S(1)}, u32[]{:S(2)}, u32[]{:S(2)}) collective-permute-start(f32[2,16,1,128]{3,2,1,0:T(1,128)S(1)} %slice.268), channel_id=1, source_target_pairs={{0,1},{1,2},{2,3},{4,5},{5,6},{6,7},{8,9},{9,10},{10,11},{12,13},{... | collective-permute-start | bytes 49160 | tf_op jit(solution)/shard_map/ppermute | solution.py:13
  26.2 0.1 broadcast_in_dim.154
  26.3 0.1 broadcast_in_dim.164
  26.4 0.7 %collective-permute-done.5 = f32[2,16,1,128]{3,2,1,0:T(1,128)S(1)} collective-permute-done((f32[2,16,1,128]{3,2,1,0:T(1,128)S(1)}, f32[2,16,1,128]{3,2,1,0:T(1,128)S(1)}, u32[]{:S(2)}, u32[]{:S(2)}) %collective-permute-start.5) | collective-permute-done | bytes 16416 | tf_op jit(solution)/shard_map/ppermute | solution.py:13
  27.1 0.8 %fusion.34 = f32[1,16,16,128]{3,2,1,0:T(8,128)} fusion(f32[2,16,16,128]{3,2,1,0:T(8,128)S(1)} %get-tuple-element.45, f32[15,16,128]{2,1,0:T(8,128)S(1)} %get-tuple-element.62, f32[1,16,128]{2,1,0:T(8,128)S(1)} %get-tuple-element.60, f32[16,15,128]{2,1,0:T(8,128)S(1)} %bitcast.308, f32[16,16,127]{2,1,0:T(8,128)S(1)} %bitcast.307, f32[16,128]{1,0:T(8,128)S(1)} %bitcast.312, ...), kind=kLoop, calls=%fused_computation.83 | loop fusion | flops 294912 | bytes 935424 | tf_op jit(solution)/shard_map/broadcast_in_dim | solution.py:100
  27.9 0.8 %fusion.32 = f32[1,16,16,128]{3,2,1,0:T(8,128)} fusion(f32[2,16,16,128]{3,2,1,0:T(8,128)S(1)} %get-tuple-element.45, f32[15,16,128]{2,1,0:T(8,128)S(1)} %get-tuple-element.61, f32[1,16,128]{2,1,0:T(8,128)S(1)} %get-tuple-element.59, f32[16,15,128]{2,1,0:T(8,128)S(1)} %bitcast.306, f32[16,16,127]{2,1,0:T(8,128)S(1)} %bitcast.305, f32[16,128]{1,0:T(8,128)S(1)} %bitcast.311, ...), kind=kLoop, calls=%fused_computation.78 | loop fusion | flops 294912 | bytes 935424 | tf_op jit(solution)/shard_map/broadcast_in_dim | solution.py:100
  (39 shorter events, 0.6 us)
Async XLA Ops:
  0.6 7.3 %copy-start = (f32[2]{0:T(128)S(1)}, f32[2]{0:T(128)}, u32[]{:S(2)}) copy-start(f32[2]{0:T(128)} %param.6) | copy-start | bytes 28
  0.6 2.9 %copy-start.1 = (f32[1,16,16,128]{3,2,1,0:T(8,128)S(1)}, f32[1,16,16,128]{3,2,1,0:T(8,128)}, u32[]{:S(2)}) copy-start(f32[1,16,16,128]{3,2,1,0:T(8,128)} %param.4) | copy-start | bytes 393220
  0.7 2.9 %copy-start.2 = (f32[1,16,16,128]{3,2,1,0:T(8,128)S(1)}, f32[1,16,16,128]{3,2,1,0:T(8,128)}, u32[]{:S(2)}) copy-start(f32[1,16,16,128]{3,2,1,0:T(8,128)} %param.5) | copy-start | bytes 393220
  1.6 8.1 %collective-permute-start.2 = (f32[1,2,16,1,128]{4,3,2,0,1:T(1,128)S(1)}, f32[1,2,16,1,128]{4,3,2,0,1:T(1,128)S(1)}, u32[]{:S(2)}, u32[]{:S(2)}) collective-permute-start(f32[1,2,16,1,128]{4,3,2,0,1:T(1,128)S(1)} %fusion.67), channel_id=1, source_target_pairs={{1,0},{2,1},{3,2},{5,4},{6,5},{7,6},{9,8},{10,9},{11,10},{13,12},{... | collective-permute-start | bytes 49160 | tf_op jit(solution)/shard_map/ppermute | solution.py:13
  3.8 5.9 %collective-permute-start.1 = (f32[4,128]{1,0:T(4,128)S(1)}, f32[4,128]{1,0:T(4,128)S(1)}, u32[]{:S(2)}, u32[]{:S(2)}) collective-permute-start(f32[4,128]{1,0:T(4,128)S(1)} %reshape.562), channel_id=1, source_target_pairs={{4,0},{8,4},{12,8},{5,1},{9,5},{13,9},{6,2},{10,6},{14,10},{7,3},{... | collective-permute-start | bytes 6152 | tf_op jit(solution)/shard_map/ppermute | solution.py:13
  5.1 9.9 %collective-permute-start = (f32[1,2,16,16,128]{4,3,2,0,1:T(8,128)S(1)}, f32[1,2,16,16,128]{4,3,2,0,1:T(8,128)S(1)}, u32[]{:S(2)}, u32[]{:S(2)}) collective-permute-start(f32[1,2,16,16,128]{4,3,2,0,1:T(8,128)S(1)} %pad_maximum_fusion.5), channel_id=1, source_target_pairs={{0,16},{16,0},{1,17},{17,1},{2,18},{18,2},{3,19},{19,3},{4,20},{20... | collective-permute-start | bytes 786440 | tf_op jit(solution)/shard_map/ppermute | solution.py:122
  9.7 4.7 %collective-permute-start.3 = (f32[36,128]{1,0:T(8,128)S(1)}, f32[36,128]{1,0:T(8,128)S(1)}, u32[]{:S(2)}, u32[]{:S(2)}) collective-permute-start(f32[36,128]{1,0:T(8,128)S(1)} %maximum_bitcast_fusion), channel_id=1, source_target_pairs={{0,16},{16,0},{1,17},{17,1},{2,18},{18,2},{3,19},{19,3},{4,20},{20... | collective-permute-start | bytes 55304 | tf_op jit(solution)/shard_map/ppermute | solution.py:123
  11.3 0.7 %copy-start.3 = (f32[2]{0:T(128)S(1)}, f32[2]{0:T(128)}, u32[]{:S(2)}) copy-start(f32[2]{0:T(128)} %param.7) | copy-start | bytes 28
  17.6 8.7 %collective-permute-start.4 = (f32[4,128]{1,0:T(4,128)S(1)}, f32[4,128]{1,0:T(4,128)S(1)}, u32[]{:S(2)}, u32[]{:S(2)}) collective-permute-start(f32[4,128]{1,0:T(4,128)S(1)} %reshape.568), channel_id=1, source_target_pairs={{0,4},{4,8},{8,12},{1,5},{5,9},{9,13},{2,6},{6,10},{10,14},{3,7},{... | collective-permute-start | bytes 6152 | tf_op jit(solution)/shard_map/ppermute | solution.py:13
  22.1 5.0 %collective-permute-start.5 = (f32[2,16,1,128]{3,2,1,0:T(1,128)S(1)}, f32[2,16,1,128]{3,2,1,0:T(1,128)S(1)}, u32[]{:S(2)}, u32[]{:S(2)}) collective-permute-start(f32[2,16,1,128]{3,2,1,0:T(1,128)S(1)} %slice.268), channel_id=1, source_target_pairs={{0,1},{1,2},{2,3},{4,5},{5,6},{6,7},{8,9},{9,10},{10,11},{12,13},{... | collective-permute-start | bytes 49160 | tf_op jit(solution)/shard_map/ppermute | solution.py:13

commit v18 on v15

--- a/solution.py
+++ b/solution.py
@@ -102,9 +102,10 @@
     local = models.shape[0]
     order = (member - jnp.arange(mp)) % mp
     picks = (order[:, None] * local + jnp.arange(local)[None, :]).reshape(-1)
-    weights = jnp.take(coupling, picks)
+    values = jnp.take(jnp.concatenate([coupling, tv_weight]), jnp.append(picks, picks[0] + coupling.size))
+    weights = values[:-1]
     alpha = weights[0]
-    beta = jnp.take(tv_weight, picks[:1])[0]
+    beta = values[-1]
     own = jnp.stack([models, direction], 1)
     rim_x = passed_dense(own[..., :1], "tx", -1)
     rim_y = passed_along(own[..., :1, :], "ty", -1)

time: 28.2 us -> 29.4 us (1.043)
  other arithmetic: 3.77 us -> 5.23 us
  waiting for transfers between devices: 2.59 us -> 3.52 us
  between operations: 1.76 us -> 1 us
  starting transfers between devices: 16.1 us -> 15.7 us
    ppermute x1, waiting for transfers between devices: 1.17 us -> 3.18 us  [shards(): theirs = lax.ppermute(rims, 'mp', pairs).reshape(-1)]
    add x1, other arithmetic: 0.2 us -> 1.46 us  [model_split(): beta * grad_own / size + alpha * cross_q]
    ppermute x4, waiting for transfers between devices: 1.42 us -> 0.34 us  [passed_along(): return lax.ppermute(array, axis, pairs)]
    slice x0 -> x1, local copies, waits for them, and re-layouts: none -> 0.59 us  [shards(): beta = values[-1]]
    gather x2 -> x1, local copies, waits for them, and re-layouts: 1.22 us -> 0.64 us  [shards(): jnp.take(jnp.concatenate([coupling, tv_weight]), jnp.append(picks, picks[...]
    ppermute x1, starting transfers between devices: 1.46 us -> 1.06 us  [shards(): theirs = lax.ppermute(rims, 'mp', pairs).reshape(-1)]
  transfers between devices with their start and end apart: 6 -> 6, of which waited for: 3 -> 2; matrix products, arithmetic and copies ran while one was open for 9% -> 10% of each run, Pallas kernels for 0% -> 0%
where the time goes in v18:
time: 29.4 us; the launch traced here: 29.2 us
  starting transfers between devices  15.7 us (53%)
  other arithmetic  5.23 us (18%)
  local copies, waits for them, and re-layouts  3.78 us (13%)
  waiting for transfers between devices  3.52 us (12%)
  between operations  1 us (3%)
    ppermute x4, starting transfers between devices, passed_along(): return lax.ppermute(array, axis, pairs)  11.8 us
    ppermute x1, waiting for transfers between devices, shards(): theirs = lax.ppermute(rims, 'mp', pairs).reshape(-1)  3.18 us
    ppermute x1, starting transfers between devices, shards(): tiles.append(lax.ppermute(own, 'mp', pairs))  2.78 us
    add x1, other arithmetic, model_split(): beta * grad_own / size + alpha * cross_q  1.46 us
    ppermute x1, starting transfers between devices, shards(): theirs = lax.ppermute(rims, 'mp', pairs).reshape(-1)  1.06 us
    another operation x2, other arithmetic, shards(): own = jnp.stack([models, direction], 1)  0.94 us
    sub x1, other arithmetic, adjoint_one(): return (res + below - fz)[None]  0.88 us
    unnamed x8, local copies, waits for them, and re-layouts  0.67 us
  transfers between devices with their start and end apart: 6, of which 2 were waited for; matrix products, arithmetic and copies ran while one was open for 10% of the time, Pallas kernels for 0%

profile of v18, /device:TPU:1, one launch (start us, length us, event | category | flops | bytes accessed | tf_op | source)
XLA Modules:
  0.0 29.2 jit_solution(16340766157615292780)
XLA Ops:
  0.6 0.9 %fusion.67 = f32[1,2,16,1,128]{4,3,2,0,1:T(1,128)S(1)} fusion(f32[1,1,16,16,128]{4,3,2,0,1:T(8,128)} %bitcast.267, f32[1,1,16,16,128]{4,3,2,0,1:T(8,128)} %bitcast.272), kind=kLoop, calls=%fused_computation.160 | loop fusion | flops 4096 | bytes 278528 | tf_op jit(solution)/shard_map/stack | solution.py:109
  1.6 1.9 %collective-permute-start.2 = (f32[1,2,16,1,128]{4,3,2,0,1:T(1,128)S(1)}, f32[1,2,16,1,128]{4,3,2,0,1:T(1,128)S(1)}, u32[]{:S(2)}, u32[]{:S(2)}) collective-permute-start(f32[1,2,16,1,128]{4,3,2,0,1:T(1,128)S(1)} %fusion.67), channel_id=1, source_target_pairs={{1,0},{2,1},{3,2},{5,4},{6,5},{7,6},{9,8},{10,9},{11,10},{13,12},{... | collective-permute-start | bytes 49160 | tf_op jit(solution)/shard_map/ppermute | solution.py:13
  3.5 0.1 fusion.10
  3.7 0.1 reshape.618
  3.8 1.3 %collective-permute-start.1 = (f32[4,128]{1,0:T(4,128)S(1)}, f32[4,128]{1,0:T(4,128)S(1)}, u32[]{:S(2)}, u32[]{:S(2)}) collective-permute-start(f32[4,128]{1,0:T(4,128)S(1)} %reshape.618), channel_id=1, source_target_pairs={{4,0},{8,4},{12,8},{5,1},{9,5},{13,9},{6,2},{10,6},{14,10},{7,3},{... | collective-permute-start | bytes 6152 | tf_op jit(solution)/shard_map/ppermute | solution.py:13
  5.1 2.8 %collective-permute-start = (f32[1,2,16,16,128]{4,3,2,0,1:T(8,128)S(1)}, f32[1,2,16,16,128]{4,3,2,0,1:T(8,128)S(1)}, u32[]{:S(2)}, u32[]{:S(2)}) collective-permute-start(f32[1,2,16,16,128]{4,3,2,0,1:T(8,128)S(1)} %pad_maximum_fusion.5), channel_id=1, source_target_pairs={{0,16},{16,0},{1,17},{17,1},{2,18},{18,2},{3,19},{19,3},{4,20},{20... | collective-permute-start | bytes 786440 | tf_op jit(solution)/shard_map/ppermute | solution.py:117
  7.9 0.1 fusion.69
  8.0 0.6 %copy-done.2 = f32[2]{0:T(128)S(1)} copy-done((f32[2]{0:T(128)S(1)}, f32[2]{0:T(128)}, u32[]{:S(2)}) %copy-start.2) | copy-done | bytes 32
  8.8 0.6 %gather_fusion = f32[3]{0:T(128)S(1)} fusion(f32[4]{0:T(128)S(1)} %pad_maximum_fusion.8, s32[1024]{0:T(1024)S(1)} %pad_clamp_fusion), kind=kCustom, calls=%fused_computation | custom fusion | bytes 36 | tf_op jit(solution)/shard_map/jit(_take)/gather | solution.py:105
  9.4 0.1 and_select_fusion
  9.5 0.6 %fusion.77 = (f32[1]{0:T(128)}, f32[1]{0:T(128)}) fusion(f32[3]{0:T(128)S(1)} %and_select_fusion), kind=kLoop, calls=%fused_computation.182 | loop fusion | bytes 16 | tf_op jit(solution)/shard_map/slice | solution.py:108
  10.1 1.1 %collective-permute-start.3 = (f32[36,128]{1,0:T(8,128)S(1)}, f32[36,128]{1,0:T(8,128)S(1)}, u32[]{:S(2)}, u32[]{:S(2)}) collective-permute-start(f32[36,128]{1,0:T(8,128)S(1)} %maximum_bitcast_fusion), channel_id=1, source_target_pairs={{0,16},{16,0},{1,17},{17,1},{2,18},{18,2},{3,19},{19,3},{4,20},{20... | collective-permute-start | bytes 55304 | tf_op jit(solution)/shard_map/ppermute | solution.py:118
  11.2 0.1 reshape.619
  11.3 3.2 %collective-permute-done.3 = f32[36,128]{1,0:T(8,128)S(1)} collective-permute-done((f32[36,128]{1,0:T(8,128)S(1)}, f32[36,128]{1,0:T(8,128)S(1)}, u32[]{:S(2)}, u32[]{:S(2)}) %collective-permute-start.3) | collective-permute-done | bytes 18464 | tf_op jit(solution)/shard_map/ppermute | solution.py:118
  14.4 0.1 reshape.622
  14.5 0.4 %copy.6 = f32[2,2,16,16,1]{4,3,2,0,1:T(8,128)S(1)} copy(f32[2,2,16,16,1]{3,2,1,4,0:T(8,128)S(1)} %pad_maximum_fusion.7) | data formatting | bytes 8192 | tf_op jit(solution)/shard_map/concatenate | solution.py:122
  15.0 0.2 slice.235
  15.4 0.3 %fusion = (f32[2,2,16,16,128]{4,3,2,0,1:T(8,128)S(1)}, f32[2,2,16,16,128]{4,3,2,0,1:T(8,128)S(1)}) fusion(f32[2,2,16,16,1]{4,3,2,0,1:T(8,128)S(1)} %copy.6, f32[2,2,16,16,127]{4,3,2,0,1:T(8,128)S(1)} %slice.235, pred[128]{0:T(512)(128)(4,1)S(1)} %compare_and_fusion, f32[1,2,16,16,128]{4,3,2,0,1:T(8,128)S(1)} %collective-permute-done, ...), kind=kLoop, calls=%fused_computation.7 | loop fusion | flops 1179648 | bytes 2621584 | tf_op jit(solution)/shard_map/jit(_where)/select_n | solution.py:33
  15.8 0.5 %fusion.26 = (f32[16,16,128]{2,1,0:T(8,128)S(1)}, f32[16,16,128]{2,1,0:T(8,128)S(1)}, f32[16,16,128]{2,1,0:T(8,128)S(1)}, f32[16,16,128]{2,1,0:T(8,128)S(1)}, f3...) fusion(f32[2]{0:T(128)S(1)} %bitcast.279, ...), kind=kLoop, calls=%fused_computation.68 | loop fusion | flops 1998848 | bytes 3506184 | tf_op jit(solution)/shard_map/reduce_sum | solution.py:49
  16.4 0.1 fusion.44
  16.5 0.1 fusion.50
  16.7 0.1 fusion.47
  16.8 1.5 %fusion.5 = (f32[1,3,16,16,128]{4,3,2,0,1:T(8,128)S(1)}, f32[1,3,16,16,128]{4,3,2,0,1:T(8,128)S(1)}) fusion(f32[1,1,16,16,128]{4,3,2,0,1:T(8,128)S(1)} %get-tuple-element.26, f32[1,1,16,16,128]{4,3,2,0,1:T(8,128)S(1)} %get-tuple-element.24, f32[1,1,16,16,128]{4,3,2,0,1:T(8,128)S(1)} %get-tuple-element.20, f32[]{:T(128)} %bitcast.10, ...), kind=kLoop, calls=%fused_computation.23 | loop fusion | flops 1572864 | bytes 3276808 | tf_op jit(solution)/shard_map/add | solution.py:79
  18.3 0.1 fusion.16
  18.4 0.2 slice_reduce_fusion
  18.7 0.1 reshape.624
  18.8 4.5 %collective-permute-start.4 = (f32[4,128]{1,0:T(4,128)S(1)}, f32[4,128]{1,0:T(4,128)S(1)}, u32[]{:S(2)}, u32[]{:S(2)}) collective-permute-start(f32[4,128]{1,0:T(4,128)S(1)} %reshape.624), channel_id=1, source_target_pairs={{0,4},{4,8},{8,12},{1,5},{5,9},{9,13},{2,6},{6,10},{10,14},{3,7},{... | collective-permute-start | bytes 6152 | tf_op jit(solution)/shard_map/ppermute | solution.py:13
  23.3 4.1 %collective-permute-start.5 = (f32[2,16,1,128]{3,2,1,0:T(1,128)S(1)}, f32[2,16,1,128]{3,2,1,0:T(1,128)S(1)}, u32[]{:S(2)}, u32[]{:S(2)}) collective-permute-start(f32[2,16,1,128]{3,2,1,0:T(1,128)S(1)} %slice.260), channel_id=1, source_target_pairs={{0,1},{1,2},{2,3},{4,5},{5,6},{6,7},{8,9},{9,10},{10,11},{12,13},{... | collective-permute-start | bytes 49160 | tf_op jit(solution)/shard_map/ppermute | solution.py:13
  27.6 0.2 concatenate.142
  27.8 0.2 concatenate.141
  28.0 0.3 %collective-permute-done.5 = f32[2,16,1,128]{3,2,1,0:T(1,128)S(1)} collective-permute-done((f32[2,16,1,128]{3,2,1,0:T(1,128)S(1)}, f32[2,16,1,128]{3,2,1,0:T(1,128)S(1)}, u32[]{:S(2)}, u32[]{:S(2)}) %collective-permute-start.5) | collective-permute-done | bytes 16416 | tf_op jit(solution)/shard_map/ppermute | solution.py:13
  28.3 0.9 %slice_subtract_fusion.1 = (f32[1,16,16,128]{3,2,1,0:T(8,128)}, f32[1,16,16,128]{3,2,1,0:T(8,128)}) fusion(f32[2,16,16,128]{3,2,1,0:T(8,128)S(1)} %get-tuple-element.37, f32[1,16,16,127]{3,2,1,0:T(8,128)S(1)} %slice_bitcast_fusion.1, f32[1,16,16,1]{3,2,1,0:T(8,128)S(1)} %concatenate.142, f32[1,16,15,128]{3,2,1,0:T(8,128)S(1)} %slice_bitcast_fusion, ...), kind=kLoop, calls=%fused_computation.76 | loop fusion | flops 589824 | bytes 1835024 | tf_op jit(solution)/shard_map/sub | solution.py:94
  (43 shorter events, 0.7 us)
Async XLA Ops:
  0.6 2.9 %copy-start = (f32[1,16,16,128]{3,2,1,0:T(8,128)S(1)}, f32[1,16,16,128]{3,2,1,0:T(8,128)}, u32[]{:S(2)}) copy-start(f32[1,16,16,128]{3,2,1,0:T(8,128)} %param.4) | copy-start | bytes 393220
  0.6 2.9 %copy-start.1 = (f32[1,16,16,128]{3,2,1,0:T(8,128)S(1)}, f32[1,16,16,128]{3,2,1,0:T(8,128)}, u32[]{:S(2)}) copy-start(f32[1,16,16,128]{3,2,1,0:T(8,128)} %param.5) | copy-start | bytes 393220
  1.6 8.5 %collective-permute-start.2 = (f32[1,2,16,1,128]{4,3,2,0,1:T(1,128)S(1)}, f32[1,2,16,1,128]{4,3,2,0,1:T(1,128)S(1)}, u32[]{:S(2)}, u32[]{:S(2)}) collective-permute-start(f32[1,2,16,1,128]{4,3,2,0,1:T(1,128)S(1)} %fusion.67), channel_id=1, source_target_pairs={{1,0},{2,1},{3,2},{5,4},{6,5},{7,6},{9,8},{10,9},{11,10},{13,12},{... | collective-permute-start | bytes 49160 | tf_op jit(solution)/shard_map/ppermute | solution.py:13
  3.8 6.3 %collective-permute-start.1 = (f32[4,128]{1,0:T(4,128)S(1)}, f32[4,128]{1,0:T(4,128)S(1)}, u32[]{:S(2)}, u32[]{:S(2)}) collective-permute-start(f32[4,128]{1,0:T(4,128)S(1)} %reshape.618), channel_id=1, source_target_pairs={{4,0},{8,4},{12,8},{5,1},{9,5},{13,9},{6,2},{10,6},{14,10},{7,3},{... | collective-permute-start | bytes 6152 | tf_op jit(solution)/shard_map/ppermute | solution.py:13
  5.1 9.9 %collective-permute-start = (f32[1,2,16,16,128]{4,3,2,0,1:T(8,128)S(1)}, f32[1,2,16,16,128]{4,3,2,0,1:T(8,128)S(1)}, u32[]{:S(2)}, u32[]{:S(2)}) collective-permute-start(f32[1,2,16,16,128]{4,3,2,0,1:T(8,128)S(1)} %pad_maximum_fusion.5), channel_id=1, source_target_pairs={{0,16},{16,0},{1,17},{17,1},{2,18},{18,2},{3,19},{19,3},{4,20},{20... | collective-permute-start | bytes 786440 | tf_op jit(solution)/shard_map/ppermute | solution.py:117
  8.0 0.7 %copy-start.2 = (f32[2]{0:T(128)S(1)}, f32[2]{0:T(128)}, u32[]{:S(2)}) copy-start(f32[2]{0:T(128)} %param.7) | copy-start | bytes 28
  8.0 0.7 %copy-start.3 = (f32[2]{0:T(128)S(1)}, f32[2]{0:T(128)}, u32[]{:S(2)}) copy-start(f32[2]{0:T(128)} %param.6) | copy-start | bytes 28
  10.1 4.3 %collective-permute-start.3 = (f32[36,128]{1,0:T(8,128)S(1)}, f32[36,128]{1,0:T(8,128)S(1)}, u32[]{:S(2)}, u32[]{:S(2)}) collective-permute-start(f32[36,128]{1,0:T(8,128)S(1)} %maximum_bitcast_fusion), channel_id=1, source_target_pairs={{0,16},{16,0},{1,17},{17,1},{2,18},{18,2},{3,19},{19,3},{4,20},{20... | collective-permute-start | bytes 55304 | tf_op jit(solution)/shard_map/ppermute | solution.py:118
  18.8 8.7 %collective-permute-start.4 = (f32[4,128]{1,0:T(4,128)S(1)}, f32[4,128]{1,0:T(4,128)S(1)}, u32[]{:S(2)}, u32[]{:S(2)}) collective-permute-start(f32[4,128]{1,0:T(4,128)S(1)} %reshape.624), channel_id=1, source_target_pairs={{0,4},{4,8},{8,12},{1,5},{5,9},{9,13},{2,6},{6,10},{10,14},{3,7},{... | collective-permute-start | bytes 6152 | tf_op jit(solution)/shard_map/ppermute | solution.py:13
  23.3 5.0 %collective-permute-start.5 = (f32[2,16,1,128]{3,2,1,0:T(1,128)S(1)}, f32[2,16,1,128]{3,2,1,0:T(1,128)S(1)}, u32[]{:S(2)}, u32[]{:S(2)}) collective-permute-start(f32[2,16,1,128]{3,2,1,0:T(1,128)S(1)} %slice.260), channel_id=1, source_target_pairs={{0,1},{1,2},{2,3},{4,5},{5,6},{6,7},{8,9},{9,10},{10,11},{12,13},{... | collective-permute-start | bytes 49160 | tf_op jit(solution)/shard_map/ppermute | solution.py:13
